TPU v7x, 32 devices: a whole 2x2x4 slice. The times are simulated.
32 devices in a mesh: cases: 2 (over y), blk: 8 (over z, x), state: 2 (over core).
Axes of the slice: x: 2, y: 2, z: 4, core: 2. Of those that a mesh axis runs over, the one named last changes fastest.
Arguments:
- base_real: float32 [32768], P(('cases', 'blk', 'state')), parts along dimension 0, may hold values from -6 to 6
- base_reactive: float32 [32768], P(('cases', 'blk', 'state')), parts along dimension 0, may hold values from 0.2 to 1
- voltage: float32 [32768], P(('cases', 'blk', 'state')), parts along dimension 0, may hold values from 0.9 to 1.1
- rating: float32 [32768], P(('cases', 'blk', 'state')), parts along dimension 0, may hold values from 1 to 4
- monitored: int32 [16384], P(('cases', 'blk', 'state')), parts along dimension 0, may hold values from 0 to 2047, as said below
- tile_ids: int32 [128, 4], P(('cases', 'blk', 'state')), parts along dimension 0, may hold values from -1 to 7, as said below
- tile_values: bfloat16 [128, 4, 128, 128], P(('cases', 'blk', 'state')), parts along dimension 0, may hold values from -0.5 to 0.5
- outage_ids: int32 [16, 128], P(('cases', 'blk')), parts along dimension 0, may hold values from 0 to 2047, as said below
- coupling: bfloat16 [16, 128, 128], P(('cases', 'blk')), parts along dimension 0, may hold values from -0.5 to 0.5
- outage_pairs: int32 [16, 2, 128], P(('cases', 'blk')), parts along dimension 0, may hold values from 0 to 127, as said below
Outputs:
- branch_peak: float32 [16384], P(('cases', 'blk', 'state')), parts along dimension 0
- worst_loading: float32 [16, 128], P(('cases', 'blk'), 'state'), parts along dimension 0
There are 2 independent parts, one for each index of `cases`. A program takes and returns all parts, laid end to end along the dimension named above; each array names one. Nothing has to cross between parts.
Inputs may be any that keep to these rules, and one draw needn't show every extreme that they name: `monitored`: the 1024 entries of one cycle position (entry index // 1024) are distinct. `outage_ids`: each row holds 128 distinct indices. `tile_ids`: each row names between 2 and 4 distinct outage blocks in its first slots and holds -1 in the remaining slots; some row is full. `outage_pairs`: the two branches of a pair differ.
All inputs are finite; a program needn't handle non-finite values.
Results may differ from a plain program's by a relative error of at most 0.0019.
Values may be sent and summed in bfloat16 or wider, within the bound.
No kernel may reach another device: no remote copies, remote signals or barrier semaphores. Data moves between devices by JAX's collectives and lax.ppermute only.
A program may use at most 64 MiB of HBM per device.

v0:
```python
import jax
import jax.numpy as jnp
from jax import lax
from jax.sharding import PartitionSpec as P


def solve_pairs(flows_block, coupling_block, pair_block):
    first_idx = pair_block[0]
    second_idx = pair_block[1]
    flow_first = jnp.take(flows_block, first_idx).astype(jnp.float32)
    flow_second = jnp.take(flows_block, second_idx).astype(jnp.float32)
    s_first_second = coupling_block[first_idx, second_idx].astype(jnp.float32)
    s_second_first = coupling_block[second_idx, first_idx].astype(jnp.float32)
    determinant = 1.0 - s_first_second * s_second_first
    w_first = (flow_first + s_first_second * flow_second) / determinant
    w_second = (flow_second + s_second_first * flow_first) / determinant
    return (w_first, w_second)


def body(
    base_real,
    base_reactive,
    voltage,
    rating,
    monitored,
    tile_ids,
    tile_values,
    outage_ids,
    coupling,
    outage_pairs,
):
    real_pos, reactive_pos, volt_pos, rating_pos = (
        lax.all_gather(base_real, "state", axis=0, tiled=True),
        lax.all_gather(base_reactive, "state", axis=0, tiled=True),
        lax.all_gather(voltage, "state", axis=0, tiled=True),
        lax.all_gather(rating, "state", axis=0, tiled=True),
    )
    tiles_dev = tile_ids.shape[0]
    slot_count = tile_ids.shape[1]
    tile_size = tile_values.shape[2]
    pair_count = outage_pairs.shape[2]
    blocks = lax.axis_size("blk")
    halves = lax.axis_size("state")
    half_width = pair_count // halves
    mon_real = jnp.take(real_pos, monitored).reshape(tiles_dev, tile_size)
    mon_reactive = jnp.take(reactive_pos, monitored).reshape(tiles_dev, tile_size)
    mon_limit = (jnp.take(volt_pos, monitored) * jnp.take(rating_pos, monitored)).reshape(
        tiles_dev, tile_size
    )
    react_sq = mon_reactive * mon_reactive
    matches = tile_ids[:, :, None] == jnp.arange(blocks, dtype=jnp.int32)[None, None, :]
    slot_table = jnp.sum(
        jnp.where(matches, jnp.arange(slot_count, dtype=jnp.int32)[None, :, None], 0), axis=1
    )
    present = jnp.any(matches, axis=1)
    outage_flow = jnp.take(real_pos, outage_ids).astype(jnp.bfloat16)
    rows_iota = lax.broadcasted_iota(jnp.int32, (tile_size, pair_count), 0)
    tile_rows = jnp.arange(tiles_dev, dtype=jnp.int32)

    def absorb(running, w_first, w_second, pair_block, block_now):
        weights = (
            jnp.where(rows_iota == pair_block[0][None, :], w_first[None, :], 0.0)
            + jnp.where(rows_iota == pair_block[1][None, :], w_second[None, :], 0.0)
        ).astype(jnp.bfloat16)
        slots = lax.dynamic_index_in_dim(slot_table, block_now, 1, keepdims=False)
        has_tile = lax.dynamic_index_in_dim(present, block_now, 1, keepdims=False)
        chosen = tile_values[tile_rows, slots]
        delta = jnp.einsum("tmi,ip->tmp", chosen, weights, preferred_element_type=jnp.float32)
        delta = jnp.where(has_tile[:, None, None], delta, 0.0)
        post = mon_real[:, :, None] + delta
        loading = jnp.sqrt(post * post + react_sq[:, :, None]) / mon_limit[:, :, None]
        peak_load = jnp.maximum(running[0], jnp.max(loading, axis=2))
        block_max = jnp.max(loading, axis=(0, 1))
        worst_load = lax.dynamic_update_slice(
            running[1], block_max[None, :], (block_now, jnp.int32(0))
        )
        return (peak_load, worst_load)

    initial = (
        jnp.zeros((tiles_dev, tile_size), jnp.float32),
        jnp.zeros((blocks, pair_count), jnp.float32),
    )
    own_first, own_second = solve_pairs(outage_flow[0], coupling[0], outage_pairs[0])
    own_weights = jnp.stack([own_first, own_second])[None]
    weight_shard = lax.all_gather(own_weights, "blk", axis=0, tiled=True)
    pair_shard = lax.all_gather(outage_pairs, "blk", axis=0, tiled=True)

    def one_block(position, carried):
        return absorb(
            carried,
            weight_shard[position, 0],
            weight_shard[position, 1],
            pair_shard[position],
            position,
        )

    peak_load, worst_load = lax.fori_loop(0, weight_shard.shape[0], one_block, initial)
    total_max = lax.pmax(worst_load, ("blk", "state"))
    worst_own = lax.dynamic_slice(
        total_max, (lax.axis_index("blk"), lax.axis_index("state") * half_width), (1, half_width)
    )
    return (peak_load.reshape(-1), worst_own)


def solution(mesh):
    return jax.shard_map(
        body,
        mesh=mesh,
        in_specs=(
            P(("cases", "blk", "state")),
            P(("cases", "blk", "state")),
            P(("cases", "blk", "state")),
            P(("cases", "blk", "state")),
            P(("cases", "blk", "state")),
            P(("cases", "blk", "state"), None),
            P(("cases", "blk", "state"), None, None, None),
            P(("cases", "blk"), None),
            P(("cases", "blk"), None, None),
            P(("cases", "blk"), None, None),
        ),
        out_specs=(P(("cases", "blk", "state")), P(("cases", "blk"), "state")),
        check_vma=False,
    )
```

profile of v0, /device:TPU:0, one launch (start us, length us, event | category | flops | bytes accessed | tf_op | source)
XLA Modules:
  0.0 117.3 jit_solution(10796585060166182035)
XLA Ops:
  2.1 2.1 %all_gather.18 = f32[2048]{0:T(1024)S(1)} all-gather(f32[1024]{0:T(1024)S(1)} %copy-done.5), channel_id=1, replica_groups=mesh['cases'=2,'blk'=8,'state'=2] {'state'}, dimensions={0}, use_global_device_ids=true | all-gather | bytes 12288 | tf_op jit(solution)/shard_map/all_gather | solution.py:33
  5.4 1.2 %gather_fusion.5 = bf16[128]{0:T(256)(128)(2,1)S(1)} fusion(bf16[128]{0:T(256)(128)(2,1)S(1)} %convert_bitcast_fusion, s32[1024]{0:T(1024)S(1)} %get-tuple-element.344), kind=kCustom, calls=%fused_computation.clone | custom fusion | bytes 1024 | tf_op jit(solution)/shard_map/jit(_take)/gather | solution.py:10
  6.6 1.2 %gather_fusion.6 = bf16[128]{0:T(256)(128)(2,1)S(1)} fusion(bf16[128]{0:T(256)(128)(2,1)S(1)} %convert_bitcast_fusion, s32[1024]{0:T(1024)S(1)} %get-tuple-element.343), kind=kCustom, calls=%fused_computation.3.clone | custom fusion | bytes 1024 | tf_op jit(solution)/shard_map/jit(_take)/gather | solution.py:11
  7.9 1.5 %gather_fusion.2 = bf16[128]{0:T(256)(128)(2,1)S(1)} fusion(bf16[128,128]{1,0:T(8,128)(2,1)S(1)} %bitcast.84, s32[128]{0:T(128)S(1)} %get-tuple-element.339), kind=kCustom, calls=%fused_computation.8 | custom fusion | bytes 1536 | tf_op jit(solution)/shard_map/gather | solution.py:12
  9.4 1.5 %gather_fusion.3 = bf16[128]{0:T(256)(128)(2,1)S(1)} fusion(bf16[128,128]{1,0:T(8,128)(2,1)S(1)} %bitcast.85, s32[128]{0:T(128)S(1)} %get-tuple-element.340), kind=kCustom, calls=%fused_computation.9 | custom fusion | bytes 1536 | tf_op jit(solution)/shard_map/gather | solution.py:13
  11.0 22.2 %all-gather.1 = f32[8,2,128]{2,1,0:T(2,128)S(1)} all-gather(f32[1,2,128]{2,1,0:T(2,128)S(1)} %maximum_bitcast_fusion), channel_id=2, replica_groups=mesh['cases'=2,'blk'=8,'state'=2] {'blk'}, dimensions={0}, use_global_device_ids=true | all-gather | bytes 9216 | tf_op jit(solution)/shard_map/all_gather | solution.py:85
  33.8 1.8 %all_gather.22 = f32[2048]{0:T(1024)S(1)} all-gather(f32[1024]{0:T(1024)S(1)} %copy-done.6), channel_id=1, replica_groups=mesh['cases'=2,'blk'=8,'state'=2] {'state'}, dimensions={0}, use_global_device_ids=true | all-gather | bytes 12288 | tf_op jit(solution)/shard_map/all_gather | solution.py:35
  35.6 3.1 %gather_fusion.8 = f32[512]{0:T(512)S(1)} fusion(f32[2048]{0:T(1024)S(1)} %all_gather.22, s32[1024]{0:T(1024)S(1)} %pad_clamp_fusion.3), kind=kCustom, calls=%fused_computation.5.clone | custom fusion | bytes 6144 | tf_op jit(solution)/shard_map/jit(_take)/gather | solution.py:47
  38.8 1.8 %all_gather.23 = f32[2048]{0:T(1024)S(1)} all-gather(f32[1024]{0:T(1024)S(1)} %copy-done.7), channel_id=1, replica_groups=mesh['cases'=2,'blk'=8,'state'=2] {'state'}, dimensions={0}, use_global_device_ids=true | all-gather | bytes 12288 | tf_op jit(solution)/shard_map/all_gather | solution.py:36
  40.6 3.1 %gather_fusion.9 = f32[512]{0:T(512)S(1)} fusion(f32[2048]{0:T(1024)S(1)} %all_gather.23, s32[1024]{0:T(1024)S(1)} %pad_clamp_fusion.3), kind=kCustom, calls=%fused_computation.6.clone | custom fusion | bytes 6144 | tf_op jit(solution)/shard_map/jit(_take)/gather | solution.py:47
  43.8 3.1 %gather_fusion.4 = f32[512]{0:T(512)S(1)} fusion(f32[2048]{0:T(1024)S(1)} %all_gather.18, s32[1024]{0:T(1024)S(1)} %pad_clamp_fusion.3), kind=kCustom, calls=%fused_computation.1.clone | custom fusion | bytes 6144 | tf_op jit(solution)/shard_map/jit(_take)/gather | solution.py:45
  46.9 1.8 %all_gather.21 = f32[2048]{0:T(1024)S(1)} all-gather(f32[1024]{0:T(1024)S(1)} %copy-done.8), channel_id=1, replica_groups=mesh['cases'=2,'blk'=8,'state'=2] {'state'}, dimensions={0}, use_global_device_ids=true | all-gather | bytes 12288 | tf_op jit(solution)/shard_map/all_gather | solution.py:34
  48.7 3.1 %gather_fusion.7 = f32[512]{0:T(512)S(1)} fusion(f32[2048]{0:T(1024)S(1)} %all_gather.21, s32[1024]{0:T(1024)S(1)} %pad_clamp_fusion.3), kind=kCustom, calls=%fused_computation.4.clone | custom fusion | bytes 6144 | tf_op jit(solution)/shard_map/jit(_take)/gather | solution.py:46
  51.9 16.3 %all_gather.19 = s32[8,2,128]{2,1,0:T(2,128)S(1)} all-gather(s32[1,2,128]{2,1,0:T(2,128)S(1)} %copy-done.2), channel_id=1, replica_groups=mesh['cases'=2,'blk'=8,'state'=2] {'blk'}, dimensions={0}, use_global_device_ids=true | all-gather | bytes 9216 | tf_op jit(solution)/shard_map/all_gather | solution.py:86
  68.5 18.8 %while.17 = (s32[]{:T(128)}, f32[4,128]{1,0:T(4,128)S(1)}, f32[8,128]{1,0:T(8,128)S(1)}, f32[512]{0:T(512)S(1)}, pred[4,8]{1,0:T(4,128)(4,1)S(1)}, /*index=5*/s3...) while((s32[]{:T(128)}, f32[4,128]{1,0:T(4,128)S(1)}, ...), condition=%wide.region_5.8_spmd.clone.clone, body=%wide.region_2.7_spmd.clone.clone.sunk | while | flops 17334688 | bytes 417519 | solution.py:97
  68.5 1.6 %gather_fusion = bf16[4,128,128]{2,1,0:T(8,128)(2,1)S(1)} fusion(bf16[4,4,128,128]{3,2,1,0:T(8,128)(2,1)} %get-tuple-element.456, s32[4]{0:T(128)S(1)} %fusion.36), kind=kCustom, calls=%fused_computation.2.clone.clone.1 | custom fusion | bytes 262176 | tf_op jit(solution)/shard_map/while/body/eval_jaxpr/gather | solution.py:67
  70.8 1.6 %gather_fusion = bf16[4,128,128]{2,1,0:T(8,128)(2,1)S(1)} fusion(bf16[4,4,128,128]{3,2,1,0:T(8,128)(2,1)} %get-tuple-element.456, s32[4]{0:T(128)S(1)} %fusion.36), kind=kCustom, calls=%fused_computation.2.clone.clone.1 | custom fusion | bytes 262176 | tf_op jit(solution)/shard_map/while/body/eval_jaxpr/gather | solution.py:67
  73.2 1.6 %gather_fusion = bf16[4,128,128]{2,1,0:T(8,128)(2,1)S(1)} fusion(bf16[4,4,128,128]{3,2,1,0:T(8,128)(2,1)} %get-tuple-element.456, s32[4]{0:T(128)S(1)} %fusion.36), kind=kCustom, calls=%fused_computation.2.clone.clone.1 | custom fusion | bytes 262176 | tf_op jit(solution)/shard_map/while/body/eval_jaxpr/gather | solution.py:67
  75.5 1.6 %gather_fusion = bf16[4,128,128]{2,1,0:T(8,128)(2,1)S(1)} fusion(bf16[4,4,128,128]{3,2,1,0:T(8,128)(2,1)} %get-tuple-element.456, s32[4]{0:T(128)S(1)} %fusion.36), kind=kCustom, calls=%fused_computation.2.clone.clone.1 | custom fusion | bytes 262176 | tf_op jit(solution)/shard_map/while/body/eval_jaxpr/gather | solution.py:67
  77.9 1.6 %gather_fusion = bf16[4,128,128]{2,1,0:T(8,128)(2,1)S(1)} fusion(bf16[4,4,128,128]{3,2,1,0:T(8,128)(2,1)} %get-tuple-element.456, s32[4]{0:T(128)S(1)} %fusion.36), kind=kCustom, calls=%fused_computation.2.clone.clone.1 | custom fusion | bytes 262176 | tf_op jit(solution)/shard_map/while/body/eval_jaxpr/gather | solution.py:67
  80.2 1.6 %gather_fusion = bf16[4,128,128]{2,1,0:T(8,128)(2,1)S(1)} fusion(bf16[4,4,128,128]{3,2,1,0:T(8,128)(2,1)} %get-tuple-element.456, s32[4]{0:T(128)S(1)} %fusion.36), kind=kCustom, calls=%fused_computation.2.clone.clone.1 | custom fusion | bytes 262176 | tf_op jit(solution)/shard_map/while/body/eval_jaxpr/gather | solution.py:67
  82.6 1.6 %gather_fusion = bf16[4,128,128]{2,1,0:T(8,128)(2,1)S(1)} fusion(bf16[4,4,128,128]{3,2,1,0:T(8,128)(2,1)} %get-tuple-element.456, s32[4]{0:T(128)S(1)} %fusion.36), kind=kCustom, calls=%fused_computation.2.clone.clone.1 | custom fusion | bytes 262176 | tf_op jit(solution)/shard_map/while/body/eval_jaxpr/gather | solution.py:67
  84.9 1.6 %gather_fusion = bf16[4,128,128]{2,1,0:T(8,128)(2,1)S(1)} fusion(bf16[4,4,128,128]{3,2,1,0:T(8,128)(2,1)} %get-tuple-element.456, s32[4]{0:T(128)S(1)} %fusion.36), kind=kCustom, calls=%fused_computation.2.clone.clone.1 | custom fusion | bytes 262176 | tf_op jit(solution)/shard_map/while/body/eval_jaxpr/gather | solution.py:67
  87.3 29.5 %pmax.7 = f32[8,128]{1,0:T(8,128)S(1)} all-reduce(f32[8,128]{1,0:T(8,128)S(1)} %get-tuple-element.223), channel_id=1, replica_groups=mesh['cases'=2,'blk'=8,'state'=2] {'blk','state'}, use_global_device_ids=true, to_apply=%region_6.9 | all-reduce | flops 1024 | bytes 8192 | tf_op jit(solution)/shard_map/pmax | solution.py:98
  (111 shorter events, 9.6 us)
Async XLA Ops:
  0.6 7.3 %copy-start = (bf16[1,128,128]{2,1,0:T(8,128)(2,1)S(1)}, bf16[1,128,128]{2,1,0:T(8,128)(2,1)}, u32[]{:S(2)}) copy-start(bf16[1,128,128]{2,1,0:T(8,128)(2,1)} %param.24) | copy-start | bytes 98308
  1.4 0.7 copy-start.5
  2.1 2.1 %copy-start.9 = (s32[1,128]{1,0:T(1,128)S(1)}, s32[1,128]{1,0:T(1,128)}, u32[]{:S(2)}) copy-start(s32[1,128]{1,0:T(1,128)} %param.23) | copy-start | bytes 1540
  6.6 1.3 %copy-start.2 = (s32[1,2,128]{2,1,0:T(2,128)S(1)}, s32[1,2,128]{2,1,0:T(2,128)}, u32[]{:S(2)}) copy-start(s32[1,2,128]{2,1,0:T(2,128)} %param.25) | copy-start | bytes 3076
  10.9 22.2 %copy-start.3 = (s32[512]{0:T(512)S(1)}, s32[512]{0:T(512)}, u32[]{:S(2)}) copy-start(s32[512]{0:T(512)} %param.20) | copy-start | bytes 6148
  33.1 0.7 copy-start.6
  35.6 3.2 %copy-start.7 = (f32[1024]{0:T(1024)S(1)}, f32[1024]{0:T(1024)}, u32[]{:S(2)}) copy-start(f32[1024]{0:T(1024)} %param.19) | copy-start | bytes 12292
  43.8 3.2 %copy-start.8 = (f32[1024]{0:T(1024)S(1)}, f32[1024]{0:T(1024)}, u32[]{:S(2)}) copy-start(f32[1024]{0:T(1024)} %param.17) | copy-start | bytes 12292
  51.9 16.3 %copy-start.4 = (s32[4,4]{1,0:T(4,128)S(1)}, s32[4,4]{1,0:T(4,128)}, u32[]{:S(2)}) copy-start(s32[4,4]{1,0:T(4,128)} %param.21) | copy-start | bytes 196
  87.2 29.5 %copy-start.1 = (f32[4,128]{1,0:T(4,128)}, f32[4,128]{1,0:T(4,128)S(1)}, u32[]{:S(2)}) copy-start(f32[4,128]{1,0:T(4,128)S(1)} %get-tuple-element.222) | copy-start | bytes 6148
where the time goes:
time: 118 us; the launch traced here: 117 us
  blocking collectives  75.5 us (64%)
  local copies, waits for them, and re-layouts  36.2 us (31%)
  matrix products  3.15 us (3%)
  other arithmetic  1.22 us (1%)
    pmax x1, blocking collectives, body(): total_max = lax.pmax(worst_load, ('blk', 'state'))  29.5 us
    all_gather x1, blocking collectives, body(): weight_shard = lax.all_gather(own_weights, 'blk', axis=0, tiled=True)  22.2 us
    all_gather x1, blocking collectives, body(): pair_shard = lax.all_gather(outage_pairs, 'blk', axis=0, tiled=True)  16.3 us
    gather x8, local copies, waits for them, and re-layouts, absorb(): chosen = tile_values[tile_rows, slots]  12.9 us
    dot_general x8, matrix products, absorb(): jnp.einsum('tmi,ip->tmp', chosen, weights, preferred_element_type=jnp.flo...  3.15 us
    gather x1, local copies, waits for them, and re-layouts, body(): jnp.take(volt_pos, monitored) * jnp.take(rating_pos, monitored)  3.14 us
    gather x1, local copies, waits for them, and re-layouts, body(): mon_real = jnp.take(real_pos, monitored).reshape(tiles_dev, tile_size)  3.14 us
    gather x1, local copies, waits for them, and re-layouts, body(): jnp.take(rating_pos, monitored)  3.14 us

commit v1 on v0

v1 whole, which is shorter than its diff:
```python
import jax
import jax.numpy as jnp
from jax import lax
from jax.sharding import PartitionSpec as P


def gather_shifts(x, axis):
    n = lax.axis_size(axis)
    parts = [x]
    for k in range(1, n):
        perm = [(j, (j + k) % n) for j in range(n)]
        parts.append(lax.ppermute(x, axis, perm))
    return jnp.stack(parts)


def gather_ordered(x, axis):
    n = lax.axis_size(axis)
    me = lax.axis_index(axis)
    stacked = gather_shifts(x, axis)
    return jnp.take(stacked, (me - jnp.arange(n)) % n, axis=0)


def scatter_max(x, axis):
    n = lax.axis_size(axis)
    me = lax.axis_index(axis)
    result = lax.dynamic_index_in_dim(x, me, 0, keepdims=False)
    for k in range(1, n):
        perm = [(j, (j + k) % n) for j in range(n)]
        piece = lax.dynamic_index_in_dim(x, (me + k) % n, 0, keepdims=False)
        result = jnp.maximum(result, lax.ppermute(piece, axis, perm))
    return result


def solve_pairs(flows_block, coupling_block, pair_block):
    first_idx = pair_block[0]
    second_idx = pair_block[1]
    flow_first = jnp.take(flows_block, first_idx).astype(jnp.float32)
    flow_second = jnp.take(flows_block, second_idx).astype(jnp.float32)
    s_first_second = coupling_block[first_idx, second_idx].astype(jnp.float32)
    s_second_first = coupling_block[second_idx, first_idx].astype(jnp.float32)
    determinant = 1.0 - s_first_second * s_second_first
    w_first = (flow_first + s_first_second * flow_second) / determinant
    w_second = (flow_second + s_second_first * flow_first) / determinant
    return (w_first, w_second)


def body(
    base_real,
    base_reactive,
    voltage,
    rating,
    monitored,
    tile_ids,
    tile_values,
    outage_ids,
    coupling,
    outage_pairs,
):
    tiles_dev, slot_count, tile_size, _ = tile_values.shape
    pair_count = outage_pairs.shape[2]
    blocks = lax.axis_size("blk")
    halves = lax.axis_size("state")
    half_width = pair_count // halves
    me_blk = lax.axis_index("blk")

    state_local = jnp.stack([base_real, base_reactive, voltage, rating])
    state_pos = gather_ordered(state_local, "state")
    state_pos = jnp.moveaxis(state_pos, 0, 1).reshape(4, -1)
    real_pos = state_pos[0]

    outage_flow = jnp.take(real_pos, outage_ids[0]).astype(jnp.bfloat16)
    own_first, own_second = solve_pairs(outage_flow, coupling[0], outage_pairs[0])
    packed = jnp.stack(
        [
            own_first,
            own_second,
            outage_pairs[0, 0].astype(jnp.float32),
            outage_pairs[0, 1].astype(jnp.float32),
        ]
    )
    shifted = gather_shifts(packed, "blk")

    mon_vals = jnp.take(state_pos, monitored, axis=1).reshape(4, tiles_dev, tile_size)
    mon_real = mon_vals[0]
    react_sq = mon_vals[1] * mon_vals[1]
    mon_limit = mon_vals[2] * mon_vals[3]

    valid = tile_ids >= 0
    block_of = jnp.clip(tile_ids, 0, blocks - 1)
    chosen = jnp.take(shifted, (me_blk - block_of) % blocks, axis=0)
    rows_iota = lax.broadcasted_iota(jnp.int32, (1, 1, tile_size, pair_count), 2)
    first_at = chosen[:, :, 2].astype(jnp.int32)[:, :, None, :]
    second_at = chosen[:, :, 3].astype(jnp.int32)[:, :, None, :]
    w_first = chosen[:, :, 0].astype(jnp.bfloat16)[:, :, None, :]
    w_second = chosen[:, :, 1].astype(jnp.bfloat16)[:, :, None, :]
    zero = jnp.zeros((), jnp.bfloat16)
    weights = jnp.where(rows_iota == first_at, w_first, zero) + jnp.where(
        rows_iota == second_at, w_second, zero
    )
    delta = jnp.einsum(
        "tkmi,tkip->tkmp", tile_values, weights, preferred_element_type=jnp.float32
    )
    post = mon_real[:, None, :, None] + delta
    loading = jnp.sqrt(post * post + react_sq[:, None, :, None]) / mon_limit[:, None, :, None]
    neg = jnp.float32(-jnp.inf)
    loading = jnp.where(valid[:, :, None, None], loading, neg)

    base_load = jnp.sqrt(mon_real * mon_real + react_sq) / mon_limit
    block_iota = jnp.arange(blocks, dtype=jnp.int32)
    matches = tile_ids[:, :, None] == block_iota[None, None, :]
    absent = jnp.logical_not(jnp.any(matches, axis=1))
    any_absent = jnp.any(absent, axis=1)

    peak_load = jnp.max(loading, axis=(1, 3))
    peak_load = jnp.maximum(peak_load, jnp.where(any_absent[:, None], base_load, neg))

    col_max = jnp.max(loading, axis=2)
    worst_local = jnp.max(
        jnp.where(matches[:, :, :, None], col_max[:, :, None, :], neg), axis=(0, 1)
    )
    base_max = jnp.max(base_load, axis=1)
    absent_max = jnp.max(jnp.where(absent, base_max[:, None], neg), axis=0)
    worst_local = jnp.maximum(worst_local, absent_max[:, None])

    by_half = worst_local.reshape(blocks, halves, half_width).transpose(1, 0, 2)
    half_max = scatter_max(by_half, "state")
    worst_own = scatter_max(half_max, "blk")[None, :]
    return (peak_load.reshape(-1), worst_own)


def solution(mesh):
    return jax.shard_map(
        body,
        mesh=mesh,
        in_specs=(
            P(("cases", "blk", "state")),
            P(("cases", "blk", "state")),
            P(("cases", "blk", "state")),
            P(("cases", "blk", "state")),
            P(("cases", "blk", "state")),
            P(("cases", "blk", "state"), None),
            P(("cases", "blk", "state"), None, None, None),
            P(("cases", "blk"), None),
            P(("cases", "blk"), None, None),
            P(("cases", "blk"), None, None),
        ),
        out_specs=(P(("cases", "blk", "state")), P(("cases", "blk"), "state")),
        check_vma=False,
    )
```

time: 118 us -> 52.8 us (0.45)
  blocking collectives: 75.5 us -> 0 us
  starting transfers between devices: 0 us -> 24.3 us
  local copies, waits for them, and re-layouts: 36.2 us -> 13 us
  waiting for transfers between devices: 0 us -> 8.34 us
  other arithmetic: 1.22 us -> 3.6 us
    all_gather x6 -> x0, blocking collectives: 46 us -> none  [the longest x1 22.2 us: body(): weight_shard = lax.all_gather(own_weights, 'blk', axis=0, tiled=True)]
    pmax x1 -> x0, blocking collectives: 29.5 us -> none  [body(): total_max = lax.pmax(worst_load, ('blk', 'state'))]
    ppermute x0 -> x16, starting transfers between devices: none -> 24.3 us  [the longest x8 14.4 us: gather_shifts(): parts.append(lax.ppermute(x, axis, perm))]
    gather x13 -> x4, local copies, waits for them, and re-layouts: 26.7 us -> 3.35 us  [the longest x1 1.15 us: body(): outage_flow = jnp.take(real_pos, outage_ids[0]).astype(jnp.bfloat16)]
    ppermute x0 -> x16, waiting for transfers between devices: none -> 8.34 us  [the longest x8 6.24 us: scatter_max(): result = jnp.maximum(result, lax.ppermute(piece, axis, perm))]
    dynamic_slice x25 -> x0, local copies, waits for them, and re-layouts: 2.18 us -> none  [the longest x16 1.51 us: absorb(): has_tile = lax.dynamic_index_in_dim(present, block_now, 1, keepdims=False)]
    unnamed x21 -> x20, local copies, waits for them, and re-layouts: 1.48 us -> 3.62 us
    dot_general x8 -> x1, matrix products: 3.15 us -> 2.22 us  [body(): jnp.einsum('tkmi,tkip->tkmp', tile_values, weights, preferred_element_typ...]
  transfers between devices with their start and end apart: 0 -> 16, of which waited for: 0 -> 5; matrix products, arithmetic and copies ran while one was open for 0% -> 12% of each run, Pallas kernels for 0% -> 0%
where the time goes in v1:
time: 52.8 us; the launch traced here: 52.5 us
  starting transfers between devices  24.3 us (46%)
  local copies, waits for them, and re-layouts  13 us (25%)
  waiting for transfers between devices  8.34 us (16%)
  other arithmetic  3.6 us (7%)
  matrix products  2.22 us (4%)
  between operations  1.09 us (2%)
    ppermute x8, starting transfers between devices, gather_shifts(): parts.append(lax.ppermute(x, axis, perm))  14.4 us
    ppermute x8, starting transfers between devices, scatter_max(): result = jnp.maximum(result, lax.ppermute(piece, axis, perm))  9.89 us
    ppermute x8, waiting for transfers between devices, scatter_max(): result = jnp.maximum(result, lax.ppermute(piece, axis, perm))  6.24 us
    unnamed x20, local copies, waits for them, and re-layouts  3.62 us
    dot_general x1, matrix products, body(): jnp.einsum('tkmi,tkip->tkmp', tile_values, weights, preferred_element_typ...  2.22 us
    ppermute x8, waiting for transfers between devices, gather_shifts(): parts.append(lax.ppermute(x, axis, perm))  2.1 us
    gather x1, local copies, waits for them, and re-layouts, solve_pairs(): s_second_first = coupling_block[second_idx, first_idx].astype(jnp.float32)  1.5 us
    gather x1, local copies, waits for them, and re-layouts, solve_pairs(): s_first_second = coupling_block[first_idx, second_idx].astype(jnp.float32)  1.5 us
  transfers between devices with their start and end apart: 16, of which 5 were waited for; matrix products, arithmetic and copies ran while one was open for 12% of the time, Pallas kernels for 0%

profile of v1, /device:TPU:0, one launch (start us, length us, event | category | flops | bytes accessed | tf_op | source)
XLA Modules:
  0.0 52.5 jit_solution(5764604094622918353)
XLA Ops:
  1.4 0.7 %fusion.43 = (f32[1,4,1024]{2,1,0:T(4,128)S(1)}, f32[4,1024]{1,0:T(4,128)S(1)}) fusion(f32[1,1024]{1,0:T(1,128)S(1)} %bitcast.135, f32[1,1024]{1,0:T(1,128)} %bitcast.136, f32[1,1024]{1,0:T(1,128)} %bitcast.137, f32[1,1024]{1,0:T(1,128)} %bitcast.138), kind=kLoop, calls=%fused_computation.131 | loop fusion | flops 12288 | bytes 49152 | tf_op jit(solution)/shard_map/stack | solution.py:13
  6.1 1.5 %gather_fusion.3 = bf16[128]{0:T(256)(128)(2,1)S(1)} fusion(bf16[128,128]{1,0:T(8,128)(2,1)S(1)} %bitcast.126, s32[128]{0:T(128)S(1)} %get-tuple-element.35), kind=kCustom, calls=%fused_computation.5 | custom fusion | bytes 1536 | tf_op jit(solution)/shard_map/gather | solution.py:39
  7.6 1.5 %gather_fusion.4 = bf16[128]{0:T(256)(128)(2,1)S(1)} fusion(bf16[128,128]{1,0:T(8,128)(2,1)S(1)} %bitcast.127, s32[128]{0:T(128)S(1)} %get-tuple-element.36), kind=kCustom, calls=%fused_computation.6 | custom fusion | bytes 1536 | tf_op jit(solution)/shard_map/gather | solution.py:40
  9.8 1.1 %gather_fusion.2 = bf16[128]{0:T(256)(128)(2,1)S(1)} fusion(f32[2048]{0:T(1024)S(1)} %bitcast.125, s32[1024]{0:T(1024)S(1)} %pad_clamp_fusion.3), kind=kCustom, calls=%fused_computation.4 | custom fusion | bytes 1024 | tf_op jit(solution)/shard_map/jit(_take)/gather | solution.py:71
  11.0 1.2 %gather_fusion.6 = bf16[128]{0:T(256)(128)(2,1)S(1)} fusion(bf16[128]{0:T(256)(128)(2,1)S(1)} %fusion.39, s32[1024]{0:T(1024)S(1)} %get-tuple-element.41), kind=kCustom, calls=%fused_computation.clone | custom fusion | bytes 1024 | tf_op jit(solution)/shard_map/jit(_take)/gather | solution.py:37
  12.2 1.2 %gather_fusion.7 = bf16[128]{0:T(256)(128)(2,1)S(1)} fusion(bf16[128]{0:T(256)(128)(2,1)S(1)} %fusion.39, s32[1024]{0:T(1024)S(1)} %get-tuple-element.40), kind=kCustom, calls=%fused_computation.1.clone | custom fusion | bytes 1024 | tf_op jit(solution)/shard_map/jit(_take)/gather | solution.py:38
  13.5 3.0 %collective-permute-start.1 = (f32[4,128]{1,0:T(4,128)S(1)}, f32[4,128]{1,0:T(4,128)S(1)}, u32[]{:S(2)}, u32[]{:S(2)}) collective-permute-start(f32[4,128]{1,0:T(4,128)S(1)} %pad_maximum_fusion.2), channel_id=1, source_target_pairs={{0,2},{2,4},{4,6},{6,8},{8,10},{10,12},{12,14},{14,0},{1,3},{3,5},... | collective-permute-start | bytes 6152 | tf_op jit(solution)/shard_map/ppermute | solution.py:12
  16.5 1.6 %collective-permute-start.2 = (f32[4,128]{1,0:T(4,128)S(1)}, f32[4,128]{1,0:T(4,128)S(1)}, u32[]{:S(2)}, u32[]{:S(2)}) collective-permute-start(f32[4,128]{1,0:T(4,128)S(1)} %pad_maximum_fusion.2), channel_id=1, source_target_pairs={{0,4},{2,6},{4,8},{6,10},{8,12},{10,14},{12,0},{14,2},{1,5},{3,7},... | collective-permute-start | bytes 6152 | tf_op jit(solution)/shard_map/ppermute | solution.py:12
  18.5 1.0 %gather_fusion.1 = f32[512,4]{1,0:T(8,128)S(1)} fusion(f32[4,2048]{0,1:T(8,128)S(1)} %copy.15, s32[1024]{0:T(1024)S(1)} %pad_clamp_fusion.4), kind=kCustom, calls=%fused_computation.3 | custom fusion | bytes 18432 | tf_op jit(solution)/shard_map/jit(_take)/gather | solution.py:83
  20.5 2.6 %collective-permute-start.3 = (f32[4,128]{1,0:T(4,128)S(1)}, f32[4,128]{1,0:T(4,128)S(1)}, u32[]{:S(2)}, u32[]{:S(2)}) collective-permute-start(f32[4,128]{1,0:T(4,128)S(1)} %pad_maximum_fusion.2), channel_id=1, source_target_pairs={{0,6},{2,8},{4,10},{6,12},{8,14},{10,0},{12,2},{14,4},{1,7},{3,9},... | collective-permute-start | bytes 6152 | tf_op jit(solution)/shard_map/ppermute | solution.py:12
  23.1 1.2 %collective-permute-start.4 = (f32[4,128]{1,0:T(4,128)S(1)}, f32[4,128]{1,0:T(4,128)S(1)}, u32[]{:S(2)}, u32[]{:S(2)}) collective-permute-start(f32[4,128]{1,0:T(4,128)S(1)} %pad_maximum_fusion.2), channel_id=1, source_target_pairs={{0,8},{2,10},{4,12},{6,14},{8,0},{10,2},{12,4},{14,6},{1,9},{3,11}... | collective-permute-start | bytes 6152 | tf_op jit(solution)/shard_map/ppermute | solution.py:12
  24.4 2.6 %collective-permute-start.5 = (f32[4,128]{1,0:T(4,128)S(1)}, f32[4,128]{1,0:T(4,128)S(1)}, u32[]{:S(2)}, u32[]{:S(2)}) collective-permute-start(f32[4,128]{1,0:T(4,128)S(1)} %pad_maximum_fusion.2), channel_id=1, source_target_pairs={{0,10},{2,12},{4,14},{6,0},{8,2},{10,4},{12,6},{14,8},{1,11},{3,13... | collective-permute-start | bytes 6152 | tf_op jit(solution)/shard_map/ppermute | solution.py:12
  27.0 1.3 %collective-permute-start.6 = (f32[4,128]{1,0:T(4,128)S(1)}, f32[4,128]{1,0:T(4,128)S(1)}, u32[]{:S(2)}, u32[]{:S(2)}) collective-permute-start(f32[4,128]{1,0:T(4,128)S(1)} %pad_maximum_fusion.2), channel_id=1, source_target_pairs={{0,12},{2,14},{4,0},{6,2},{8,4},{10,6},{12,8},{14,10},{1,13},{3,15... | collective-permute-start | bytes 6152 | tf_op jit(solution)/shard_map/ppermute | solution.py:12
  28.4 1.4 %collective-permute-start.7 = (f32[4,128]{1,0:T(4,128)S(1)}, f32[4,128]{1,0:T(4,128)S(1)}, u32[]{:S(2)}, u32[]{:S(2)}) collective-permute-start(f32[4,128]{1,0:T(4,128)S(1)} %pad_maximum_fusion.2), channel_id=1, source_target_pairs={{0,14},{2,0},{4,2},{6,4},{8,6},{10,8},{12,10},{14,12},{1,15},{3,1}... | collective-permute-start | bytes 6152 | tf_op jit(solution)/shard_map/ppermute | solution.py:12
  30.6 1.4 %collective-permute-done.7 = f32[4,128]{1,0:T(4,128)S(1)} collective-permute-done((f32[4,128]{1,0:T(4,128)S(1)}, f32[4,128]{1,0:T(4,128)S(1)}, u32[]{:S(2)}, u32[]{:S(2)}) %collective-permute-start.7) | collective-permute-done | bytes 2080 | tf_op jit(solution)/shard_map/ppermute | solution.py:12
  32.7 2.2 %fusion.44 = (f32[4,4,128]{2,1,0:T(4,128)S(1)}, f32[4,128]{1,0:T(4,128)S(1)}) fusion(f32[4,128]{1,0:T(4,128)S(1)} %bitcast.132, f32[4,128]{1,0:T(4,128)S(1)} %bitcast.133, bf16[4,4,128,128]{3,2,1,0:T(8,128)(2,1)S(1)} %copy-done, s32[4,4,128]{2,1,0:T(4,128)S(1)} %get-tuple-element.16, s32[4,4,128]{2,1,0:T(4,128)S(1)} %get-tuple-element.15, ...), kind=kOutput, calls=%fused_computation.132 | convolution fusion | flops 71038464 | bytes 565264 | tf_op jit(solution)/shard_map/tkmi,tkip->tkmp/dot_general | solution.py:100
  35.3 1.1 %collective-permute-done.8 = f32[8,64]{1,0:T(8,128)S(1)} collective-permute-done((f32[8,64]{1,0:T(8,128)S(1)}, f32[8,64]{1,0:T(8,128)S(1)}, u32[]{:S(2)}, u32[]{:S(2)}) %collective-permute-start.8) | collective-permute-done | bytes 2080 | tf_op jit(solution)/shard_map/ppermute | solution.py:30
  37.1 1.2 %collective-permute-start.11 = (f32[64]{0:T(128)S(1)}, f32[64]{0:T(128)S(1)}, u32[]{:S(2)}, u32[]{:S(2)}) collective-permute-start(f32[64]{0:T(128)S(1)} %get-tuple-element.28), channel_id=1, source_target_pairs={{0,6},{2,8},{4,10},{6,12},{8,14},{10,0},{12,2},{14,4},{1,7},{3,9},... | collective-permute-start | bytes 776 | tf_op jit(solution)/shard_map/ppermute | solution.py:30
  38.3 3.5 %collective-permute-start.12 = (f32[64]{0:T(128)S(1)}, f32[64]{0:T(128)S(1)}, u32[]{:S(2)}, u32[]{:S(2)}) collective-permute-start(f32[64]{0:T(128)S(1)} %get-tuple-element.27), channel_id=1, source_target_pairs={{0,8},{2,10},{4,12},{6,14},{8,0},{10,2},{12,4},{14,6},{1,9},{3,11}... | collective-permute-start | bytes 776 | tf_op jit(solution)/shard_map/ppermute | solution.py:30
  41.8 0.8 %collective-permute-start.13 = (f32[64]{0:T(128)S(1)}, f32[64]{0:T(128)S(1)}, u32[]{:S(2)}, u32[]{:S(2)}) collective-permute-start(f32[64]{0:T(128)S(1)} %get-tuple-element.26), channel_id=1, source_target_pairs={{0,10},{2,12},{4,14},{6,0},{8,2},{10,4},{12,6},{14,8},{1,11},{3,13... | collective-permute-start | bytes 776 | tf_op jit(solution)/shard_map/ppermute | solution.py:30
  42.6 1.5 %collective-permute-start.14 = (f32[64]{0:T(128)S(1)}, f32[64]{0:T(128)S(1)}, u32[]{:S(2)}, u32[]{:S(2)}) collective-permute-start(f32[64]{0:T(128)S(1)} %get-tuple-element.25), channel_id=1, source_target_pairs={{0,12},{2,14},{4,0},{6,2},{8,4},{10,6},{12,8},{14,10},{1,13},{3,15... | collective-permute-start | bytes 776 | tf_op jit(solution)/shard_map/ppermute | solution.py:30
  44.2 1.6 %collective-permute-start.15 = (f32[64]{0:T(128)S(1)}, f32[64]{0:T(128)S(1)}, u32[]{:S(2)}, u32[]{:S(2)}) collective-permute-start(f32[64]{0:T(128)S(1)} %get-tuple-element.24), channel_id=1, source_target_pairs={{0,14},{2,0},{4,2},{6,4},{8,6},{10,8},{12,10},{14,12},{1,15},{3,1}... | collective-permute-start | bytes 776 | tf_op jit(solution)/shard_map/ppermute | solution.py:30
  46.9 0.9 %collective-permute-done.15 = f32[64]{0:T(128)S(1)} collective-permute-done((f32[64]{0:T(128)S(1)}, f32[64]{0:T(128)S(1)}, u32[]{:S(2)}, u32[]{:S(2)}) %collective-permute-start.15) | collective-permute-done | bytes 288 | tf_op jit(solution)/shard_map/ppermute | solution.py:30
  47.8 4.3 %collective-permute-done.9 = f32[64]{0:T(128)S(1)} collective-permute-done((f32[64]{0:T(128)S(1)}, f32[64]{0:T(128)S(1)}, u32[]{:S(2)}, u32[]{:S(2)}) %collective-permute-start.9) | collective-permute-done | bytes 288 | tf_op jit(solution)/shard_map/ppermute | solution.py:30
  (79 shorter events, 10.8 us)
Async XLA Ops:
  0.6 32.0 %copy-start = (bf16[4,4,128,128]{3,2,1,0:T(8,128)(2,1)S(1)}, bf16[4,4,128,128]{3,2,1,0:T(8,128)(2,1)}, u32[]{:S(2)}) copy-start(bf16[4,4,128,128]{3,2,1,0:T(8,128)(2,1)} %param.18) | copy-start | bytes 1572868
  0.6 0.7 %copy-start.5 = (f32[1024]{0:T(1024)S(1)}, f32[1024]{0:T(1024)}, u32[]{:S(2)}) copy-start(f32[1024]{0:T(1024)} %param.15) | copy-start | bytes 12292
  2.1 0.7 %copy-start.2 = (s32[1,2,128]{2,1,0:T(2,128)S(1)}, s32[1,2,128]{2,1,0:T(2,128)}, u32[]{:S(2)}) copy-start(s32[1,2,128]{2,1,0:T(2,128)} %param.21) | copy-start | bytes 3076
  2.1 7.0 %collective-permute-start = (f32[4,1024]{1,0:T(4,128)S(1)}, f32[4,1024]{1,0:T(4,128)S(1)}, u32[]{:S(2)}, u32[]{:S(2)}) collective-permute-start(f32[4,1024]{1,0:T(4,128)S(1)} %get-tuple-element.20), channel_id=1, source_target_pairs={{0,1},{1,0},{2,3},{3,2},{4,5},{5,4},{6,7},{7,6},{8,9},{9,8},{10,11... | collective-permute-start | bytes 49160 | tf_op jit(solution)/shard_map/ppermute | solution.py:12
  2.8 0.7 %copy-start.3 = (s32[512]{0:T(512)S(1)}, s32[512]{0:T(512)}, u32[]{:S(2)}) copy-start(s32[512]{0:T(512)} %param.16) | copy-start | bytes 6148
  3.5 0.7 %copy-start.6 = (s32[1,128]{1,0:T(1,128)S(1)}, s32[1,128]{1,0:T(1,128)}, u32[]{:S(2)}) copy-start(s32[1,128]{1,0:T(1,128)} %param.19) | copy-start | bytes 1540
  4.2 0.7 %copy-start.4 = (s32[4,4]{1,0:T(4,128)S(1)}, s32[4,4]{1,0:T(4,128)}, u32[]{:S(2)}) copy-start(s32[4,4]{1,0:T(4,128)} %param.17) | copy-start | bytes 196
  5.3 0.8 %copy-start.1 = (bf16[1,128,128]{2,1,0:T(8,128)(2,1)S(1)}, bf16[1,128,128]{2,1,0:T(8,128)(2,1)}, u32[]{:S(2)}) copy-start(bf16[1,128,128]{2,1,0:T(8,128)(2,1)} %param.20) | copy-start | bytes 98308
  13.5 13.5 %collective-permute-start.1 = (f32[4,128]{1,0:T(4,128)S(1)}, f32[4,128]{1,0:T(4,128)S(1)}, u32[]{:S(2)}, u32[]{:S(2)}) collective-permute-start(f32[4,128]{1,0:T(4,128)S(1)} %pad_maximum_fusion.2), channel_id=1, source_target_pairs={{0,2},{2,4},{4,6},{6,8},{8,10},{10,12},{12,14},{14,0},{1,3},{3,5},... | collective-permute-start | bytes 6152 | tf_op jit(solution)/shard_map/ppermute | solution.py:12
  16.5 11.8 %collective-permute-start.2 = (f32[4,128]{1,0:T(4,128)S(1)}, f32[4,128]{1,0:T(4,128)S(1)}, u32[]{:S(2)}, u32[]{:S(2)}) collective-permute-start(f32[4,128]{1,0:T(4,128)S(1)} %pad_maximum_fusion.2), channel_id=1, source_target_pairs={{0,4},{2,6},{4,8},{6,10},{8,12},{10,14},{12,0},{14,2},{1,5},{3,7},... | collective-permute-start | bytes 6152 | tf_op jit(solution)/shard_map/ppermute | solution.py:12
  20.5 9.3 %collective-permute-start.3 = (f32[4,128]{1,0:T(4,128)S(1)}, f32[4,128]{1,0:T(4,128)S(1)}, u32[]{:S(2)}, u32[]{:S(2)}) collective-permute-start(f32[4,128]{1,0:T(4,128)S(1)} %pad_maximum_fusion.2), channel_id=1, source_target_pairs={{0,6},{2,8},{4,10},{6,12},{8,14},{10,0},{12,2},{14,4},{1,7},{3,9},... | collective-permute-start | bytes 6152 | tf_op jit(solution)/shard_map/ppermute | solution.py:12
  23.1 6.7 %collective-permute-start.4 = (f32[4,128]{1,0:T(4,128)S(1)}, f32[4,128]{1,0:T(4,128)S(1)}, u32[]{:S(2)}, u32[]{:S(2)}) collective-permute-start(f32[4,128]{1,0:T(4,128)S(1)} %pad_maximum_fusion.2), channel_id=1, source_target_pairs={{0,8},{2,10},{4,12},{6,14},{8,0},{10,2},{12,4},{14,6},{1,9},{3,11}... | collective-permute-start | bytes 6152 | tf_op jit(solution)/shard_map/ppermute | solution.py:12
  24.4 5.5 %collective-permute-start.5 = (f32[4,128]{1,0:T(4,128)S(1)}, f32[4,128]{1,0:T(4,128)S(1)}, u32[]{:S(2)}, u32[]{:S(2)}) collective-permute-start(f32[4,128]{1,0:T(4,128)S(1)} %pad_maximum_fusion.2), channel_id=1, source_target_pairs={{0,10},{2,12},{4,14},{6,0},{8,2},{10,4},{12,6},{14,8},{1,11},{3,13... | collective-permute-start | bytes 6152 | tf_op jit(solution)/shard_map/ppermute | solution.py:12
  27.0 3.6 %collective-permute-start.6 = (f32[4,128]{1,0:T(4,128)S(1)}, f32[4,128]{1,0:T(4,128)S(1)}, u32[]{:S(2)}, u32[]{:S(2)}) collective-permute-start(f32[4,128]{1,0:T(4,128)S(1)} %pad_maximum_fusion.2), channel_id=1, source_target_pairs={{0,12},{2,14},{4,0},{6,2},{8,4},{10,6},{12,8},{14,10},{1,13},{3,15... | collective-permute-start | bytes 6152 | tf_op jit(solution)/shard_map/ppermute | solution.py:12
  28.4 3.6 %collective-permute-start.7 = (f32[4,128]{1,0:T(4,128)S(1)}, f32[4,128]{1,0:T(4,128)S(1)}, u32[]{:S(2)}, u32[]{:S(2)}) collective-permute-start(f32[4,128]{1,0:T(4,128)S(1)} %pad_maximum_fusion.2), channel_id=1, source_target_pairs={{0,14},{2,0},{4,2},{6,4},{8,6},{10,8},{12,10},{14,12},{1,15},{3,1}... | collective-permute-start | bytes 6152 | tf_op jit(solution)/shard_map/ppermute | solution.py:12
  35.1 1.2 %collective-permute-start.8 = (f32[8,64]{1,0:T(8,128)S(1)}, f32[8,64]{1,0:T(8,128)S(1)}, u32[]{:S(2)}, u32[]{:S(2)}) collective-permute-start(f32[8,64]{1,0:T(8,128)S(1)} %bitcast.139), channel_id=1, source_target_pairs={{0,1},{1,0},{2,3},{3,2},{4,5},{5,4},{6,7},{7,6},{8,9},{9,8},{10,11... | collective-permute-start | bytes 6152 | tf_op jit(solution)/shard_map/ppermute | solution.py:30
  36.4 7.8 %collective-permute-start.10 = (f32[64]{0:T(128)S(1)}, f32[64]{0:T(128)S(1)}, u32[]{:S(2)}, u32[]{:S(2)}) collective-permute-start(f32[64]{0:T(128)S(1)} %get-tuple-element.29), channel_id=1, source_target_pairs={{0,4},{2,6},{4,8},{6,10},{8,12},{10,14},{12,0},{14,2},{1,5},{3,7},... | collective-permute-start | bytes 776 | tf_op jit(solution)/shard_map/ppermute | solution.py:30
  37.1 8.6 %collective-permute-start.11 = (f32[64]{0:T(128)S(1)}, f32[64]{0:T(128)S(1)}, u32[]{:S(2)}, u32[]{:S(2)}) collective-permute-start(f32[64]{0:T(128)S(1)} %get-tuple-element.28), channel_id=1, source_target_pairs={{0,6},{2,8},{4,10},{6,12},{8,14},{10,0},{12,2},{14,4},{1,7},{3,9},... | collective-permute-start | bytes 776 | tf_op jit(solution)/shard_map/ppermute | solution.py:30
  38.3 8.5 %collective-permute-start.12 = (f32[64]{0:T(128)S(1)}, f32[64]{0:T(128)S(1)}, u32[]{:S(2)}, u32[]{:S(2)}) collective-permute-start(f32[64]{0:T(128)S(1)} %get-tuple-element.27), channel_id=1, source_target_pairs={{0,8},{2,10},{4,12},{6,14},{8,0},{10,2},{12,4},{14,6},{1,9},{3,11}... | collective-permute-start | bytes 776 | tf_op jit(solution)/shard_map/ppermute | solution.py:30
  41.8 5.1 %collective-permute-start.13 = (f32[64]{0:T(128)S(1)}, f32[64]{0:T(128)S(1)}, u32[]{:S(2)}, u32[]{:S(2)}) collective-permute-start(f32[64]{0:T(128)S(1)} %get-tuple-element.26), channel_id=1, source_target_pairs={{0,10},{2,12},{4,14},{6,0},{8,2},{10,4},{12,6},{14,8},{1,11},{3,13... | collective-permute-start | bytes 776 | tf_op jit(solution)/shard_map/ppermute | solution.py:30
  42.6 4.2 %collective-permute-start.14 = (f32[64]{0:T(128)S(1)}, f32[64]{0:T(128)S(1)}, u32[]{:S(2)}, u32[]{:S(2)}) collective-permute-start(f32[64]{0:T(128)S(1)} %get-tuple-element.25), channel_id=1, source_target_pairs={{0,12},{2,14},{4,0},{6,2},{8,4},{10,6},{12,8},{14,10},{1,13},{3,15... | collective-permute-start | bytes 776 | tf_op jit(solution)/shard_map/ppermute | solution.py:30
  44.2 3.6 %collective-permute-start.15 = (f32[64]{0:T(128)S(1)}, f32[64]{0:T(128)S(1)}, u32[]{:S(2)}, u32[]{:S(2)}) collective-permute-start(f32[64]{0:T(128)S(1)} %get-tuple-element.24), channel_id=1, source_target_pairs={{0,14},{2,0},{4,2},{6,4},{8,6},{10,8},{12,10},{14,12},{1,15},{3,1}... | collective-permute-start | bytes 776 | tf_op jit(solution)/shard_map/ppermute | solution.py:30
  45.8 6.3 %collective-permute-start.9 = (f32[64]{0:T(128)S(1)}, f32[64]{0:T(128)S(1)}, u32[]{:S(2)}, u32[]{:S(2)}) collective-permute-start(f32[64]{0:T(128)S(1)} %get-tuple-element.23), channel_id=1, source_target_pairs={{0,2},{2,4},{4,6},{6,8},{8,10},{10,12},{12,14},{14,0},{1,3},{3,5},... | collective-permute-start | bytes 776 | tf_op jit(solution)/shard_map/ppermute | solution.py:30

commit v2 on v1

v2 whole, which is shorter than its diff:
```python
import jax
import jax.numpy as jnp
from jax import lax
from jax.sharding import PartitionSpec as P


def axes_size(axes):
    size = 1
    for axis in axes:
        size *= lax.axis_size(axis)
    return size


def gather_doubling(x, axes):
    n = axes_size(axes)
    me = lax.axis_index(axes)
    cur = x[None]
    bit = 1
    while bit < n:
        other = lax.ppermute(cur, axes, [(j, j ^ bit) for j in range(n)])
        low = (me & bit) == 0
        cur = jnp.where(low, jnp.concatenate([cur, other]), jnp.concatenate([other, cur]))
        bit *= 2
    return cur


def scatter_max(x, axes):
    n = axes_size(axes)
    me = lax.axis_index(axes)
    cur = x
    bit = 1
    while bit < n:
        pairs = cur.reshape((cur.shape[0] // 2, 2) + cur.shape[1:])
        mine = (me // bit) % 2
        keep = lax.dynamic_index_in_dim(pairs, mine, 1, keepdims=False)
        send = lax.dynamic_index_in_dim(pairs, 1 - mine, 1, keepdims=False)
        cur = jnp.maximum(keep, lax.ppermute(send, axes, [(j, j ^ bit) for j in range(n)]))
        bit *= 2
    return cur[0]


def body(
    base_real,
    base_reactive,
    voltage,
    rating,
    monitored,
    tile_ids,
    tile_values,
    outage_ids,
    coupling,
    outage_pairs,
):
    tiles_dev, slot_count, tile_size, _ = tile_values.shape
    pair_count = outage_pairs.shape[2]
    blocks = lax.axis_size("blk")
    halves = lax.axis_size("state")
    half_width = pair_count // halves
    half_len = base_real.shape[0]
    me_state = lax.axis_index("state")
    both = ("blk", "state")

    first_idx = outage_pairs[0, 0]
    second_idx = outage_pairs[0, 1]
    local_at = outage_ids[0] - me_state * half_len
    in_half = (local_at >= 0) & (local_at < half_len)
    flow_part = jnp.where(in_half, jnp.take(base_real, jnp.clip(local_at, 0, half_len - 1)), 0.0)
    flow_part = flow_part.astype(jnp.bfloat16).astype(jnp.float32)
    pair_at = jnp.concatenate([first_idx, second_idx])
    flow_pairs = jnp.take(flow_part, pair_at).reshape(2, pair_count)
    coupled = coupling[0][pair_at, jnp.concatenate([second_idx, first_idx])]
    coupled = coupled.astype(jnp.float32).reshape(2, pair_count)
    packed = jnp.concatenate(
        [flow_pairs, coupled, outage_pairs[0].astype(jnp.float32)]
    )
    known = gather_doubling(packed, both).reshape(blocks, halves, 6, pair_count)

    state_local = jnp.stack([base_real, base_reactive, voltage, rating])
    other_half = lax.ppermute(
        state_local, "state", [(j, (j + 1) % halves) for j in range(halves)]
    )
    state_pos = jnp.where(
        me_state == 0,
        jnp.concatenate([state_local, other_half], axis=1),
        jnp.concatenate([other_half, state_local], axis=1),
    )
    mon_vals = jnp.take(state_pos, monitored, axis=1).reshape(4, tiles_dev, tile_size)
    mon_real = mon_vals[0]
    react_sq = mon_vals[1] * mon_vals[1]
    mon_limit = mon_vals[2] * mon_vals[3]

    flow_first = jnp.sum(known[:, :, 0], axis=1)
    flow_second = jnp.sum(known[:, :, 1], axis=1)
    s_first_second = known[:, 0, 2]
    s_second_first = known[:, 0, 3]
    determinant = 1.0 - s_first_second * s_second_first
    w_first_all = (flow_first + s_first_second * flow_second) / determinant
    w_second_all = (flow_second + s_second_first * flow_first) / determinant
    table = jnp.stack([w_first_all, w_second_all, known[:, 0, 4], known[:, 0, 5]], axis=1)

    valid = tile_ids >= 0
    block_of = jnp.clip(tile_ids, 0, blocks - 1)
    chosen = jnp.take(table, block_of, axis=0)
    rows_iota = lax.broadcasted_iota(jnp.int32, (1, 1, tile_size, pair_count), 2)
    first_at = chosen[:, :, 2].astype(jnp.int32)[:, :, None, :]
    second_at = chosen[:, :, 3].astype(jnp.int32)[:, :, None, :]
    w_first = chosen[:, :, 0].astype(jnp.bfloat16)[:, :, None, :]
    w_second = chosen[:, :, 1].astype(jnp.bfloat16)[:, :, None, :]
    zero = jnp.zeros((), jnp.bfloat16)
    weights = jnp.where(rows_iota == first_at, w_first, zero) + jnp.where(
        rows_iota == second_at, w_second, zero
    )
    delta = jnp.einsum(
        "tkmi,tkip->tkmp", tile_values, weights, preferred_element_type=jnp.float32
    )
    post = mon_real[:, None, :, None] + delta
    loading = jnp.sqrt(post * post + react_sq[:, None, :, None]) / mon_limit[:, None, :, None]
    neg = jnp.float32(-jnp.inf)
    loading = jnp.where(valid[:, :, None, None], loading, neg)

    base_load = jnp.sqrt(mon_real * mon_real + react_sq) / mon_limit
    block_iota = jnp.arange(blocks, dtype=jnp.int32)
    matches = tile_ids[:, :, None] == block_iota[None, None, :]
    absent = jnp.logical_not(jnp.any(matches, axis=1))
    any_absent = jnp.any(absent, axis=1)

    peak_load = jnp.max(loading, axis=(1, 3))
    peak_load = jnp.maximum(peak_load, jnp.where(any_absent[:, None], base_load, neg))

    col_max = jnp.max(loading, axis=2)
    worst_local = jnp.max(
        jnp.where(matches[:, :, :, None], col_max[:, :, None, :], neg), axis=(0, 1)
    )
    base_max = jnp.max(base_load, axis=1)
    absent_max = jnp.max(jnp.where(absent, base_max[:, None], neg), axis=0)
    worst_local = jnp.maximum(worst_local, absent_max[:, None])

    worst_own = scatter_max(worst_local.reshape(blocks * halves, half_width), both)[None, :]
    return (peak_load.reshape(-1), worst_own)


def solution(mesh):
    return jax.shard_map(
        body,
        mesh=mesh,
        in_specs=(
            P(("cases", "blk", "state")),
            P(("cases", "blk", "state")),
            P(("cases", "blk", "state")),
            P(("cases", "blk", "state")),
            P(("cases", "blk", "state")),
            P(("cases", "blk", "state"), None),
            P(("cases", "blk", "state"), None, None, None),
            P(("cases", "blk"), None),
            P(("cases", "blk"), None, None),
            P(("cases", "blk"), None, None),
        ),
        out_specs=(P(("cases", "blk", "state")), P(("cases", "blk"), "state")),
        check_vma=False,
    )
```

time: 52.8 us -> 44.4 us (0.84)
  starting transfers between devices: 24.3 us -> 13.6 us
  waiting for transfers between devices: 8.34 us -> 11.4 us
  local copies, waits for them, and re-layouts: 13 us -> 11.3 us
  other arithmetic: 3.6 us -> 4.66 us
    ppermute x16 -> x9, starting transfers between devices: 24.3 us -> 13.6 us  [the longest x4 8.41 us: gather_doubling(): other = lax.ppermute(cur, axes, [(j, j ^ bit) for j in range(n)])]
    ppermute x16 -> x9, waiting for transfers between devices: 8.34 us -> 11.4 us  [the longest x4 7.72 us: scatter_max(): lax.ppermute(send, axes, [(j, j ^ bit) for j in range(n)])]
    gather x7 -> x4, local copies, waits for them, and re-layouts: 7.78 us -> 5.83 us  [the longest x1 2.4 us: body(): coupled = coupling[0][pair_at, jnp.concatenate([second_idx, first_idx])]]
    unnamed x20, local copies, waits for them, and re-layouts: 3.62 us -> 2.3 us
    gather x1, local copies, waits for them, and re-layouts: 1.04 us -> 2.25 us  [body(): jnp.take(state_pos, monitored, axis=1).reshape(4, tiles_dev, tile_size)]
    select_n x4 -> x8, other arithmetic: 0.17 us -> 1.18 us  [the longest x1 1.11 us: body(): jnp.where(me_state == 0, jnp.concatenate([state_local, other_half], axis=...]
    concatenate x0 -> x3, local copies, waits for them, and re-layouts: none -> 0.73 us  [the longest x1 0.36 us: body(): jnp.concatenate([other_half, state_local], axis=1)]
  transfers between devices with their start and end apart: 16 -> 9, of which waited for: 5 -> 6; matrix products, arithmetic and copies ran while one was open for 12% -> 26% of each run, Pallas kernels for 0% -> 0%
where the time goes in v2:
time: 44.4 us; the launch traced here: 44.2 us
  starting transfers between devices  13.6 us (31%)
  waiting for transfers between devices  11.4 us (26%)
  local copies, waits for them, and re-layouts  11.3 us (25%)
  other arithmetic  4.66 us (10%)
  matrix products  2.22 us (5%)
  between operations  1.01 us (2%)
    ppermute x4, starting transfers between devices, gather_doubling(): other = lax.ppermute(cur, axes, [(j, j ^ bit) for j in range(n)])  8.41 us
    ppermute x4, waiting for transfers between devices, scatter_max(): lax.ppermute(send, axes, [(j, j ^ bit) for j in range(n)])  7.72 us
    ppermute x4, starting transfers between devices, scatter_max(): lax.ppermute(send, axes, [(j, j ^ bit) for j in range(n)])  4.61 us
    ppermute x4, waiting for transfers between devices, gather_doubling(): other = lax.ppermute(cur, axes, [(j, j ^ bit) for j in range(n)])  3.64 us
    gather x1, local copies, waits for them, and re-layouts, body(): coupled = coupling[0][pair_at, jnp.concatenate([second_idx, first_idx])]  2.4 us
    unnamed x20, local copies, waits for them, and re-layouts  2.3 us
    gather x1, local copies, waits for them, and re-layouts, body(): jnp.take(state_pos, monitored, axis=1).reshape(4, tiles_dev, tile_size)  2.25 us
    dot_general x1, matrix products, body(): jnp.einsum('tkmi,tkip->tkmp', tile_values, weights, preferred_element_typ...  2.22 us
  transfers between devices with their start and end apart: 9, of which 6 were waited for; matrix products, arithmetic and copies ran while one was open for 26% of the time, Pallas kernels for 0%

profile of v2, /device:TPU:0, one launch (start us, length us, event | category | flops | bytes accessed | tf_op | source)
XLA Modules:
  0.0 44.2 jit_solution(16267011736411949864)
XLA Ops:
  0.7 0.7 %copy-done.1 = f32[1024]{0:T(1024)S(1)} copy-done((f32[1024]{0:T(1024)S(1)}, f32[1024]{0:T(1024)}, u32[]{:S(2)}) %copy-start.1) | copy-done | bytes 4120
  1.4 0.7 %pad_maximum_fusion.1 = f32[4,1024]{1,0:T(4,128)S(1)} fusion(f32[1,1024]{1,0:T(1,128)} %bitcast.113, f32[1,1024]{1,0:T(1,128)} %bitcast.115, f32[1,1024]{1,0:T(1,128)} %bitcast.117, f32[1,1024]{1,0:T(1,128)S(1)} %bitcast.103), kind=kLoop, calls=%fused_computation.36 | loop fusion | flops 12288 | bytes 32768 | tf_op jit(solution)/shard_map/stack | solution.py:78
  2.8 2.4 %gather_fusion.3 = bf16[256]{0:T(256)(128)(2,1)S(1)} fusion(bf16[128,128]{1,0:T(8,128)(2,1)S(1)} %bitcast.106, s32[256]{0:T(256)S(1)} %bitcast.105), kind=kCustom, calls=%fused_computation.3 | custom fusion | bytes 3072 | tf_op jit(solution)/shard_map/gather | solution.py:71
  5.3 0.6 %copy-done.9 = s32[1,128]{1,0:T(1,128)S(1)} copy-done((s32[1,128]{1,0:T(1,128)S(1)}, s32[1,128]{1,0:T(1,128)}, u32[]{:S(2)}) %copy-start.9) | copy-done | bytes 536
  5.9 1.0 %gather_fusion.1 = bf16[128]{0:T(256)(128)(2,1)S(1)} fusion(f32[1024]{0:T(1024)S(1)} %copy-done.1, s32[1024]{0:T(1024)S(1)} %pad_clamp_fusion.2), kind=kCustom, calls=%fused_computation.1 | custom fusion | bytes 1024 | tf_op jit(solution)/shard_map/jit(_take)/gather | solution.py:67
  6.9 1.9 %gather_fusion.2 = f32[256]{0:T(256)S(1)} fusion(f32[128]{0:T(128)S(1)} %convert_convert_fusion, s32[1024]{0:T(1024)S(1)} %pad_clamp_fusion.1), kind=kCustom, calls=%fused_computation.2 | custom fusion | bytes 3072 | tf_op jit(solution)/shard_map/jit(_take)/gather | solution.py:70
  9.6 0.7 %copy-done.3 = s32[4,4]{1,0:T(4,128)S(1)} copy-done((s32[4,4]{1,0:T(4,128)S(1)}, s32[4,4]{1,0:T(4,128)}, u32[]{:S(2)}) %copy-start.3) | copy-done | bytes 88
  10.6 3.0 %collective-permute-start.2 = (f32[2,6,128]{2,0,1:T(2,128)S(1)}, f32[2,6,128]{2,0,1:T(2,128)S(1)}, u32[]{:S(2)}, u32[]{:S(2)}) collective-permute-start(f32[2,6,128]{2,0,1:T(2,128)S(1)} %maximum_select_fusion.3), channel_id=1, source_target_pairs={{0,2},{1,3},{2,0},{3,1},{4,6},{5,7},{6,4},{7,5},{8,10},{9,11},{10,... | collective-permute-start | bytes 18440 | tf_op jit(solution)/shard_map/ppermute | solution.py:20
  13.6 1.6 %collective-permute-done.2 = f32[2,6,128]{2,0,1:T(2,128)S(1)} collective-permute-done((f32[2,6,128]{2,0,1:T(2,128)S(1)}, f32[2,6,128]{2,0,1:T(2,128)S(1)}, u32[]{:S(2)}, u32[]{:S(2)}) %collective-permute-start.2) | collective-permute-done | bytes 6176 | tf_op jit(solution)/shard_map/ppermute | solution.py:20
  15.2 2.2 %collective-permute-start.3 = (f32[4,6,128]{2,0,1:T(4,128)S(1)}, f32[4,6,128]{2,0,1:T(4,128)S(1)}, u32[]{:S(2)}, u32[]{:S(2)}) collective-permute-start(f32[4,6,128]{2,0,1:T(4,128)S(1)} %maximum_select_fusion.2), channel_id=1, source_target_pairs={{0,4},{1,5},{2,6},{3,7},{4,0},{5,1},{6,2},{7,3},{8,12},{9,13},{10,... | collective-permute-start | bytes 36872 | tf_op jit(solution)/shard_map/ppermute | solution.py:20
  18.2 1.1 %broadcast_select_fusion = f32[4,2048]{0,1:T(8,128)} fusion(f32[4,2048]{0,1:T(8,128)S(1)} %copy.47, f32[4,2048]{0,1:T(8,128)S(1)} %copy.48, pred[]{:T(512)S(6)} %eq.57), kind=kLoop, calls=%fused_computation.18 | loop fusion | flops 8192 | bytes 98305 | tf_op jit(solution)/shard_map/jit(_where)/select_n | solution.py:82
  19.3 2.3 %gather_fusion = f32[512,4]{1,0:T(8,128)S(1)} fusion(f32[4,2048]{0,1:T(8,128)} %broadcast_select_fusion, s32[1024]{0:T(1024)S(1)} %pad_clamp_fusion.3), kind=kCustom, calls=%fused_computation | custom fusion | bytes 18432 | tf_op jit(solution)/shard_map/jit(_take)/gather | solution.py:87
  21.7 0.6 %fusion.15 = (f32[512]{0:T(512)S(1)}, f32[512]{0:T(512)S(1)}, f32[512]{0:T(512)S(1)}, f32[512]{0:T(512)S(1)}) fusion(f32[4,512]{0,1:T(8,128)S(1)} %select_bitcast_fusion), kind=kLoop, calls=%fused_computation.26 | loop fusion | flops 2560 | bytes 16384 | tf_op jit(solution)/shard_map/div | solution.py:121
  22.5 2.7 %collective-permute-start.4 = (f32[8,6,128]{2,0,1:T(8,128)S(1)}, f32[8,6,128]{2,0,1:T(8,128)S(1)}, u32[]{:S(2)}, u32[]{:S(2)}) collective-permute-start(f32[8,6,128]{2,0,1:T(8,128)S(1)} %maximum_select_fusion.1), channel_id=1, source_target_pairs={{0,8},{1,9},{2,10},{3,11},{4,12},{5,13},{6,14},{7,15},{8,0},{9,1},... | collective-permute-start | bytes 73736 | tf_op jit(solution)/shard_map/ppermute | solution.py:20
  25.2 2.1 %collective-permute-done.4 = f32[8,6,128]{2,0,1:T(8,128)S(1)} collective-permute-done((f32[8,6,128]{2,0,1:T(8,128)S(1)}, f32[8,6,128]{2,0,1:T(8,128)S(1)}, u32[]{:S(2)}, u32[]{:S(2)}) %collective-permute-start.4) | collective-permute-done | bytes 24608 | tf_op jit(solution)/shard_map/ppermute | solution.py:20
  27.3 0.6 %gather_fusion.4 = f32[16,4,128]{2,1,0:T(4,128)S(1)} fusion(f32[8,4,128]{2,1,0:T(4,128)S(1)} %pad_maximum_fusion.2, s32[1024]{0:T(1024)S(1)} %pad_clamp_fusion), kind=kCustom, calls=%fused_computation.4 | custom fusion | bytes 65600 | tf_op jit(solution)/shard_map/jit(_take)/gather | solution.py:103
  28.1 2.2 %fusion.27 = (f32[4,4,128]{2,1,0:T(4,128)S(1)}, f32[4,128]{1,0:T(4,128)S(1)}) fusion(f32[4,128]{1,0:T(4,128)S(1)} %bitcast.121, f32[4,128]{1,0:T(4,128)S(1)} %bitcast.122, bf16[4,4,128,128]{3,2,1,0:T(8,128)(2,1)S(1)} %copy-done, s32[4,4,128]{2,1,0:T(4,128)S(1)} %get-tuple-element.21, s32[4,4,128]{2,1,0:T(4,128)S(1)} %get-tuple-element.20, ...), kind=kOutput, calls=%fused_computation.102 | convolution fusion | flops 71038464 | bytes 565264 | tf_op jit(solution)/shard_map/tkmi,tkip->tkmp/dot_general | solution.py:113
  30.7 1.1 %collective-permute-done.5 = f32[8,64]{1,0:T(8,128)S(1)} collective-permute-done((f32[8,64]{1,0:T(8,128)S(1)}, f32[8,64]{1,0:T(8,128)S(1)}, u32[]{:S(2)}, u32[]{:S(2)}) %collective-permute-start.5) | collective-permute-done | bytes 2080 | tf_op jit(solution)/shard_map/ppermute | solution.py:37
  31.8 1.7 %collective-permute-start.6 = (f32[4,64]{1,0:T(4,128)S(1)}, f32[4,64]{1,0:T(4,128)S(1)}, u32[]{:S(2)}, u32[]{:S(2)}) collective-permute-start(f32[4,64]{1,0:T(4,128)S(1)} %bitcast.129), channel_id=1, source_target_pairs={{0,2},{1,3},{2,0},{3,1},{4,6},{5,7},{6,4},{7,5},{8,10},{9,11},{10,... | collective-permute-start | bytes 3080 | tf_op jit(solution)/shard_map/ppermute | solution.py:37
  33.5 1.9 %collective-permute-done.6 = f32[4,64]{1,0:T(4,128)S(1)} collective-permute-done((f32[4,64]{1,0:T(4,128)S(1)}, f32[4,64]{1,0:T(4,128)S(1)}, u32[]{:S(2)}, u32[]{:S(2)}) %collective-permute-start.6) | collective-permute-done | bytes 1056 | tf_op jit(solution)/shard_map/ppermute | solution.py:37
  35.7 3.5 %collective-permute-done.7 = f32[2,64]{1,0:T(2,128)S(1)} collective-permute-done((f32[2,64]{1,0:T(2,128)S(1)}, f32[2,64]{1,0:T(2,128)S(1)}, u32[]{:S(2)}, u32[]{:S(2)}) %collective-permute-start.7) | collective-permute-done | bytes 544 | tf_op jit(solution)/shard_map/ppermute | solution.py:37
  39.1 2.7 %collective-permute-start.8 = (f32[1,64]{1,0:T(1,128)S(1)}, f32[1,64]{1,0:T(1,128)S(1)}, u32[]{:S(2)}, u32[]{:S(2)}) collective-permute-start(f32[1,64]{1,0:T(1,128)S(1)} %constant_dynamic-slice_fusion), channel_id=1, source_target_pairs={{0,8},{1,9},{2,10},{3,11},{4,12},{5,13},{6,14},{7,15},{8,0},{9,1},... | collective-permute-start | bytes 776 | tf_op jit(solution)/shard_map/ppermute | solution.py:37
  41.8 0.6 %bitcast_maximum_fusion = f32[512]{0:T(512)} fusion(f32[4,128]{1,0:T(4,128)S(1)} %get-tuple-element.3, f32[512]{0:T(512)S(1)} %get-tuple-element.4, pred[4]{0:T(512)(128)(4,1)S(1)} %not_reduce_fusion), kind=kLoop, calls=%fused_computation.69 | loop fusion | flops 1024 | bytes 6148 | tf_op jit(solution)/shard_map/max | solution.py:128
  42.4 1.2 %collective-permute-done.8 = f32[1,64]{1,0:T(1,128)S(1)} collective-permute-done((f32[1,64]{1,0:T(1,128)S(1)}, f32[1,64]{1,0:T(1,128)S(1)}, u32[]{:S(2)}, u32[]{:S(2)}) %collective-permute-start.8) | collective-permute-done | bytes 288 | tf_op jit(solution)/shard_map/ppermute | solution.py:37
  (72 shorter events, 4.2 us)
Async XLA Ops:
  0.6 27.4 %copy-start = (bf16[4,4,128,128]{3,2,1,0:T(8,128)(2,1)S(1)}, bf16[4,4,128,128]{3,2,1,0:T(8,128)(2,1)}, u32[]{:S(2)}) copy-start(bf16[4,4,128,128]{3,2,1,0:T(8,128)(2,1)} %param.16) | copy-start | bytes 1572868
  0.6 0.7 %copy-start.1 = (f32[1024]{0:T(1024)S(1)}, f32[1024]{0:T(1024)}, u32[]{:S(2)}) copy-start(f32[1024]{0:T(1024)} %param.10) | copy-start | bytes 12292
  0.7 2.2 %copy-start.2 = (bf16[1,128,128]{2,1,0:T(8,128)(2,1)S(1)}, bf16[1,128,128]{2,1,0:T(8,128)(2,1)}, u32[]{:S(2)}) copy-start(bf16[1,128,128]{2,1,0:T(8,128)(2,1)} %param.18) | copy-start | bytes 98308
  2.1 0.7 %copy-start.8 = (s32[1,2,128]{2,1,0:T(2,128)S(1)}, s32[1,2,128]{2,1,0:T(2,128)}, u32[]{:S(2)}) copy-start(s32[1,2,128]{2,1,0:T(2,128)} %param.19) | copy-start | bytes 3076
  2.1 15.3 %collective-permute-start = (f32[4,1024]{1,0:T(4,128)S(1)}, f32[4,1024]{1,0:T(4,128)S(1)}, u32[]{:S(2)}, u32[]{:S(2)}) collective-permute-start(f32[4,1024]{1,0:T(4,128)S(1)} %pad_maximum_fusion.1), channel_id=1, source_target_pairs={{0,1},{1,0},{2,3},{3,2},{4,5},{5,4},{6,7},{7,6},{8,9},{9,8},{10,11... | collective-permute-start | bytes 49160 | tf_op jit(solution)/shard_map/ppermute | solution.py:79
  5.3 0.7 %copy-start.9 = (s32[1,128]{1,0:T(1,128)S(1)}, s32[1,128]{1,0:T(1,128)}, u32[]{:S(2)}) copy-start(s32[1,128]{1,0:T(1,128)} %param.17) | copy-start | bytes 1540
  8.9 0.7 %copy-start.7 = (s32[512]{0:T(512)S(1)}, s32[512]{0:T(512)}, u32[]{:S(2)}) copy-start(s32[512]{0:T(512)} %param.14) | copy-start | bytes 6148
  8.9 1.7 %collective-permute-start.1 = (f32[1,6,128]{2,0,1:T(1,128)S(1)}, f32[1,6,128]{2,0,1:T(1,128)S(1)}, u32[]{:S(2)}, u32[]{:S(2)}) collective-permute-start(f32[1,6,128]{2,0,1:T(1,128)S(1)} %broadcast_in_dim.147), channel_id=1, source_target_pairs={{0,1},{1,0},{2,3},{3,2},{4,5},{5,4},{6,7},{7,6},{8,9},{9,8},{10,11... | collective-permute-start | bytes 9224 | tf_op jit(solution)/shard_map/ppermute | solution.py:20
  9.5 0.7 %copy-start.3 = (s32[4,4]{1,0:T(4,128)S(1)}, s32[4,4]{1,0:T(4,128)}, u32[]{:S(2)}) copy-start(s32[4,4]{1,0:T(4,128)} %param.15) | copy-start | bytes 196
  10.6 4.6 %collective-permute-start.2 = (f32[2,6,128]{2,0,1:T(2,128)S(1)}, f32[2,6,128]{2,0,1:T(2,128)S(1)}, u32[]{:S(2)}, u32[]{:S(2)}) collective-permute-start(f32[2,6,128]{2,0,1:T(2,128)S(1)} %maximum_select_fusion.3), channel_id=1, source_target_pairs={{0,2},{1,3},{2,0},{3,1},{4,6},{5,7},{6,4},{7,5},{8,10},{9,11},{10,... | collective-permute-start | bytes 18440 | tf_op jit(solution)/shard_map/ppermute | solution.py:20
  13.6 3.8 %copy-start.4 = (f32[1024]{0:T(1024)S(1)}, f32[1024]{0:T(1024)}, u32[]{:S(2)}) copy-start(f32[1024]{0:T(1024)} %param.13) | copy-start | bytes 12292
  13.6 3.8 %copy-start.5 = (f32[1024]{0:T(1024)S(1)}, f32[1024]{0:T(1024)}, u32[]{:S(2)}) copy-start(f32[1024]{0:T(1024)} %param.12) | copy-start | bytes 12292
  13.6 3.8 %copy-start.6 = (f32[1024]{0:T(1024)S(1)}, f32[1024]{0:T(1024)}, u32[]{:S(2)}) copy-start(f32[1024]{0:T(1024)} %param.11) | copy-start | bytes 12292
  15.2 7.2 %collective-permute-start.3 = (f32[4,6,128]{2,0,1:T(4,128)S(1)}, f32[4,6,128]{2,0,1:T(4,128)S(1)}, u32[]{:S(2)}, u32[]{:S(2)}) collective-permute-start(f32[4,6,128]{2,0,1:T(4,128)S(1)} %maximum_select_fusion.2), channel_id=1, source_target_pairs={{0,4},{1,5},{2,6},{3,7},{4,0},{5,1},{6,2},{7,3},{8,12},{9,13},{10,... | collective-permute-start | bytes 36872 | tf_op jit(solution)/shard_map/ppermute | solution.py:20
  22.5 4.8 %collective-permute-start.4 = (f32[8,6,128]{2,0,1:T(8,128)S(1)}, f32[8,6,128]{2,0,1:T(8,128)S(1)}, u32[]{:S(2)}, u32[]{:S(2)}) collective-permute-start(f32[8,6,128]{2,0,1:T(8,128)S(1)} %maximum_select_fusion.1), channel_id=1, source_target_pairs={{0,8},{1,9},{2,10},{3,11},{4,12},{5,13},{6,14},{7,15},{8,0},{9,1},... | collective-permute-start | bytes 73736 | tf_op jit(solution)/shard_map/ppermute | solution.py:20
  30.6 1.2 %collective-permute-start.5 = (f32[8,64]{1,0:T(8,128)S(1)}, f32[8,64]{1,0:T(8,128)S(1)}, u32[]{:S(2)}, u32[]{:S(2)}) collective-permute-start(f32[8,64]{1,0:T(8,128)S(1)} %bitcast.126), channel_id=1, source_target_pairs={{0,1},{1,0},{2,3},{3,2},{4,5},{5,4},{6,7},{7,6},{8,9},{9,8},{10,11... | collective-permute-start | bytes 6152 | tf_op jit(solution)/shard_map/ppermute | solution.py:37
  31.8 3.6 %collective-permute-start.6 = (f32[4,64]{1,0:T(4,128)S(1)}, f32[4,64]{1,0:T(4,128)S(1)}, u32[]{:S(2)}, u32[]{:S(2)}) collective-permute-start(f32[4,64]{1,0:T(4,128)S(1)} %bitcast.129), channel_id=1, source_target_pairs={{0,2},{1,3},{2,0},{3,1},{4,6},{5,7},{6,4},{7,5},{8,10},{9,11},{10,... | collective-permute-start | bytes 3080 | tf_op jit(solution)/shard_map/ppermute | solution.py:37
  35.5 3.6 %collective-permute-start.7 = (f32[2,64]{1,0:T(2,128)S(1)}, f32[2,64]{1,0:T(2,128)S(1)}, u32[]{:S(2)}, u32[]{:S(2)}) collective-permute-start(f32[2,64]{1,0:T(2,128)S(1)} %bitcast.130), channel_id=1, source_target_pairs={{0,4},{1,5},{2,6},{3,7},{4,0},{5,1},{6,2},{7,3},{8,12},{9,13},{10,... | collective-permute-start | bytes 1544 | tf_op jit(solution)/shard_map/ppermute | solution.py:37
  39.1 4.5 %collective-permute-start.8 = (f32[1,64]{1,0:T(1,128)S(1)}, f32[1,64]{1,0:T(1,128)S(1)}, u32[]{:S(2)}, u32[]{:S(2)}) collective-permute-start(f32[1,64]{1,0:T(1,128)S(1)} %constant_dynamic-slice_fusion), channel_id=1, source_target_pairs={{0,8},{1,9},{2,10},{3,11},{4,12},{5,13},{6,14},{7,15},{8,0},{9,1},... | collective-permute-start | bytes 776 | tf_op jit(solution)/shard_map/ppermute | solution.py:37

commit v3 on v2

--- a/solution.py
+++ b/solution.py
@@ -63,13 +63,22 @@
     first_idx = outage_pairs[0, 0]
     second_idx = outage_pairs[0, 1]
     local_at = outage_ids[0] - me_state * half_len
-    in_half = (local_at >= 0) & (local_at < half_len)
-    flow_part = jnp.where(in_half, jnp.take(base_real, jnp.clip(local_at, 0, half_len - 1)), 0.0)
-    flow_part = flow_part.astype(jnp.bfloat16).astype(jnp.float32)
+    branch_iota = lax.broadcasted_iota(jnp.int32, (pair_count, half_len), 1)
+    pick_branch = (branch_iota == local_at[:, None]).astype(jnp.bfloat16)
+    flow_part = jnp.dot(
+        pick_branch, base_real.astype(jnp.bfloat16), preferred_element_type=jnp.float32
+    )
     pair_at = jnp.concatenate([first_idx, second_idx])
-    flow_pairs = jnp.take(flow_part, pair_at).reshape(2, pair_count)
-    coupled = coupling[0][pair_at, jnp.concatenate([second_idx, first_idx])]
-    coupled = coupled.astype(jnp.float32).reshape(2, pair_count)
+    pair_to = jnp.concatenate([second_idx, first_idx])
+    outage_iota = lax.broadcasted_iota(jnp.int32, (2 * pair_count, pair_count), 1)
+    pick_at = (outage_iota == pair_at[:, None]).astype(jnp.bfloat16)
+    flow_pairs = jnp.dot(
+        pick_at, flow_part.astype(jnp.bfloat16), preferred_element_type=jnp.float32
+    ).reshape(2, pair_count)
+    coupled_rows = jnp.dot(pick_at, coupling[0], preferred_element_type=jnp.float32)
+    coupled = jnp.sum(
+        jnp.where(outage_iota == pair_to[:, None], coupled_rows, 0.0), axis=1
+    ).reshape(2, pair_count)
     packed = jnp.concatenate(
         [flow_pairs, coupled, outage_pairs[0].astype(jnp.float32)]
     )

time: 44.4 us -> 39.8 us (0.90)
  local copies, waits for them, and re-layouts: 11.3 us -> 6.11 us
  matrix products: 2.22 us -> 2.87 us
    gather x3 -> x0, local copies, waits for them, and re-layouts: 5.24 us -> none  [the longest x1 2.4 us: body(): coupled = coupling[0][pair_at, jnp.concatenate([second_idx, first_idx])]]
    dot_general x0 -> x2, matrix products: none -> 0.65 us  [the longest x1 0.37 us: body(): jnp.dot(pick_at, flow_part.astype(jnp.bfloat16), preferred_element_type=j...]
  transfers between devices with their start and end apart: 9 -> 9, of which waited for: 6 -> 6; matrix products, arithmetic and copies ran while one was open for 26% -> 17% of each run, Pallas kernels for 0% -> 0%
where the time goes in v3:
time: 39.8 us; the launch traced here: 39.5 us
  starting transfers between devices  13.6 us (34%)
  waiting for transfers between devices  11.4 us (29%)
  local copies, waits for them, and re-layouts  6.11 us (15%)
  other arithmetic  4.62 us (12%)
  matrix products  2.87 us (7%)
  between operations  1 us (3%)
    ppermute x4, starting transfers between devices, gather_doubling(): other = lax.ppermute(cur, axes, [(j, j ^ bit) for j in range(n)])  8.41 us
    ppermute x4, waiting for transfers between devices, scatter_max(): lax.ppermute(send, axes, [(j, j ^ bit) for j in range(n)])  7.73 us
    ppermute x4, starting transfers between devices, scatter_max(): lax.ppermute(send, axes, [(j, j ^ bit) for j in range(n)])  4.61 us
    ppermute x4, waiting for transfers between devices, gather_doubling(): other = lax.ppermute(cur, axes, [(j, j ^ bit) for j in range(n)])  3.64 us
    unnamed x20, local copies, waits for them, and re-layouts  2.31 us
    gather x1, local copies, waits for them, and re-layouts, body(): jnp.take(state_pos, monitored, axis=1).reshape(4, tiles_dev, tile_size)  2.25 us
    dot_general x1, matrix products, body(): jnp.einsum('tkmi,tkip->tkmp', tile_values, weights, preferred_element_typ...  2.22 us
    select_n x1, other arithmetic, body(): jnp.where(me_state == 0, jnp.concatenate([state_local, other_half], axis=...  1.11 us
  transfers between devices with their start and end apart: 9, of which 6 were waited for; matrix products, arithmetic and copies ran while one was open for 17% of the time, Pallas kernels for 0%

profile of v3, /device:TPU:0, one launch (start us, length us, event | category | flops | bytes accessed | tf_op | source)
XLA Modules:
  0.0 39.5 jit_solution(5229275642322122969)
XLA Ops:
  0.7 0.7 %copy-done.1 = f32[1024]{0:T(1024)S(1)} copy-done((f32[1024]{0:T(1024)S(1)}, f32[1024]{0:T(1024)}, u32[]{:S(2)}) %copy-start.1) | copy-done | bytes 4120
  1.4 0.7 %pad_maximum_fusion.1 = f32[4,1024]{1,0:T(4,128)S(1)} fusion(f32[1,1024]{1,0:T(1,128)} %bitcast.105, f32[1,1024]{1,0:T(1,128)} %bitcast.107, f32[1,1024]{1,0:T(1,128)} %bitcast.109, f32[1,1024]{1,0:T(1,128)S(1)} %bitcast.101), kind=kLoop, calls=%fused_computation.46 | loop fusion | flops 12288 | bytes 32768 | tf_op jit(solution)/shard_map/stack | solution.py:87
  2.2 0.6 %collective-permute-start = (f32[4,1024]{1,0:T(4,128)S(1)}, f32[4,1024]{1,0:T(4,128)S(1)}, u32[]{:S(2)}, u32[]{:S(2)}) collective-permute-start(f32[4,1024]{1,0:T(4,128)S(1)} %pad_maximum_fusion.1), channel_id=1, source_target_pairs={{0,1},{1,0},{2,3},{3,2},{4,5},{5,4},{6,7},{7,6},{8,9},{9,8},{10,11... | collective-permute-start | bytes 49160 | tf_op jit(solution)/shard_map/ppermute | solution.py:88
  2.9 0.6 %copy-done.9 = s32[1,128]{1,0:T(1,128)S(1)} copy-done((s32[1,128]{1,0:T(1,128)S(1)}, s32[1,128]{1,0:T(1,128)}, u32[]{:S(2)}) %copy-start.9) | copy-done | bytes 536
  4.2 0.6 %collective-permute-start.1 = (f32[1,6,128]{2,0,1:T(1,128)S(1)}, f32[1,6,128]{2,0,1:T(1,128)S(1)}, u32[]{:S(2)}, u32[]{:S(2)}) collective-permute-start(f32[1,6,128]{2,0,1:T(1,128)S(1)} %broadcast_in_dim.134), channel_id=1, source_target_pairs={{0,1},{1,0},{2,3},{3,2},{4,5},{5,4},{6,7},{7,6},{8,9},{9,8},{10,11... | collective-permute-start | bytes 9224 | tf_op jit(solution)/shard_map/ppermute | solution.py:20
  4.9 0.7 %copy-done.2 = s32[4,4]{1,0:T(4,128)S(1)} copy-done((s32[4,4]{1,0:T(4,128)S(1)}, s32[4,4]{1,0:T(4,128)}, u32[]{:S(2)}) %copy-start.2) | copy-done | bytes 88
  5.9 3.0 %collective-permute-start.2 = (f32[2,6,128]{2,0,1:T(2,128)S(1)}, f32[2,6,128]{2,0,1:T(2,128)S(1)}, u32[]{:S(2)}, u32[]{:S(2)}) collective-permute-start(f32[2,6,128]{2,0,1:T(2,128)S(1)} %maximum_select_fusion.3), channel_id=1, source_target_pairs={{0,2},{1,3},{2,0},{3,1},{4,6},{5,7},{6,4},{7,5},{8,10},{9,11},{10,... | collective-permute-start | bytes 18440 | tf_op jit(solution)/shard_map/ppermute | solution.py:20
  9.0 1.6 %collective-permute-done.2 = f32[2,6,128]{2,0,1:T(2,128)S(1)} collective-permute-done((f32[2,6,128]{2,0,1:T(2,128)S(1)}, f32[2,6,128]{2,0,1:T(2,128)S(1)}, u32[]{:S(2)}, u32[]{:S(2)}) %collective-permute-start.2) | collective-permute-done | bytes 6176 | tf_op jit(solution)/shard_map/ppermute | solution.py:20
  10.6 2.2 %collective-permute-start.3 = (f32[4,6,128]{2,0,1:T(4,128)S(1)}, f32[4,6,128]{2,0,1:T(4,128)S(1)}, u32[]{:S(2)}, u32[]{:S(2)}) collective-permute-start(f32[4,6,128]{2,0,1:T(4,128)S(1)} %maximum_select_fusion.2), channel_id=1, source_target_pairs={{0,4},{1,5},{2,6},{3,7},{4,0},{5,1},{6,2},{7,3},{8,12},{9,13},{10,... | collective-permute-start | bytes 36872 | tf_op jit(solution)/shard_map/ppermute | solution.py:20
  13.6 1.1 %broadcast_select_fusion = f32[4,2048]{0,1:T(8,128)} fusion(f32[4,2048]{0,1:T(8,128)S(1)} %copy.47, f32[4,2048]{0,1:T(8,128)S(1)} %copy.48, pred[]{:T(512)S(6)} %eq.81), kind=kLoop, calls=%fused_computation.22 | loop fusion | flops 8192 | bytes 98305 | tf_op jit(solution)/shard_map/jit(_where)/select_n | solution.py:91
  14.7 2.3 %gather_fusion = f32[512,4]{1,0:T(8,128)S(1)} fusion(f32[4,2048]{0,1:T(8,128)} %broadcast_select_fusion, s32[1024]{0:T(1024)S(1)} %pad_clamp_fusion.1), kind=kCustom, calls=%fused_computation | custom fusion | bytes 18432 | tf_op jit(solution)/shard_map/jit(_take)/gather | solution.py:96
  17.1 0.6 %fusion.21 = (f32[512]{0:T(512)S(1)}, f32[512]{0:T(512)S(1)}, f32[512]{0:T(512)S(1)}, f32[512]{0:T(512)S(1)}) fusion(f32[4,512]{0,1:T(8,128)S(1)} %select_bitcast_fusion), kind=kLoop, calls=%fused_computation.31 | loop fusion | flops 2560 | bytes 16384 | tf_op jit(solution)/shard_map/div | solution.py:130
  17.8 2.7 %collective-permute-start.4 = (f32[8,6,128]{2,0,1:T(8,128)S(1)}, f32[8,6,128]{2,0,1:T(8,128)S(1)}, u32[]{:S(2)}, u32[]{:S(2)}) collective-permute-start(f32[8,6,128]{2,0,1:T(8,128)S(1)} %maximum_select_fusion.1), channel_id=1, source_target_pairs={{0,8},{1,9},{2,10},{3,11},{4,12},{5,13},{6,14},{7,15},{8,0},{9,1},... | collective-permute-start | bytes 73736 | tf_op jit(solution)/shard_map/ppermute | solution.py:20
  20.6 2.1 %collective-permute-done.4 = f32[8,6,128]{2,0,1:T(8,128)S(1)} collective-permute-done((f32[8,6,128]{2,0,1:T(8,128)S(1)}, f32[8,6,128]{2,0,1:T(8,128)S(1)}, u32[]{:S(2)}, u32[]{:S(2)}) %collective-permute-start.4) | collective-permute-done | bytes 24608 | tf_op jit(solution)/shard_map/ppermute | solution.py:20
  22.7 0.6 %gather_fusion.1 = f32[16,4,128]{2,1,0:T(4,128)S(1)} fusion(f32[8,4,128]{2,1,0:T(4,128)S(1)} %pad_maximum_fusion.2, s32[1024]{0:T(1024)S(1)} %pad_clamp_fusion), kind=kCustom, calls=%fused_computation.1 | custom fusion | bytes 65600 | tf_op jit(solution)/shard_map/jit(_take)/gather | solution.py:112
  23.4 2.2 %fusion.32 = (f32[4,4,128]{2,1,0:T(4,128)S(1)}, f32[4,128]{1,0:T(4,128)S(1)}) fusion(f32[4,128]{1,0:T(4,128)S(1)} %bitcast.113, f32[4,128]{1,0:T(4,128)S(1)} %bitcast.114, bf16[4,4,128,128]{3,2,1,0:T(8,128)(2,1)S(1)} %copy-done, s32[4,4,128]{2,1,0:T(4,128)S(1)} %get-tuple-element.19, s32[4,4,128]{2,1,0:T(4,128)S(1)} %get-tuple-element.18, ...), kind=kOutput, calls=%fused_computation.96 | convolution fusion | flops 71038464 | bytes 565264 | tf_op jit(solution)/shard_map/tkmi,tkip->tkmp/dot_general | solution.py:122
  26.1 1.1 %collective-permute-done.5 = f32[8,64]{1,0:T(8,128)S(1)} collective-permute-done((f32[8,64]{1,0:T(8,128)S(1)}, f32[8,64]{1,0:T(8,128)S(1)}, u32[]{:S(2)}, u32[]{:S(2)}) %collective-permute-start.5) | collective-permute-done | bytes 2080 | tf_op jit(solution)/shard_map/ppermute | solution.py:37
  27.2 1.7 %collective-permute-start.6 = (f32[4,64]{1,0:T(4,128)S(1)}, f32[4,64]{1,0:T(4,128)S(1)}, u32[]{:S(2)}, u32[]{:S(2)}) collective-permute-start(f32[4,64]{1,0:T(4,128)S(1)} %bitcast.120), channel_id=1, source_target_pairs={{0,2},{1,3},{2,0},{3,1},{4,6},{5,7},{6,4},{7,5},{8,10},{9,11},{10,... | collective-permute-start | bytes 3080 | tf_op jit(solution)/shard_map/ppermute | solution.py:37
  28.9 1.9 %collective-permute-done.6 = f32[4,64]{1,0:T(4,128)S(1)} collective-permute-done((f32[4,64]{1,0:T(4,128)S(1)}, f32[4,64]{1,0:T(4,128)S(1)}, u32[]{:S(2)}, u32[]{:S(2)}) %collective-permute-start.6) | collective-permute-done | bytes 1056 | tf_op jit(solution)/shard_map/ppermute | solution.py:37
  31.0 3.5 %collective-permute-done.7 = f32[2,64]{1,0:T(2,128)S(1)} collective-permute-done((f32[2,64]{1,0:T(2,128)S(1)}, f32[2,64]{1,0:T(2,128)S(1)}, u32[]{:S(2)}, u32[]{:S(2)}) %collective-permute-start.7) | collective-permute-done | bytes 544 | tf_op jit(solution)/shard_map/ppermute | solution.py:37
  34.5 2.7 %collective-permute-start.8 = (f32[1,64]{1,0:T(1,128)S(1)}, f32[1,64]{1,0:T(1,128)S(1)}, u32[]{:S(2)}, u32[]{:S(2)}) collective-permute-start(f32[1,64]{1,0:T(1,128)S(1)} %constant_dynamic-slice_fusion), channel_id=1, source_target_pairs={{0,8},{1,9},{2,10},{3,11},{4,12},{5,13},{6,14},{7,15},{8,0},{9,1},... | collective-permute-start | bytes 776 | tf_op jit(solution)/shard_map/ppermute | solution.py:37
  37.1 0.6 %bitcast_maximum_fusion = f32[512]{0:T(512)} fusion(f32[4,128]{1,0:T(4,128)S(1)} %get-tuple-element.3, f32[512]{0:T(512)S(1)} %get-tuple-element.4, pred[4]{0:T(512)(128)(4,1)S(1)} %not_reduce_fusion), kind=kLoop, calls=%fused_computation.72 | loop fusion | flops 1024 | bytes 6148 | tf_op jit(solution)/shard_map/max | solution.py:137
  37.8 1.2 %collective-permute-done.8 = f32[1,64]{1,0:T(1,128)S(1)} collective-permute-done((f32[1,64]{1,0:T(1,128)S(1)}, f32[1,64]{1,0:T(1,128)S(1)}, u32[]{:S(2)}, u32[]{:S(2)}) %collective-permute-start.8) | collective-permute-done | bytes 288 | tf_op jit(solution)/shard_map/ppermute | solution.py:37
  39.0 0.5 %fusion.30 = f32[1,64]{1,0:T(1,128)} fusion(f32[1,64]{1,0:T(1,128)S(1)} %collective-permute-done.8, f32[2,64]{1,0:T(2,128)S(1)} %max.34, s32[]{:T(128)S(6)} %select_n.183), kind=kLoop, calls=%fused_computation.91 | loop fusion | flops 64 | bytes 772 | tf_op jit(solution)/shard_map/max | solution.py:37
  (68 shorter events, 3.1 us)
Async XLA Ops:
  0.6 22.8 %copy-start = (bf16[4,4,128,128]{3,2,1,0:T(8,128)(2,1)S(1)}, bf16[4,4,128,128]{3,2,1,0:T(8,128)(2,1)}, u32[]{:S(2)}) copy-start(bf16[4,4,128,128]{3,2,1,0:T(8,128)(2,1)} %param.16) | copy-start | bytes 1572868
  0.6 0.7 %copy-start.1 = (f32[1024]{0:T(1024)S(1)}, f32[1024]{0:T(1024)}, u32[]{:S(2)}) copy-start(f32[1024]{0:T(1024)} %param.10) | copy-start | bytes 12292
  1.4 2.1 %copy-start.8 = (bf16[1,128,128]{2,1,0:T(8,128)(2,1)S(1)}, bf16[1,128,128]{2,1,0:T(8,128)(2,1)}, u32[]{:S(2)}) copy-start(bf16[1,128,128]{2,1,0:T(8,128)(2,1)} %param.18) | copy-start | bytes 98308
  2.1 0.7 %copy-start.7 = (s32[1,2,128]{2,1,0:T(2,128)S(1)}, s32[1,2,128]{2,1,0:T(2,128)}, u32[]{:S(2)}) copy-start(s32[1,2,128]{2,1,0:T(2,128)} %param.19) | copy-start | bytes 3076
  2.2 10.6 %collective-permute-start = (f32[4,1024]{1,0:T(4,128)S(1)}, f32[4,1024]{1,0:T(4,128)S(1)}, u32[]{:S(2)}, u32[]{:S(2)}) collective-permute-start(f32[4,1024]{1,0:T(4,128)S(1)} %pad_maximum_fusion.1), channel_id=1, source_target_pairs={{0,1},{1,0},{2,3},{3,2},{4,5},{5,4},{6,7},{7,6},{8,9},{9,8},{10,11... | collective-permute-start | bytes 49160 | tf_op jit(solution)/shard_map/ppermute | solution.py:88
  2.9 0.7 %copy-start.9 = (s32[1,128]{1,0:T(1,128)S(1)}, s32[1,128]{1,0:T(1,128)}, u32[]{:S(2)}) copy-start(s32[1,128]{1,0:T(1,128)} %param.17) | copy-start | bytes 1540
  4.2 0.7 %copy-start.6 = (s32[512]{0:T(512)S(1)}, s32[512]{0:T(512)}, u32[]{:S(2)}) copy-start(s32[512]{0:T(512)} %param.14) | copy-start | bytes 6148
  4.2 1.7 %collective-permute-start.1 = (f32[1,6,128]{2,0,1:T(1,128)S(1)}, f32[1,6,128]{2,0,1:T(1,128)S(1)}, u32[]{:S(2)}, u32[]{:S(2)}) collective-permute-start(f32[1,6,128]{2,0,1:T(1,128)S(1)} %broadcast_in_dim.134), channel_id=1, source_target_pairs={{0,1},{1,0},{2,3},{3,2},{4,5},{5,4},{6,7},{7,6},{8,9},{9,8},{10,11... | collective-permute-start | bytes 9224 | tf_op jit(solution)/shard_map/ppermute | solution.py:20
  4.9 0.7 %copy-start.2 = (s32[4,4]{1,0:T(4,128)S(1)}, s32[4,4]{1,0:T(4,128)}, u32[]{:S(2)}) copy-start(s32[4,4]{1,0:T(4,128)} %param.15) | copy-start | bytes 196
  5.9 4.6 %collective-permute-start.2 = (f32[2,6,128]{2,0,1:T(2,128)S(1)}, f32[2,6,128]{2,0,1:T(2,128)S(1)}, u32[]{:S(2)}, u32[]{:S(2)}) collective-permute-start(f32[2,6,128]{2,0,1:T(2,128)S(1)} %maximum_select_fusion.3), channel_id=1, source_target_pairs={{0,2},{1,3},{2,0},{3,1},{4,6},{5,7},{6,4},{7,5},{8,10},{9,11},{10,... | collective-permute-start | bytes 18440 | tf_op jit(solution)/shard_map/ppermute | solution.py:20
  9.0 3.8 %copy-start.3 = (f32[1024]{0:T(1024)S(1)}, f32[1024]{0:T(1024)}, u32[]{:S(2)}) copy-start(f32[1024]{0:T(1024)} %param.13) | copy-start | bytes 12292
  9.0 3.8 %copy-start.4 = (f32[1024]{0:T(1024)S(1)}, f32[1024]{0:T(1024)}, u32[]{:S(2)}) copy-start(f32[1024]{0:T(1024)} %param.12) | copy-start | bytes 12292
  9.0 3.8 %copy-start.5 = (f32[1024]{0:T(1024)S(1)}, f32[1024]{0:T(1024)}, u32[]{:S(2)}) copy-start(f32[1024]{0:T(1024)} %param.11) | copy-start | bytes 12292
  10.6 7.2 %collective-permute-start.3 = (f32[4,6,128]{2,0,1:T(4,128)S(1)}, f32[4,6,128]{2,0,1:T(4,128)S(1)}, u32[]{:S(2)}, u32[]{:S(2)}) collective-permute-start(f32[4,6,128]{2,0,1:T(4,128)S(1)} %maximum_select_fusion.2), channel_id=1, source_target_pairs={{0,4},{1,5},{2,6},{3,7},{4,0},{5,1},{6,2},{7,3},{8,12},{9,13},{10,... | collective-permute-start | bytes 36872 | tf_op jit(solution)/shard_map/ppermute | solution.py:20
  17.8 4.8 %collective-permute-start.4 = (f32[8,6,128]{2,0,1:T(8,128)S(1)}, f32[8,6,128]{2,0,1:T(8,128)S(1)}, u32[]{:S(2)}, u32[]{:S(2)}) collective-permute-start(f32[8,6,128]{2,0,1:T(8,128)S(1)} %maximum_select_fusion.1), channel_id=1, source_target_pairs={{0,8},{1,9},{2,10},{3,11},{4,12},{5,13},{6,14},{7,15},{8,0},{9,1},... | collective-permute-start | bytes 73736 | tf_op jit(solution)/shard_map/ppermute | solution.py:20
  25.9 1.2 %collective-permute-start.5 = (f32[8,64]{1,0:T(8,128)S(1)}, f32[8,64]{1,0:T(8,128)S(1)}, u32[]{:S(2)}, u32[]{:S(2)}) collective-permute-start(f32[8,64]{1,0:T(8,128)S(1)} %bitcast.118), channel_id=1, source_target_pairs={{0,1},{1,0},{2,3},{3,2},{4,5},{5,4},{6,7},{7,6},{8,9},{9,8},{10,11... | collective-permute-start | bytes 6152 | tf_op jit(solution)/shard_map/ppermute | solution.py:37
  27.2 3.6 %collective-permute-start.6 = (f32[4,64]{1,0:T(4,128)S(1)}, f32[4,64]{1,0:T(4,128)S(1)}, u32[]{:S(2)}, u32[]{:S(2)}) collective-permute-start(f32[4,64]{1,0:T(4,128)S(1)} %bitcast.120), channel_id=1, source_target_pairs={{0,2},{1,3},{2,0},{3,1},{4,6},{5,7},{6,4},{7,5},{8,10},{9,11},{10,... | collective-permute-start | bytes 3080 | tf_op jit(solution)/shard_map/ppermute | solution.py:37
  30.8 3.6 %collective-permute-start.7 = (f32[2,64]{1,0:T(2,128)S(1)}, f32[2,64]{1,0:T(2,128)S(1)}, u32[]{:S(2)}, u32[]{:S(2)}) collective-permute-start(f32[2,64]{1,0:T(2,128)S(1)} %bitcast.121), channel_id=1, source_target_pairs={{0,4},{1,5},{2,6},{3,7},{4,0},{5,1},{6,2},{7,3},{8,12},{9,13},{10,... | collective-permute-start | bytes 1544 | tf_op jit(solution)/shard_map/ppermute | solution.py:37
  34.5 4.5 %collective-permute-start.8 = (f32[1,64]{1,0:T(1,128)S(1)}, f32[1,64]{1,0:T(1,128)S(1)}, u32[]{:S(2)}, u32[]{:S(2)}) collective-permute-start(f32[1,64]{1,0:T(1,128)S(1)} %constant_dynamic-slice_fusion), channel_id=1, source_target_pairs={{0,8},{1,9},{2,10},{3,11},{4,12},{5,13},{6,14},{7,15},{8,0},{9,1},... | collective-permute-start | bytes 776 | tf_op jit(solution)/shard_map/ppermute | solution.py:37

commit v4 on v3

--- a/solution.py
+++ b/solution.py
@@ -84,19 +84,18 @@
     )
     known = gather_doubling(packed, both).reshape(blocks, halves, 6, pair_count)
 
-    state_local = jnp.stack([base_real, base_reactive, voltage, rating])
+    state_local = jnp.stack(
+        [base_real, base_reactive * base_reactive, voltage * rating], axis=1
+    )
     other_half = lax.ppermute(
         state_local, "state", [(j, (j + 1) % halves) for j in range(halves)]
     )
-    state_pos = jnp.where(
-        me_state == 0,
-        jnp.concatenate([state_local, other_half], axis=1),
-        jnp.concatenate([other_half, state_local], axis=1),
-    )
-    mon_vals = jnp.take(state_pos, monitored, axis=1).reshape(4, tiles_dev, tile_size)
-    mon_real = mon_vals[0]
-    react_sq = mon_vals[1] * mon_vals[1]
-    mon_limit = mon_vals[2] * mon_vals[3]
+    state_pos = jnp.concatenate([state_local, other_half])
+    mon_at = (monitored - me_state * half_len) % (halves * half_len)
+    mon_vals = jnp.take(state_pos, mon_at, axis=0, mode="clip")
+    mon_real = mon_vals[:, 0].reshape(tiles_dev, tile_size)
+    react_sq = mon_vals[:, 1].reshape(tiles_dev, tile_size)
+    mon_limit = mon_vals[:, 2].reshape(tiles_dev, tile_size)
 
     flow_first = jnp.sum(known[:, :, 0], axis=1)
     flow_second = jnp.sum(known[:, :, 1], axis=1)

time: 39.8 us -> 36.2 us (0.910)
  local copies, waits for them, and re-layouts: 6.11 us -> 3.75 us
  waiting for transfers between devices: 11.4 us -> 9.95 us
  starting transfers between devices: 13.6 us -> 15 us
  other arithmetic: 4.62 us -> 3.33 us
    ppermute x4, waiting for transfers between devices: 7.73 us -> 6.31 us  [scatter_max(): lax.ppermute(send, axes, [(j, j ^ bit) for j in range(n)])]
    ppermute x4, starting transfers between devices: 4.61 us -> 6.02 us  [scatter_max(): lax.ppermute(send, axes, [(j, j ^ bit) for j in range(n)])]
    select_n x3 -> x1, other arithmetic: 1.24 us -> 0.01 us  [body(): mon_at = (monitored - me_state * half_len) % (halves * half_len)]
    gather x1, local copies, waits for them, and re-layouts: 2.25 us -> 1.04 us  [body(): mon_vals = jnp.take(state_pos, mon_at, axis=0, mode='clip')]
    unnamed x20 -> x18, local copies, waits for them, and re-layouts: 2.31 us -> 1.54 us
    mul x0 -> x2, other arithmetic: none -> 0.77 us  [the longest x1 0.77 us: body(): base_reactive * base_reactive]
    another operation x2, other arithmetic: 0.83 us -> 0.1 us  [the longest x1 0.75 us: body(): state_local = jnp.stack([base_real, base_reactive, voltage, rating])]
  transfers between devices with their start and end apart: 9 -> 9, of which waited for: 6 -> 6; matrix products, arithmetic and copies ran while one was open for 17% -> 11% of each run, Pallas kernels for 0% -> 0%
where the time goes in v4:
time: 36.2 us; the launch traced here: 35.9 us
  starting transfers between devices  15 us (41%)
  waiting for transfers between devices  9.95 us (27%)
  local copies, waits for them, and re-layouts  3.75 us (10%)
  other arithmetic  3.33 us (9%)
  matrix products  2.87 us (8%)
  between operations  0.98 us (3%)
    ppermute x4, starting transfers between devices, gather_doubling(): other = lax.ppermute(cur, axes, [(j, j ^ bit) for j in range(n)])  8.44 us
    ppermute x4, waiting for transfers between devices, scatter_max(): lax.ppermute(send, axes, [(j, j ^ bit) for j in range(n)])  6.31 us
    ppermute x4, starting transfers between devices, scatter_max(): lax.ppermute(send, axes, [(j, j ^ bit) for j in range(n)])  6.02 us
    ppermute x4, waiting for transfers between devices, gather_doubling(): other = lax.ppermute(cur, axes, [(j, j ^ bit) for j in range(n)])  3.63 us
    dot_general x1, matrix products, body(): jnp.einsum('tkmi,tkip->tkmp', tile_values, weights, preferred_element_typ...  2.22 us
    unnamed x18, local copies, waits for them, and re-layouts  1.54 us
    gather x1, local copies, waits for them, and re-layouts, body(): mon_vals = jnp.take(state_pos, mon_at, axis=0, mode='clip')  1.04 us
    mul x1, other arithmetic, body(): base_reactive * base_reactive  0.77 us
  transfers between devices with their start and end apart: 9, of which 6 were waited for; matrix products, arithmetic and copies ran while one was open for 11% of the time, Pallas kernels for 0%

profile of v4, /device:TPU:0, one launch (start us, length us, event | category | flops | bytes accessed | tf_op | source)
XLA Modules:
  0.0 35.9 jit_solution(10343681183967739155)
XLA Ops:
  0.7 0.8 %mul.63 = f32[1024]{0:T(1024)S(1)} multiply(f32[1024]{0:T(1024)} %param.11, f32[1024]{0:T(1024)} %param.11) | non-fusion elementwise | flops 1024 | bytes 12288 | tf_op jit(solution)/shard_map/mul | solution.py:88
  1.5 0.7 %copy-done.1 = f32[1024]{0:T(1024)S(1)} copy-done((f32[1024]{0:T(1024)S(1)}, f32[1024]{0:T(1024)}, u32[]{:S(2)}) %copy-start.1) | copy-done | bytes 4120
  2.2 0.6 %collective-permute-start = (f32[1024,3]{0,1:T(4,128)S(1)}, f32[1024,3]{0,1:T(4,128)S(1)}, u32[]{:S(2)}, u32[]{:S(2)}) collective-permute-start(f32[1024,3]{0,1:T(4,128)S(1)} %pad_maximum_fusion.1), channel_id=1, source_target_pairs={{0,1},{1,0},{2,3},{3,2},{4,5},{5,4},{6,7},{7,6},{8,9},{9,8},{10,11... | collective-permute-start | bytes 36872 | tf_op jit(solution)/shard_map/ppermute | solution.py:90
  3.2 0.4 %fusion.10 = f32[1,256]{1,0:T(1,128)S(1)} fusion(bf16[1024,1]{0,1:T(2,128)(2,1)S(1)} %reshape.166, s32[128]{0:T(128)S(1)} %subtract_bitcast_fusion, s32[256]{0:T(256)S(1)} %get-tuple-element.30), kind=kOutput, calls=%fused_computation.17 | convolution fusion | flops 491648 | bytes 4608 | tf_op jit(solution)/shard_map/dot_general | solution.py:75
  3.6 0.6 %collective-permute-start.1 = (f32[1,6,128]{2,0,1:T(1,128)S(1)}, f32[1,6,128]{2,0,1:T(1,128)S(1)}, u32[]{:S(2)}, u32[]{:S(2)}) collective-permute-start(f32[1,6,128]{2,0,1:T(1,128)S(1)} %broadcast_in_dim.122), channel_id=1, source_target_pairs={{0,1},{1,0},{2,3},{3,2},{4,5},{5,4},{6,7},{7,6},{8,9},{9,8},{10,11... | collective-permute-start | bytes 9224 | tf_op jit(solution)/shard_map/ppermute | solution.py:20
  4.4 0.6 %copy-done.6 = s32[512]{0:T(512)S(1)} copy-done((s32[512]{0:T(512)S(1)}, s32[512]{0:T(512)}, u32[]{:S(2)}) %copy-start.6) | copy-done | bytes 2072
  5.3 3.0 %collective-permute-start.2 = (f32[2,6,128]{2,0,1:T(2,128)S(1)}, f32[2,6,128]{2,0,1:T(2,128)S(1)}, u32[]{:S(2)}, u32[]{:S(2)}) collective-permute-start(f32[2,6,128]{2,0,1:T(2,128)S(1)} %maximum_select_fusion.3), channel_id=1, source_target_pairs={{0,2},{1,3},{2,0},{3,1},{4,6},{5,7},{6,4},{7,5},{8,10},{9,11},{10,... | collective-permute-start | bytes 18440 | tf_op jit(solution)/shard_map/ppermute | solution.py:20
  8.3 1.6 %collective-permute-done.2 = f32[2,6,128]{2,0,1:T(2,128)S(1)} collective-permute-done((f32[2,6,128]{2,0,1:T(2,128)S(1)}, f32[2,6,128]{2,0,1:T(2,128)S(1)}, u32[]{:S(2)}, u32[]{:S(2)}) %collective-permute-start.2) | collective-permute-done | bytes 6176 | tf_op jit(solution)/shard_map/ppermute | solution.py:20
  9.9 2.2 %collective-permute-start.3 = (f32[4,6,128]{2,0,1:T(4,128)S(1)}, f32[4,6,128]{2,0,1:T(4,128)S(1)}, u32[]{:S(2)}, u32[]{:S(2)}) collective-permute-start(f32[4,6,128]{2,0,1:T(4,128)S(1)} %maximum_select_fusion.2), channel_id=1, source_target_pairs={{0,4},{1,5},{2,6},{3,7},{4,0},{5,1},{6,2},{7,3},{8,12},{9,13},{10,... | collective-permute-start | bytes 36872 | tf_op jit(solution)/shard_map/ppermute | solution.py:20
  12.5 1.0 %gather_fusion = f32[512,3]{1,0:T(8,128)S(1)} fusion(f32[2048,3]{1,0:T(8,128)S(1)} %copy.43, s32[1024]{0:T(1024)S(1)} %pad_clamp_fusion.1), kind=kCustom, calls=%fused_computation | custom fusion | bytes 14336 | tf_op jit(solution)/shard_map/jit(_take)/gather | solution.py:95
  13.5 0.5 %fusion.21 = (f32[512]{0:T(512)S(1)}, f32[512]{0:T(512)S(1)}, f32[512]{0:T(512)S(1)}, f32[512]{0:T(512)S(1)}) fusion(f32[512,3]{1,0:T(8,128)S(1)} %gather_fusion), kind=kLoop, calls=%fused_computation.27 | loop fusion | flops 1536 | bytes 14336 | tf_op jit(solution)/shard_map/div | solution.py:129
  14.2 2.7 %collective-permute-start.4 = (f32[8,6,128]{2,0,1:T(8,128)S(1)}, f32[8,6,128]{2,0,1:T(8,128)S(1)}, u32[]{:S(2)}, u32[]{:S(2)}) collective-permute-start(f32[8,6,128]{2,0,1:T(8,128)S(1)} %maximum_select_fusion.1), channel_id=1, source_target_pairs={{0,8},{1,9},{2,10},{3,11},{4,12},{5,13},{6,14},{7,15},{8,0},{9,1},... | collective-permute-start | bytes 73736 | tf_op jit(solution)/shard_map/ppermute | solution.py:20
  17.0 2.0 %collective-permute-done.4 = f32[8,6,128]{2,0,1:T(8,128)S(1)} collective-permute-done((f32[8,6,128]{2,0,1:T(8,128)S(1)}, f32[8,6,128]{2,0,1:T(8,128)S(1)}, u32[]{:S(2)}, u32[]{:S(2)}) %collective-permute-start.4) | collective-permute-done | bytes 24608 | tf_op jit(solution)/shard_map/ppermute | solution.py:20
  19.1 0.6 %gather_fusion.1 = f32[16,4,128]{2,1,0:T(4,128)S(1)} fusion(f32[8,4,128]{2,1,0:T(4,128)S(1)} %pad_maximum_fusion.2, s32[1024]{0:T(1024)S(1)} %pad_clamp_fusion), kind=kCustom, calls=%fused_computation.1 | custom fusion | bytes 65600 | tf_op jit(solution)/shard_map/jit(_take)/gather | solution.py:111
  19.8 2.2 %fusion.31 = (f32[4,4,128]{2,1,0:T(4,128)S(1)}, f32[4,128]{1,0:T(4,128)S(1)}) fusion(f32[4,128]{1,0:T(4,128)S(1)} %bitcast.110, f32[4,128]{1,0:T(4,128)S(1)} %bitcast.108, bf16[4,4,128,128]{3,2,1,0:T(8,128)(2,1)S(1)} %copy-done, s32[4,4,128]{2,1,0:T(4,128)S(1)} %get-tuple-element.19, s32[4,4,128]{2,1,0:T(4,128)S(1)} %get-tuple-element.18, ...), kind=kOutput, calls=%fused_computation.93 | convolution fusion | flops 71038464 | bytes 565264 | tf_op jit(solution)/shard_map/tkmi,tkip->tkmp/dot_general | solution.py:121
  22.4 1.1 %collective-permute-done.5 = f32[8,64]{1,0:T(8,128)S(1)} collective-permute-done((f32[8,64]{1,0:T(8,128)S(1)}, f32[8,64]{1,0:T(8,128)S(1)}, u32[]{:S(2)}, u32[]{:S(2)}) %collective-permute-start.5) | collective-permute-done | bytes 2080 | tf_op jit(solution)/shard_map/ppermute | solution.py:37
  23.5 1.6 %collective-permute-start.6 = (f32[4,64]{1,0:T(4,128)S(1)}, f32[4,64]{1,0:T(4,128)S(1)}, u32[]{:S(2)}, u32[]{:S(2)}) collective-permute-start(f32[4,64]{1,0:T(4,128)S(1)} %bitcast.115), channel_id=1, source_target_pairs={{0,2},{1,3},{2,0},{3,1},{4,6},{5,7},{6,4},{7,5},{8,10},{9,11},{10,... | collective-permute-start | bytes 3080 | tf_op jit(solution)/shard_map/ppermute | solution.py:37
  25.1 2.1 %collective-permute-done.6 = f32[4,64]{1,0:T(4,128)S(1)} collective-permute-done((f32[4,64]{1,0:T(4,128)S(1)}, f32[4,64]{1,0:T(4,128)S(1)}, u32[]{:S(2)}, u32[]{:S(2)}) %collective-permute-start.6) | collective-permute-done | bytes 1056 | tf_op jit(solution)/shard_map/ppermute | solution.py:37
  27.2 1.7 %collective-permute-start.7 = (f32[2,64]{1,0:T(2,128)S(1)}, f32[2,64]{1,0:T(2,128)S(1)}, u32[]{:S(2)}, u32[]{:S(2)}) collective-permute-start(f32[2,64]{1,0:T(2,128)S(1)} %bitcast.116), channel_id=1, source_target_pairs={{0,4},{1,5},{2,6},{3,7},{4,0},{5,1},{6,2},{7,3},{8,12},{9,13},{10,... | collective-permute-start | bytes 1544 | tf_op jit(solution)/shard_map/ppermute | solution.py:37
  28.9 2.0 %collective-permute-done.7 = f32[2,64]{1,0:T(2,128)S(1)} collective-permute-done((f32[2,64]{1,0:T(2,128)S(1)}, f32[2,64]{1,0:T(2,128)S(1)}, u32[]{:S(2)}, u32[]{:S(2)}) %collective-permute-start.7) | collective-permute-done | bytes 544 | tf_op jit(solution)/shard_map/ppermute | solution.py:37
  30.9 2.7 %collective-permute-start.8 = (f32[1,64]{1,0:T(1,128)S(1)}, f32[1,64]{1,0:T(1,128)S(1)}, u32[]{:S(2)}, u32[]{:S(2)}) collective-permute-start(f32[1,64]{1,0:T(1,128)S(1)} %constant_dynamic-slice_fusion), channel_id=1, source_target_pairs={{0,8},{1,9},{2,10},{3,11},{4,12},{5,13},{6,14},{7,15},{8,0},{9,1},... | collective-permute-start | bytes 776 | tf_op jit(solution)/shard_map/ppermute | solution.py:37
  33.6 0.6 %bitcast_maximum_fusion = f32[512]{0:T(512)} fusion(f32[4,128]{1,0:T(4,128)S(1)} %get-tuple-element.3, f32[512]{0:T(512)S(1)} %get-tuple-element.4, pred[4]{0:T(512)(128)(4,1)S(1)} %not_reduce_fusion), kind=kLoop, calls=%fused_computation.70 | loop fusion | flops 1024 | bytes 6148 | tf_op jit(solution)/shard_map/max | solution.py:136
  34.2 1.2 %collective-permute-done.8 = f32[1,64]{1,0:T(1,128)S(1)} collective-permute-done((f32[1,64]{1,0:T(1,128)S(1)}, f32[1,64]{1,0:T(1,128)S(1)}, u32[]{:S(2)}, u32[]{:S(2)}) %collective-permute-start.8) | collective-permute-done | bytes 288 | tf_op jit(solution)/shard_map/ppermute | solution.py:37
  35.4 0.5 %fusion.29 = f32[1,64]{1,0:T(1,128)} fusion(f32[1,64]{1,0:T(1,128)S(1)} %collective-permute-done.8, f32[2,64]{1,0:T(2,128)S(1)} %max.34, s32[]{:T(128)S(6)} %select_n.169), kind=kLoop, calls=%fused_computation.88 | loop fusion | flops 64 | bytes 772 | tf_op jit(solution)/shard_map/max | solution.py:37
  (64 shorter events, 2.1 us)
Async XLA Ops:
  0.6 19.2 %copy-start = (bf16[4,4,128,128]{3,2,1,0:T(8,128)(2,1)S(1)}, bf16[4,4,128,128]{3,2,1,0:T(8,128)(2,1)}, u32[]{:S(2)}) copy-start(bf16[4,4,128,128]{3,2,1,0:T(8,128)(2,1)} %param.16) | copy-start | bytes 1572868
  0.6 0.8 %copy-start.3 = (f32[1024]{0:T(1024)S(1)}, f32[1024]{0:T(1024)}, u32[]{:S(2)}) copy-start(f32[1024]{0:T(1024)} %param.12) | copy-start | bytes 12292
  0.7 0.8 %copy-start.4 = (f32[1024]{0:T(1024)S(1)}, f32[1024]{0:T(1024)}, u32[]{:S(2)}) copy-start(f32[1024]{0:T(1024)} %param.13) | copy-start | bytes 12292
  1.4 0.7 %copy-start.1 = (f32[1024]{0:T(1024)S(1)}, f32[1024]{0:T(1024)}, u32[]{:S(2)}) copy-start(f32[1024]{0:T(1024)} %param.10) | copy-start | bytes 12292
  2.1 0.8 %copy-start.8 = (s32[1,128]{1,0:T(1,128)S(1)}, s32[1,128]{1,0:T(1,128)}, u32[]{:S(2)}) copy-start(s32[1,128]{1,0:T(1,128)} %param.17) | copy-start | bytes 1540
  2.2 0.7 %copy-start.5 = (s32[1,2,128]{2,1,0:T(2,128)S(1)}, s32[1,2,128]{2,1,0:T(2,128)}, u32[]{:S(2)}) copy-start(s32[1,2,128]{2,1,0:T(2,128)} %param.19) | copy-start | bytes 3076
  2.2 0.8 %copy-start.7 = (bf16[1,128,128]{2,1,0:T(8,128)(2,1)S(1)}, bf16[1,128,128]{2,1,0:T(8,128)(2,1)}, u32[]{:S(2)}) copy-start(bf16[1,128,128]{2,1,0:T(8,128)(2,1)} %param.18) | copy-start | bytes 98308
  2.2 9.9 %collective-permute-start = (f32[1024,3]{0,1:T(4,128)S(1)}, f32[1024,3]{0,1:T(4,128)S(1)}, u32[]{:S(2)}, u32[]{:S(2)}) collective-permute-start(f32[1024,3]{0,1:T(4,128)S(1)} %pad_maximum_fusion.1), channel_id=1, source_target_pairs={{0,1},{1,0},{2,3},{3,2},{4,5},{5,4},{6,7},{7,6},{8,9},{9,8},{10,11... | collective-permute-start | bytes 36872 | tf_op jit(solution)/shard_map/ppermute | solution.py:90
  3.6 0.7 %copy-start.2 = (s32[4,4]{1,0:T(4,128)S(1)}, s32[4,4]{1,0:T(4,128)}, u32[]{:S(2)}) copy-start(s32[4,4]{1,0:T(4,128)} %param.15) | copy-start | bytes 196
  3.6 1.6 %collective-permute-start.1 = (f32[1,6,128]{2,0,1:T(1,128)S(1)}, f32[1,6,128]{2,0,1:T(1,128)S(1)}, u32[]{:S(2)}, u32[]{:S(2)}) collective-permute-start(f32[1,6,128]{2,0,1:T(1,128)S(1)} %broadcast_in_dim.122), channel_id=1, source_target_pairs={{0,1},{1,0},{2,3},{3,2},{4,5},{5,4},{6,7},{7,6},{8,9},{9,8},{10,11... | collective-permute-start | bytes 9224 | tf_op jit(solution)/shard_map/ppermute | solution.py:20
  4.3 0.7 %copy-start.6 = (s32[512]{0:T(512)S(1)}, s32[512]{0:T(512)}, u32[]{:S(2)}) copy-start(s32[512]{0:T(512)} %param.14) | copy-start | bytes 6148
  5.3 4.6 %collective-permute-start.2 = (f32[2,6,128]{2,0,1:T(2,128)S(1)}, f32[2,6,128]{2,0,1:T(2,128)S(1)}, u32[]{:S(2)}, u32[]{:S(2)}) collective-permute-start(f32[2,6,128]{2,0,1:T(2,128)S(1)} %maximum_select_fusion.3), channel_id=1, source_target_pairs={{0,2},{1,3},{2,0},{3,1},{4,6},{5,7},{6,4},{7,5},{8,10},{9,11},{10,... | collective-permute-start | bytes 18440 | tf_op jit(solution)/shard_map/ppermute | solution.py:20
  9.9 4.2 %collective-permute-start.3 = (f32[4,6,128]{2,0,1:T(4,128)S(1)}, f32[4,6,128]{2,0,1:T(4,128)S(1)}, u32[]{:S(2)}, u32[]{:S(2)}) collective-permute-start(f32[4,6,128]{2,0,1:T(4,128)S(1)} %maximum_select_fusion.2), channel_id=1, source_target_pairs={{0,4},{1,5},{2,6},{3,7},{4,0},{5,1},{6,2},{7,3},{8,12},{9,13},{10,... | collective-permute-start | bytes 36872 | tf_op jit(solution)/shard_map/ppermute | solution.py:20
  14.2 4.8 %collective-permute-start.4 = (f32[8,6,128]{2,0,1:T(8,128)S(1)}, f32[8,6,128]{2,0,1:T(8,128)S(1)}, u32[]{:S(2)}, u32[]{:S(2)}) collective-permute-start(f32[8,6,128]{2,0,1:T(8,128)S(1)} %maximum_select_fusion.1), channel_id=1, source_target_pairs={{0,8},{1,9},{2,10},{3,11},{4,12},{5,13},{6,14},{7,15},{8,0},{9,1},... | collective-permute-start | bytes 73736 | tf_op jit(solution)/shard_map/ppermute | solution.py:20
  22.3 1.2 %collective-permute-start.5 = (f32[8,64]{1,0:T(8,128)S(1)}, f32[8,64]{1,0:T(8,128)S(1)}, u32[]{:S(2)}, u32[]{:S(2)}) collective-permute-start(f32[8,64]{1,0:T(8,128)S(1)} %bitcast.113), channel_id=1, source_target_pairs={{0,1},{1,0},{2,3},{3,2},{4,5},{5,4},{6,7},{7,6},{8,9},{9,8},{10,11... | collective-permute-start | bytes 6152 | tf_op jit(solution)/shard_map/ppermute | solution.py:37
  23.5 3.6 %collective-permute-start.6 = (f32[4,64]{1,0:T(4,128)S(1)}, f32[4,64]{1,0:T(4,128)S(1)}, u32[]{:S(2)}, u32[]{:S(2)}) collective-permute-start(f32[4,64]{1,0:T(4,128)S(1)} %bitcast.115), channel_id=1, source_target_pairs={{0,2},{1,3},{2,0},{3,1},{4,6},{5,7},{6,4},{7,5},{8,10},{9,11},{10,... | collective-permute-start | bytes 3080 | tf_op jit(solution)/shard_map/ppermute | solution.py:37
  27.2 3.6 %collective-permute-start.7 = (f32[2,64]{1,0:T(2,128)S(1)}, f32[2,64]{1,0:T(2,128)S(1)}, u32[]{:S(2)}, u32[]{:S(2)}) collective-permute-start(f32[2,64]{1,0:T(2,128)S(1)} %bitcast.116), channel_id=1, source_target_pairs={{0,4},{1,5},{2,6},{3,7},{4,0},{5,1},{6,2},{7,3},{8,12},{9,13},{10,... | collective-permute-start | bytes 1544 | tf_op jit(solution)/shard_map/ppermute | solution.py:37
  30.9 4.5 %collective-permute-start.8 = (f32[1,64]{1,0:T(1,128)S(1)}, f32[1,64]{1,0:T(1,128)S(1)}, u32[]{:S(2)}, u32[]{:S(2)}) collective-permute-start(f32[1,64]{1,0:T(1,128)S(1)} %constant_dynamic-slice_fusion), channel_id=1, source_target_pairs={{0,8},{1,9},{2,10},{3,11},{4,12},{5,13},{6,14},{7,15},{8,0},{9,1},... | collective-permute-start | bytes 776 | tf_op jit(solution)/shard_map/ppermute | solution.py:37

commit v5 on v4

--- a/solution.py
+++ b/solution.py
@@ -121,29 +121,32 @@
     delta = jnp.einsum(
         "tkmi,tkip->tkmp", tile_values, weights, preferred_element_type=jnp.float32
     )
+    inv_limit_sq = 1.0 / (mon_limit * mon_limit)
     post = mon_real[:, None, :, None] + delta
-    loading = jnp.sqrt(post * post + react_sq[:, None, :, None]) / mon_limit[:, None, :, None]
+    squared = (post * post + react_sq[:, None, :, None]) * inv_limit_sq[:, None, :, None]
     neg = jnp.float32(-jnp.inf)
-    loading = jnp.where(valid[:, :, None, None], loading, neg)
+    squared = jnp.where(valid[:, :, None, None], squared, neg)
 
-    base_load = jnp.sqrt(mon_real * mon_real + react_sq) / mon_limit
+    base_sq = (mon_real * mon_real + react_sq) * inv_limit_sq
     block_iota = jnp.arange(blocks, dtype=jnp.int32)
     matches = tile_ids[:, :, None] == block_iota[None, None, :]
     absent = jnp.logical_not(jnp.any(matches, axis=1))
     any_absent = jnp.any(absent, axis=1)
 
-    peak_load = jnp.max(loading, axis=(1, 3))
-    peak_load = jnp.maximum(peak_load, jnp.where(any_absent[:, None], base_load, neg))
+    peak_sq = jnp.max(squared, axis=(1, 3))
+    peak_sq = jnp.maximum(peak_sq, jnp.where(any_absent[:, None], base_sq, neg))
+    peak_load = jnp.sqrt(peak_sq)
 
-    col_max = jnp.max(loading, axis=2)
+    col_max = jnp.max(squared, axis=2)
     worst_local = jnp.max(
         jnp.where(matches[:, :, :, None], col_max[:, :, None, :], neg), axis=(0, 1)
     )
-    base_max = jnp.max(base_load, axis=1)
+    base_max = jnp.max(base_sq, axis=1)
     absent_max = jnp.max(jnp.where(absent, base_max[:, None], neg), axis=0)
     worst_local = jnp.maximum(worst_local, absent_max[:, None])
 
-    worst_own = scatter_max(worst_local.reshape(blocks * halves, half_width), both)[None, :]
+    worst_sq = scatter_max(worst_local.reshape(blocks * halves, half_width), both)
+    worst_own = jnp.sqrt(worst_sq)[None, :]
     return (peak_load.reshape(-1), worst_own)
 
 

time: 36.2 us -> 36.1 us (level)
    sqrt x0 -> x2, other arithmetic: none -> 1.18 us  [the longest x1 0.66 us: body(): peak_load = jnp.sqrt(peak_sq)]
    max x1 -> x0, other arithmetic: 0.65 us -> none  [body(): jnp.maximum(peak_load, jnp.where(any_absent[:, None], base_load, neg))]
    max x4 -> x3, other arithmetic: 0.53 us -> 0.01 us  [scatter_max(): jnp.maximum(keep, lax.ppermute(send, axes, [(j, j ^ bit) for j in range(n...]
    mul x0 -> x1, other arithmetic: none -> 0.51 us  [body(): base_sq = (mon_real * mon_real + react_sq) * inv_limit_sq]
    div x1 -> x0, other arithmetic: 0.51 us -> none  [body(): base_load = jnp.sqrt(mon_real * mon_real + react_sq) / mon_limit]
where the time goes in v5:
time: 36.1 us; the launch traced here: 35.9 us
  starting transfers between devices  15.1 us (42%)
  waiting for transfers between devices  9.9 us (27%)
  local copies, waits for them, and re-layouts  3.75 us (10%)
  other arithmetic  3.34 us (9%)
  matrix products  2.84 us (8%)
  between operations  0.98 us (3%)
    ppermute x4, starting transfers between devices, gather_doubling(): other = lax.ppermute(cur, axes, [(j, j ^ bit) for j in range(n)])  8.45 us
    ppermute x4, waiting for transfers between devices, scatter_max(): lax.ppermute(send, axes, [(j, j ^ bit) for j in range(n)])  6.28 us
    ppermute x4, starting transfers between devices, scatter_max(): lax.ppermute(send, axes, [(j, j ^ bit) for j in range(n)])  6.05 us
    ppermute x4, waiting for transfers between devices, gather_doubling(): other = lax.ppermute(cur, axes, [(j, j ^ bit) for j in range(n)])  3.62 us
    dot_general x1, matrix products, body(): jnp.einsum('tkmi,tkip->tkmp', tile_values, weights, preferred_element_typ...  2.19 us
    unnamed x18, local copies, waits for them, and re-layouts  1.54 us
    gather x1, local copies, waits for them, and re-layouts, body(): mon_vals = jnp.take(state_pos, mon_at, axis=0, mode='clip')  1.04 us
    mul x1, other arithmetic, body(): base_reactive * base_reactive  0.77 us
  transfers between devices with their start and end apart: 9, of which 6 were waited for; matrix products, arithmetic and copies ran while one was open for 11% of the time, Pallas kernels for 0%

profile of v5, /device:TPU:0, one launch (start us, length us, event | category | flops | bytes accessed | tf_op | source)
XLA Modules:
  0.0 35.9 jit_solution(9242651678964031936)
XLA Ops:
  0.7 0.8 %mul.101 = f32[1024]{0:T(1024)S(1)} multiply(f32[1024]{0:T(1024)} %param.11, f32[1024]{0:T(1024)} %param.11) | non-fusion elementwise | flops 1024 | bytes 12288 | tf_op jit(solution)/shard_map/mul | solution.py:88
  1.5 0.7 %copy-done.1 = f32[1024]{0:T(1024)S(1)} copy-done((f32[1024]{0:T(1024)S(1)}, f32[1024]{0:T(1024)}, u32[]{:S(2)}) %copy-start.1) | copy-done | bytes 4120
  2.2 0.6 %collective-permute-start = (f32[1024,3]{0,1:T(4,128)S(1)}, f32[1024,3]{0,1:T(4,128)S(1)}, u32[]{:S(2)}, u32[]{:S(2)}) collective-permute-start(f32[1024,3]{0,1:T(4,128)S(1)} %pad_maximum_fusion.1), channel_id=1, source_target_pairs={{0,1},{1,0},{2,3},{3,2},{4,5},{5,4},{6,7},{7,6},{8,9},{9,8},{10,11... | collective-permute-start | bytes 36872 | tf_op jit(solution)/shard_map/ppermute | solution.py:90
  3.2 0.4 %fusion.9 = f32[1,256]{1,0:T(1,128)S(1)} fusion(bf16[1024,1]{0,1:T(2,128)(2,1)S(1)} %reshape.176, s32[128]{0:T(128)S(1)} %subtract_bitcast_fusion, s32[256]{0:T(256)S(1)} %get-tuple-element.30), kind=kOutput, calls=%fused_computation.16 | convolution fusion | flops 491648 | bytes 4608 | tf_op jit(solution)/shard_map/dot_general | solution.py:75
  3.6 0.6 %collective-permute-start.1 = (f32[1,6,128]{2,0,1:T(1,128)S(1)}, f32[1,6,128]{2,0,1:T(1,128)S(1)}, u32[]{:S(2)}, u32[]{:S(2)}) collective-permute-start(f32[1,6,128]{2,0,1:T(1,128)S(1)} %broadcast_in_dim.124), channel_id=1, source_target_pairs={{0,1},{1,0},{2,3},{3,2},{4,5},{5,4},{6,7},{7,6},{8,9},{9,8},{10,11... | collective-permute-start | bytes 9224 | tf_op jit(solution)/shard_map/ppermute | solution.py:20
  4.4 0.6 %copy-done.6 = s32[512]{0:T(512)S(1)} copy-done((s32[512]{0:T(512)S(1)}, s32[512]{0:T(512)}, u32[]{:S(2)}) %copy-start.6) | copy-done | bytes 2072
  5.3 3.0 %collective-permute-start.2 = (f32[2,6,128]{2,0,1:T(2,128)S(1)}, f32[2,6,128]{2,0,1:T(2,128)S(1)}, u32[]{:S(2)}, u32[]{:S(2)}) collective-permute-start(f32[2,6,128]{2,0,1:T(2,128)S(1)} %maximum_select_fusion.3), channel_id=1, source_target_pairs={{0,2},{1,3},{2,0},{3,1},{4,6},{5,7},{6,4},{7,5},{8,10},{9,11},{10,... | collective-permute-start | bytes 18440 | tf_op jit(solution)/shard_map/ppermute | solution.py:20
  8.3 1.6 %collective-permute-done.2 = f32[2,6,128]{2,0,1:T(2,128)S(1)} collective-permute-done((f32[2,6,128]{2,0,1:T(2,128)S(1)}, f32[2,6,128]{2,0,1:T(2,128)S(1)}, u32[]{:S(2)}, u32[]{:S(2)}) %collective-permute-start.2) | collective-permute-done | bytes 6176 | tf_op jit(solution)/shard_map/ppermute | solution.py:20
  9.9 2.2 %collective-permute-start.3 = (f32[4,6,128]{2,0,1:T(4,128)S(1)}, f32[4,6,128]{2,0,1:T(4,128)S(1)}, u32[]{:S(2)}, u32[]{:S(2)}) collective-permute-start(f32[4,6,128]{2,0,1:T(4,128)S(1)} %maximum_select_fusion.2), channel_id=1, source_target_pairs={{0,4},{1,5},{2,6},{3,7},{4,0},{5,1},{6,2},{7,3},{8,12},{9,13},{10,... | collective-permute-start | bytes 36872 | tf_op jit(solution)/shard_map/ppermute | solution.py:20
  12.5 1.0 %gather_fusion = f32[512,3]{1,0:T(8,128)S(1)} fusion(f32[2048,3]{1,0:T(8,128)S(1)} %copy.43, s32[1024]{0:T(1024)S(1)} %pad_clamp_fusion.1), kind=kCustom, calls=%fused_computation | custom fusion | bytes 14336 | tf_op jit(solution)/shard_map/jit(_take)/gather | solution.py:95
  13.5 0.5 %multiply_reduce_fusion = (f32[512]{0:T(512)S(1)}, f32[512]{0:T(512)S(1)}, f32[512]{0:T(512)S(1)}, f32[512]{0:T(512)S(1)}) fusion(f32[512,3]{1,0:T(8,128)S(1)} %gather_fusion), kind=kLoop, calls=%fused_computation.23 | loop fusion | flops 2560 | bytes 14336 | tf_op jit(solution)/shard_map/mul | solution.py:130
  14.2 2.7 %collective-permute-start.4 = (f32[8,6,128]{2,0,1:T(8,128)S(1)}, f32[8,6,128]{2,0,1:T(8,128)S(1)}, u32[]{:S(2)}, u32[]{:S(2)}) collective-permute-start(f32[8,6,128]{2,0,1:T(8,128)S(1)} %maximum_select_fusion.1), channel_id=1, source_target_pairs={{0,8},{1,9},{2,10},{3,11},{4,12},{5,13},{6,14},{7,15},{8,0},{9,1},... | collective-permute-start | bytes 73736 | tf_op jit(solution)/shard_map/ppermute | solution.py:20
  17.0 2.0 %collective-permute-done.4 = f32[8,6,128]{2,0,1:T(8,128)S(1)} collective-permute-done((f32[8,6,128]{2,0,1:T(8,128)S(1)}, f32[8,6,128]{2,0,1:T(8,128)S(1)}, u32[]{:S(2)}, u32[]{:S(2)}) %collective-permute-start.4) | collective-permute-done | bytes 24608 | tf_op jit(solution)/shard_map/ppermute | solution.py:20
  19.1 0.6 %gather_fusion.1 = f32[16,4,128]{2,1,0:T(4,128)S(1)} fusion(f32[8,4,128]{2,1,0:T(4,128)S(1)} %pad_maximum_fusion.2, s32[1024]{0:T(1024)S(1)} %pad_clamp_fusion), kind=kCustom, calls=%fused_computation.1 | custom fusion | bytes 65600 | tf_op jit(solution)/shard_map/jit(_take)/gather | solution.py:111
  19.8 2.2 %fusion.32 = (f32[4,4,128]{2,1,0:T(4,128)S(1)}, f32[4,128]{1,0:T(4,128)S(1)}) fusion(f32[4,128]{1,0:T(4,128)S(1)} %bitcast.112, f32[4,128]{1,0:T(4,128)S(1)} %bitcast.110, bf16[4,4,128,128]{3,2,1,0:T(8,128)(2,1)S(1)} %copy-done, s32[4,4,128]{2,1,0:T(4,128)S(1)} %get-tuple-element.19, s32[4,4,128]{2,1,0:T(4,128)S(1)} %get-tuple-element.18, ...), kind=kOutput, calls=%fused_computation.94 | convolution fusion | flops 71038464 | bytes 565264 | tf_op jit(solution)/shard_map/tkmi,tkip->tkmp/dot_general | solution.py:121
  22.4 1.1 %collective-permute-done.5 = f32[8,64]{1,0:T(8,128)S(1)} collective-permute-done((f32[8,64]{1,0:T(8,128)S(1)}, f32[8,64]{1,0:T(8,128)S(1)}, u32[]{:S(2)}, u32[]{:S(2)}) %collective-permute-start.5) | collective-permute-done | bytes 2080 | tf_op jit(solution)/shard_map/ppermute | solution.py:37
  23.5 1.6 %collective-permute-start.6 = (f32[4,64]{1,0:T(4,128)S(1)}, f32[4,64]{1,0:T(4,128)S(1)}, u32[]{:S(2)}, u32[]{:S(2)}) collective-permute-start(f32[4,64]{1,0:T(4,128)S(1)} %bitcast.117), channel_id=1, source_target_pairs={{0,2},{1,3},{2,0},{3,1},{4,6},{5,7},{6,4},{7,5},{8,10},{9,11},{10,... | collective-permute-start | bytes 3080 | tf_op jit(solution)/shard_map/ppermute | solution.py:37
  25.1 2.1 %collective-permute-done.6 = f32[4,64]{1,0:T(4,128)S(1)} collective-permute-done((f32[4,64]{1,0:T(4,128)S(1)}, f32[4,64]{1,0:T(4,128)S(1)}, u32[]{:S(2)}, u32[]{:S(2)}) %collective-permute-start.6) | collective-permute-done | bytes 1056 | tf_op jit(solution)/shard_map/ppermute | solution.py:37
  27.2 1.7 %collective-permute-start.7 = (f32[2,64]{1,0:T(2,128)S(1)}, f32[2,64]{1,0:T(2,128)S(1)}, u32[]{:S(2)}, u32[]{:S(2)}) collective-permute-start(f32[2,64]{1,0:T(2,128)S(1)} %bitcast.118), channel_id=1, source_target_pairs={{0,4},{1,5},{2,6},{3,7},{4,0},{5,1},{6,2},{7,3},{8,12},{9,13},{10,... | collective-permute-start | bytes 1544 | tf_op jit(solution)/shard_map/ppermute | solution.py:37
  28.8 2.0 %collective-permute-done.7 = f32[2,64]{1,0:T(2,128)S(1)} collective-permute-done((f32[2,64]{1,0:T(2,128)S(1)}, f32[2,64]{1,0:T(2,128)S(1)}, u32[]{:S(2)}, u32[]{:S(2)}) %collective-permute-start.7) | collective-permute-done | bytes 544 | tf_op jit(solution)/shard_map/ppermute | solution.py:37
  30.8 2.7 %collective-permute-start.8 = (f32[1,64]{1,0:T(1,128)S(1)}, f32[1,64]{1,0:T(1,128)S(1)}, u32[]{:S(2)}, u32[]{:S(2)}) collective-permute-start(f32[1,64]{1,0:T(1,128)S(1)} %constant_dynamic-slice_fusion), channel_id=1, source_target_pairs={{0,8},{1,9},{2,10},{3,11},{4,12},{5,13},{6,14},{7,15},{8,0},{9,1},... | collective-permute-start | bytes 776 | tf_op jit(solution)/shard_map/ppermute | solution.py:37
  33.5 0.7 %fusion.28 = f32[512]{0:T(512)} fusion(f32[4,128]{1,0:T(4,128)S(1)} %get-tuple-element.3, f32[512]{0:T(512)S(1)} %get-tuple-element.4, pred[4]{0:T(512)(128)(4,1)S(1)} %not_reduce_fusion), kind=kLoop, calls=%fused_computation.71 | loop fusion | flops 1024 | bytes 6148 | tf_op jit(solution)/shard_map/sqrt | solution.py:138
  34.2 1.2 %collective-permute-done.8 = f32[1,64]{1,0:T(1,128)S(1)} collective-permute-done((f32[1,64]{1,0:T(1,128)S(1)}, f32[1,64]{1,0:T(1,128)S(1)}, u32[]{:S(2)}, u32[]{:S(2)}) %collective-permute-start.8) | collective-permute-done | bytes 288 | tf_op jit(solution)/shard_map/ppermute | solution.py:37
  35.4 0.5 %fusion.30 = f32[1,64]{1,0:T(1,128)} fusion(f32[1,64]{1,0:T(1,128)S(1)} %collective-permute-done.8, f32[2,64]{1,0:T(2,128)S(1)} %max.34, s32[]{:T(128)S(6)} %select_n.169), kind=kLoop, calls=%fused_computation.89 | loop fusion | flops 64 | bytes 772 | tf_op jit(solution)/shard_map/sqrt | solution.py:149
  (64 shorter events, 2.1 us)
Async XLA Ops:
  0.6 19.2 %copy-start = (bf16[4,4,128,128]{3,2,1,0:T(8,128)(2,1)S(1)}, bf16[4,4,128,128]{3,2,1,0:T(8,128)(2,1)}, u32[]{:S(2)}) copy-start(bf16[4,4,128,128]{3,2,1,0:T(8,128)(2,1)} %param.16) | copy-start | bytes 1572868
  0.6 0.8 %copy-start.3 = (f32[1024]{0:T(1024)S(1)}, f32[1024]{0:T(1024)}, u32[]{:S(2)}) copy-start(f32[1024]{0:T(1024)} %param.12) | copy-start | bytes 12292
  0.7 0.8 %copy-start.4 = (f32[1024]{0:T(1024)S(1)}, f32[1024]{0:T(1024)}, u32[]{:S(2)}) copy-start(f32[1024]{0:T(1024)} %param.13) | copy-start | bytes 12292
  1.4 0.7 %copy-start.1 = (f32[1024]{0:T(1024)S(1)}, f32[1024]{0:T(1024)}, u32[]{:S(2)}) copy-start(f32[1024]{0:T(1024)} %param.10) | copy-start | bytes 12292
  2.1 0.8 %copy-start.8 = (s32[1,128]{1,0:T(1,128)S(1)}, s32[1,128]{1,0:T(1,128)}, u32[]{:S(2)}) copy-start(s32[1,128]{1,0:T(1,128)} %param.17) | copy-start | bytes 1540
  2.2 0.7 %copy-start.5 = (s32[1,2,128]{2,1,0:T(2,128)S(1)}, s32[1,2,128]{2,1,0:T(2,128)}, u32[]{:S(2)}) copy-start(s32[1,2,128]{2,1,0:T(2,128)} %param.19) | copy-start | bytes 3076
  2.2 0.8 %copy-start.7 = (bf16[1,128,128]{2,1,0:T(8,128)(2,1)S(1)}, bf16[1,128,128]{2,1,0:T(8,128)(2,1)}, u32[]{:S(2)}) copy-start(bf16[1,128,128]{2,1,0:T(8,128)(2,1)} %param.18) | copy-start | bytes 98308
  2.2 9.9 %collective-permute-start = (f32[1024,3]{0,1:T(4,128)S(1)}, f32[1024,3]{0,1:T(4,128)S(1)}, u32[]{:S(2)}, u32[]{:S(2)}) collective-permute-start(f32[1024,3]{0,1:T(4,128)S(1)} %pad_maximum_fusion.1), channel_id=1, source_target_pairs={{0,1},{1,0},{2,3},{3,2},{4,5},{5,4},{6,7},{7,6},{8,9},{9,8},{10,11... | collective-permute-start | bytes 36872 | tf_op jit(solution)/shard_map/ppermute | solution.py:90
  3.6 0.7 %copy-start.2 = (s32[4,4]{1,0:T(4,128)S(1)}, s32[4,4]{1,0:T(4,128)}, u32[]{:S(2)}) copy-start(s32[4,4]{1,0:T(4,128)} %param.15) | copy-start | bytes 196
  3.6 1.6 %collective-permute-start.1 = (f32[1,6,128]{2,0,1:T(1,128)S(1)}, f32[1,6,128]{2,0,1:T(1,128)S(1)}, u32[]{:S(2)}, u32[]{:S(2)}) collective-permute-start(f32[1,6,128]{2,0,1:T(1,128)S(1)} %broadcast_in_dim.124), channel_id=1, source_target_pairs={{0,1},{1,0},{2,3},{3,2},{4,5},{5,4},{6,7},{7,6},{8,9},{9,8},{10,11... | collective-permute-start | bytes 9224 | tf_op jit(solution)/shard_map/ppermute | solution.py:20
  4.3 0.7 %copy-start.6 = (s32[512]{0:T(512)S(1)}, s32[512]{0:T(512)}, u32[]{:S(2)}) copy-start(s32[512]{0:T(512)} %param.14) | copy-start | bytes 6148
  5.3 4.6 %collective-permute-start.2 = (f32[2,6,128]{2,0,1:T(2,128)S(1)}, f32[2,6,128]{2,0,1:T(2,128)S(1)}, u32[]{:S(2)}, u32[]{:S(2)}) collective-permute-start(f32[2,6,128]{2,0,1:T(2,128)S(1)} %maximum_select_fusion.3), channel_id=1, source_target_pairs={{0,2},{1,3},{2,0},{3,1},{4,6},{5,7},{6,4},{7,5},{8,10},{9,11},{10,... | collective-permute-start | bytes 18440 | tf_op jit(solution)/shard_map/ppermute | solution.py:20
  9.9 4.2 %collective-permute-start.3 = (f32[4,6,128]{2,0,1:T(4,128)S(1)}, f32[4,6,128]{2,0,1:T(4,128)S(1)}, u32[]{:S(2)}, u32[]{:S(2)}) collective-permute-start(f32[4,6,128]{2,0,1:T(4,128)S(1)} %maximum_select_fusion.2), channel_id=1, source_target_pairs={{0,4},{1,5},{2,6},{3,7},{4,0},{5,1},{6,2},{7,3},{8,12},{9,13},{10,... | collective-permute-start | bytes 36872 | tf_op jit(solution)/shard_map/ppermute | solution.py:20
  14.2 4.8 %collective-permute-start.4 = (f32[8,6,128]{2,0,1:T(8,128)S(1)}, f32[8,6,128]{2,0,1:T(8,128)S(1)}, u32[]{:S(2)}, u32[]{:S(2)}) collective-permute-start(f32[8,6,128]{2,0,1:T(8,128)S(1)} %maximum_select_fusion.1), channel_id=1, source_target_pairs={{0,8},{1,9},{2,10},{3,11},{4,12},{5,13},{6,14},{7,15},{8,0},{9,1},... | collective-permute-start | bytes 73736 | tf_op jit(solution)/shard_map/ppermute | solution.py:20
  22.3 1.2 %collective-permute-start.5 = (f32[8,64]{1,0:T(8,128)S(1)}, f32[8,64]{1,0:T(8,128)S(1)}, u32[]{:S(2)}, u32[]{:S(2)}) collective-permute-start(f32[8,64]{1,0:T(8,128)S(1)} %bitcast.115), channel_id=1, source_target_pairs={{0,1},{1,0},{2,3},{3,2},{4,5},{5,4},{6,7},{7,6},{8,9},{9,8},{10,11... | collective-permute-start | bytes 6152 | tf_op jit(solution)/shard_map/ppermute | solution.py:37
  23.5 3.6 %collective-permute-start.6 = (f32[4,64]{1,0:T(4,128)S(1)}, f32[4,64]{1,0:T(4,128)S(1)}, u32[]{:S(2)}, u32[]{:S(2)}) collective-permute-start(f32[4,64]{1,0:T(4,128)S(1)} %bitcast.117), channel_id=1, source_target_pairs={{0,2},{1,3},{2,0},{3,1},{4,6},{5,7},{6,4},{7,5},{8,10},{9,11},{10,... | collective-permute-start | bytes 3080 | tf_op jit(solution)/shard_map/ppermute | solution.py:37
  27.2 3.6 %collective-permute-start.7 = (f32[2,64]{1,0:T(2,128)S(1)}, f32[2,64]{1,0:T(2,128)S(1)}, u32[]{:S(2)}, u32[]{:S(2)}) collective-permute-start(f32[2,64]{1,0:T(2,128)S(1)} %bitcast.118), channel_id=1, source_target_pairs={{0,4},{1,5},{2,6},{3,7},{4,0},{5,1},{6,2},{7,3},{8,12},{9,13},{10,... | collective-permute-start | bytes 1544 | tf_op jit(solution)/shard_map/ppermute | solution.py:37
  30.8 4.5 %collective-permute-start.8 = (f32[1,64]{1,0:T(1,128)S(1)}, f32[1,64]{1,0:T(1,128)S(1)}, u32[]{:S(2)}, u32[]{:S(2)}) collective-permute-start(f32[1,64]{1,0:T(1,128)S(1)} %constant_dynamic-slice_fusion), channel_id=1, source_target_pairs={{0,8},{1,9},{2,10},{3,11},{4,12},{5,13},{6,14},{7,15},{8,0},{9,1},... | collective-permute-start | bytes 776 | tf_op jit(solution)/shard_map/ppermute | solution.py:37

commit v6 on v5

--- a/solution.py
+++ b/solution.py
@@ -75,14 +75,19 @@
     flow_pairs = jnp.dot(
         pick_at, flow_part.astype(jnp.bfloat16), preferred_element_type=jnp.float32
     ).reshape(2, pair_count)
+    flow_other = lax.ppermute(
+        flow_pairs, "state", [(j, (j + 1) % halves) for j in range(halves)]
+    )
     coupled_rows = jnp.dot(pick_at, coupling[0], preferred_element_type=jnp.float32)
     coupled = jnp.sum(
         jnp.where(outage_iota == pair_to[:, None], coupled_rows, 0.0), axis=1
     ).reshape(2, pair_count)
-    packed = jnp.concatenate(
-        [flow_pairs, coupled, outage_pairs[0].astype(jnp.float32)]
-    )
-    known = gather_doubling(packed, both).reshape(blocks, halves, 6, pair_count)
+    flows = flow_pairs + flow_other
+    determinant = 1.0 - coupled[0] * coupled[1]
+    w_first = (flows[0] + coupled[0] * flows[1]) / determinant
+    w_second = (flows[1] + coupled[1] * flows[0]) / determinant
+    packed = jnp.stack([w_first, w_second, first_idx.astype(jnp.float32), second_idx.astype(jnp.float32)])
+    table = gather_doubling(packed.astype(jnp.bfloat16), ("blk",))
 
     state_local = jnp.stack(
         [base_real, base_reactive * base_reactive, voltage * rating], axis=1
@@ -97,23 +102,14 @@
     react_sq = mon_vals[:, 1].reshape(tiles_dev, tile_size)
     mon_limit = mon_vals[:, 2].reshape(tiles_dev, tile_size)
 
-    flow_first = jnp.sum(known[:, :, 0], axis=1)
-    flow_second = jnp.sum(known[:, :, 1], axis=1)
-    s_first_second = known[:, 0, 2]
-    s_second_first = known[:, 0, 3]
-    determinant = 1.0 - s_first_second * s_second_first
-    w_first_all = (flow_first + s_first_second * flow_second) / determinant
-    w_second_all = (flow_second + s_second_first * flow_first) / determinant
-    table = jnp.stack([w_first_all, w_second_all, known[:, 0, 4], known[:, 0, 5]], axis=1)
-
     valid = tile_ids >= 0
     block_of = jnp.clip(tile_ids, 0, blocks - 1)
     chosen = jnp.take(table, block_of, axis=0)
     rows_iota = lax.broadcasted_iota(jnp.int32, (1, 1, tile_size, pair_count), 2)
     first_at = chosen[:, :, 2].astype(jnp.int32)[:, :, None, :]
     second_at = chosen[:, :, 3].astype(jnp.int32)[:, :, None, :]
-    w_first = chosen[:, :, 0].astype(jnp.bfloat16)[:, :, None, :]
-    w_second = chosen[:, :, 1].astype(jnp.bfloat16)[:, :, None, :]
+    w_first = chosen[:, :, 0][:, :, None, :]
+    w_second = chosen[:, :, 1][:, :, None, :]
     zero = jnp.zeros((), jnp.bfloat16)
     weights = jnp.where(rows_iota == first_at, w_first, zero) + jnp.where(
         rows_iota == second_at, w_second, zero

time: 36.1 us -> 37.8 us (1.047)
  local copies, waits for them, and re-layouts: 3.75 us -> 5.04 us
  starting transfers between devices: 15.1 us -> 15.6 us
    unnamed x18, local copies, waits for them, and re-layouts: 1.54 us -> 2.85 us
    ppermute x4 -> x3, waiting for transfers between devices: 3.62 us -> 4.49 us  [gather_doubling(): other = lax.ppermute(cur, axes, [(j, j ^ bit) for j in range(n)])]
    ppermute x4, starting transfers between devices: 6.05 us -> 6.91 us  [scatter_max(): lax.ppermute(send, axes, [(j, j ^ bit) for j in range(n)])]
    ppermute x4, waiting for transfers between devices: 6.28 us -> 5.42 us  [scatter_max(): lax.ppermute(send, axes, [(j, j ^ bit) for j in range(n)])]
    ppermute x4 -> x3, starting transfers between devices: 8.45 us -> 8.05 us  [gather_doubling(): other = lax.ppermute(cur, axes, [(j, j ^ bit) for j in range(n)])]
  transfers between devices with their start and end apart: 9 -> 9, of which waited for: 6 -> 7; matrix products, arithmetic and copies ran while one was open for 11% -> 6% of each run, Pallas kernels for 0% -> 0%
where the time goes in v6:
time: 37.8 us; the launch traced here: 37.6 us
  starting transfers between devices  15.6 us (41%)
  waiting for transfers between devices  9.91 us (26%)
  local copies, waits for them, and re-layouts  5.04 us (13%)
  other arithmetic  3.29 us (9%)
  matrix products  2.83 us (7%)
  between operations  0.89 us (2%)
    ppermute x3, starting transfers between devices, gather_doubling(): other = lax.ppermute(cur, axes, [(j, j ^ bit) for j in range(n)])  8.05 us
    ppermute x4, starting transfers between devices, scatter_max(): lax.ppermute(send, axes, [(j, j ^ bit) for j in range(n)])  6.91 us
    ppermute x4, waiting for transfers between devices, scatter_max(): lax.ppermute(send, axes, [(j, j ^ bit) for j in range(n)])  5.42 us
    ppermute x3, waiting for transfers between devices, gather_doubling(): other = lax.ppermute(cur, axes, [(j, j ^ bit) for j in range(n)])  4.49 us
    unnamed x18, local copies, waits for them, and re-layouts  2.85 us
    dot_general x1, matrix products, body(): jnp.einsum('tkmi,tkip->tkmp', tile_values, weights, preferred_element_typ...  2.19 us
    gather x1, local copies, waits for them, and re-layouts, body(): mon_vals = jnp.take(state_pos, mon_at, axis=0, mode='clip')  1.04 us
    mul x1, other arithmetic, body(): base_reactive * base_reactive  0.77 us
  transfers between devices with their start and end apart: 9, of which 7 were waited for; matrix products, arithmetic and copies ran while one was open for 6% of the time, Pallas kernels for 0%

profile of v6, /device:TPU:0, one launch (start us, length us, event | category | flops | bytes accessed | tf_op | source)
XLA Modules:
  0.0 37.6 jit_solution(311897640114754409)
XLA Ops:
  0.7 0.8 %mul.75 = f32[1024]{0:T(1024)S(1)} multiply(f32[1024]{0:T(1024)} %param.11, f32[1024]{0:T(1024)} %param.11) | non-fusion elementwise | flops 1024 | bytes 12288 | tf_op jit(solution)/shard_map/mul | solution.py:93
  1.5 0.7 %copy-done.1 = f32[1024]{0:T(1024)S(1)} copy-done((f32[1024]{0:T(1024)S(1)}, f32[1024]{0:T(1024)}, u32[]{:S(2)}) %copy-start.1) | copy-done | bytes 4120
  2.2 0.6 %collective-permute-start = (f32[1024,3]{0,1:T(4,128)S(1)}, f32[1024,3]{0,1:T(4,128)S(1)}, u32[]{:S(2)}, u32[]{:S(2)}) collective-permute-start(f32[1024,3]{0,1:T(4,128)S(1)} %pad_maximum_fusion.1), channel_id=1, source_target_pairs={{0,1},{1,0},{2,3},{3,2},{4,5},{5,4},{6,7},{7,6},{8,9},{9,8},{10,11... | collective-permute-start | bytes 36872 | tf_op jit(solution)/shard_map/ppermute | solution.py:95
  2.7 0.7 %copy-done.6 = s32[1,2,128]{2,1,0:T(2,128)S(1)} copy-done((s32[1,2,128]{2,1,0:T(2,128)S(1)}, s32[1,2,128]{2,1,0:T(2,128)}, u32[]{:S(2)}) %copy-start.6) | copy-done | bytes 1048
  3.4 0.6 %copy-done.8 = s32[1,128]{1,0:T(1,128)S(1)} copy-done((s32[1,128]{1,0:T(1,128)S(1)}, s32[1,128]{1,0:T(1,128)}, u32[]{:S(2)}) %copy-start.8) | copy-done | bytes 536
  4.9 0.6 %copy-done.5 = s32[512]{0:T(512)S(1)} copy-done((s32[512]{0:T(512)S(1)}, s32[512]{0:T(512)}, u32[]{:S(2)}) %copy-start.5) | copy-done | bytes 2072
  5.8 2.8 %collective-permute-start.2 = (bf16[1,4,128]{2,1,0:T(4,128)(2,1)S(1)}, bf16[1,4,128]{2,1,0:T(4,128)(2,1)S(1)}, u32[]{:S(2)}, u32[]{:S(2)}) collective-permute-start(bf16[1,4,128]{2,1,0:T(4,128)(2,1)S(1)} %pad_maximum_fusion.2), channel_id=1, source_target_pairs={{0,2},{2,0},{4,6},{6,4},{8,10},{10,8},{12,14},{14,12},{1,3},{3,1},... | collective-permute-start | bytes 3080 | tf_op jit(solution)/shard_map/ppermute | solution.py:20
  8.7 1.4 %collective-permute-done.2 = bf16[1,4,128]{2,1,0:T(4,128)(2,1)S(1)} collective-permute-done((bf16[1,4,128]{2,1,0:T(4,128)(2,1)S(1)}, bf16[1,4,128]{2,1,0:T(4,128)(2,1)S(1)}, u32[]{:S(2)}, u32[]{:S(2)}) %collective-permute-start.2) | collective-permute-done | bytes 1056 | tf_op jit(solution)/shard_map/ppermute | solution.py:20
  10.2 2.2 %collective-permute-start.3 = (bf16[2,4,128]{2,1,0:T(4,128)(2,1)S(1)}, bf16[2,4,128]{2,1,0:T(4,128)(2,1)S(1)}, u32[]{:S(2)}, u32[]{:S(2)}) collective-permute-start(bf16[2,4,128]{2,1,0:T(4,128)(2,1)S(1)} %maximum_select_fusion.2), channel_id=1, source_target_pairs={{0,4},{2,6},{4,0},{6,2},{8,12},{10,14},{12,8},{14,10},{1,5},{3,7},... | collective-permute-start | bytes 6152 | tf_op jit(solution)/shard_map/ppermute | solution.py:20
  12.4 1.5 %collective-permute-done.3 = bf16[2,4,128]{2,1,0:T(4,128)(2,1)S(1)} collective-permute-done((bf16[2,4,128]{2,1,0:T(4,128)(2,1)S(1)}, bf16[2,4,128]{2,1,0:T(4,128)(2,1)S(1)}, u32[]{:S(2)}, u32[]{:S(2)}) %collective-permute-start.3) | collective-permute-done | bytes 2080 | tf_op jit(solution)/shard_map/ppermute | solution.py:20
  13.9 3.1 %collective-permute-start.4 = (bf16[4,4,128]{2,1,0:T(4,128)(2,1)S(1)}, bf16[4,4,128]{2,1,0:T(4,128)(2,1)S(1)}, u32[]{:S(2)}, u32[]{:S(2)}) collective-permute-start(bf16[4,4,128]{2,1,0:T(4,128)(2,1)S(1)} %maximum_select_fusion.1), channel_id=1, source_target_pairs={{0,8},{2,10},{4,12},{6,14},{8,0},{10,2},{12,4},{14,6},{1,9},{3,11}... | collective-permute-start | bytes 12296 | tf_op jit(solution)/shard_map/ppermute | solution.py:20
  17.0 1.6 %collective-permute-done.4 = bf16[4,4,128]{2,1,0:T(4,128)(2,1)S(1)} collective-permute-done((bf16[4,4,128]{2,1,0:T(4,128)(2,1)S(1)}, bf16[4,4,128]{2,1,0:T(4,128)(2,1)S(1)}, u32[]{:S(2)}, u32[]{:S(2)}) %collective-permute-start.4) | collective-permute-done | bytes 4128 | tf_op jit(solution)/shard_map/ppermute | solution.py:20
  18.6 0.6 %gather_fusion.1 = bf16[16,4,128]{2,1,0:T(4,128)(2,1)S(1)} fusion(bf16[8,4,128]{2,1,0:T(4,128)(2,1)S(1)} %maximum_select_fusion, s32[1024]{0:T(1024)S(1)} %pad_clamp_fusion), kind=kCustom, calls=%fused_computation.1 | custom fusion | bytes 32832 | tf_op jit(solution)/shard_map/jit(_take)/gather | solution.py:107
  19.7 1.0 %gather_fusion = f32[512,3]{1,0:T(8,128)S(1)} fusion(f32[2048,3]{1,0:T(8,128)S(1)} %copy.26, s32[1024]{0:T(1024)S(1)} %pad_clamp_fusion.1), kind=kCustom, calls=%fused_computation | custom fusion | bytes 14336 | tf_op jit(solution)/shard_map/jit(_take)/gather | solution.py:100
  21.4 2.2 %fusion.35 = (f32[4,4,128]{2,1,0:T(4,128)S(1)}, f32[4,128]{1,0:T(4,128)S(1)}) fusion(f32[4,128]{1,0:T(4,128)S(1)} %bitcast.101, f32[4,128]{1,0:T(4,128)S(1)} %bitcast.99, bf16[4,4,128,128]{3,2,1,0:T(8,128)(2,1)S(1)} %copy-done, s32[4,4,128]{2,1,0:T(4,128)S(1)} %get-tuple-element.12, s32[4,4,128]{2,1,0:T(4,128)S(1)} %get-tuple-element.13, ...), kind=kOutput, calls=%fused_computation.93 | convolution fusion | flops 71038464 | bytes 565264 | tf_op jit(solution)/shard_map/tkmi,tkip->tkmp/dot_general | solution.py:117
  24.1 1.1 %collective-permute-done.5 = f32[8,64]{1,0:T(8,128)S(1)} collective-permute-done((f32[8,64]{1,0:T(8,128)S(1)}, f32[8,64]{1,0:T(8,128)S(1)}, u32[]{:S(2)}, u32[]{:S(2)}) %collective-permute-start.5) | collective-permute-done | bytes 2080 | tf_op jit(solution)/shard_map/ppermute | solution.py:37
  25.2 1.9 %collective-permute-start.6 = (f32[4,64]{1,0:T(4,128)S(1)}, f32[4,64]{1,0:T(4,128)S(1)}, u32[]{:S(2)}, u32[]{:S(2)}) collective-permute-start(f32[4,64]{1,0:T(4,128)S(1)} %bitcast.106), channel_id=1, source_target_pairs={{0,2},{1,3},{2,0},{3,1},{4,6},{5,7},{6,4},{7,5},{8,10},{9,11},{10,... | collective-permute-start | bytes 3080 | tf_op jit(solution)/shard_map/ppermute | solution.py:37
  27.1 1.8 %collective-permute-done.6 = f32[4,64]{1,0:T(4,128)S(1)} collective-permute-done((f32[4,64]{1,0:T(4,128)S(1)}, f32[4,64]{1,0:T(4,128)S(1)}, u32[]{:S(2)}, u32[]{:S(2)}) %collective-permute-start.6) | collective-permute-done | bytes 1056 | tf_op jit(solution)/shard_map/ppermute | solution.py:37
  28.8 2.0 %collective-permute-start.7 = (f32[2,64]{1,0:T(2,128)S(1)}, f32[2,64]{1,0:T(2,128)S(1)}, u32[]{:S(2)}, u32[]{:S(2)}) collective-permute-start(f32[2,64]{1,0:T(2,128)S(1)} %bitcast.107), channel_id=1, source_target_pairs={{0,4},{1,5},{2,6},{3,7},{4,0},{5,1},{6,2},{7,3},{8,12},{9,13},{10,... | collective-permute-start | bytes 1544 | tf_op jit(solution)/shard_map/ppermute | solution.py:37
  30.8 1.7 %collective-permute-done.7 = f32[2,64]{1,0:T(2,128)S(1)} collective-permute-done((f32[2,64]{1,0:T(2,128)S(1)}, f32[2,64]{1,0:T(2,128)S(1)}, u32[]{:S(2)}, u32[]{:S(2)}) %collective-permute-start.7) | collective-permute-done | bytes 544 | tf_op jit(solution)/shard_map/ppermute | solution.py:37
  32.5 3.0 %collective-permute-start.8 = (f32[1,64]{1,0:T(1,128)S(1)}, f32[1,64]{1,0:T(1,128)S(1)}, u32[]{:S(2)}, u32[]{:S(2)}) collective-permute-start(f32[1,64]{1,0:T(1,128)S(1)} %constant_dynamic-slice_fusion), channel_id=1, source_target_pairs={{0,8},{1,9},{2,10},{3,11},{4,12},{5,13},{6,14},{7,15},{8,0},{9,1},... | collective-permute-start | bytes 776 | tf_op jit(solution)/shard_map/ppermute | solution.py:37
  35.5 0.7 %fusion.28 = f32[512]{0:T(512)} fusion(f32[4,128]{1,0:T(4,128)S(1)} %get-tuple-element.3, f32[512]{0:T(512)S(1)} %get-tuple-element.4, pred[4]{0:T(512)(128)(4,1)S(1)} %not_reduce_fusion), kind=kLoop, calls=%fused_computation.59 | loop fusion | flops 1024 | bytes 6148 | tf_op jit(solution)/shard_map/sqrt | solution.py:134
  36.1 0.9 %collective-permute-done.8 = f32[1,64]{1,0:T(1,128)S(1)} collective-permute-done((f32[1,64]{1,0:T(1,128)S(1)}, f32[1,64]{1,0:T(1,128)S(1)}, u32[]{:S(2)}, u32[]{:S(2)}) %collective-permute-start.8) | collective-permute-done | bytes 288 | tf_op jit(solution)/shard_map/ppermute | solution.py:37
  37.0 0.5 %fusion.30 = f32[1,64]{1,0:T(1,128)} fusion(f32[1,64]{1,0:T(1,128)S(1)} %collective-permute-done.8, f32[2,64]{1,0:T(2,128)S(1)} %max.34, s32[]{:T(128)S(6)} %select_n.154), kind=kLoop, calls=%fused_computation.77 | loop fusion | flops 64 | bytes 772 | tf_op jit(solution)/shard_map/sqrt | solution.py:145
  (58 shorter events, 3.0 us)
Async XLA Ops:
  0.6 20.8 %copy-start = (bf16[4,4,128,128]{3,2,1,0:T(8,128)(2,1)S(1)}, bf16[4,4,128,128]{3,2,1,0:T(8,128)(2,1)}, u32[]{:S(2)}) copy-start(bf16[4,4,128,128]{3,2,1,0:T(8,128)(2,1)} %param.16) | copy-start | bytes 1572868
  0.6 0.8 %copy-start.3 = (f32[1024]{0:T(1024)S(1)}, f32[1024]{0:T(1024)}, u32[]{:S(2)}) copy-start(f32[1024]{0:T(1024)} %param.12) | copy-start | bytes 12292
  0.7 0.8 %copy-start.4 = (f32[1024]{0:T(1024)S(1)}, f32[1024]{0:T(1024)}, u32[]{:S(2)}) copy-start(f32[1024]{0:T(1024)} %param.13) | copy-start | bytes 12292
  1.4 0.7 %copy-start.1 = (f32[1024]{0:T(1024)S(1)}, f32[1024]{0:T(1024)}, u32[]{:S(2)}) copy-start(f32[1024]{0:T(1024)} %param.10) | copy-start | bytes 12292
  2.2 17.2 %collective-permute-start = (f32[1024,3]{0,1:T(4,128)S(1)}, f32[1024,3]{0,1:T(4,128)S(1)}, u32[]{:S(2)}, u32[]{:S(2)}) collective-permute-start(f32[1024,3]{0,1:T(4,128)S(1)} %pad_maximum_fusion.1), channel_id=1, source_target_pairs={{0,1},{1,0},{2,3},{3,2},{4,5},{5,4},{6,7},{7,6},{8,9},{9,8},{10,11... | collective-permute-start | bytes 36872 | tf_op jit(solution)/shard_map/ppermute | solution.py:95
  2.7 0.7 %copy-start.6 = (s32[1,2,128]{2,1,0:T(2,128)S(1)}, s32[1,2,128]{2,1,0:T(2,128)}, u32[]{:S(2)}) copy-start(s32[1,2,128]{2,1,0:T(2,128)} %param.19) | copy-start | bytes 3076
  3.4 0.7 %copy-start.8 = (s32[1,128]{1,0:T(1,128)S(1)}, s32[1,128]{1,0:T(1,128)}, u32[]{:S(2)}) copy-start(s32[1,128]{1,0:T(1,128)} %param.17) | copy-start | bytes 1540
  4.1 0.7 %copy-start.2 = (s32[4,4]{1,0:T(4,128)S(1)}, s32[4,4]{1,0:T(4,128)}, u32[]{:S(2)}) copy-start(s32[4,4]{1,0:T(4,128)} %param.15) | copy-start | bytes 196
  4.1 1.4 %copy-start.7 = (bf16[1,128,128]{2,1,0:T(8,128)(2,1)S(1)}, bf16[1,128,128]{2,1,0:T(8,128)(2,1)}, u32[]{:S(2)}) copy-start(bf16[1,128,128]{2,1,0:T(8,128)(2,1)} %param.18) | copy-start | bytes 98308
  4.4 1.3 %collective-permute-start.1 = (f32[2,128]{1,0:T(2,128)S(1)}, f32[2,128]{1,0:T(2,128)S(1)}, u32[]{:S(2)}, u32[]{:S(2)}) collective-permute-start(f32[2,128]{1,0:T(2,128)S(1)} %bitcast.108), channel_id=1, source_target_pairs={{0,1},{1,0},{2,3},{3,2},{4,5},{5,4},{6,7},{7,6},{8,9},{9,8},{10,11... | collective-permute-start | bytes 3080 | tf_op jit(solution)/shard_map/ppermute | solution.py:78
  4.8 0.7 %copy-start.5 = (s32[512]{0:T(512)S(1)}, s32[512]{0:T(512)}, u32[]{:S(2)}) copy-start(s32[512]{0:T(512)} %param.14) | copy-start | bytes 6148
  5.8 4.3 %collective-permute-start.2 = (bf16[1,4,128]{2,1,0:T(4,128)(2,1)S(1)}, bf16[1,4,128]{2,1,0:T(4,128)(2,1)S(1)}, u32[]{:S(2)}, u32[]{:S(2)}) collective-permute-start(bf16[1,4,128]{2,1,0:T(4,128)(2,1)S(1)} %pad_maximum_fusion.2), channel_id=1, source_target_pairs={{0,2},{2,0},{4,6},{6,4},{8,10},{10,8},{12,14},{14,12},{1,3},{3,1},... | collective-permute-start | bytes 3080 | tf_op jit(solution)/shard_map/ppermute | solution.py:20
  10.2 3.7 %collective-permute-start.3 = (bf16[2,4,128]{2,1,0:T(4,128)(2,1)S(1)}, bf16[2,4,128]{2,1,0:T(4,128)(2,1)S(1)}, u32[]{:S(2)}, u32[]{:S(2)}) collective-permute-start(bf16[2,4,128]{2,1,0:T(4,128)(2,1)S(1)} %maximum_select_fusion.2), channel_id=1, source_target_pairs={{0,4},{2,6},{4,0},{6,2},{8,12},{10,14},{12,8},{14,10},{1,5},{3,7},... | collective-permute-start | bytes 6152 | tf_op jit(solution)/shard_map/ppermute | solution.py:20
  13.9 4.7 %collective-permute-start.4 = (bf16[4,4,128]{2,1,0:T(4,128)(2,1)S(1)}, bf16[4,4,128]{2,1,0:T(4,128)(2,1)S(1)}, u32[]{:S(2)}, u32[]{:S(2)}) collective-permute-start(bf16[4,4,128]{2,1,0:T(4,128)(2,1)S(1)} %maximum_select_fusion.1), channel_id=1, source_target_pairs={{0,8},{2,10},{4,12},{6,14},{8,0},{10,2},{12,4},{14,6},{1,9},{3,11}... | collective-permute-start | bytes 12296 | tf_op jit(solution)/shard_map/ppermute | solution.py:20
  23.9 1.2 %collective-permute-start.5 = (f32[8,64]{1,0:T(8,128)S(1)}, f32[8,64]{1,0:T(8,128)S(1)}, u32[]{:S(2)}, u32[]{:S(2)}) collective-permute-start(f32[8,64]{1,0:T(8,128)S(1)} %bitcast.104), channel_id=1, source_target_pairs={{0,1},{1,0},{2,3},{3,2},{4,5},{5,4},{6,7},{7,6},{8,9},{9,8},{10,11... | collective-permute-start | bytes 6152 | tf_op jit(solution)/shard_map/ppermute | solution.py:37
  25.2 3.6 %collective-permute-start.6 = (f32[4,64]{1,0:T(4,128)S(1)}, f32[4,64]{1,0:T(4,128)S(1)}, u32[]{:S(2)}, u32[]{:S(2)}) collective-permute-start(f32[4,64]{1,0:T(4,128)S(1)} %bitcast.106), channel_id=1, source_target_pairs={{0,2},{1,3},{2,0},{3,1},{4,6},{5,7},{6,4},{7,5},{8,10},{9,11},{10,... | collective-permute-start | bytes 3080 | tf_op jit(solution)/shard_map/ppermute | solution.py:37
  28.8 3.6 %collective-permute-start.7 = (f32[2,64]{1,0:T(2,128)S(1)}, f32[2,64]{1,0:T(2,128)S(1)}, u32[]{:S(2)}, u32[]{:S(2)}) collective-permute-start(f32[2,64]{1,0:T(2,128)S(1)} %bitcast.107), channel_id=1, source_target_pairs={{0,4},{1,5},{2,6},{3,7},{4,0},{5,1},{6,2},{7,3},{8,12},{9,13},{10,... | collective-permute-start | bytes 1544 | tf_op jit(solution)/shard_map/ppermute | solution.py:37
  32.5 4.5 %collective-permute-start.8 = (f32[1,64]{1,0:T(1,128)S(1)}, f32[1,64]{1,0:T(1,128)S(1)}, u32[]{:S(2)}, u32[]{:S(2)}) collective-permute-start(f32[1,64]{1,0:T(1,128)S(1)} %constant_dynamic-slice_fusion), channel_id=1, source_target_pairs={{0,8},{1,9},{2,10},{3,11},{4,12},{5,13},{6,14},{7,15},{8,0},{9,1},... | collective-permute-start | bytes 776 | tf_op jit(solution)/shard_map/ppermute | solution.py:37

commit v7 on v6

--- a/solution.py
+++ b/solution.py
@@ -51,7 +51,7 @@
     coupling,
     outage_pairs,
 ):
-    tiles_dev, slot_count, tile_size, _ = tile_values.shape
+    tiles_dev, _, tile_size, _ = tile_values.shape
     pair_count = outage_pairs.shape[2]
     blocks = lax.axis_size("blk")
     halves = lax.axis_size("state")
@@ -89,18 +89,16 @@
     packed = jnp.stack([w_first, w_second, first_idx.astype(jnp.float32), second_idx.astype(jnp.float32)])
     table = gather_doubling(packed.astype(jnp.bfloat16), ("blk",))
 
-    state_local = jnp.stack(
-        [base_real, base_reactive * base_reactive, voltage * rating], axis=1
-    )
-    other_half = lax.ppermute(
-        state_local, "state", [(j, (j + 1) % halves) for j in range(halves)]
-    )
+    state_local = jnp.stack([base_real, base_reactive * base_reactive, voltage * rating], axis=1)
+    other_half = lax.ppermute(state_local, "state", [(j, (j + 1) % halves) for j in range(halves)])
     state_pos = jnp.concatenate([state_local, other_half])
     mon_at = (monitored - me_state * half_len) % (halves * half_len)
     mon_vals = jnp.take(state_pos, mon_at, axis=0, mode="clip")
     mon_real = mon_vals[:, 0].reshape(tiles_dev, tile_size)
     react_sq = mon_vals[:, 1].reshape(tiles_dev, tile_size)
     mon_limit = mon_vals[:, 2].reshape(tiles_dev, tile_size)
+    inv_limit_sq = 1.0 / (mon_limit * mon_limit)
+    base_sq = (mon_real * mon_real + react_sq) * inv_limit_sq
 
     valid = tile_ids >= 0
     block_of = jnp.clip(tile_ids, 0, blocks - 1)
@@ -117,13 +115,11 @@
     delta = jnp.einsum(
         "tkmi,tkip->tkmp", tile_values, weights, preferred_element_type=jnp.float32
     )
-    inv_limit_sq = 1.0 / (mon_limit * mon_limit)
     post = mon_real[:, None, :, None] + delta
     squared = (post * post + react_sq[:, None, :, None]) * inv_limit_sq[:, None, :, None]
     neg = jnp.float32(-jnp.inf)
     squared = jnp.where(valid[:, :, None, None], squared, neg)
 
-    base_sq = (mon_real * mon_real + react_sq) * inv_limit_sq
     block_iota = jnp.arange(blocks, dtype=jnp.int32)
     matches = tile_ids[:, :, None] == block_iota[None, None, :]
     absent = jnp.logical_not(jnp.any(matches, axis=1))

time: 37.8 us -> 37.8 us (level)
  no operation moved by 1% of the time
where the time goes in v7:
time: 37.8 us; the launch traced here: 37.6 us
  starting transfers between devices  15.6 us (41%)
  waiting for transfers between devices  9.92 us (26%)
  local copies, waits for them, and re-layouts  5.04 us (13%)
  other arithmetic  3.29 us (9%)
  matrix products  2.83 us (7%)
  between operations  0.89 us (2%)
    ppermute x3, starting transfers between devices, gather_doubling(): other = lax.ppermute(cur, axes, [(j, j ^ bit) for j in range(n)])  8.05 us
    ppermute x4, starting transfers between devices, scatter_max(): lax.ppermute(send, axes, [(j, j ^ bit) for j in range(n)])  6.91 us
    ppermute x4, waiting for transfers between devices, scatter_max(): lax.ppermute(send, axes, [(j, j ^ bit) for j in range(n)])  5.42 us
    ppermute x3, waiting for transfers between devices, gather_doubling(): other = lax.ppermute(cur, axes, [(j, j ^ bit) for j in range(n)])  4.49 us
    unnamed x18, local copies, waits for them, and re-layouts  2.85 us
    dot_general x1, matrix products, body(): jnp.einsum('tkmi,tkip->tkmp', tile_values, weights, preferred_element_typ...  2.19 us
    gather x1, local copies, waits for them, and re-layouts, body(): mon_vals = jnp.take(state_pos, mon_at, axis=0, mode='clip')  1.04 us
    mul x1, other arithmetic, body(): base_reactive * base_reactive  0.77 us
  transfers between devices with their start and end apart: 9, of which 7 were waited for; matrix products, arithmetic and copies ran while one was open for 6% of the time, Pallas kernels for 0%

profile of v7, /device:TPU:0, one launch (start us, length us, event | category | flops | bytes accessed | tf_op | source)
XLA Modules:
  0.0 37.6 jit_solution(311897640114754409)
XLA Ops:
  0.7 0.8 %mul.75 = f32[1024]{0:T(1024)S(1)} multiply(f32[1024]{0:T(1024)} %param.11, f32[1024]{0:T(1024)} %param.11) | non-fusion elementwise | flops 1024 | bytes 12288 | tf_op jit(solution)/shard_map/mul | solution.py:92
  1.5 0.7 %copy-done.1 = f32[1024]{0:T(1024)S(1)} copy-done((f32[1024]{0:T(1024)S(1)}, f32[1024]{0:T(1024)}, u32[]{:S(2)}) %copy-start.1) | copy-done | bytes 4120
  2.2 0.6 %collective-permute-start = (f32[1024,3]{0,1:T(4,128)S(1)}, f32[1024,3]{0,1:T(4,128)S(1)}, u32[]{:S(2)}, u32[]{:S(2)}) collective-permute-start(f32[1024,3]{0,1:T(4,128)S(1)} %pad_maximum_fusion.1), channel_id=1, source_target_pairs={{0,1},{1,0},{2,3},{3,2},{4,5},{5,4},{6,7},{7,6},{8,9},{9,8},{10,11... | collective-permute-start | bytes 36872 | tf_op jit(solution)/shard_map/ppermute | solution.py:93
  2.7 0.7 %copy-done.6 = s32[1,2,128]{2,1,0:T(2,128)S(1)} copy-done((s32[1,2,128]{2,1,0:T(2,128)S(1)}, s32[1,2,128]{2,1,0:T(2,128)}, u32[]{:S(2)}) %copy-start.6) | copy-done | bytes 1048
  3.4 0.6 %copy-done.8 = s32[1,128]{1,0:T(1,128)S(1)} copy-done((s32[1,128]{1,0:T(1,128)S(1)}, s32[1,128]{1,0:T(1,128)}, u32[]{:S(2)}) %copy-start.8) | copy-done | bytes 536
  4.9 0.6 %copy-done.5 = s32[512]{0:T(512)S(1)} copy-done((s32[512]{0:T(512)S(1)}, s32[512]{0:T(512)}, u32[]{:S(2)}) %copy-start.5) | copy-done | bytes 2072
  5.8 2.8 %collective-permute-start.2 = (bf16[1,4,128]{2,1,0:T(4,128)(2,1)S(1)}, bf16[1,4,128]{2,1,0:T(4,128)(2,1)S(1)}, u32[]{:S(2)}, u32[]{:S(2)}) collective-permute-start(bf16[1,4,128]{2,1,0:T(4,128)(2,1)S(1)} %pad_maximum_fusion.2), channel_id=1, source_target_pairs={{0,2},{2,0},{4,6},{6,4},{8,10},{10,8},{12,14},{14,12},{1,3},{3,1},... | collective-permute-start | bytes 3080 | tf_op jit(solution)/shard_map/ppermute | solution.py:20
  8.7 1.4 %collective-permute-done.2 = bf16[1,4,128]{2,1,0:T(4,128)(2,1)S(1)} collective-permute-done((bf16[1,4,128]{2,1,0:T(4,128)(2,1)S(1)}, bf16[1,4,128]{2,1,0:T(4,128)(2,1)S(1)}, u32[]{:S(2)}, u32[]{:S(2)}) %collective-permute-start.2) | collective-permute-done | bytes 1056 | tf_op jit(solution)/shard_map/ppermute | solution.py:20
  10.2 2.2 %collective-permute-start.3 = (bf16[2,4,128]{2,1,0:T(4,128)(2,1)S(1)}, bf16[2,4,128]{2,1,0:T(4,128)(2,1)S(1)}, u32[]{:S(2)}, u32[]{:S(2)}) collective-permute-start(bf16[2,4,128]{2,1,0:T(4,128)(2,1)S(1)} %maximum_select_fusion.2), channel_id=1, source_target_pairs={{0,4},{2,6},{4,0},{6,2},{8,12},{10,14},{12,8},{14,10},{1,5},{3,7},... | collective-permute-start | bytes 6152 | tf_op jit(solution)/shard_map/ppermute | solution.py:20
  12.4 1.5 %collective-permute-done.3 = bf16[2,4,128]{2,1,0:T(4,128)(2,1)S(1)} collective-permute-done((bf16[2,4,128]{2,1,0:T(4,128)(2,1)S(1)}, bf16[2,4,128]{2,1,0:T(4,128)(2,1)S(1)}, u32[]{:S(2)}, u32[]{:S(2)}) %collective-permute-start.3) | collective-permute-done | bytes 2080 | tf_op jit(solution)/shard_map/ppermute | solution.py:20
  13.9 3.1 %collective-permute-start.4 = (bf16[4,4,128]{2,1,0:T(4,128)(2,1)S(1)}, bf16[4,4,128]{2,1,0:T(4,128)(2,1)S(1)}, u32[]{:S(2)}, u32[]{:S(2)}) collective-permute-start(bf16[4,4,128]{2,1,0:T(4,128)(2,1)S(1)} %maximum_select_fusion.1), channel_id=1, source_target_pairs={{0,8},{2,10},{4,12},{6,14},{8,0},{10,2},{12,4},{14,6},{1,9},{3,11}... | collective-permute-start | bytes 12296 | tf_op jit(solution)/shard_map/ppermute | solution.py:20
  17.0 1.6 %collective-permute-done.4 = bf16[4,4,128]{2,1,0:T(4,128)(2,1)S(1)} collective-permute-done((bf16[4,4,128]{2,1,0:T(4,128)(2,1)S(1)}, bf16[4,4,128]{2,1,0:T(4,128)(2,1)S(1)}, u32[]{:S(2)}, u32[]{:S(2)}) %collective-permute-start.4) | collective-permute-done | bytes 4128 | tf_op jit(solution)/shard_map/ppermute | solution.py:20
  18.6 0.6 %gather_fusion.1 = bf16[16,4,128]{2,1,0:T(4,128)(2,1)S(1)} fusion(bf16[8,4,128]{2,1,0:T(4,128)(2,1)S(1)} %maximum_select_fusion, s32[1024]{0:T(1024)S(1)} %pad_clamp_fusion), kind=kCustom, calls=%fused_computation.1 | custom fusion | bytes 32832 | tf_op jit(solution)/shard_map/jit(_take)/gather | solution.py:105
  19.7 1.0 %gather_fusion = f32[512,3]{1,0:T(8,128)S(1)} fusion(f32[2048,3]{1,0:T(8,128)S(1)} %copy.26, s32[1024]{0:T(1024)S(1)} %pad_clamp_fusion.1), kind=kCustom, calls=%fused_computation | custom fusion | bytes 14336 | tf_op jit(solution)/shard_map/jit(_take)/gather | solution.py:96
  21.4 2.2 %fusion.35 = (f32[4,4,128]{2,1,0:T(4,128)S(1)}, f32[4,128]{1,0:T(4,128)S(1)}) fusion(f32[4,128]{1,0:T(4,128)S(1)} %bitcast.101, f32[4,128]{1,0:T(4,128)S(1)} %bitcast.99, bf16[4,4,128,128]{3,2,1,0:T(8,128)(2,1)S(1)} %copy-done, s32[4,4,128]{2,1,0:T(4,128)S(1)} %get-tuple-element.12, s32[4,4,128]{2,1,0:T(4,128)S(1)} %get-tuple-element.13, ...), kind=kOutput, calls=%fused_computation.93 | convolution fusion | flops 71038464 | bytes 565264 | tf_op jit(solution)/shard_map/tkmi,tkip->tkmp/dot_general | solution.py:115
  24.1 1.1 %collective-permute-done.5 = f32[8,64]{1,0:T(8,128)S(1)} collective-permute-done((f32[8,64]{1,0:T(8,128)S(1)}, f32[8,64]{1,0:T(8,128)S(1)}, u32[]{:S(2)}, u32[]{:S(2)}) %collective-permute-start.5) | collective-permute-done | bytes 2080 | tf_op jit(solution)/shard_map/ppermute | solution.py:37
  25.2 1.9 %collective-permute-start.6 = (f32[4,64]{1,0:T(4,128)S(1)}, f32[4,64]{1,0:T(4,128)S(1)}, u32[]{:S(2)}, u32[]{:S(2)}) collective-permute-start(f32[4,64]{1,0:T(4,128)S(1)} %bitcast.106), channel_id=1, source_target_pairs={{0,2},{1,3},{2,0},{3,1},{4,6},{5,7},{6,4},{7,5},{8,10},{9,11},{10,... | collective-permute-start | bytes 3080 | tf_op jit(solution)/shard_map/ppermute | solution.py:37
  27.1 1.8 %collective-permute-done.6 = f32[4,64]{1,0:T(4,128)S(1)} collective-permute-done((f32[4,64]{1,0:T(4,128)S(1)}, f32[4,64]{1,0:T(4,128)S(1)}, u32[]{:S(2)}, u32[]{:S(2)}) %collective-permute-start.6) | collective-permute-done | bytes 1056 | tf_op jit(solution)/shard_map/ppermute | solution.py:37
  28.8 2.0 %collective-permute-start.7 = (f32[2,64]{1,0:T(2,128)S(1)}, f32[2,64]{1,0:T(2,128)S(1)}, u32[]{:S(2)}, u32[]{:S(2)}) collective-permute-start(f32[2,64]{1,0:T(2,128)S(1)} %bitcast.107), channel_id=1, source_target_pairs={{0,4},{1,5},{2,6},{3,7},{4,0},{5,1},{6,2},{7,3},{8,12},{9,13},{10,... | collective-permute-start | bytes 1544 | tf_op jit(solution)/shard_map/ppermute | solution.py:37
  30.8 1.7 %collective-permute-done.7 = f32[2,64]{1,0:T(2,128)S(1)} collective-permute-done((f32[2,64]{1,0:T(2,128)S(1)}, f32[2,64]{1,0:T(2,128)S(1)}, u32[]{:S(2)}, u32[]{:S(2)}) %collective-permute-start.7) | collective-permute-done | bytes 544 | tf_op jit(solution)/shard_map/ppermute | solution.py:37
  32.5 3.0 %collective-permute-start.8 = (f32[1,64]{1,0:T(1,128)S(1)}, f32[1,64]{1,0:T(1,128)S(1)}, u32[]{:S(2)}, u32[]{:S(2)}) collective-permute-start(f32[1,64]{1,0:T(1,128)S(1)} %constant_dynamic-slice_fusion), channel_id=1, source_target_pairs={{0,8},{1,9},{2,10},{3,11},{4,12},{5,13},{6,14},{7,15},{8,0},{9,1},... | collective-permute-start | bytes 776 | tf_op jit(solution)/shard_map/ppermute | solution.py:37
  35.5 0.7 %fusion.28 = f32[512]{0:T(512)} fusion(f32[4,128]{1,0:T(4,128)S(1)} %get-tuple-element.3, f32[512]{0:T(512)S(1)} %get-tuple-element.4, pred[4]{0:T(512)(128)(4,1)S(1)} %not_reduce_fusion), kind=kLoop, calls=%fused_computation.59 | loop fusion | flops 1024 | bytes 6148 | tf_op jit(solution)/shard_map/sqrt | solution.py:130
  36.1 0.9 %collective-permute-done.8 = f32[1,64]{1,0:T(1,128)S(1)} collective-permute-done((f32[1,64]{1,0:T(1,128)S(1)}, f32[1,64]{1,0:T(1,128)S(1)}, u32[]{:S(2)}, u32[]{:S(2)}) %collective-permute-start.8) | collective-permute-done | bytes 288 | tf_op jit(solution)/shard_map/ppermute | solution.py:37
  37.0 0.5 %fusion.30 = f32[1,64]{1,0:T(1,128)} fusion(f32[1,64]{1,0:T(1,128)S(1)} %collective-permute-done.8, f32[2,64]{1,0:T(2,128)S(1)} %max.34, s32[]{:T(128)S(6)} %select_n.154), kind=kLoop, calls=%fused_computation.77 | loop fusion | flops 64 | bytes 772 | tf_op jit(solution)/shard_map/sqrt | solution.py:141
  (58 shorter events, 3.0 us)
Async XLA Ops:
  0.6 20.8 %copy-start = (bf16[4,4,128,128]{3,2,1,0:T(8,128)(2,1)S(1)}, bf16[4,4,128,128]{3,2,1,0:T(8,128)(2,1)}, u32[]{:S(2)}) copy-start(bf16[4,4,128,128]{3,2,1,0:T(8,128)(2,1)} %param.16) | copy-start | bytes 1572868
  0.6 0.8 %copy-start.3 = (f32[1024]{0:T(1024)S(1)}, f32[1024]{0:T(1024)}, u32[]{:S(2)}) copy-start(f32[1024]{0:T(1024)} %param.12) | copy-start | bytes 12292
  0.7 0.8 %copy-start.4 = (f32[1024]{0:T(1024)S(1)}, f32[1024]{0:T(1024)}, u32[]{:S(2)}) copy-start(f32[1024]{0:T(1024)} %param.13) | copy-start | bytes 12292
  1.4 0.7 %copy-start.1 = (f32[1024]{0:T(1024)S(1)}, f32[1024]{0:T(1024)}, u32[]{:S(2)}) copy-start(f32[1024]{0:T(1024)} %param.10) | copy-start | bytes 12292
  2.2 17.2 %collective-permute-start = (f32[1024,3]{0,1:T(4,128)S(1)}, f32[1024,3]{0,1:T(4,128)S(1)}, u32[]{:S(2)}, u32[]{:S(2)}) collective-permute-start(f32[1024,3]{0,1:T(4,128)S(1)} %pad_maximum_fusion.1), channel_id=1, source_target_pairs={{0,1},{1,0},{2,3},{3,2},{4,5},{5,4},{6,7},{7,6},{8,9},{9,8},{10,11... | collective-permute-start | bytes 36872 | tf_op jit(solution)/shard_map/ppermute | solution.py:93
  2.7 0.7 %copy-start.6 = (s32[1,2,128]{2,1,0:T(2,128)S(1)}, s32[1,2,128]{2,1,0:T(2,128)}, u32[]{:S(2)}) copy-start(s32[1,2,128]{2,1,0:T(2,128)} %param.19) | copy-start | bytes 3076
  3.4 0.7 %copy-start.8 = (s32[1,128]{1,0:T(1,128)S(1)}, s32[1,128]{1,0:T(1,128)}, u32[]{:S(2)}) copy-start(s32[1,128]{1,0:T(1,128)} %param.17) | copy-start | bytes 1540
  4.1 0.7 %copy-start.2 = (s32[4,4]{1,0:T(4,128)S(1)}, s32[4,4]{1,0:T(4,128)}, u32[]{:S(2)}) copy-start(s32[4,4]{1,0:T(4,128)} %param.15) | copy-start | bytes 196
  4.1 1.4 %copy-start.7 = (bf16[1,128,128]{2,1,0:T(8,128)(2,1)S(1)}, bf16[1,128,128]{2,1,0:T(8,128)(2,1)}, u32[]{:S(2)}) copy-start(bf16[1,128,128]{2,1,0:T(8,128)(2,1)} %param.18) | copy-start | bytes 98308
  4.4 1.3 %collective-permute-start.1 = (f32[2,128]{1,0:T(2,128)S(1)}, f32[2,128]{1,0:T(2,128)S(1)}, u32[]{:S(2)}, u32[]{:S(2)}) collective-permute-start(f32[2,128]{1,0:T(2,128)S(1)} %bitcast.108), channel_id=1, source_target_pairs={{0,1},{1,0},{2,3},{3,2},{4,5},{5,4},{6,7},{7,6},{8,9},{9,8},{10,11... | collective-permute-start | bytes 3080 | tf_op jit(solution)/shard_map/ppermute | solution.py:78
  4.8 0.7 %copy-start.5 = (s32[512]{0:T(512)S(1)}, s32[512]{0:T(512)}, u32[]{:S(2)}) copy-start(s32[512]{0:T(512)} %param.14) | copy-start | bytes 6148
  5.8 4.3 %collective-permute-start.2 = (bf16[1,4,128]{2,1,0:T(4,128)(2,1)S(1)}, bf16[1,4,128]{2,1,0:T(4,128)(2,1)S(1)}, u32[]{:S(2)}, u32[]{:S(2)}) collective-permute-start(bf16[1,4,128]{2,1,0:T(4,128)(2,1)S(1)} %pad_maximum_fusion.2), channel_id=1, source_target_pairs={{0,2},{2,0},{4,6},{6,4},{8,10},{10,8},{12,14},{14,12},{1,3},{3,1},... | collective-permute-start | bytes 3080 | tf_op jit(solution)/shard_map/ppermute | solution.py:20
  10.2 3.7 %collective-permute-start.3 = (bf16[2,4,128]{2,1,0:T(4,128)(2,1)S(1)}, bf16[2,4,128]{2,1,0:T(4,128)(2,1)S(1)}, u32[]{:S(2)}, u32[]{:S(2)}) collective-permute-start(bf16[2,4,128]{2,1,0:T(4,128)(2,1)S(1)} %maximum_select_fusion.2), channel_id=1, source_target_pairs={{0,4},{2,6},{4,0},{6,2},{8,12},{10,14},{12,8},{14,10},{1,5},{3,7},... | collective-permute-start | bytes 6152 | tf_op jit(solution)/shard_map/ppermute | solution.py:20
  13.9 4.7 %collective-permute-start.4 = (bf16[4,4,128]{2,1,0:T(4,128)(2,1)S(1)}, bf16[4,4,128]{2,1,0:T(4,128)(2,1)S(1)}, u32[]{:S(2)}, u32[]{:S(2)}) collective-permute-start(bf16[4,4,128]{2,1,0:T(4,128)(2,1)S(1)} %maximum_select_fusion.1), channel_id=1, source_target_pairs={{0,8},{2,10},{4,12},{6,14},{8,0},{10,2},{12,4},{14,6},{1,9},{3,11}... | collective-permute-start | bytes 12296 | tf_op jit(solution)/shard_map/ppermute | solution.py:20
  23.9 1.2 %collective-permute-start.5 = (f32[8,64]{1,0:T(8,128)S(1)}, f32[8,64]{1,0:T(8,128)S(1)}, u32[]{:S(2)}, u32[]{:S(2)}) collective-permute-start(f32[8,64]{1,0:T(8,128)S(1)} %bitcast.104), channel_id=1, source_target_pairs={{0,1},{1,0},{2,3},{3,2},{4,5},{5,4},{6,7},{7,6},{8,9},{9,8},{10,11... | collective-permute-start | bytes 6152 | tf_op jit(solution)/shard_map/ppermute | solution.py:37
  25.2 3.6 %collective-permute-start.6 = (f32[4,64]{1,0:T(4,128)S(1)}, f32[4,64]{1,0:T(4,128)S(1)}, u32[]{:S(2)}, u32[]{:S(2)}) collective-permute-start(f32[4,64]{1,0:T(4,128)S(1)} %bitcast.106), channel_id=1, source_target_pairs={{0,2},{1,3},{2,0},{3,1},{4,6},{5,7},{6,4},{7,5},{8,10},{9,11},{10,... | collective-permute-start | bytes 3080 | tf_op jit(solution)/shard_map/ppermute | solution.py:37
  28.8 3.6 %collective-permute-start.7 = (f32[2,64]{1,0:T(2,128)S(1)}, f32[2,64]{1,0:T(2,128)S(1)}, u32[]{:S(2)}, u32[]{:S(2)}) collective-permute-start(f32[2,64]{1,0:T(2,128)S(1)} %bitcast.107), channel_id=1, source_target_pairs={{0,4},{1,5},{2,6},{3,7},{4,0},{5,1},{6,2},{7,3},{8,12},{9,13},{10,... | collective-permute-start | bytes 1544 | tf_op jit(solution)/shard_map/ppermute | solution.py:37
  32.5 4.5 %collective-permute-start.8 = (f32[1,64]{1,0:T(1,128)S(1)}, f32[1,64]{1,0:T(1,128)S(1)}, u32[]{:S(2)}, u32[]{:S(2)}) collective-permute-start(f32[1,64]{1,0:T(1,128)S(1)} %constant_dynamic-slice_fusion), channel_id=1, source_target_pairs={{0,8},{1,9},{2,10},{3,11},{4,12},{5,13},{6,14},{7,15},{8,0},{9,1},... | collective-permute-start | bytes 776 | tf_op jit(solution)/shard_map/ppermute | solution.py:37

commit v8 on v6

--- a/solution.py
+++ b/solution.py
@@ -1,6 +1,8 @@
 import jax
 import jax.numpy as jnp
 from jax import lax
+from jax.experimental import pallas as pl
+from jax.experimental.pallas import tpu as pltpu
 from jax.sharding import PartitionSpec as P
 
 
@@ -39,6 +41,42 @@
     return cur[0]
 
 
+def prep_kernel(me_ref, real_ref, ids_ref, pairs_ref, coupling_ref, flow_ref, coupled_ref):
+    half_len = real_ref.shape[1]
+    outages = ids_ref.shape[1]
+    local_at = ids_ref[...] - me_ref[0] * half_len
+    branch_iota = lax.broadcasted_iota(jnp.int32, (half_len, outages), 0)
+    pick_branch = (branch_iota == local_at).astype(jnp.bfloat16)
+    real = real_ref[...].astype(jnp.bfloat16)
+    flow_part = jnp.dot(real, pick_branch, preferred_element_type=jnp.float32)
+    pairs = pairs_ref[0]
+    pair_at = jnp.concatenate([pairs[0:1], pairs[1:2]], axis=1)
+    pair_to = jnp.concatenate([pairs[1:2], pairs[0:1]], axis=1)
+    outage_iota = lax.broadcasted_iota(jnp.int32, (outages, pair_at.shape[1]), 0)
+    pick_at = (outage_iota == pair_at).astype(jnp.bfloat16)
+    flow_ref[...] = jnp.dot(
+        flow_part.astype(jnp.bfloat16), pick_at, preferred_element_type=jnp.float32
+    )
+    columns = jnp.dot(coupling_ref[0], pick_at, preferred_element_type=jnp.float32)
+    rows = (outage_iota == pair_to).astype(jnp.float32)
+    coupled_ref[...] = jnp.sum(columns * rows, axis=0, keepdims=True)
+
+
+def prep_call(me_state, base_real, outage_ids, outage_pairs, coupling):
+    pair_count = outage_pairs.shape[2]
+    vmem = pl.BlockSpec(memory_space=pltpu.VMEM)
+    flow, coupled = pl.pallas_call(
+        prep_kernel,
+        out_shape=(
+            jax.ShapeDtypeStruct((1, 2 * pair_count), jnp.float32),
+            jax.ShapeDtypeStruct((1, 2 * pair_count), jnp.float32),
+        ),
+        in_specs=[pl.BlockSpec(memory_space=pltpu.SMEM), vmem, vmem, vmem, vmem],
+        out_specs=(vmem, vmem),
+    )(me_state.reshape(1), base_real.reshape(1, -1), outage_ids, outage_pairs, coupling)
+    return flow.reshape(2, pair_count), coupled.reshape(2, pair_count)[::-1]
+
+
 def body(
     base_real,
     base_reactive,
@@ -62,26 +100,10 @@
 
     first_idx = outage_pairs[0, 0]
     second_idx = outage_pairs[0, 1]
-    local_at = outage_ids[0] - me_state * half_len
-    branch_iota = lax.broadcasted_iota(jnp.int32, (pair_count, half_len), 1)
-    pick_branch = (branch_iota == local_at[:, None]).astype(jnp.bfloat16)
-    flow_part = jnp.dot(
-        pick_branch, base_real.astype(jnp.bfloat16), preferred_element_type=jnp.float32
-    )
-    pair_at = jnp.concatenate([first_idx, second_idx])
-    pair_to = jnp.concatenate([second_idx, first_idx])
-    outage_iota = lax.broadcasted_iota(jnp.int32, (2 * pair_count, pair_count), 1)
-    pick_at = (outage_iota == pair_at[:, None]).astype(jnp.bfloat16)
-    flow_pairs = jnp.dot(
-        pick_at, flow_part.astype(jnp.bfloat16), preferred_element_type=jnp.float32
-    ).reshape(2, pair_count)
+    flow_pairs, coupled = prep_call(me_state, base_real, outage_ids, outage_pairs, coupling)
     flow_other = lax.ppermute(
         flow_pairs, "state", [(j, (j + 1) % halves) for j in range(halves)]
     )
-    coupled_rows = jnp.dot(pick_at, coupling[0], preferred_element_type=jnp.float32)
-    coupled = jnp.sum(
-        jnp.where(outage_iota == pair_to[:, None], coupled_rows, 0.0), axis=1
-    ).reshape(2, pair_count)
     flows = flow_pairs + flow_other
     determinant = 1.0 - coupled[0] * coupled[1]
     w_first = (flows[0] + coupled[0] * flows[1]) / determinant
@@ -101,10 +123,14 @@
     mon_real = mon_vals[:, 0].reshape(tiles_dev, tile_size)
     react_sq = mon_vals[:, 1].reshape(tiles_dev, tile_size)
     mon_limit = mon_vals[:, 2].reshape(tiles_dev, tile_size)
+    inv_limit_sq = 1.0 / (mon_limit * mon_limit)
+    base_sq = (mon_real * mon_real + react_sq) * inv_limit_sq
 
     valid = tile_ids >= 0
     block_of = jnp.clip(tile_ids, 0, blocks - 1)
-    chosen = jnp.take(table, block_of, axis=0)
+    pick_block = (block_of.reshape(-1, 1) == jnp.arange(blocks, dtype=jnp.int32)[None, :]).astype(jnp.bfloat16)
+    chosen = jnp.dot(pick_block, table.reshape(blocks, -1), preferred_element_type=jnp.float32)
+    chosen = chosen.astype(jnp.bfloat16).reshape(tiles_dev, slot_count, 4, pair_count)
     rows_iota = lax.broadcasted_iota(jnp.int32, (1, 1, tile_size, pair_count), 2)
     first_at = chosen[:, :, 2].astype(jnp.int32)[:, :, None, :]
     second_at = chosen[:, :, 3].astype(jnp.int32)[:, :, None, :]
@@ -117,13 +143,11 @@
     delta = jnp.einsum(
         "tkmi,tkip->tkmp", tile_values, weights, preferred_element_type=jnp.float32
     )
-    inv_limit_sq = 1.0 / (mon_limit * mon_limit)
     post = mon_real[:, None, :, None] + delta
     squared = (post * post + react_sq[:, None, :, None]) * inv_limit_sq[:, None, :, None]
     neg = jnp.float32(-jnp.inf)
     squared = jnp.where(valid[:, :, None, None], squared, neg)
 
-    base_sq = (mon_real * mon_real + react_sq) * inv_limit_sq
     block_iota = jnp.arange(blocks, dtype=jnp.int32)
     matches = tile_ids[:, :, None] == block_iota[None, None, :]
     absent = jnp.logical_not(jnp.any(matches, axis=1))

time: 37.8 us -> 39.6 us (1.048)
  Pallas kernels: 0 us -> 1.66 us
  local copies, waits for them, and re-layouts: 5.04 us -> 5.68 us
  matrix products: 2.83 us -> 2.38 us
    pallas_call x0 -> x1, Pallas kernels: none -> 1.66 us  [prep_call(): pl.pallas_call(prep_kernel, out_shape=(jax.ShapeDtypeStruct((1, 2 * pair_...]
    unnamed x18 -> x24, local copies, waits for them, and re-layouts: 2.85 us -> 4.06 us
    gather x1 -> x0, local copies, waits for them, and re-layouts: 0.59 us -> none  [body(): chosen = jnp.take(table, block_of, axis=0)]
    dot_general x2 -> x1, matrix products: 0.65 us -> 0.19 us  [body(): jnp.dot(pick_block, table.reshape(blocks, -1), preferred_element_type=jnp...]
  transfers between devices with their start and end apart: 9 -> 9, of which waited for: 7 -> 7; matrix products, arithmetic and copies ran while one was open for 6% -> 3% of each run, Pallas kernels for 0% -> 4%
where the time goes in v8:
time: 39.6 us; the launch traced here: 39.2 us
  starting transfers between devices  15.3 us (39%)
  waiting for transfers between devices  10.1 us (26%)
  local copies, waits for them, and re-layouts  5.68 us (14%)
  other arithmetic  3.24 us (8%)
  matrix products  2.38 us (6%)
  Pallas kernels  1.66 us (4%)
  between operations  0.91 us (2%)
    ppermute x3, starting transfers between devices, gather_doubling(): other = lax.ppermute(cur, axes, [(j, j ^ bit) for j in range(n)])  7.83 us
    ppermute x4, starting transfers between devices, scatter_max(): lax.ppermute(send, axes, [(j, j ^ bit) for j in range(n)])  6.91 us
    ppermute x4, waiting for transfers between devices, scatter_max(): lax.ppermute(send, axes, [(j, j ^ bit) for j in range(n)])  5.42 us
    ppermute x3, waiting for transfers between devices, gather_doubling(): other = lax.ppermute(cur, axes, [(j, j ^ bit) for j in range(n)])  4.63 us
    unnamed x24, local copies, waits for them, and re-layouts  4.06 us
    dot_general x1, matrix products, body(): jnp.einsum('tkmi,tkip->tkmp', tile_values, weights, preferred_element_typ...  2.19 us
    pallas_call x1, Pallas kernels, prep_call(): pl.pallas_call(prep_kernel, out_shape=(jax.ShapeDtypeStruct((1, 2 * pair_...  1.66 us
    gather x1, local copies, waits for them, and re-layouts, body(): mon_vals = jnp.take(state_pos, mon_at, axis=0, mode='clip')  1.04 us
  transfers between devices with their start and end apart: 9, of which 7 were waited for; matrix products, arithmetic and copies ran while one was open for 3% of the time, Pallas kernels for 4%

profile of v8, /device:TPU:0, one launch (start us, length us, event | category | flops | bytes accessed | tf_op | source)
XLA Modules:
  0.0 39.2 jit_solution(11164686044014961988)
XLA Ops:
  0.7 0.8 %mul.78 = f32[1024]{0:T(1024)S(1)} multiply(f32[1024]{0:T(1024)} %param.11, f32[1024]{0:T(1024)} %param.11) | non-fusion elementwise | flops 1024 | bytes 12288 | tf_op jit(solution)/shard_map/mul | solution.py:115
  1.5 0.7 %copy-done.1 = f32[1024]{0:T(1024)S(1)} copy-done((f32[1024]{0:T(1024)S(1)}, f32[1024]{0:T(1024)}, u32[]{:S(2)}) %copy-start.1) | copy-done | bytes 4120
  2.7 1.7 %shard_map.113 = (f32[1,256]{1,0:T(1,128)}, f32[1,256]{1,0:T(1,128)}) custom-call(s32[1]{0:T(128)} %bitcast.3.me_ref, f32[1,1024]{1,0:T(1,128)} %bitcast.54, s32[1,128]{1,0:T(1,128)} %ids_ref.1, s32[1,2,128]{2,1,0:T(2,128)} %pairs_ref.1, bf16[1,128,128]{2,1,0:T(8,128)(2,1)} %coupling_ref.1), custom_call_target="tpu_custom_call" | custom-call | tf_op jit(solution)/shard_map/pallas_call | solution.py:68
  4.4 0.7 %copy-done.9 = f32[1,256]{1,0:T(1,128)S(1)} copy-done((f32[1,256]{1,0:T(1,128)S(1)}, f32[1,256]{1,0:T(1,128)}, u32[]{:S(2)}) %copy-start.9) | copy-done | bytes 1048
  5.1 0.6 %copy-done.3 = s32[4,4]{1,0:T(4,128)S(1)} copy-done((s32[4,4]{1,0:T(4,128)S(1)}, s32[4,4]{1,0:T(4,128)}, u32[]{:S(2)}) %copy-start.3) | copy-done | bytes 88
  5.9 0.7 %copy-done.7 = s32[512]{0:T(512)S(1)} copy-done((s32[512]{0:T(512)S(1)}, s32[512]{0:T(512)}, u32[]{:S(2)}) %copy-start.7) | copy-done | bytes 2072
  6.8 0.7 %copy-done.8 = f32[1,256]{1,0:T(1,128)S(1)} copy-done((f32[1,256]{1,0:T(1,128)S(1)}, f32[1,256]{1,0:T(1,128)}, u32[]{:S(2)}) %copy-start.8) | copy-done | bytes 1048
  7.5 2.6 %collective-permute-start.2 = (bf16[1,4,128]{2,1,0:T(4,128)(2,1)S(1)}, bf16[1,4,128]{2,1,0:T(4,128)(2,1)S(1)}, u32[]{:S(2)}, u32[]{:S(2)}) collective-permute-start(bf16[1,4,128]{2,1,0:T(4,128)(2,1)S(1)} %maximum_convert_fusion), channel_id=1, source_target_pairs={{0,2},{2,0},{4,6},{6,4},{8,10},{10,8},{12,14},{14,12},{1,3},{3,1},... | collective-permute-start | bytes 3080 | tf_op jit(solution)/shard_map/ppermute | solution.py:22
  10.1 1.5 %collective-permute-done.2 = bf16[1,4,128]{2,1,0:T(4,128)(2,1)S(1)} collective-permute-done((bf16[1,4,128]{2,1,0:T(4,128)(2,1)S(1)}, bf16[1,4,128]{2,1,0:T(4,128)(2,1)S(1)}, u32[]{:S(2)}, u32[]{:S(2)}) %collective-permute-start.2) | collective-permute-done | bytes 1056 | tf_op jit(solution)/shard_map/ppermute | solution.py:22
  11.6 2.2 %collective-permute-start.3 = (bf16[2,4,128]{2,1,0:T(4,128)(2,1)S(1)}, bf16[2,4,128]{2,1,0:T(4,128)(2,1)S(1)}, u32[]{:S(2)}, u32[]{:S(2)}) collective-permute-start(bf16[2,4,128]{2,1,0:T(4,128)(2,1)S(1)} %maximum_select_fusion.4), channel_id=1, source_target_pairs={{0,4},{2,6},{4,0},{6,2},{8,12},{10,14},{12,8},{14,10},{1,5},{3,7},... | collective-permute-start | bytes 6152 | tf_op jit(solution)/shard_map/ppermute | solution.py:22
  13.8 1.5 %collective-permute-done.3 = bf16[2,4,128]{2,1,0:T(4,128)(2,1)S(1)} collective-permute-done((bf16[2,4,128]{2,1,0:T(4,128)(2,1)S(1)}, bf16[2,4,128]{2,1,0:T(4,128)(2,1)S(1)}, u32[]{:S(2)}, u32[]{:S(2)}) %collective-permute-start.3) | collective-permute-done | bytes 2080 | tf_op jit(solution)/shard_map/ppermute | solution.py:22
  15.4 3.1 %collective-permute-start.4 = (bf16[4,4,128]{2,1,0:T(4,128)(2,1)S(1)}, bf16[4,4,128]{2,1,0:T(4,128)(2,1)S(1)}, u32[]{:S(2)}, u32[]{:S(2)}) collective-permute-start(bf16[4,4,128]{2,1,0:T(4,128)(2,1)S(1)} %maximum_select_fusion.3), channel_id=1, source_target_pairs={{0,8},{2,10},{4,12},{6,14},{8,0},{10,2},{12,4},{14,6},{1,9},{3,11}... | collective-permute-start | bytes 12296 | tf_op jit(solution)/shard_map/ppermute | solution.py:22
  18.5 1.6 %collective-permute-done.4 = bf16[4,4,128]{2,1,0:T(4,128)(2,1)S(1)} collective-permute-done((bf16[4,4,128]{2,1,0:T(4,128)(2,1)S(1)}, bf16[4,4,128]{2,1,0:T(4,128)(2,1)S(1)}, u32[]{:S(2)}, u32[]{:S(2)}) %collective-permute-start.4) | collective-permute-done | bytes 4128 | tf_op jit(solution)/shard_map/ppermute | solution.py:22
  20.4 0.7 %copy-done.2 = f32[1024]{0:T(1024)S(1)} copy-done((f32[1024]{0:T(1024)S(1)}, f32[1024]{0:T(1024)}, u32[]{:S(2)}) %copy-start.2) | copy-done | bytes 4120
  21.4 1.0 %gather_fusion = f32[512,3]{1,0:T(8,128)S(1)} fusion(f32[2048,3]{1,0:T(8,128)S(1)} %copy.30, s32[1024]{0:T(1024)S(1)} %pad_clamp_fusion), kind=kCustom, calls=%fused_computation | custom fusion | bytes 14336 | tf_op jit(solution)/shard_map/jit(_take)/gather | solution.py:122
  23.1 2.2 %fusion.31 = (f32[4,4,128]{2,1,0:T(4,128)S(1)}, f32[4,128]{1,0:T(4,128)S(1)}) fusion(f32[4,128]{1,0:T(4,128)S(1)} %bitcast.65, f32[4,128]{1,0:T(4,128)S(1)} %bitcast.63, bf16[4,4,128,128]{3,2,1,0:T(8,128)(2,1)S(1)} %copy-done, s32[4,4,128]{2,1,0:T(4,128)S(1)} %bitcast.72, s32[4,4,128]{2,1,0:T(4,128)S(1)} %bitcast.73, ...), kind=kOutput, calls=%fused_computation.81 | convolution fusion | flops 71038464 | bytes 565264 | tf_op jit(solution)/shard_map/tkmi,tkip->tkmp/dot_general | solution.py:143
  25.8 1.1 %collective-permute-done.5 = f32[8,64]{1,0:T(8,128)S(1)} collective-permute-done((f32[8,64]{1,0:T(8,128)S(1)}, f32[8,64]{1,0:T(8,128)S(1)}, u32[]{:S(2)}, u32[]{:S(2)}) %collective-permute-start.5) | collective-permute-done | bytes 2080 | tf_op jit(solution)/shard_map/ppermute | solution.py:39
  26.9 1.9 %collective-permute-start.6 = (f32[4,64]{1,0:T(4,128)S(1)}, f32[4,64]{1,0:T(4,128)S(1)}, u32[]{:S(2)}, u32[]{:S(2)}) collective-permute-start(f32[4,64]{1,0:T(4,128)S(1)} %bitcast.79), channel_id=1, source_target_pairs={{0,2},{1,3},{2,0},{3,1},{4,6},{5,7},{6,4},{7,5},{8,10},{9,11},{10,... | collective-permute-start | bytes 3080 | tf_op jit(solution)/shard_map/ppermute | solution.py:39
  28.8 1.8 %collective-permute-done.6 = f32[4,64]{1,0:T(4,128)S(1)} collective-permute-done((f32[4,64]{1,0:T(4,128)S(1)}, f32[4,64]{1,0:T(4,128)S(1)}, u32[]{:S(2)}, u32[]{:S(2)}) %collective-permute-start.6) | collective-permute-done | bytes 1056 | tf_op jit(solution)/shard_map/ppermute | solution.py:39
  30.5 2.0 %collective-permute-start.7 = (f32[2,64]{1,0:T(2,128)S(1)}, f32[2,64]{1,0:T(2,128)S(1)}, u32[]{:S(2)}, u32[]{:S(2)}) collective-permute-start(f32[2,64]{1,0:T(2,128)S(1)} %bitcast.82), channel_id=1, source_target_pairs={{0,4},{1,5},{2,6},{3,7},{4,0},{5,1},{6,2},{7,3},{8,12},{9,13},{10,... | collective-permute-start | bytes 1544 | tf_op jit(solution)/shard_map/ppermute | solution.py:39
  32.5 1.7 %collective-permute-done.7 = f32[2,64]{1,0:T(2,128)S(1)} collective-permute-done((f32[2,64]{1,0:T(2,128)S(1)}, f32[2,64]{1,0:T(2,128)S(1)}, u32[]{:S(2)}, u32[]{:S(2)}) %collective-permute-start.7) | collective-permute-done | bytes 544 | tf_op jit(solution)/shard_map/ppermute | solution.py:39
  34.2 3.0 %collective-permute-start.8 = (f32[1,64]{1,0:T(1,128)S(1)}, f32[1,64]{1,0:T(1,128)S(1)}, u32[]{:S(2)}, u32[]{:S(2)}) collective-permute-start(f32[1,64]{1,0:T(1,128)S(1)} %constant_dynamic-slice_fusion), channel_id=1, source_target_pairs={{0,8},{1,9},{2,10},{3,11},{4,12},{5,13},{6,14},{7,15},{8,0},{9,1},... | collective-permute-start | bytes 776 | tf_op jit(solution)/shard_map/ppermute | solution.py:39
  37.2 0.7 %fusion.24 = f32[512]{0:T(512)} fusion(f32[4,128]{1,0:T(4,128)S(1)} %get-tuple-element.7, f32[512]{0:T(512)S(1)} %get-tuple-element.8, pred[4]{0:T(512)(128)(4,1)S(1)} %not_reduce_fusion), kind=kLoop, calls=%fused_computation.56 | loop fusion | flops 1024 | bytes 6148 | tf_op jit(solution)/shard_map/sqrt | solution.py:158
  37.8 0.9 %collective-permute-done.8 = f32[1,64]{1,0:T(1,128)S(1)} collective-permute-done((f32[1,64]{1,0:T(1,128)S(1)}, f32[1,64]{1,0:T(1,128)S(1)}, u32[]{:S(2)}, u32[]{:S(2)}) %collective-permute-start.8) | collective-permute-done | bytes 288 | tf_op jit(solution)/shard_map/ppermute | solution.py:39
  (61 shorter events, 3.3 us)
Async XLA Ops:
  0.6 22.4 %copy-start = (bf16[4,4,128,128]{3,2,1,0:T(8,128)(2,1)S(1)}, bf16[4,4,128,128]{3,2,1,0:T(8,128)(2,1)}, u32[]{:S(2)}) copy-start(bf16[4,4,128,128]{3,2,1,0:T(8,128)(2,1)} %param.16) | copy-start | bytes 1572868
  0.6 0.8 %copy-start.4 = (f32[1024]{0:T(1024)S(1)}, f32[1024]{0:T(1024)}, u32[]{:S(2)}) copy-start(f32[1024]{0:T(1024)} %param.12) | copy-start | bytes 12292
  0.7 0.8 %copy-start.5 = (f32[1024]{0:T(1024)S(1)}, f32[1024]{0:T(1024)}, u32[]{:S(2)}) copy-start(f32[1024]{0:T(1024)} %param.13) | copy-start | bytes 12292
  1.4 0.7 %copy-start.1 = (f32[1024]{0:T(1024)S(1)}, f32[1024]{0:T(1024)}, u32[]{:S(2)}) copy-start(f32[1024]{0:T(1024)} %param.10) | copy-start | bytes 12292
  2.2 18.2 %collective-permute-start = (f32[1024,3]{0,1:T(4,128)S(1)}, f32[1024,3]{0,1:T(4,128)S(1)}, u32[]{:S(2)}, u32[]{:S(2)}) collective-permute-start(f32[1024,3]{0,1:T(4,128)S(1)} %pad_maximum_fusion.1), channel_id=1, source_target_pairs={{0,1},{1,0},{2,3},{3,2},{4,5},{5,4},{6,7},{7,6},{8,9},{9,8},{10,11... | collective-permute-start | bytes 36872 | tf_op jit(solution)/shard_map/ppermute | solution.py:117
  4.4 0.7 %copy-start.9 = (f32[1,256]{1,0:T(1,128)S(1)}, f32[1,256]{1,0:T(1,128)}, u32[]{:S(2)}) copy-start(f32[1,256]{1,0:T(1,128)} %get-tuple-element.4) | copy-start | bytes 3076
  4.4 0.7 %copy-start.6 = (s32[1,2,128]{2,1,0:T(2,128)S(1)}, s32[1,2,128]{2,1,0:T(2,128)}, u32[]{:S(2)}) copy-start(s32[1,2,128]{2,1,0:T(2,128)} %pairs_ref.1) | copy-start | bytes 3076
  5.1 0.7 %copy-start.3 = (s32[4,4]{1,0:T(4,128)S(1)}, s32[4,4]{1,0:T(4,128)}, u32[]{:S(2)}) copy-start(s32[4,4]{1,0:T(4,128)} %param.15) | copy-start | bytes 196
  5.1 1.7 %collective-permute-start.1 = (f32[2,128]{1,0:T(2,128)S(1)}, f32[2,128]{1,0:T(2,128)S(1)}, u32[]{:S(2)}, u32[]{:S(2)}) collective-permute-start(f32[2,128]{1,0:T(2,128)S(1)} %bitcast.80), channel_id=1, source_target_pairs={{0,1},{1,0},{2,3},{3,2},{4,5},{5,4},{6,7},{7,6},{8,9},{9,8},{10,11... | collective-permute-start | bytes 3080 | tf_op jit(solution)/shard_map/ppermute | solution.py:104
  5.9 0.7 %copy-start.7 = (s32[512]{0:T(512)S(1)}, s32[512]{0:T(512)}, u32[]{:S(2)}) copy-start(s32[512]{0:T(512)} %param.14) | copy-start | bytes 6148
  6.8 0.7 %copy-start.8 = (f32[1,256]{1,0:T(1,128)S(1)}, f32[1,256]{1,0:T(1,128)}, u32[]{:S(2)}) copy-start(f32[1,256]{1,0:T(1,128)} %get-tuple-element.5) | copy-start | bytes 3076
  7.5 4.1 %collective-permute-start.2 = (bf16[1,4,128]{2,1,0:T(4,128)(2,1)S(1)}, bf16[1,4,128]{2,1,0:T(4,128)(2,1)S(1)}, u32[]{:S(2)}, u32[]{:S(2)}) collective-permute-start(bf16[1,4,128]{2,1,0:T(4,128)(2,1)S(1)} %maximum_convert_fusion), channel_id=1, source_target_pairs={{0,2},{2,0},{4,6},{6,4},{8,10},{10,8},{12,14},{14,12},{1,3},{3,1},... | collective-permute-start | bytes 3080 | tf_op jit(solution)/shard_map/ppermute | solution.py:22
  11.6 3.7 %collective-permute-start.3 = (bf16[2,4,128]{2,1,0:T(4,128)(2,1)S(1)}, bf16[2,4,128]{2,1,0:T(4,128)(2,1)S(1)}, u32[]{:S(2)}, u32[]{:S(2)}) collective-permute-start(bf16[2,4,128]{2,1,0:T(4,128)(2,1)S(1)} %maximum_select_fusion.4), channel_id=1, source_target_pairs={{0,4},{2,6},{4,0},{6,2},{8,12},{10,14},{12,8},{14,10},{1,5},{3,7},... | collective-permute-start | bytes 6152 | tf_op jit(solution)/shard_map/ppermute | solution.py:22
  15.4 4.7 %collective-permute-start.4 = (bf16[4,4,128]{2,1,0:T(4,128)(2,1)S(1)}, bf16[4,4,128]{2,1,0:T(4,128)(2,1)S(1)}, u32[]{:S(2)}, u32[]{:S(2)}) collective-permute-start(bf16[4,4,128]{2,1,0:T(4,128)(2,1)S(1)} %maximum_select_fusion.3), channel_id=1, source_target_pairs={{0,8},{2,10},{4,12},{6,14},{8,0},{10,2},{12,4},{14,6},{1,9},{3,11}... | collective-permute-start | bytes 12296 | tf_op jit(solution)/shard_map/ppermute | solution.py:22
  20.3 0.7 %copy-start.2 = (f32[1024]{0:T(1024)S(1)}, f32[1024]{0:T(1024)}, u32[]{:S(2)}) copy-start(f32[1024]{0:T(1024)} %param.10) | copy-start | bytes 12292
  25.6 1.2 %collective-permute-start.5 = (f32[8,64]{1,0:T(8,128)S(1)}, f32[8,64]{1,0:T(8,128)S(1)}, u32[]{:S(2)}, u32[]{:S(2)}) collective-permute-start(f32[8,64]{1,0:T(8,128)S(1)} %bitcast.74), channel_id=1, source_target_pairs={{0,1},{1,0},{2,3},{3,2},{4,5},{5,4},{6,7},{7,6},{8,9},{9,8},{10,11... | collective-permute-start | bytes 6152 | tf_op jit(solution)/shard_map/ppermute | solution.py:39
  26.9 3.6 %collective-permute-start.6 = (f32[4,64]{1,0:T(4,128)S(1)}, f32[4,64]{1,0:T(4,128)S(1)}, u32[]{:S(2)}, u32[]{:S(2)}) collective-permute-start(f32[4,64]{1,0:T(4,128)S(1)} %bitcast.79), channel_id=1, source_target_pairs={{0,2},{1,3},{2,0},{3,1},{4,6},{5,7},{6,4},{7,5},{8,10},{9,11},{10,... | collective-permute-start | bytes 3080 | tf_op jit(solution)/shard_map/ppermute | solution.py:39
  30.5 3.6 %collective-permute-start.7 = (f32[2,64]{1,0:T(2,128)S(1)}, f32[2,64]{1,0:T(2,128)S(1)}, u32[]{:S(2)}, u32[]{:S(2)}) collective-permute-start(f32[2,64]{1,0:T(2,128)S(1)} %bitcast.82), channel_id=1, source_target_pairs={{0,4},{1,5},{2,6},{3,7},{4,0},{5,1},{6,2},{7,3},{8,12},{9,13},{10,... | collective-permute-start | bytes 1544 | tf_op jit(solution)/shard_map/ppermute | solution.py:39
  34.2 4.5 %collective-permute-start.8 = (f32[1,64]{1,0:T(1,128)S(1)}, f32[1,64]{1,0:T(1,128)S(1)}, u32[]{:S(2)}, u32[]{:S(2)}) collective-permute-start(f32[1,64]{1,0:T(1,128)S(1)} %constant_dynamic-slice_fusion), channel_id=1, source_target_pairs={{0,8},{1,9},{2,10},{3,11},{4,12},{5,13},{6,14},{7,15},{8,0},{9,1},... | collective-permute-start | bytes 776 | tf_op jit(solution)/shard_map/ppermute | solution.py:39

commit v9 on v7

--- a/solution.py
+++ b/solution.py
@@ -51,7 +51,7 @@
     coupling,
     outage_pairs,
 ):
-    tiles_dev, _, tile_size, _ = tile_values.shape
+    tiles_dev, slot_count, tile_size, _ = tile_values.shape
     pair_count = outage_pairs.shape[2]
     blocks = lax.axis_size("blk")
     halves = lax.axis_size("state")
@@ -102,7 +102,9 @@
 
     valid = tile_ids >= 0
     block_of = jnp.clip(tile_ids, 0, blocks - 1)
-    chosen = jnp.take(table, block_of, axis=0)
+    pick_block = (block_of.reshape(-1, 1) == jnp.arange(blocks, dtype=jnp.int32)[None, :]).astype(jnp.bfloat16)
+    chosen = jnp.dot(pick_block, table.reshape(blocks, -1), preferred_element_type=jnp.float32)
+    chosen = chosen.astype(jnp.bfloat16).reshape(tiles_dev, slot_count, 4, pair_count)
     rows_iota = lax.broadcasted_iota(jnp.int32, (1, 1, tile_size, pair_count), 2)
     first_at = chosen[:, :, 2].astype(jnp.int32)[:, :, None, :]
     second_at = chosen[:, :, 3].astype(jnp.int32)[:, :, None, :]

time: 37.8 us -> 37.9 us (level)
    gather x1 -> x0, local copies, waits for them, and re-layouts: 0.59 us -> none  [body(): chosen = jnp.take(table, block_of, axis=0)]
    unnamed x18 -> x22, local copies, waits for them, and re-layouts: 2.85 us -> 3.37 us
  transfers between devices with their start and end apart: 9 -> 9, of which waited for: 7 -> 7; matrix products, arithmetic and copies ran while one was open for 6% -> 5% of each run, Pallas kernels for 0% -> 0%
where the time goes in v9:
time: 37.9 us; the launch traced here: 37.6 us
  starting transfers between devices  15.4 us (41%)
  waiting for transfers between devices  10.1 us (27%)
  local copies, waits for them, and re-layouts  4.99 us (13%)
  other arithmetic  3.26 us (9%)
  matrix products  3.03 us (8%)
  between operations  0.94 us (2%)
    ppermute x3, starting transfers between devices, gather_doubling(): other = lax.ppermute(cur, axes, [(j, j ^ bit) for j in range(n)])  7.84 us
    ppermute x4, starting transfers between devices, scatter_max(): lax.ppermute(send, axes, [(j, j ^ bit) for j in range(n)])  6.91 us
    ppermute x4, waiting for transfers between devices, scatter_max(): lax.ppermute(send, axes, [(j, j ^ bit) for j in range(n)])  5.42 us
    ppermute x3, waiting for transfers between devices, gather_doubling(): other = lax.ppermute(cur, axes, [(j, j ^ bit) for j in range(n)])  4.63 us
    unnamed x22, local copies, waits for them, and re-layouts  3.37 us
    dot_general x1, matrix products, body(): jnp.einsum('tkmi,tkip->tkmp', tile_values, weights, preferred_element_typ...  2.19 us
    gather x1, local copies, waits for them, and re-layouts, body(): mon_vals = jnp.take(state_pos, mon_at, axis=0, mode='clip')  1.04 us
    mul x1, other arithmetic, body(): base_reactive * base_reactive  0.77 us
  transfers between devices with their start and end apart: 9, of which 7 were waited for; matrix products, arithmetic and copies ran while one was open for 5% of the time, Pallas kernels for 0%

profile of v9, /device:TPU:0, one launch (start us, length us, event | category | flops | bytes accessed | tf_op | source)
XLA Modules:
  0.0 37.6 jit_solution(6764887873429208008)
XLA Ops:
  0.7 0.8 %mul.75 = f32[1024]{0:T(1024)S(1)} multiply(f32[1024]{0:T(1024)} %param.11, f32[1024]{0:T(1024)} %param.11) | non-fusion elementwise | flops 1024 | bytes 12288 | tf_op jit(solution)/shard_map/mul | solution.py:92
  1.5 0.7 %copy-done.1 = f32[1024]{0:T(1024)S(1)} copy-done((f32[1024]{0:T(1024)S(1)}, f32[1024]{0:T(1024)}, u32[]{:S(2)}) %copy-start.1) | copy-done | bytes 4120
  2.2 0.6 %collective-permute-start = (f32[1024,3]{0,1:T(4,128)S(1)}, f32[1024,3]{0,1:T(4,128)S(1)}, u32[]{:S(2)}, u32[]{:S(2)}) collective-permute-start(f32[1024,3]{0,1:T(4,128)S(1)} %pad_maximum_fusion.1), channel_id=1, source_target_pairs={{0,1},{1,0},{2,3},{3,2},{4,5},{5,4},{6,7},{7,6},{8,9},{9,8},{10,11... | collective-permute-start | bytes 36872 | tf_op jit(solution)/shard_map/ppermute | solution.py:93
  2.7 0.7 %copy-done.6 = s32[1,2,128]{2,1,0:T(2,128)S(1)} copy-done((s32[1,2,128]{2,1,0:T(2,128)S(1)}, s32[1,2,128]{2,1,0:T(2,128)}, u32[]{:S(2)}) %copy-start.6) | copy-done | bytes 1048
  3.4 0.6 %copy-done.8 = s32[1,128]{1,0:T(1,128)S(1)} copy-done((s32[1,128]{1,0:T(1,128)S(1)}, s32[1,128]{1,0:T(1,128)}, u32[]{:S(2)}) %copy-start.8) | copy-done | bytes 536
  4.5 0.7 %copy-done.2 = s32[4,4]{1,0:T(4,128)S(1)} copy-done((s32[4,4]{1,0:T(4,128)S(1)}, s32[4,4]{1,0:T(4,128)}, u32[]{:S(2)}) %copy-start.2) | copy-done | bytes 88
  5.3 0.7 %copy-done.5 = s32[512]{0:T(512)S(1)} copy-done((s32[512]{0:T(512)S(1)}, s32[512]{0:T(512)}, u32[]{:S(2)}) %copy-start.5) | copy-done | bytes 2072
  6.6 2.6 %collective-permute-start.2 = (bf16[1,4,128]{2,1,0:T(4,128)(2,1)S(1)}, bf16[1,4,128]{2,1,0:T(4,128)(2,1)S(1)}, u32[]{:S(2)}, u32[]{:S(2)}) collective-permute-start(bf16[1,4,128]{2,1,0:T(4,128)(2,1)S(1)} %maximum_convert_fusion), channel_id=1, source_target_pairs={{0,2},{2,0},{4,6},{6,4},{8,10},{10,8},{12,14},{14,12},{1,3},{3,1},... | collective-permute-start | bytes 3080 | tf_op jit(solution)/shard_map/ppermute | solution.py:20
  9.1 1.5 %collective-permute-done.2 = bf16[1,4,128]{2,1,0:T(4,128)(2,1)S(1)} collective-permute-done((bf16[1,4,128]{2,1,0:T(4,128)(2,1)S(1)}, bf16[1,4,128]{2,1,0:T(4,128)(2,1)S(1)}, u32[]{:S(2)}, u32[]{:S(2)}) %collective-permute-start.2) | collective-permute-done | bytes 1056 | tf_op jit(solution)/shard_map/ppermute | solution.py:20
  10.7 2.2 %collective-permute-start.3 = (bf16[2,4,128]{2,1,0:T(4,128)(2,1)S(1)}, bf16[2,4,128]{2,1,0:T(4,128)(2,1)S(1)}, u32[]{:S(2)}, u32[]{:S(2)}) collective-permute-start(bf16[2,4,128]{2,1,0:T(4,128)(2,1)S(1)} %maximum_select_fusion.4), channel_id=1, source_target_pairs={{0,4},{2,6},{4,0},{6,2},{8,12},{10,14},{12,8},{14,10},{1,5},{3,7},... | collective-permute-start | bytes 6152 | tf_op jit(solution)/shard_map/ppermute | solution.py:20
  12.9 1.5 %collective-permute-done.3 = bf16[2,4,128]{2,1,0:T(4,128)(2,1)S(1)} collective-permute-done((bf16[2,4,128]{2,1,0:T(4,128)(2,1)S(1)}, bf16[2,4,128]{2,1,0:T(4,128)(2,1)S(1)}, u32[]{:S(2)}, u32[]{:S(2)}) %collective-permute-start.3) | collective-permute-done | bytes 2080 | tf_op jit(solution)/shard_map/ppermute | solution.py:20
  14.4 3.1 %collective-permute-start.4 = (bf16[4,4,128]{2,1,0:T(4,128)(2,1)S(1)}, bf16[4,4,128]{2,1,0:T(4,128)(2,1)S(1)}, u32[]{:S(2)}, u32[]{:S(2)}) collective-permute-start(bf16[4,4,128]{2,1,0:T(4,128)(2,1)S(1)} %maximum_select_fusion.3), channel_id=1, source_target_pairs={{0,8},{2,10},{4,12},{6,14},{8,0},{10,2},{12,4},{14,6},{1,9},{3,11}... | collective-permute-start | bytes 12296 | tf_op jit(solution)/shard_map/ppermute | solution.py:20
  17.6 1.6 %collective-permute-done.4 = bf16[4,4,128]{2,1,0:T(4,128)(2,1)S(1)} collective-permute-done((bf16[4,4,128]{2,1,0:T(4,128)(2,1)S(1)}, bf16[4,4,128]{2,1,0:T(4,128)(2,1)S(1)}, u32[]{:S(2)}, u32[]{:S(2)}) %collective-permute-start.4) | collective-permute-done | bytes 4128 | tf_op jit(solution)/shard_map/ppermute | solution.py:20
  19.8 1.0 %gather_fusion = f32[512,3]{1,0:T(8,128)S(1)} fusion(f32[2048,3]{1,0:T(8,128)S(1)} %copy.30, s32[1024]{0:T(1024)S(1)} %pad_clamp_fusion), kind=kCustom, calls=%fused_computation | custom fusion | bytes 14336 | tf_op jit(solution)/shard_map/jit(_take)/gather | solution.py:96
  21.5 2.2 %fusion.43 = (f32[4,4,128]{2,1,0:T(4,128)S(1)}, f32[4,128]{1,0:T(4,128)S(1)}) fusion(f32[4,128]{1,0:T(4,128)S(1)} %bitcast.108, f32[4,128]{1,0:T(4,128)S(1)} %bitcast.106, bf16[4,4,128,128]{3,2,1,0:T(8,128)(2,1)S(1)} %copy-done, s32[4,4,128]{2,1,0:T(4,128)S(1)} %bitcast.115, s32[4,4,128]{2,1,0:T(4,128)S(1)} %bitcast.116, ...), kind=kOutput, calls=%fused_computation.103 | convolution fusion | flops 71038464 | bytes 565264 | tf_op jit(solution)/shard_map/tkmi,tkip->tkmp/dot_general | solution.py:117
  24.2 1.1 %collective-permute-done.5 = f32[8,64]{1,0:T(8,128)S(1)} collective-permute-done((f32[8,64]{1,0:T(8,128)S(1)}, f32[8,64]{1,0:T(8,128)S(1)}, u32[]{:S(2)}, u32[]{:S(2)}) %collective-permute-start.5) | collective-permute-done | bytes 2080 | tf_op jit(solution)/shard_map/ppermute | solution.py:37
  25.3 1.9 %collective-permute-start.6 = (f32[4,64]{1,0:T(4,128)S(1)}, f32[4,64]{1,0:T(4,128)S(1)}, u32[]{:S(2)}, u32[]{:S(2)}) collective-permute-start(f32[4,64]{1,0:T(4,128)S(1)} %bitcast.122), channel_id=1, source_target_pairs={{0,2},{1,3},{2,0},{3,1},{4,6},{5,7},{6,4},{7,5},{8,10},{9,11},{10,... | collective-permute-start | bytes 3080 | tf_op jit(solution)/shard_map/ppermute | solution.py:37
  27.2 1.8 %collective-permute-done.6 = f32[4,64]{1,0:T(4,128)S(1)} collective-permute-done((f32[4,64]{1,0:T(4,128)S(1)}, f32[4,64]{1,0:T(4,128)S(1)}, u32[]{:S(2)}, u32[]{:S(2)}) %collective-permute-start.6) | collective-permute-done | bytes 1056 | tf_op jit(solution)/shard_map/ppermute | solution.py:37
  28.9 2.0 %collective-permute-start.7 = (f32[2,64]{1,0:T(2,128)S(1)}, f32[2,64]{1,0:T(2,128)S(1)}, u32[]{:S(2)}, u32[]{:S(2)}) collective-permute-start(f32[2,64]{1,0:T(2,128)S(1)} %bitcast.125), channel_id=1, source_target_pairs={{0,4},{1,5},{2,6},{3,7},{4,0},{5,1},{6,2},{7,3},{8,12},{9,13},{10,... | collective-permute-start | bytes 1544 | tf_op jit(solution)/shard_map/ppermute | solution.py:37
  30.9 1.7 %collective-permute-done.7 = f32[2,64]{1,0:T(2,128)S(1)} collective-permute-done((f32[2,64]{1,0:T(2,128)S(1)}, f32[2,64]{1,0:T(2,128)S(1)}, u32[]{:S(2)}, u32[]{:S(2)}) %collective-permute-start.7) | collective-permute-done | bytes 544 | tf_op jit(solution)/shard_map/ppermute | solution.py:37
  32.6 3.0 %collective-permute-start.8 = (f32[1,64]{1,0:T(1,128)S(1)}, f32[1,64]{1,0:T(1,128)S(1)}, u32[]{:S(2)}, u32[]{:S(2)}) collective-permute-start(f32[1,64]{1,0:T(1,128)S(1)} %constant_dynamic-slice_fusion), channel_id=1, source_target_pairs={{0,8},{1,9},{2,10},{3,11},{4,12},{5,13},{6,14},{7,15},{8,0},{9,1},... | collective-permute-start | bytes 776 | tf_op jit(solution)/shard_map/ppermute | solution.py:37
  35.6 0.7 %fusion.33 = f32[512]{0:T(512)} fusion(f32[4,128]{1,0:T(4,128)S(1)} %get-tuple-element.3, f32[512]{0:T(512)S(1)} %get-tuple-element.4, pred[4]{0:T(512)(128)(4,1)S(1)} %not_reduce_fusion), kind=kLoop, calls=%fused_computation.69 | loop fusion | flops 1024 | bytes 6148 | tf_op jit(solution)/shard_map/sqrt | solution.py:132
  36.2 0.9 %collective-permute-done.8 = f32[1,64]{1,0:T(1,128)S(1)} collective-permute-done((f32[1,64]{1,0:T(1,128)S(1)}, f32[1,64]{1,0:T(1,128)S(1)}, u32[]{:S(2)}, u32[]{:S(2)}) %collective-permute-start.8) | collective-permute-done | bytes 288 | tf_op jit(solution)/shard_map/ppermute | solution.py:37
  37.1 0.5 %fusion.35 = f32[1,64]{1,0:T(1,128)} fusion(f32[1,64]{1,0:T(1,128)S(1)} %collective-permute-done.8, f32[2,64]{1,0:T(2,128)S(1)} %max.34, s32[]{:T(128)S(6)} %select_n.158), kind=kLoop, calls=%fused_computation.86 | loop fusion | flops 64 | bytes 772 | tf_op jit(solution)/shard_map/sqrt | solution.py:143
  (64 shorter events, 2.9 us)
Async XLA Ops:
  0.6 20.8 %copy-start = (bf16[4,4,128,128]{3,2,1,0:T(8,128)(2,1)S(1)}, bf16[4,4,128,128]{3,2,1,0:T(8,128)(2,1)}, u32[]{:S(2)}) copy-start(bf16[4,4,128,128]{3,2,1,0:T(8,128)(2,1)} %param.16) | copy-start | bytes 1572868
  0.6 0.8 %copy-start.3 = (f32[1024]{0:T(1024)S(1)}, f32[1024]{0:T(1024)}, u32[]{:S(2)}) copy-start(f32[1024]{0:T(1024)} %param.12) | copy-start | bytes 12292
  0.7 0.8 %copy-start.4 = (f32[1024]{0:T(1024)S(1)}, f32[1024]{0:T(1024)}, u32[]{:S(2)}) copy-start(f32[1024]{0:T(1024)} %param.13) | copy-start | bytes 12292
  1.4 0.7 %copy-start.1 = (f32[1024]{0:T(1024)S(1)}, f32[1024]{0:T(1024)}, u32[]{:S(2)}) copy-start(f32[1024]{0:T(1024)} %param.10) | copy-start | bytes 12292
  2.2 17.2 %collective-permute-start = (f32[1024,3]{0,1:T(4,128)S(1)}, f32[1024,3]{0,1:T(4,128)S(1)}, u32[]{:S(2)}, u32[]{:S(2)}) collective-permute-start(f32[1024,3]{0,1:T(4,128)S(1)} %pad_maximum_fusion.1), channel_id=1, source_target_pairs={{0,1},{1,0},{2,3},{3,2},{4,5},{5,4},{6,7},{7,6},{8,9},{9,8},{10,11... | collective-permute-start | bytes 36872 | tf_op jit(solution)/shard_map/ppermute | solution.py:93
  2.7 0.7 %copy-start.6 = (s32[1,2,128]{2,1,0:T(2,128)S(1)}, s32[1,2,128]{2,1,0:T(2,128)}, u32[]{:S(2)}) copy-start(s32[1,2,128]{2,1,0:T(2,128)} %param.19) | copy-start | bytes 3076
  3.4 0.7 %copy-start.8 = (s32[1,128]{1,0:T(1,128)S(1)}, s32[1,128]{1,0:T(1,128)}, u32[]{:S(2)}) copy-start(s32[1,128]{1,0:T(1,128)} %param.17) | copy-start | bytes 1540
  4.4 0.7 %copy-start.2 = (s32[4,4]{1,0:T(4,128)S(1)}, s32[4,4]{1,0:T(4,128)}, u32[]{:S(2)}) copy-start(s32[4,4]{1,0:T(4,128)} %param.15) | copy-start | bytes 196
  4.5 2.1 %collective-permute-start.1 = (f32[2,128]{1,0:T(2,128)S(1)}, f32[2,128]{1,0:T(2,128)S(1)}, u32[]{:S(2)}, u32[]{:S(2)}) collective-permute-start(f32[2,128]{1,0:T(2,128)S(1)} %bitcast.123), channel_id=1, source_target_pairs={{0,1},{1,0},{2,3},{3,2},{4,5},{5,4},{6,7},{7,6},{8,9},{9,8},{10,11... | collective-permute-start | bytes 3080 | tf_op jit(solution)/shard_map/ppermute | solution.py:78
  5.2 0.9 %copy-start.7 = (bf16[1,128,128]{2,1,0:T(8,128)(2,1)S(1)}, bf16[1,128,128]{2,1,0:T(8,128)(2,1)}, u32[]{:S(2)}) copy-start(bf16[1,128,128]{2,1,0:T(8,128)(2,1)} %param.18) | copy-start | bytes 98308
  5.3 0.7 %copy-start.5 = (s32[512]{0:T(512)S(1)}, s32[512]{0:T(512)}, u32[]{:S(2)}) copy-start(s32[512]{0:T(512)} %param.14) | copy-start | bytes 6148
  6.6 4.1 %collective-permute-start.2 = (bf16[1,4,128]{2,1,0:T(4,128)(2,1)S(1)}, bf16[1,4,128]{2,1,0:T(4,128)(2,1)S(1)}, u32[]{:S(2)}, u32[]{:S(2)}) collective-permute-start(bf16[1,4,128]{2,1,0:T(4,128)(2,1)S(1)} %maximum_convert_fusion), channel_id=1, source_target_pairs={{0,2},{2,0},{4,6},{6,4},{8,10},{10,8},{12,14},{14,12},{1,3},{3,1},... | collective-permute-start | bytes 3080 | tf_op jit(solution)/shard_map/ppermute | solution.py:20
  10.7 3.7 %collective-permute-start.3 = (bf16[2,4,128]{2,1,0:T(4,128)(2,1)S(1)}, bf16[2,4,128]{2,1,0:T(4,128)(2,1)S(1)}, u32[]{:S(2)}, u32[]{:S(2)}) collective-permute-start(bf16[2,4,128]{2,1,0:T(4,128)(2,1)S(1)} %maximum_select_fusion.4), channel_id=1, source_target_pairs={{0,4},{2,6},{4,0},{6,2},{8,12},{10,14},{12,8},{14,10},{1,5},{3,7},... | collective-permute-start | bytes 6152 | tf_op jit(solution)/shard_map/ppermute | solution.py:20
  14.4 4.7 %collective-permute-start.4 = (bf16[4,4,128]{2,1,0:T(4,128)(2,1)S(1)}, bf16[4,4,128]{2,1,0:T(4,128)(2,1)S(1)}, u32[]{:S(2)}, u32[]{:S(2)}) collective-permute-start(bf16[4,4,128]{2,1,0:T(4,128)(2,1)S(1)} %maximum_select_fusion.3), channel_id=1, source_target_pairs={{0,8},{2,10},{4,12},{6,14},{8,0},{10,2},{12,4},{14,6},{1,9},{3,11}... | collective-permute-start | bytes 12296 | tf_op jit(solution)/shard_map/ppermute | solution.py:20
  24.0 1.2 %collective-permute-start.5 = (f32[8,64]{1,0:T(8,128)S(1)}, f32[8,64]{1,0:T(8,128)S(1)}, u32[]{:S(2)}, u32[]{:S(2)}) collective-permute-start(f32[8,64]{1,0:T(8,128)S(1)} %bitcast.117), channel_id=1, source_target_pairs={{0,1},{1,0},{2,3},{3,2},{4,5},{5,4},{6,7},{7,6},{8,9},{9,8},{10,11... | collective-permute-start | bytes 6152 | tf_op jit(solution)/shard_map/ppermute | solution.py:37
  25.3 3.6 %collective-permute-start.6 = (f32[4,64]{1,0:T(4,128)S(1)}, f32[4,64]{1,0:T(4,128)S(1)}, u32[]{:S(2)}, u32[]{:S(2)}) collective-permute-start(f32[4,64]{1,0:T(4,128)S(1)} %bitcast.122), channel_id=1, source_target_pairs={{0,2},{1,3},{2,0},{3,1},{4,6},{5,7},{6,4},{7,5},{8,10},{9,11},{10,... | collective-permute-start | bytes 3080 | tf_op jit(solution)/shard_map/ppermute | solution.py:37
  28.9 3.6 %collective-permute-start.7 = (f32[2,64]{1,0:T(2,128)S(1)}, f32[2,64]{1,0:T(2,128)S(1)}, u32[]{:S(2)}, u32[]{:S(2)}) collective-permute-start(f32[2,64]{1,0:T(2,128)S(1)} %bitcast.125), channel_id=1, source_target_pairs={{0,4},{1,5},{2,6},{3,7},{4,0},{5,1},{6,2},{7,3},{8,12},{9,13},{10,... | collective-permute-start | bytes 1544 | tf_op jit(solution)/shard_map/ppermute | solution.py:37
  32.6 4.5 %collective-permute-start.8 = (f32[1,64]{1,0:T(1,128)S(1)}, f32[1,64]{1,0:T(1,128)S(1)}, u32[]{:S(2)}, u32[]{:S(2)}) collective-permute-start(f32[1,64]{1,0:T(1,128)S(1)} %constant_dynamic-slice_fusion), channel_id=1, source_target_pairs={{0,8},{1,9},{2,10},{3,11},{4,12},{5,13},{6,14},{7,15},{8,0},{9,1},... | collective-permute-start | bytes 776 | tf_op jit(solution)/shard_map/ppermute | solution.py:37

commit v10 on v9

--- a/solution.py
+++ b/solution.py
@@ -34,7 +34,8 @@
         mine = (me // bit) % 2
         keep = lax.dynamic_index_in_dim(pairs, mine, 1, keepdims=False)
         send = lax.dynamic_index_in_dim(pairs, 1 - mine, 1, keepdims=False)
-        cur = jnp.maximum(keep, lax.ppermute(send, axes, [(j, j ^ bit) for j in range(n)]))
+        got = lax.ppermute(send, axes, [(j, j ^ bit) for j in range(n)])
+        cur = jnp.maximum(keep, got)
         bit *= 2
     return cur[0]
 
@@ -105,31 +106,30 @@
     pick_block = (block_of.reshape(-1, 1) == jnp.arange(blocks, dtype=jnp.int32)[None, :]).astype(jnp.bfloat16)
     chosen = jnp.dot(pick_block, table.reshape(blocks, -1), preferred_element_type=jnp.float32)
     chosen = chosen.astype(jnp.bfloat16).reshape(tiles_dev, slot_count, 4, pair_count)
-    rows_iota = lax.broadcasted_iota(jnp.int32, (1, 1, tile_size, pair_count), 2)
-    first_at = chosen[:, :, 2].astype(jnp.int32)[:, :, None, :]
-    second_at = chosen[:, :, 3].astype(jnp.int32)[:, :, None, :]
-    w_first = chosen[:, :, 0][:, :, None, :]
-    w_second = chosen[:, :, 1][:, :, None, :]
-    zero = jnp.zeros((), jnp.bfloat16)
-    weights = jnp.where(rows_iota == first_at, w_first, zero) + jnp.where(
-        rows_iota == second_at, w_second, zero
-    )
-    delta = jnp.einsum(
-        "tkmi,tkip->tkmp", tile_values, weights, preferred_element_type=jnp.float32
-    )
-    post = mon_real[:, None, :, None] + delta
-    squared = (post * post + react_sq[:, None, :, None]) * inv_limit_sq[:, None, :, None]
     neg = jnp.float32(-jnp.inf)
-    squared = jnp.where(valid[:, :, None, None], squared, neg)
+
+    def slot_squares(values, rows):
+        rows_iota = lax.broadcasted_iota(jnp.int32, (1, 1, tile_size, pair_count), 2)
+        first_at = rows[:, :, 2].astype(jnp.int32)[:, :, None, :]
+        second_at = rows[:, :, 3].astype(jnp.int32)[:, :, None, :]
+        zero = jnp.zeros((), jnp.bfloat16)
+        weights = jnp.where(rows_iota == first_at, rows[:, :, 0][:, :, None, :], zero) + jnp.where(
+            rows_iota == second_at, rows[:, :, 1][:, :, None, :], zero
+        )
+        delta = jnp.einsum(
+            "tkmi,tkip->tkmp", values, weights, preferred_element_type=jnp.float32
+        )
+        post = mon_real[:, None, :, None] + delta
+        squared = (post * post + react_sq[:, None, :, None]) * inv_limit_sq[:, None, :, None]
+        return jnp.where(valid[:, :, None, None], squared, neg)
+
+    squared = slot_squares(tile_values, chosen)
 
     block_iota = jnp.arange(blocks, dtype=jnp.int32)
     matches = tile_ids[:, :, None] == block_iota[None, None, :]
     absent = jnp.logical_not(jnp.any(matches, axis=1))
     any_absent = jnp.any(absent, axis=1)
 
-    peak_sq = jnp.max(squared, axis=(1, 3))
-    peak_sq = jnp.maximum(peak_sq, jnp.where(any_absent[:, None], base_sq, neg))
-    peak_load = jnp.sqrt(peak_sq)
 
     col_max = jnp.max(squared, axis=2)
     worst_local = jnp.max(
@@ -141,6 +141,10 @@
 
     worst_sq = scatter_max(worst_local.reshape(blocks * halves, half_width), both)
     worst_own = jnp.sqrt(worst_sq)[None, :]
+    values_again, rows_again = lax.optimization_barrier((tile_values, chosen))
+    peak_sq = jnp.max(slot_squares(values_again, rows_again), axis=(1, 3))
+    peak_sq = jnp.maximum(peak_sq, jnp.where(any_absent[:, None], base_sq, neg))
+    peak_load = jnp.sqrt(peak_sq)
     return (peak_load.reshape(-1), worst_own)
 
 

time: 37.9 us -> 35.5 us (0.937)
  local copies, waits for them, and re-layouts: 4.99 us -> 3.31 us
  matrix products: 3.03 us -> 1.95 us
  starting transfers between devices: 15.4 us -> 16.3 us
  waiting for transfers between devices: 10.1 us -> 9.48 us
    unnamed x22, local copies, waits for them, and re-layouts: 3.37 us -> 1.67 us
    dot_general x1 -> x2, matrix products: 2.19 us -> 1.11 us  [slot_squares(): jnp.einsum('tkmi,tkip->tkmp', values, weights, preferred_element_type=jnp...]
    mul x1, other arithmetic: 0.77 us -> 0.01 us  [body(): base_reactive * base_reactive]
    squeeze x1, other arithmetic: 0.01 us -> 0.76 us  [body(): second_idx = outage_pairs[0, 1]]
    ppermute x4, waiting for transfers between devices: 5.42 us -> 4.84 us  [scatter_max(): got = lax.ppermute(send, axes, [(j, j ^ bit) for j in range(n)])]
    ppermute x1, starting transfers between devices: 0.06 us -> 0.53 us  [body(): lax.ppermute(flow_pairs, 'state', [(j, (j + 1) % halves) for j in range(h...]
    ppermute x3, starting transfers between devices: 7.84 us -> 8.3 us  [gather_doubling(): other = lax.ppermute(cur, axes, [(j, j ^ bit) for j in range(n)])]
  transfers between devices with their start and end apart: 9 -> 9, of which waited for: 7 -> 7; matrix products, arithmetic and copies ran while one was open for 5% -> 6% of each run, Pallas kernels for 0% -> 0%
where the time goes in v10:
time: 35.5 us; the launch traced here: 35.3 us
  starting transfers between devices  16.3 us (46%)
  waiting for transfers between devices  9.48 us (27%)
  local copies, waits for them, and re-layouts  3.31 us (9%)
  other arithmetic  3.28 us (9%)
  matrix products  1.95 us (5%)
  between operations  0.95 us (3%)
    ppermute x3, starting transfers between devices, gather_doubling(): other = lax.ppermute(cur, axes, [(j, j ^ bit) for j in range(n)])  8.3 us
    ppermute x4, starting transfers between devices, scatter_max(): got = lax.ppermute(send, axes, [(j, j ^ bit) for j in range(n)])  6.91 us
    ppermute x4, waiting for transfers between devices, scatter_max(): got = lax.ppermute(send, axes, [(j, j ^ bit) for j in range(n)])  4.84 us
    ppermute x3, waiting for transfers between devices, gather_doubling(): other = lax.ppermute(cur, axes, [(j, j ^ bit) for j in range(n)])  4.63 us
    unnamed x22, local copies, waits for them, and re-layouts  1.67 us
    dot_general x2, matrix products, slot_squares(): jnp.einsum('tkmi,tkip->tkmp', values, weights, preferred_element_type=jnp...  1.11 us
    gather x1, local copies, waits for them, and re-layouts, body(): mon_vals = jnp.take(state_pos, mon_at, axis=0, mode='clip')  1.04 us
    squeeze x1, other arithmetic, body(): second_idx = outage_pairs[0, 1]  0.76 us
  transfers between devices with their start and end apart: 9, of which 7 were waited for; matrix products, arithmetic and copies ran while one was open for 6% of the time, Pallas kernels for 0%

profile of v10, /device:TPU:0, one launch (start us, length us, event | category | flops | bytes accessed | tf_op | source)
XLA Modules:
  0.0 35.3 jit_solution(1658439780125145987)
XLA Ops:
  0.7 0.8 %slice_bitcast_fusion.2 = (s32[128]{0:T(128)S(1)}, bf16[1,1,128]{2,1,0:T(2,128)(2,1)S(1)}, bf16[1,1,128]{2,1,0:T(2,128)(2,1)S(1)}, s32[128]{0:T(128)S(1)}) fusion(s32[1,2,128]{2,1,0:T(2,128)} %param.19), kind=kLoop, calls=%fused_computation.119 | loop fusion | flops 256 | bytes 2560 | tf_op jit(solution)/shard_map/squeeze | solution.py:65
  1.5 0.6 %copy-done.8 = s32[1,128]{1,0:T(1,128)S(1)} copy-done((s32[1,128]{1,0:T(1,128)S(1)}, s32[1,128]{1,0:T(1,128)}, u32[]{:S(2)}) %copy-start.8) | copy-done | bytes 536
  2.5 0.5 %collective-permute-start.1 = (f32[2,128]{1,0:T(2,128)S(1)}, f32[2,128]{1,0:T(2,128)S(1)}, u32[]{:S(2)}, u32[]{:S(2)}) collective-permute-start(f32[2,128]{1,0:T(2,128)S(1)} %bitcast.135), channel_id=1, source_target_pairs={{0,1},{1,0},{2,3},{3,2},{4,5},{5,4},{6,7},{7,6},{8,9},{9,8},{10,11... | collective-permute-start | bytes 3080 | tf_op jit(solution)/shard_map/ppermute | solution.py:79
  3.3 0.6 %collective-permute-start = (f32[1024,3]{0,1:T(4,128)S(1)}, f32[1024,3]{0,1:T(4,128)S(1)}, u32[]{:S(2)}, u32[]{:S(2)}) collective-permute-start(f32[1024,3]{0,1:T(4,128)S(1)} %pad_maximum_fusion.1), channel_id=1, source_target_pairs={{0,1},{1,0},{2,3},{3,2},{4,5},{5,4},{6,7},{7,6},{8,9},{9,8},{10,11... | collective-permute-start | bytes 36872 | tf_op jit(solution)/shard_map/ppermute | solution.py:94
  4.1 0.7 %copy-done.6 = s32[512]{0:T(512)S(1)} copy-done((s32[512]{0:T(512)S(1)}, s32[512]{0:T(512)}, u32[]{:S(2)}) %copy-start.6) | copy-done | bytes 2072
  5.4 3.0 %collective-permute-start.2 = (bf16[1,4,128]{2,1,0:T(4,128)(2,1)S(1)}, bf16[1,4,128]{2,1,0:T(4,128)(2,1)S(1)}, u32[]{:S(2)}, u32[]{:S(2)}) collective-permute-start(bf16[1,4,128]{2,1,0:T(4,128)(2,1)S(1)} %maximum_convert_fusion), channel_id=1, source_target_pairs={{0,2},{2,0},{4,6},{6,4},{8,10},{10,8},{12,14},{14,12},{1,3},{3,1},... | collective-permute-start | bytes 3080 | tf_op jit(solution)/shard_map/ppermute | solution.py:20
  8.4 1.5 %collective-permute-done.2 = bf16[1,4,128]{2,1,0:T(4,128)(2,1)S(1)} collective-permute-done((bf16[1,4,128]{2,1,0:T(4,128)(2,1)S(1)}, bf16[1,4,128]{2,1,0:T(4,128)(2,1)S(1)}, u32[]{:S(2)}, u32[]{:S(2)}) %collective-permute-start.2) | collective-permute-done | bytes 1056 | tf_op jit(solution)/shard_map/ppermute | solution.py:20
  10.0 2.2 %collective-permute-start.3 = (bf16[2,4,128]{2,1,0:T(4,128)(2,1)S(1)}, bf16[2,4,128]{2,1,0:T(4,128)(2,1)S(1)}, u32[]{:S(2)}, u32[]{:S(2)}) collective-permute-start(bf16[2,4,128]{2,1,0:T(4,128)(2,1)S(1)} %maximum_select_fusion.4), channel_id=1, source_target_pairs={{0,4},{2,6},{4,0},{6,2},{8,12},{10,14},{12,8},{14,10},{1,5},{3,7},... | collective-permute-start | bytes 6152 | tf_op jit(solution)/shard_map/ppermute | solution.py:20
  12.2 1.5 %collective-permute-done.3 = bf16[2,4,128]{2,1,0:T(4,128)(2,1)S(1)} collective-permute-done((bf16[2,4,128]{2,1,0:T(4,128)(2,1)S(1)}, bf16[2,4,128]{2,1,0:T(4,128)(2,1)S(1)}, u32[]{:S(2)}, u32[]{:S(2)}) %collective-permute-start.3) | collective-permute-done | bytes 2080 | tf_op jit(solution)/shard_map/ppermute | solution.py:20
  13.7 3.1 %collective-permute-start.4 = (bf16[4,4,128]{2,1,0:T(4,128)(2,1)S(1)}, bf16[4,4,128]{2,1,0:T(4,128)(2,1)S(1)}, u32[]{:S(2)}, u32[]{:S(2)}) collective-permute-start(bf16[4,4,128]{2,1,0:T(4,128)(2,1)S(1)} %maximum_select_fusion.3), channel_id=1, source_target_pairs={{0,8},{2,10},{4,12},{6,14},{8,0},{10,2},{12,4},{14,6},{1,9},{3,11}... | collective-permute-start | bytes 12296 | tf_op jit(solution)/shard_map/ppermute | solution.py:20
  16.8 1.6 %collective-permute-done.4 = bf16[4,4,128]{2,1,0:T(4,128)(2,1)S(1)} collective-permute-done((bf16[4,4,128]{2,1,0:T(4,128)(2,1)S(1)}, bf16[4,4,128]{2,1,0:T(4,128)(2,1)S(1)}, u32[]{:S(2)}, u32[]{:S(2)}) %collective-permute-start.4) | collective-permute-done | bytes 4128 | tf_op jit(solution)/shard_map/ppermute | solution.py:20
  19.1 1.0 %gather_fusion = f32[512,3]{1,0:T(8,128)S(1)} fusion(f32[2048,3]{1,0:T(8,128)S(1)} %copy.43, s32[1024]{0:T(1024)S(1)} %pad_clamp_fusion), kind=kCustom, calls=%fused_computation | custom fusion | bytes 14336 | tf_op jit(solution)/shard_map/jit(_take)/gather | solution.py:97
  20.1 0.5 %multiply_reduce_fusion = (f32[512]{0:T(512)S(1)}, f32[512]{0:T(512)S(1)}, f32[512]{0:T(512)S(1)}, f32[512]{0:T(512)S(1)}) fusion(f32[512,3]{1,0:T(8,128)S(1)} %gather_fusion), kind=kLoop, calls=%fused_computation.39 | loop fusion | flops 2560 | bytes 14336 | tf_op jit(solution)/shard_map/mul | solution.py:102
  20.8 0.5 %fusion.8 = f32[4,4,128]{2,1,0:T(4,128)S(1)} fusion(bf16[4,4,128,128]{3,2,1,0:T(8,128)(2,1)S(1)} %copy-done, f32[4,128]{1,0:T(4,128)S(1)} %bitcast.117, f32[4,128]{1,0:T(4,128)S(1)} %bitcast.113, s32[4,4,128]{2,1,0:T(4,128)S(1)} %bitcast.127, s32[4,4,128]{2,1,0:T(4,128)S(1)} %bitcast.128, f32[4,128]{1,0:T(4,128)S(1)} %bitcast.115, ...), kind=kOutput, calls=%fused_computation.11 | convolution fusion | flops 70776832 | bytes 563216 | tf_op jit(solution)/shard_map/tkmi,tkip->tkmp/dot_general | solution.py:119
  21.8 1.1 %collective-permute-done.5 = f32[8,64]{1,0:T(8,128)S(1)} collective-permute-done((f32[8,64]{1,0:T(8,128)S(1)}, f32[8,64]{1,0:T(8,128)S(1)}, u32[]{:S(2)}, u32[]{:S(2)}) %collective-permute-start.5) | collective-permute-done | bytes 2080 | tf_op jit(solution)/shard_map/ppermute | solution.py:37
  22.9 1.9 %collective-permute-start.6 = (f32[4,64]{1,0:T(4,128)S(1)}, f32[4,64]{1,0:T(4,128)S(1)}, u32[]{:S(2)}, u32[]{:S(2)}) collective-permute-start(f32[4,64]{1,0:T(4,128)S(1)} %bitcast.134), channel_id=1, source_target_pairs={{0,2},{1,3},{2,0},{3,1},{4,6},{5,7},{6,4},{7,5},{8,10},{9,11},{10,... | collective-permute-start | bytes 3080 | tf_op jit(solution)/shard_map/ppermute | solution.py:37
  24.8 1.8 %collective-permute-done.6 = f32[4,64]{1,0:T(4,128)S(1)} collective-permute-done((f32[4,64]{1,0:T(4,128)S(1)}, f32[4,64]{1,0:T(4,128)S(1)}, u32[]{:S(2)}, u32[]{:S(2)}) %collective-permute-start.6) | collective-permute-done | bytes 1056 | tf_op jit(solution)/shard_map/ppermute | solution.py:37
  26.6 2.0 %collective-permute-start.7 = (f32[2,64]{1,0:T(2,128)S(1)}, f32[2,64]{1,0:T(2,128)S(1)}, u32[]{:S(2)}, u32[]{:S(2)}) collective-permute-start(f32[2,64]{1,0:T(2,128)S(1)} %bitcast.137), channel_id=1, source_target_pairs={{0,4},{1,5},{2,6},{3,7},{4,0},{5,1},{6,2},{7,3},{8,12},{9,13},{10,... | collective-permute-start | bytes 1544 | tf_op jit(solution)/shard_map/ppermute | solution.py:37
  28.5 0.6 %fusion.9 = f32[4,128]{1,0:T(4,128)S(1)} fusion(bf16[4,4,128,128]{3,2,1,0:T(8,128)(2,1)S(1)} %copy-done, f32[4,128]{1,0:T(4,128)S(1)} %bitcast.118, f32[4,128]{1,0:T(4,128)S(1)} %bitcast.114, s32[4,4,128]{2,1,0:T(4,128)S(1)} %bitcast.126, s32[4,4,128]{2,1,0:T(4,128)S(1)} %bitcast.125, f32[4,128]{1,0:T(4,128)S(1)} %bitcast.116, ...), kind=kOutput, calls=%fused_computation.12 | convolution fusion | flops 70778368 | bytes 557072 | tf_op jit(solution)/shard_map/tkmi,tkip->tkmp/dot_general | solution.py:119
  29.1 1.1 %collective-permute-done.7 = f32[2,64]{1,0:T(2,128)S(1)} collective-permute-done((f32[2,64]{1,0:T(2,128)S(1)}, f32[2,64]{1,0:T(2,128)S(1)}, u32[]{:S(2)}, u32[]{:S(2)}) %collective-permute-start.7) | collective-permute-done | bytes 544 | tf_op jit(solution)/shard_map/ppermute | solution.py:37
  30.2 3.0 %collective-permute-start.8 = (f32[1,64]{1,0:T(1,128)S(1)}, f32[1,64]{1,0:T(1,128)S(1)}, u32[]{:S(2)}, u32[]{:S(2)}) collective-permute-start(f32[1,64]{1,0:T(1,128)S(1)} %constant_dynamic-slice_fusion), channel_id=1, source_target_pairs={{0,8},{1,9},{2,10},{3,11},{4,12},{5,13},{6,14},{7,15},{8,0},{9,1},... | collective-permute-start | bytes 776 | tf_op jit(solution)/shard_map/ppermute | solution.py:37
  33.2 0.7 %fusion.49 = f32[512]{0:T(512)} fusion(f32[4,128]{1,0:T(4,128)S(1)} %fusion.9, f32[512]{0:T(512)S(1)} %get-tuple-element.6, pred[4]{0:T(512)(128)(4,1)S(1)} %not_reduce_fusion), kind=kLoop, calls=%fused_computation.90 | loop fusion | flops 1024 | bytes 6148 | tf_op jit(solution)/shard_map/sqrt | solution.py:147
  33.9 0.9 %collective-permute-done.8 = f32[1,64]{1,0:T(1,128)S(1)} collective-permute-done((f32[1,64]{1,0:T(1,128)S(1)}, f32[1,64]{1,0:T(1,128)S(1)}, u32[]{:S(2)}, u32[]{:S(2)}) %collective-permute-start.8) | collective-permute-done | bytes 288 | tf_op jit(solution)/shard_map/ppermute | solution.py:37
  34.7 0.5 %fusion.51 = f32[1,64]{1,0:T(1,128)} fusion(f32[1,64]{1,0:T(1,128)S(1)} %collective-permute-done.8, f32[2,64]{1,0:T(2,128)S(1)} %max.34, s32[]{:T(128)S(6)} %select_n.170), kind=kLoop, calls=%fused_computation.107 | loop fusion | flops 64 | bytes 772 | tf_op jit(solution)/shard_map/sqrt | solution.py:143
  (68 shorter events, 2.7 us)
Async XLA Ops:
  0.6 20.1 %copy-start = (bf16[4,4,128,128]{3,2,1,0:T(8,128)(2,1)S(1)}, bf16[4,4,128,128]{3,2,1,0:T(8,128)(2,1)}, u32[]{:S(2)}) copy-start(bf16[4,4,128,128]{3,2,1,0:T(8,128)(2,1)} %param.16) | copy-start | bytes 1572868
  0.6 0.8 %copy-start.1 = (f32[1024]{0:T(1024)S(1)}, f32[1024]{0:T(1024)}, u32[]{:S(2)}) copy-start(f32[1024]{0:T(1024)} %param.10) | copy-start | bytes 12292
  1.5 0.7 %copy-start.8 = (s32[1,128]{1,0:T(1,128)S(1)}, s32[1,128]{1,0:T(1,128)}, u32[]{:S(2)}) copy-start(s32[1,128]{1,0:T(1,128)} %param.17) | copy-start | bytes 1540
  2.1 0.9 %copy-start.3 = (f32[1024]{0:T(1024)S(1)}, f32[1024]{0:T(1024)}, u32[]{:S(2)}) copy-start(f32[1024]{0:T(1024)} %param.11) | copy-start | bytes 12292
  2.5 0.7 %copy-start.4 = (f32[1024]{0:T(1024)S(1)}, f32[1024]{0:T(1024)}, u32[]{:S(2)}) copy-start(f32[1024]{0:T(1024)} %param.12) | copy-start | bytes 12292
  2.5 0.7 %copy-start.5 = (f32[1024]{0:T(1024)S(1)}, f32[1024]{0:T(1024)}, u32[]{:S(2)}) copy-start(f32[1024]{0:T(1024)} %param.13) | copy-start | bytes 12292
  2.5 2.8 %collective-permute-start.1 = (f32[2,128]{1,0:T(2,128)S(1)}, f32[2,128]{1,0:T(2,128)S(1)}, u32[]{:S(2)}, u32[]{:S(2)}) collective-permute-start(f32[2,128]{1,0:T(2,128)S(1)} %bitcast.135), channel_id=1, source_target_pairs={{0,1},{1,0},{2,3},{3,2},{4,5},{5,4},{6,7},{7,6},{8,9},{9,8},{10,11... | collective-permute-start | bytes 3080 | tf_op jit(solution)/shard_map/ppermute | solution.py:79
  3.2 0.7 %copy-start.2 = (s32[4,4]{1,0:T(4,128)S(1)}, s32[4,4]{1,0:T(4,128)}, u32[]{:S(2)}) copy-start(s32[4,4]{1,0:T(4,128)} %param.15) | copy-start | bytes 196
  3.3 15.4 %collective-permute-start = (f32[1024,3]{0,1:T(4,128)S(1)}, f32[1024,3]{0,1:T(4,128)S(1)}, u32[]{:S(2)}, u32[]{:S(2)}) collective-permute-start(f32[1024,3]{0,1:T(4,128)S(1)} %pad_maximum_fusion.1), channel_id=1, source_target_pairs={{0,1},{1,0},{2,3},{3,2},{4,5},{5,4},{6,7},{7,6},{8,9},{9,8},{10,11... | collective-permute-start | bytes 36872 | tf_op jit(solution)/shard_map/ppermute | solution.py:94
  4.1 0.9 %copy-start.7 = (bf16[1,128,128]{2,1,0:T(8,128)(2,1)S(1)}, bf16[1,128,128]{2,1,0:T(8,128)(2,1)}, u32[]{:S(2)}) copy-start(bf16[1,128,128]{2,1,0:T(8,128)(2,1)} %param.18) | copy-start | bytes 98308
  4.1 0.7 %copy-start.6 = (s32[512]{0:T(512)S(1)}, s32[512]{0:T(512)}, u32[]{:S(2)}) copy-start(s32[512]{0:T(512)} %param.14) | copy-start | bytes 6148
  5.4 4.6 %collective-permute-start.2 = (bf16[1,4,128]{2,1,0:T(4,128)(2,1)S(1)}, bf16[1,4,128]{2,1,0:T(4,128)(2,1)S(1)}, u32[]{:S(2)}, u32[]{:S(2)}) collective-permute-start(bf16[1,4,128]{2,1,0:T(4,128)(2,1)S(1)} %maximum_convert_fusion), channel_id=1, source_target_pairs={{0,2},{2,0},{4,6},{6,4},{8,10},{10,8},{12,14},{14,12},{1,3},{3,1},... | collective-permute-start | bytes 3080 | tf_op jit(solution)/shard_map/ppermute | solution.py:20
  10.0 3.7 %collective-permute-start.3 = (bf16[2,4,128]{2,1,0:T(4,128)(2,1)S(1)}, bf16[2,4,128]{2,1,0:T(4,128)(2,1)S(1)}, u32[]{:S(2)}, u32[]{:S(2)}) collective-permute-start(bf16[2,4,128]{2,1,0:T(4,128)(2,1)S(1)} %maximum_select_fusion.4), channel_id=1, source_target_pairs={{0,4},{2,6},{4,0},{6,2},{8,12},{10,14},{12,8},{14,10},{1,5},{3,7},... | collective-permute-start | bytes 6152 | tf_op jit(solution)/shard_map/ppermute | solution.py:20
  13.7 4.7 %collective-permute-start.4 = (bf16[4,4,128]{2,1,0:T(4,128)(2,1)S(1)}, bf16[4,4,128]{2,1,0:T(4,128)(2,1)S(1)}, u32[]{:S(2)}, u32[]{:S(2)}) collective-permute-start(bf16[4,4,128]{2,1,0:T(4,128)(2,1)S(1)} %maximum_select_fusion.3), channel_id=1, source_target_pairs={{0,8},{2,10},{4,12},{6,14},{8,0},{10,2},{12,4},{14,6},{1,9},{3,11}... | collective-permute-start | bytes 12296 | tf_op jit(solution)/shard_map/ppermute | solution.py:20
  21.6 1.2 %collective-permute-start.5 = (f32[8,64]{1,0:T(8,128)S(1)}, f32[8,64]{1,0:T(8,128)S(1)}, u32[]{:S(2)}, u32[]{:S(2)}) collective-permute-start(f32[8,64]{1,0:T(8,128)S(1)} %bitcast.129), channel_id=1, source_target_pairs={{0,1},{1,0},{2,3},{3,2},{4,5},{5,4},{6,7},{7,6},{8,9},{9,8},{10,11... | collective-permute-start | bytes 6152 | tf_op jit(solution)/shard_map/ppermute | solution.py:37
  22.9 3.6 %collective-permute-start.6 = (f32[4,64]{1,0:T(4,128)S(1)}, f32[4,64]{1,0:T(4,128)S(1)}, u32[]{:S(2)}, u32[]{:S(2)}) collective-permute-start(f32[4,64]{1,0:T(4,128)S(1)} %bitcast.134), channel_id=1, source_target_pairs={{0,2},{1,3},{2,0},{3,1},{4,6},{5,7},{6,4},{7,5},{8,10},{9,11},{10,... | collective-permute-start | bytes 3080 | tf_op jit(solution)/shard_map/ppermute | solution.py:37
  26.6 3.6 %collective-permute-start.7 = (f32[2,64]{1,0:T(2,128)S(1)}, f32[2,64]{1,0:T(2,128)S(1)}, u32[]{:S(2)}, u32[]{:S(2)}) collective-permute-start(f32[2,64]{1,0:T(2,128)S(1)} %bitcast.137), channel_id=1, source_target_pairs={{0,4},{1,5},{2,6},{3,7},{4,0},{5,1},{6,2},{7,3},{8,12},{9,13},{10,... | collective-permute-start | bytes 1544 | tf_op jit(solution)/shard_map/ppermute | solution.py:37
  30.2 4.5 %collective-permute-start.8 = (f32[1,64]{1,0:T(1,128)S(1)}, f32[1,64]{1,0:T(1,128)S(1)}, u32[]{:S(2)}, u32[]{:S(2)}) collective-permute-start(f32[1,64]{1,0:T(1,128)S(1)} %constant_dynamic-slice_fusion), channel_id=1, source_target_pairs={{0,8},{1,9},{2,10},{3,11},{4,12},{5,13},{6,14},{7,15},{8,0},{9,1},... | collective-permute-start | bytes 776 | tf_op jit(solution)/shard_map/ppermute | solution.py:37

commit v11 on v10

--- a/solution.py
+++ b/solution.py
@@ -52,14 +52,14 @@
     coupling,
     outage_pairs,
 ):
-    tiles_dev, slot_count, tile_size, _ = tile_values.shape
+    tiles_dev, _, tile_size, _ = tile_values.shape
     pair_count = outage_pairs.shape[2]
     blocks = lax.axis_size("blk")
     halves = lax.axis_size("state")
     half_width = pair_count // halves
     half_len = base_real.shape[0]
     me_state = lax.axis_index("state")
-    both = ("blk", "state")
+    assert halves == 2
 
     first_idx = outage_pairs[0, 0]
     second_idx = outage_pairs[0, 1]
@@ -90,26 +90,43 @@
     packed = jnp.stack([w_first, w_second, first_idx.astype(jnp.float32), second_idx.astype(jnp.float32)])
     table = gather_doubling(packed.astype(jnp.bfloat16), ("blk",))
 
-    state_local = jnp.stack([base_real, base_reactive * base_reactive, voltage * rating], axis=1)
-    other_half = lax.ppermute(state_local, "state", [(j, (j + 1) % halves) for j in range(halves)])
+    state_local = jnp.stack(
+        [base_real, base_reactive * base_reactive, voltage * rating], axis=1
+    )
+    other_half = lax.ppermute(
+        state_local, "state", [(j, (j + 1) % halves) for j in range(halves)]
+    )
+    partner = [(j, (j + 1) % halves) for j in range(halves)]
+    tiles_other = lax.ppermute(tile_values, "state", partner)
+    ints_other = lax.ppermute(jnp.concatenate([monitored, tile_ids.reshape(-1)]), "state", partner)
     state_pos = jnp.concatenate([state_local, other_half])
-    mon_at = (monitored - me_state * half_len) % (halves * half_len)
-    mon_vals = jnp.take(state_pos, mon_at, axis=0, mode="clip")
+    both_monitored = jnp.concatenate([monitored, ints_other[: monitored.shape[0]]])
+    mon_at = (both_monitored - me_state * half_len) % (halves * half_len)
+    all_vals = jnp.take(state_pos, mon_at, axis=0, mode="clip")
+    mon_vals = all_vals[: monitored.shape[0]]
+    other_vals = all_vals[monitored.shape[0]:]
+    ids_other = ints_other[monitored.shape[0]:].reshape(tile_ids.shape)
+    real_other = other_vals[:, 0].reshape(tiles_dev, tile_size)
+    q_sq_other = other_vals[:, 1].reshape(tiles_dev, tile_size)
+    inv_sq_other = 1.0 / (other_vals[:, 2] * other_vals[:, 2]).reshape(tiles_dev, tile_size)
+    base_other = (real_other * real_other + q_sq_other) * inv_sq_other
     mon_real = mon_vals[:, 0].reshape(tiles_dev, tile_size)
     react_sq = mon_vals[:, 1].reshape(tiles_dev, tile_size)
     mon_limit = mon_vals[:, 2].reshape(tiles_dev, tile_size)
     inv_limit_sq = 1.0 / (mon_limit * mon_limit)
     base_sq = (mon_real * mon_real + react_sq) * inv_limit_sq
 
-    valid = tile_ids >= 0
-    block_of = jnp.clip(tile_ids, 0, blocks - 1)
-    pick_block = (block_of.reshape(-1, 1) == jnp.arange(blocks, dtype=jnp.int32)[None, :]).astype(jnp.bfloat16)
-    chosen = jnp.dot(pick_block, table.reshape(blocks, -1), preferred_element_type=jnp.float32)
-    chosen = chosen.astype(jnp.bfloat16).reshape(tiles_dev, slot_count, 4, pair_count)
     neg = jnp.float32(-jnp.inf)
+    block_iota = jnp.arange(blocks, dtype=jnp.int32)
 
-    def slot_squares(values, rows):
-        rows_iota = lax.broadcasted_iota(jnp.int32, (1, 1, tile_size, pair_count), 2)
+    def slot_rows(ids):
+        pick_block = (jnp.clip(ids, 0, blocks - 1).reshape(-1, 1) == block_iota[None, :]).astype(jnp.bfloat16)
+        rows = jnp.dot(pick_block, table.reshape(blocks, -1), preferred_element_type=jnp.float32)
+        return rows.astype(jnp.bfloat16).reshape(ids.shape + (4, pair_count))
+
+    def slot_squares(values, rows, ids, real, q_sq, inv_sq):
+        width = rows.shape[-1]
+        rows_iota = lax.broadcasted_iota(jnp.int32, (1, 1, tile_size, width), 2)
         first_at = rows[:, :, 2].astype(jnp.int32)[:, :, None, :]
         second_at = rows[:, :, 3].astype(jnp.int32)[:, :, None, :]
         zero = jnp.zeros((), jnp.bfloat16)
@@ -119,30 +136,32 @@
         delta = jnp.einsum(
             "tkmi,tkip->tkmp", values, weights, preferred_element_type=jnp.float32
         )
-        post = mon_real[:, None, :, None] + delta
-        squared = (post * post + react_sq[:, None, :, None]) * inv_limit_sq[:, None, :, None]
-        return jnp.where(valid[:, :, None, None], squared, neg)
+        post = real[:, None, :, None] + delta
+        squared = (post * post + q_sq[:, None, :, None]) * inv_sq[:, None, :, None]
+        return jnp.where((ids >= 0)[:, :, None, None], squared, neg)
 
-    squared = slot_squares(tile_values, chosen)
+    def column_maxima(values, ids, real, q_sq, inv_sq, base):
+        rows = lax.dynamic_slice_in_dim(slot_rows(ids), me_state * half_width, half_width, axis=3)
+        col_max = jnp.max(slot_squares(values, rows, ids, real, q_sq, inv_sq), axis=2)
+        matches = ids[:, :, None] == block_iota[None, None, :]
+        worst = jnp.max(jnp.where(matches[:, :, :, None], col_max[:, :, None, :], neg), axis=(0, 1))
+        absent = jnp.logical_not(jnp.any(matches, axis=1))
+        absent_max = jnp.max(jnp.where(absent, jnp.max(base, axis=1)[:, None], neg), axis=0)
+        return jnp.maximum(worst, absent_max[:, None])
 
-    block_iota = jnp.arange(blocks, dtype=jnp.int32)
-    matches = tile_ids[:, :, None] == block_iota[None, None, :]
-    absent = jnp.logical_not(jnp.any(matches, axis=1))
-    any_absent = jnp.any(absent, axis=1)
+    worst_local = jnp.maximum(
+        column_maxima(tile_values, tile_ids, mon_real, react_sq, inv_limit_sq, base_sq),
+        column_maxima(tiles_other, ids_other, real_other, q_sq_other, inv_sq_other, base_other),
+    )
+    worst_sq = scatter_max(worst_local, ("blk",))
+    worst_own = jnp.sqrt(worst_sq)[None, :]
 
-
-    col_max = jnp.max(squared, axis=2)
-    worst_local = jnp.max(
-        jnp.where(matches[:, :, :, None], col_max[:, :, None, :], neg), axis=(0, 1)
+    any_absent = jnp.logical_not(
+        jnp.all(jnp.any(tile_ids[:, :, None] == block_iota[None, None, :], axis=1), axis=1)
     )
-    base_max = jnp.max(base_sq, axis=1)
-    absent_max = jnp.max(jnp.where(absent, base_max[:, None], neg), axis=0)
-    worst_local = jnp.maximum(worst_local, absent_max[:, None])
-
-    worst_sq = scatter_max(worst_local.reshape(blocks * halves, half_width), both)
-    worst_own = jnp.sqrt(worst_sq)[None, :]
+    chosen = slot_rows(tile_ids)
     values_again, rows_again = lax.optimization_barrier((tile_values, chosen))
-    peak_sq = jnp.max(slot_squares(values_again, rows_again), axis=(1, 3))
+    peak_sq = jnp.max(slot_squares(values_again, rows_again, tile_ids, mon_real, react_sq, inv_limit_sq), axis=(1, 3))
     peak_sq = jnp.maximum(peak_sq, jnp.where(any_absent[:, None], base_sq, neg))
     peak_load = jnp.sqrt(peak_sq)
     return (peak_load.reshape(-1), worst_own)

time: 35.5 us -> 39.1 us (1.10)
  matrix products: 1.95 us -> 5.18 us
  waiting for transfers between devices: 9.48 us -> 7.31 us
  local copies, waits for them, and re-layouts: 3.31 us -> 4.83 us
  other arithmetic: 3.28 us -> 3.95 us
    dot_general x2 -> x3, matrix products: 1.11 us -> 4.15 us  [slot_squares(): jnp.einsum('tkmi,tkip->tkmp', values, weights, preferred_element_type=jnp...]
    ppermute x4 -> x3, waiting for transfers between devices: 4.84 us -> 2.92 us  [scatter_max(): got = lax.ppermute(send, axes, [(j, j ^ bit) for j in range(n)])]
    gather x1, local copies, waits for them, and re-layouts: 1.04 us -> 2.81 us  [body(): all_vals = jnp.take(state_pos, mon_at, axis=0, mode='clip')]
    slice x1, other arithmetic: 0.04 us -> 0.85 us  [body(): real_other = other_vals[:, 0].reshape(tiles_dev, tile_size)]
    unnamed x22 -> x26, local copies, waits for them, and re-layouts: 1.67 us -> 1.01 us
    ppermute x0 -> x2, starting transfers between devices: none -> 0.64 us  [the longest x1 0.56 us: body(): lax.ppermute(jnp.concatenate([monitored, tile_ids.reshape(-1)]), 'state',...]
    mul x1 -> x0, other arithmetic: 0.51 us -> none  [body(): base_sq = (mon_real * mon_real + react_sq) * inv_limit_sq]
    ppermute x4 -> x3, starting transfers between devices: 6.91 us -> 6.57 us  [scatter_max(): got = lax.ppermute(send, axes, [(j, j ^ bit) for j in range(n)])]
  transfers between devices with their start and end apart: 9 -> 10, of which waited for: 7 -> 5; matrix products, arithmetic and copies ran while one was open for 6% -> 26% of each run, Pallas kernels for 0% -> 0%
where the time goes in v11:
time: 39.1 us; the launch traced here: 38.9 us
  starting transfers between devices  16.5 us (42%)
  waiting for transfers between devices  7.31 us (19%)
  matrix products  5.18 us (13%)
  local copies, waits for them, and re-layouts  4.83 us (12%)
  other arithmetic  3.95 us (10%)
  between operations  1.09 us (3%)
    ppermute x3, starting transfers between devices, gather_doubling(): other = lax.ppermute(cur, axes, [(j, j ^ bit) for j in range(n)])  8.24 us
    ppermute x3, starting transfers between devices, scatter_max(): got = lax.ppermute(send, axes, [(j, j ^ bit) for j in range(n)])  6.57 us
    ppermute x3, waiting for transfers between devices, gather_doubling(): other = lax.ppermute(cur, axes, [(j, j ^ bit) for j in range(n)])  4.37 us
    dot_general x3, matrix products, slot_squares(): jnp.einsum('tkmi,tkip->tkmp', values, weights, preferred_element_type=jnp...  4.15 us
    ppermute x3, waiting for transfers between devices, scatter_max(): got = lax.ppermute(send, axes, [(j, j ^ bit) for j in range(n)])  2.92 us
    gather x1, local copies, waits for them, and re-layouts, body(): all_vals = jnp.take(state_pos, mon_at, axis=0, mode='clip')  2.81 us
    unnamed x26, local copies, waits for them, and re-layouts  1.01 us
    slice x1, other arithmetic, body(): real_other = other_vals[:, 0].reshape(tiles_dev, tile_size)  0.85 us
  transfers between devices with their start and end apart: 10, of which 5 were waited for; matrix products, arithmetic and copies ran while one was open for 26% of the time, Pallas kernels for 0%

profile of v11, /device:TPU:0, one launch (start us, length us, event | category | flops | bytes accessed | tf_op | source)
XLA Modules:
  0.0 38.9 jit_solution(14391903844332793592)
XLA Ops:
  0.7 0.8 %slice_bitcast_fusion.2 = (s32[128]{0:T(128)S(1)}, bf16[1,1,128]{2,1,0:T(2,128)(2,1)S(1)}, bf16[1,1,128]{2,1,0:T(2,128)(2,1)S(1)}, s32[128]{0:T(128)S(1)}) fusion(s32[1,2,128]{2,1,0:T(2,128)} %param.19), kind=kLoop, calls=%fused_computation.156 | loop fusion | flops 256 | bytes 2560 | tf_op jit(solution)/shard_map/squeeze | solution.py:65
  1.5 0.6 %copy-done.8 = s32[1,128]{1,0:T(1,128)S(1)} copy-done((s32[1,128]{1,0:T(1,128)S(1)}, s32[1,128]{1,0:T(1,128)}, u32[]{:S(2)}) %copy-start.8) | copy-done | bytes 536
  2.1 0.4 fusion.18
  2.5 0.5 %collective-permute-start.2 = (f32[2,128]{1,0:T(2,128)S(1)}, f32[2,128]{1,0:T(2,128)S(1)}, u32[]{:S(2)}, u32[]{:S(2)}) collective-permute-start(f32[2,128]{1,0:T(2,128)S(1)} %bitcast.178), channel_id=1, source_target_pairs={{0,1},{1,0},{2,3},{3,2},{4,5},{5,4},{6,7},{7,6},{8,9},{9,8},{10,11... | collective-permute-start | bytes 3080 | tf_op jit(solution)/shard_map/ppermute | solution.py:79
  3.3 0.6 %collective-permute-start = (f32[1024,3]{0,1:T(4,128)S(1)}, f32[1024,3]{0,1:T(4,128)S(1)}, u32[]{:S(2)}, u32[]{:S(2)}) collective-permute-start(f32[1024,3]{0,1:T(4,128)S(1)} %pad_maximum_fusion.1), channel_id=1, source_target_pairs={{0,1},{1,0},{2,3},{3,2},{4,5},{5,4},{6,7},{7,6},{8,9},{9,8},{10,11... | collective-permute-start | bytes 36872 | tf_op jit(solution)/shard_map/ppermute | solution.py:96
  4.0 0.6 %collective-permute-start.1 = (s32[528]{0:T(1024)S(1)}, s32[528]{0:T(1024)S(1)}, u32[]{:S(2)}, u32[]{:S(2)}) collective-permute-start(s32[528]{0:T(1024)S(1)} %pad_add_fusion), channel_id=1, source_target_pairs={{0,1},{1,0},{2,3},{3,2},{4,5},{5,4},{6,7},{7,6},{8,9},{9,8},{10,11... | collective-permute-start | bytes 6344 | tf_op jit(solution)/shard_map/ppermute | solution.py:101
  5.4 3.0 %collective-permute-start.3 = (bf16[1,4,128]{2,1,0:T(4,128)(2,1)S(1)}, bf16[1,4,128]{2,1,0:T(4,128)(2,1)S(1)}, u32[]{:S(2)}, u32[]{:S(2)}) collective-permute-start(bf16[1,4,128]{2,1,0:T(4,128)(2,1)S(1)} %maximum_convert_fusion), channel_id=1, source_target_pairs={{0,2},{2,0},{4,6},{6,4},{8,10},{10,8},{12,14},{14,12},{1,3},{3,1},... | collective-permute-start | bytes 3080 | tf_op jit(solution)/shard_map/ppermute | solution.py:20
  8.4 1.5 %collective-permute-done.3 = bf16[1,4,128]{2,1,0:T(4,128)(2,1)S(1)} collective-permute-done((bf16[1,4,128]{2,1,0:T(4,128)(2,1)S(1)}, bf16[1,4,128]{2,1,0:T(4,128)(2,1)S(1)}, u32[]{:S(2)}, u32[]{:S(2)}) %collective-permute-start.3) | collective-permute-done | bytes 1056 | tf_op jit(solution)/shard_map/ppermute | solution.py:20
  10.0 2.2 %collective-permute-start.4 = (bf16[2,4,128]{2,1,0:T(4,128)(2,1)S(1)}, bf16[2,4,128]{2,1,0:T(4,128)(2,1)S(1)}, u32[]{:S(2)}, u32[]{:S(2)}) collective-permute-start(bf16[2,4,128]{2,1,0:T(4,128)(2,1)S(1)} %maximum_select_fusion.3), channel_id=1, source_target_pairs={{0,4},{2,6},{4,0},{6,2},{8,12},{10,14},{12,8},{14,10},{1,5},{3,7},... | collective-permute-start | bytes 6152 | tf_op jit(solution)/shard_map/ppermute | solution.py:20
  12.4 1.3 %collective-permute-done.4 = bf16[2,4,128]{2,1,0:T(4,128)(2,1)S(1)} collective-permute-done((bf16[2,4,128]{2,1,0:T(4,128)(2,1)S(1)}, bf16[2,4,128]{2,1,0:T(4,128)(2,1)S(1)}, u32[]{:S(2)}, u32[]{:S(2)}) %collective-permute-start.4) | collective-permute-done | bytes 2080 | tf_op jit(solution)/shard_map/ppermute | solution.py:20
  13.7 3.1 %collective-permute-start.5 = (bf16[4,4,128]{2,1,0:T(4,128)(2,1)S(1)}, bf16[4,4,128]{2,1,0:T(4,128)(2,1)S(1)}, u32[]{:S(2)}, u32[]{:S(2)}) collective-permute-start(bf16[4,4,128]{2,1,0:T(4,128)(2,1)S(1)} %maximum_select_fusion.2), channel_id=1, source_target_pairs={{0,8},{2,10},{4,12},{6,14},{8,0},{10,2},{12,4},{14,6},{1,9},{3,11}... | collective-permute-start | bytes 12296 | tf_op jit(solution)/shard_map/ppermute | solution.py:20
  16.8 1.6 %collective-permute-done.5 = bf16[4,4,128]{2,1,0:T(4,128)(2,1)S(1)} collective-permute-done((bf16[4,4,128]{2,1,0:T(4,128)(2,1)S(1)}, bf16[4,4,128]{2,1,0:T(4,128)(2,1)S(1)}, u32[]{:S(2)}, u32[]{:S(2)}) %collective-permute-start.5) | collective-permute-done | bytes 4128 | tf_op jit(solution)/shard_map/ppermute | solution.py:20
  19.5 2.8 %gather_fusion = f32[1024,3]{1,0:T(8,128)S(1)} fusion(f32[2048,3]{1,0:T(8,128)S(1)} %copy.33, s32[1024]{0:T(1024)S(1)} %broadcast_clamp_fusion), kind=kCustom, calls=%fused_computation | custom fusion | bytes 28672 | tf_op jit(solution)/shard_map/jit(_take)/gather | solution.py:105
  22.4 0.9 %slice_reduce_fusion.1 = (f32[512]{0:T(512)S(1)}, f32[512]{0:T(512)S(1)}, f32[512]{0:T(512)S(1)}, f32[512]{0:T(512)S(1)}, f32[512]{0:T(512)S(1)}, /*index=5*/f32[512]{0:T(512)S(1)}, f32[512]{0:T(512)S(1)}) fusion(f32[1024,3]{1,0:T(8,128)S(1)} %gather_fusion), kind=kLoop, calls=%fused_computation.47 | loop fusion | flops 3584 | bytes 26624 | tf_op jit(solution)/shard_map/slice | solution.py:109
  23.7 1.1 %fusion.12 = f32[4,4,64]{2,1,0:T(4,128)S(1)} fusion(bf16[4,4,128,128]{3,2,1,0:T(8,128)(2,1)S(1)} %copy-done.7, f32[4,128]{1,0:T(4,128)S(1)} %bitcast.149, f32[4,128]{1,0:T(4,128)S(1)} %bitcast.151, s32[4,4,64]{2,1,0:T(4,128)S(1)} %fusion.61, s32[4,4,64]{2,1,0:T(4,128)S(1)} %fusion.62, f32[4,128]{1,0:T(4,128)S(1)} %bitcast.153, ...), kind=kOutput, calls=%fused_computation.16 | convolution fusion | flops 35388416 | bytes 546832 | tf_op jit(solution)/shard_map/tkmi,tkip->tkmp/dot_general | solution.py:136
  24.9 1.1 %select_reduce_fusion = f32[4,4,64]{2,1,0:T(4,128)S(1)} fusion(pred[4,4]{1,0:T(4,128)(4,1)S(1)} %broadcast_compare_fusion, f32[4,128]{1,0:T(4,128)S(1)} %bitcast.157, f32[4,128]{1,0:T(4,128)S(1)} %bitcast.156, bf16[4,4,128,128]{3,2,1,0:T(8,128)(2,1)S(1)} %collective-permute-done.6, s32[4,4,64]{2,1,0:T(4,128)S(1)} %fusion.59, s32[4,4,64]{2,1,0:T(4,128)S(1)} %fusion.60, ...), kind=kOutput, calls=%fused_computation.30 | convolution fusion | flops 35388416 | bytes 546832 | tf_op jit(solution)/shard_map/tkmi,tkip->tkmp/dot_general | solution.py:136
  26.2 1.9 %collective-permute-start.7 = (f32[4,64]{1,0:T(4,128)S(1)}, f32[4,64]{1,0:T(4,128)S(1)}, u32[]{:S(2)}, u32[]{:S(2)}) collective-permute-start(f32[4,64]{1,0:T(4,128)S(1)} %bitcast.177), channel_id=1, source_target_pairs={{0,2},{2,0},{4,6},{6,4},{8,10},{10,8},{12,14},{14,12},{1,3},{3,1},... | collective-permute-start | bytes 3080 | tf_op jit(solution)/shard_map/ppermute | solution.py:37
  28.1 1.8 %collective-permute-done.7 = f32[4,64]{1,0:T(4,128)S(1)} collective-permute-done((f32[4,64]{1,0:T(4,128)S(1)}, f32[4,64]{1,0:T(4,128)S(1)}, u32[]{:S(2)}, u32[]{:S(2)}) %collective-permute-start.7) | collective-permute-done | bytes 1056 | tf_op jit(solution)/shard_map/ppermute | solution.py:37
  29.9 2.0 %collective-permute-start.8 = (f32[2,64]{1,0:T(2,128)S(1)}, f32[2,64]{1,0:T(2,128)S(1)}, u32[]{:S(2)}, u32[]{:S(2)}) collective-permute-start(f32[2,64]{1,0:T(2,128)S(1)} %bitcast.180), channel_id=1, source_target_pairs={{0,4},{2,6},{4,0},{6,2},{8,12},{10,14},{12,8},{14,10},{1,5},{3,7},... | collective-permute-start | bytes 1544 | tf_op jit(solution)/shard_map/ppermute | solution.py:37
  31.9 1.9 %fusion.4 = f32[4,128]{1,0:T(4,128)S(1)} fusion(bf16[4,4,128,128]{3,2,1,0:T(8,128)(2,1)S(1)} %copy-done.7, f32[4,128]{1,0:T(4,128)S(1)} %bitcast.150, f32[4,128]{1,0:T(4,128)S(1)} %bitcast.152, s32[4,4,128]{2,1,0:T(4,128)S(1)} %bitcast.167, s32[4,4,128]{2,1,0:T(4,128)S(1)} %bitcast.166, f32[4,128]{1,0:T(4,128)S(1)} %bitcast.154, ...), kind=kOutput, calls=%fused_computation.6 | convolution fusion | flops 70778368 | bytes 557072 | tf_op jit(solution)/shard_map/tkmi,tkip->tkmp/dot_general | solution.py:136
  33.8 2.7 %collective-permute-start.9 = (f32[1,64]{1,0:T(1,128)S(1)}, f32[1,64]{1,0:T(1,128)S(1)}, u32[]{:S(2)}, u32[]{:S(2)}) collective-permute-start(f32[1,64]{1,0:T(1,128)S(1)} %constant_dynamic-slice_fusion.6), channel_id=1, source_target_pairs={{0,8},{2,10},{4,12},{6,14},{8,0},{10,2},{12,4},{14,6},{1,9},{3,11}... | collective-permute-start | bytes 776 | tf_op jit(solution)/shard_map/ppermute | solution.py:37
  36.5 0.7 %fusion.65 = f32[512]{0:T(512)} fusion(f32[4,128]{1,0:T(4,128)S(1)} %fusion.4, f32[512]{0:T(512)S(1)} %get-tuple-element.7, pred[4]{0:T(512)(128)(4,1)S(1)} %not.9), kind=kLoop, calls=%fused_computation.133 | loop fusion | flops 1024 | bytes 6148 | tf_op jit(solution)/shard_map/sqrt | solution.py:166
  37.2 1.2 %collective-permute-done.9 = f32[1,64]{1,0:T(1,128)S(1)} collective-permute-done((f32[1,64]{1,0:T(1,128)S(1)}, f32[1,64]{1,0:T(1,128)S(1)}, u32[]{:S(2)}, u32[]{:S(2)}) %collective-permute-start.9) | collective-permute-done | bytes 288 | tf_op jit(solution)/shard_map/ppermute | solution.py:37
  38.4 0.5 %fusion.67 = f32[1,64]{1,0:T(1,128)} fusion(f32[1,64]{1,0:T(1,128)S(1)} %collective-permute-done.9, f32[2,64]{1,0:T(2,128)S(1)} %max.56, s32[]{:T(128)S(6)} %select_n.186), kind=kLoop, calls=%fused_computation.144 | loop fusion | flops 64 | bytes 772 | tf_op jit(solution)/shard_map/sqrt | solution.py:157
  (89 shorter events, 3.3 us)
Async XLA Ops:
  0.6 4.4 %copy-start = (bf16[1,128,128]{2,1,0:T(8,128)(2,1)S(1)}, bf16[1,128,128]{2,1,0:T(8,128)(2,1)}, u32[]{:S(2)}) copy-start(bf16[1,128,128]{2,1,0:T(8,128)(2,1)} %param.18) | copy-start | bytes 98308
  0.6 0.8 %copy-start.1 = (f32[1024]{0:T(1024)S(1)}, f32[1024]{0:T(1024)}, u32[]{:S(2)}) copy-start(f32[1024]{0:T(1024)} %param.10) | copy-start | bytes 12292
  1.5 0.7 %copy-start.8 = (s32[1,128]{1,0:T(1,128)S(1)}, s32[1,128]{1,0:T(1,128)}, u32[]{:S(2)}) copy-start(s32[1,128]{1,0:T(1,128)} %param.17) | copy-start | bytes 1540
  2.1 0.9 %copy-start.3 = (f32[1024]{0:T(1024)S(1)}, f32[1024]{0:T(1024)}, u32[]{:S(2)}) copy-start(f32[1024]{0:T(1024)} %param.11) | copy-start | bytes 12292
  2.5 0.7 %copy-start.5 = (f32[1024]{0:T(1024)S(1)}, f32[1024]{0:T(1024)}, u32[]{:S(2)}) copy-start(f32[1024]{0:T(1024)} %param.12) | copy-start | bytes 12292
  2.5 0.7 %copy-start.6 = (f32[1024]{0:T(1024)S(1)}, f32[1024]{0:T(1024)}, u32[]{:S(2)}) copy-start(f32[1024]{0:T(1024)} %param.13) | copy-start | bytes 12292
  2.5 2.9 %collective-permute-start.2 = (f32[2,128]{1,0:T(2,128)S(1)}, f32[2,128]{1,0:T(2,128)S(1)}, u32[]{:S(2)}, u32[]{:S(2)}) collective-permute-start(f32[2,128]{1,0:T(2,128)S(1)} %bitcast.178), channel_id=1, source_target_pairs={{0,1},{1,0},{2,3},{3,2},{4,5},{5,4},{6,7},{7,6},{8,9},{9,8},{10,11... | collective-permute-start | bytes 3080 | tf_op jit(solution)/shard_map/ppermute | solution.py:79
  3.2 0.7 %copy-start.2 = (s32[4,4]{1,0:T(4,128)S(1)}, s32[4,4]{1,0:T(4,128)}, u32[]{:S(2)}) copy-start(s32[4,4]{1,0:T(4,128)} %param.15) | copy-start | bytes 196
  3.3 0.7 %copy-start.4 = (s32[512]{0:T(512)S(1)}, s32[512]{0:T(512)}, u32[]{:S(2)}) copy-start(s32[512]{0:T(512)} %param.14) | copy-start | bytes 6148
  3.3 15.9 %collective-permute-start = (f32[1024,3]{0,1:T(4,128)S(1)}, f32[1024,3]{0,1:T(4,128)S(1)}, u32[]{:S(2)}, u32[]{:S(2)}) collective-permute-start(f32[1024,3]{0,1:T(4,128)S(1)} %pad_maximum_fusion.1), channel_id=1, source_target_pairs={{0,1},{1,0},{2,3},{3,2},{4,5},{5,4},{6,7},{7,6},{8,9},{9,8},{10,11... | collective-permute-start | bytes 36872 | tf_op jit(solution)/shard_map/ppermute | solution.py:96
  4.0 8.1 %collective-permute-start.1 = (s32[528]{0:T(1024)S(1)}, s32[528]{0:T(1024)S(1)}, u32[]{:S(2)}, u32[]{:S(2)}) collective-permute-start(s32[528]{0:T(1024)S(1)} %pad_add_fusion), channel_id=1, source_target_pairs={{0,1},{1,0},{2,3},{3,2},{4,5},{5,4},{6,7},{7,6},{8,9},{9,8},{10,11... | collective-permute-start | bytes 6344 | tf_op jit(solution)/shard_map/ppermute | solution.py:101
  4.6 20.4 %collective-permute-start.6 = (bf16[4,4,128,128]{3,2,1,0:T(8,128)(2,1)}, bf16[4,4,128,128]{3,2,1,0:T(8,128)(2,1)S(1)}, u32[]{:S(2)}, u32[]{:S(2)}) collective-permute-start(bf16[4,4,128,128]{3,2,1,0:T(8,128)(2,1)} %param.16), channel_id=1, source_target_pairs={{0,1},{1,0},{2,3},{3,2},{4,5},{5,4},{6,7},{7,6},{8,9},{9,8},{10,11... | collective-permute-start | bytes 1572872 | tf_op jit(solution)/shard_map/ppermute | solution.py:100
  5.4 4.5 %collective-permute-start.3 = (bf16[1,4,128]{2,1,0:T(4,128)(2,1)S(1)}, bf16[1,4,128]{2,1,0:T(4,128)(2,1)S(1)}, u32[]{:S(2)}, u32[]{:S(2)}) collective-permute-start(bf16[1,4,128]{2,1,0:T(4,128)(2,1)S(1)} %maximum_convert_fusion), channel_id=1, source_target_pairs={{0,2},{2,0},{4,6},{6,4},{8,10},{10,8},{12,14},{14,12},{1,3},{3,1},... | collective-permute-start | bytes 3080 | tf_op jit(solution)/shard_map/ppermute | solution.py:20
  10.0 3.7 %collective-permute-start.4 = (bf16[2,4,128]{2,1,0:T(4,128)(2,1)S(1)}, bf16[2,4,128]{2,1,0:T(4,128)(2,1)S(1)}, u32[]{:S(2)}, u32[]{:S(2)}) collective-permute-start(bf16[2,4,128]{2,1,0:T(4,128)(2,1)S(1)} %maximum_select_fusion.3), channel_id=1, source_target_pairs={{0,4},{2,6},{4,0},{6,2},{8,12},{10,14},{12,8},{14,10},{1,5},{3,7},... | collective-permute-start | bytes 6152 | tf_op jit(solution)/shard_map/ppermute | solution.py:20
  13.7 4.7 %collective-permute-start.5 = (bf16[4,4,128]{2,1,0:T(4,128)(2,1)S(1)}, bf16[4,4,128]{2,1,0:T(4,128)(2,1)S(1)}, u32[]{:S(2)}, u32[]{:S(2)}) collective-permute-start(bf16[4,4,128]{2,1,0:T(4,128)(2,1)S(1)} %maximum_select_fusion.2), channel_id=1, source_target_pairs={{0,8},{2,10},{4,12},{6,14},{8,0},{10,2},{12,4},{14,6},{1,9},{3,11}... | collective-permute-start | bytes 12296 | tf_op jit(solution)/shard_map/ppermute | solution.py:20
  22.3 1.4 %copy-start.7 = (bf16[4,4,128,128]{3,2,1,0:T(8,128)(2,1)S(1)}, bf16[4,4,128,128]{3,2,1,0:T(8,128)(2,1)}, u32[]{:S(2)}) copy-start(bf16[4,4,128,128]{3,2,1,0:T(8,128)(2,1)} %param.16) | copy-start | bytes 1572868
  26.2 3.7 %collective-permute-start.7 = (f32[4,64]{1,0:T(4,128)S(1)}, f32[4,64]{1,0:T(4,128)S(1)}, u32[]{:S(2)}, u32[]{:S(2)}) collective-permute-start(f32[4,64]{1,0:T(4,128)S(1)} %bitcast.177), channel_id=1, source_target_pairs={{0,2},{2,0},{4,6},{6,4},{8,10},{10,8},{12,14},{14,12},{1,3},{3,1},... | collective-permute-start | bytes 3080 | tf_op jit(solution)/shard_map/ppermute | solution.py:37
  29.9 3.9 %collective-permute-start.8 = (f32[2,64]{1,0:T(2,128)S(1)}, f32[2,64]{1,0:T(2,128)S(1)}, u32[]{:S(2)}, u32[]{:S(2)}) collective-permute-start(f32[2,64]{1,0:T(2,128)S(1)} %bitcast.180), channel_id=1, source_target_pairs={{0,4},{2,6},{4,0},{6,2},{8,12},{10,14},{12,8},{14,10},{1,5},{3,7},... | collective-permute-start | bytes 1544 | tf_op jit(solution)/shard_map/ppermute | solution.py:37
  33.8 4.5 %collective-permute-start.9 = (f32[1,64]{1,0:T(1,128)S(1)}, f32[1,64]{1,0:T(1,128)S(1)}, u32[]{:S(2)}, u32[]{:S(2)}) collective-permute-start(f32[1,64]{1,0:T(1,128)S(1)} %constant_dynamic-slice_fusion.6), channel_id=1, source_target_pairs={{0,8},{2,10},{4,12},{6,14},{8,0},{10,2},{12,4},{14,6},{1,9},{3,11}... | collective-permute-start | bytes 776 | tf_op jit(solution)/shard_map/ppermute | solution.py:37

commit v12 on v10

--- a/solution.py
+++ b/solution.py
@@ -28,15 +28,15 @@
     n = axes_size(axes)
     me = lax.axis_index(axes)
     cur = x
-    bit = 1
-    while bit < n:
-        pairs = cur.reshape((cur.shape[0] // 2, 2) + cur.shape[1:])
+    bit = n // 2
+    while bit >= 1:
+        pairs = cur.reshape((2, cur.shape[0] // 2) + cur.shape[1:])
         mine = (me // bit) % 2
-        keep = lax.dynamic_index_in_dim(pairs, mine, 1, keepdims=False)
-        send = lax.dynamic_index_in_dim(pairs, 1 - mine, 1, keepdims=False)
+        keep = lax.dynamic_index_in_dim(pairs, mine, 0, keepdims=False)
+        send = lax.dynamic_index_in_dim(pairs, 1 - mine, 0, keepdims=False)
         got = lax.ppermute(send, axes, [(j, j ^ bit) for j in range(n)])
         cur = jnp.maximum(keep, got)
-        bit *= 2
+        bit //= 2
     return cur[0]
 
 

time: 35.5 us -> 35.6 us (level)
  no operation moved by 1% of the time
where the time goes in v12:
time: 35.6 us; the launch traced here: 35.3 us
  starting transfers between devices  16.1 us (45%)
  waiting for transfers between devices  9.52 us (27%)
  local copies, waits for them, and re-layouts  3.53 us (10%)
  other arithmetic  3.28 us (9%)
  matrix products  1.95 us (5%)
  between operations  0.94 us (3%)
    ppermute x3, starting transfers between devices, gather_doubling(): other = lax.ppermute(cur, axes, [(j, j ^ bit) for j in range(n)])  8.3 us
    ppermute x4, starting transfers between devices, scatter_max(): got = lax.ppermute(send, axes, [(j, j ^ bit) for j in range(n)])  6.72 us
    ppermute x4, waiting for transfers between devices, scatter_max(): got = lax.ppermute(send, axes, [(j, j ^ bit) for j in range(n)])  4.88 us
    ppermute x3, waiting for transfers between devices, gather_doubling(): other = lax.ppermute(cur, axes, [(j, j ^ bit) for j in range(n)])  4.63 us
    unnamed x22, local copies, waits for them, and re-layouts  1.67 us
    dot_general x2, matrix products, slot_squares(): jnp.einsum('tkmi,tkip->tkmp', values, weights, preferred_element_type=jnp...  1.11 us
    gather x1, local copies, waits for them, and re-layouts, body(): mon_vals = jnp.take(state_pos, mon_at, axis=0, mode='clip')  1.04 us
    squeeze x1, other arithmetic, body(): second_idx = outage_pairs[0, 1]  0.76 us
  transfers between devices with their start and end apart: 9, of which 7 were waited for; matrix products, arithmetic and copies ran while one was open for 6% of the time, Pallas kernels for 0%

profile of v12, /device:TPU:0, one launch (start us, length us, event | category | flops | bytes accessed | tf_op | source)
XLA Modules:
  0.0 35.3 jit_solution(15788752604582779651)
XLA Ops:
  0.7 0.8 %slice_bitcast_fusion.2 = (s32[128]{0:T(128)S(1)}, bf16[1,1,128]{2,1,0:T(2,128)(2,1)S(1)}, bf16[1,1,128]{2,1,0:T(2,128)(2,1)S(1)}, s32[128]{0:T(128)S(1)}) fusion(s32[1,2,128]{2,1,0:T(2,128)} %param.19), kind=kLoop, calls=%fused_computation.122 | loop fusion | flops 256 | bytes 2560 | tf_op jit(solution)/shard_map/squeeze | solution.py:65
  1.5 0.6 %copy-done.8 = s32[1,128]{1,0:T(1,128)S(1)} copy-done((s32[1,128]{1,0:T(1,128)S(1)}, s32[1,128]{1,0:T(1,128)}, u32[]{:S(2)}) %copy-start.8) | copy-done | bytes 536
  2.5 0.5 %collective-permute-start.1 = (f32[2,128]{1,0:T(2,128)S(1)}, f32[2,128]{1,0:T(2,128)S(1)}, u32[]{:S(2)}, u32[]{:S(2)}) collective-permute-start(f32[2,128]{1,0:T(2,128)S(1)} %bitcast.140), channel_id=1, source_target_pairs={{0,1},{1,0},{2,3},{3,2},{4,5},{5,4},{6,7},{7,6},{8,9},{9,8},{10,11... | collective-permute-start | bytes 3080 | tf_op jit(solution)/shard_map/ppermute | solution.py:79
  3.3 0.6 %collective-permute-start = (f32[1024,3]{0,1:T(4,128)S(1)}, f32[1024,3]{0,1:T(4,128)S(1)}, u32[]{:S(2)}, u32[]{:S(2)}) collective-permute-start(f32[1024,3]{0,1:T(4,128)S(1)} %pad_maximum_fusion.1), channel_id=1, source_target_pairs={{0,1},{1,0},{2,3},{3,2},{4,5},{5,4},{6,7},{7,6},{8,9},{9,8},{10,11... | collective-permute-start | bytes 36872 | tf_op jit(solution)/shard_map/ppermute | solution.py:94
  4.1 0.7 %copy-done.6 = s32[512]{0:T(512)S(1)} copy-done((s32[512]{0:T(512)S(1)}, s32[512]{0:T(512)}, u32[]{:S(2)}) %copy-start.6) | copy-done | bytes 2072
  5.4 3.0 %collective-permute-start.2 = (bf16[1,4,128]{2,1,0:T(4,128)(2,1)S(1)}, bf16[1,4,128]{2,1,0:T(4,128)(2,1)S(1)}, u32[]{:S(2)}, u32[]{:S(2)}) collective-permute-start(bf16[1,4,128]{2,1,0:T(4,128)(2,1)S(1)} %maximum_convert_fusion), channel_id=1, source_target_pairs={{0,2},{2,0},{4,6},{6,4},{8,10},{10,8},{12,14},{14,12},{1,3},{3,1},... | collective-permute-start | bytes 3080 | tf_op jit(solution)/shard_map/ppermute | solution.py:20
  8.4 1.5 %collective-permute-done.2 = bf16[1,4,128]{2,1,0:T(4,128)(2,1)S(1)} collective-permute-done((bf16[1,4,128]{2,1,0:T(4,128)(2,1)S(1)}, bf16[1,4,128]{2,1,0:T(4,128)(2,1)S(1)}, u32[]{:S(2)}, u32[]{:S(2)}) %collective-permute-start.2) | collective-permute-done | bytes 1056 | tf_op jit(solution)/shard_map/ppermute | solution.py:20
  10.0 2.2 %collective-permute-start.3 = (bf16[2,4,128]{2,1,0:T(4,128)(2,1)S(1)}, bf16[2,4,128]{2,1,0:T(4,128)(2,1)S(1)}, u32[]{:S(2)}, u32[]{:S(2)}) collective-permute-start(bf16[2,4,128]{2,1,0:T(4,128)(2,1)S(1)} %maximum_select_fusion.4), channel_id=1, source_target_pairs={{0,4},{2,6},{4,0},{6,2},{8,12},{10,14},{12,8},{14,10},{1,5},{3,7},... | collective-permute-start | bytes 6152 | tf_op jit(solution)/shard_map/ppermute | solution.py:20
  12.2 1.5 %collective-permute-done.3 = bf16[2,4,128]{2,1,0:T(4,128)(2,1)S(1)} collective-permute-done((bf16[2,4,128]{2,1,0:T(4,128)(2,1)S(1)}, bf16[2,4,128]{2,1,0:T(4,128)(2,1)S(1)}, u32[]{:S(2)}, u32[]{:S(2)}) %collective-permute-start.3) | collective-permute-done | bytes 2080 | tf_op jit(solution)/shard_map/ppermute | solution.py:20
  13.7 3.1 %collective-permute-start.4 = (bf16[4,4,128]{2,1,0:T(4,128)(2,1)S(1)}, bf16[4,4,128]{2,1,0:T(4,128)(2,1)S(1)}, u32[]{:S(2)}, u32[]{:S(2)}) collective-permute-start(bf16[4,4,128]{2,1,0:T(4,128)(2,1)S(1)} %maximum_select_fusion.3), channel_id=1, source_target_pairs={{0,8},{2,10},{4,12},{6,14},{8,0},{10,2},{12,4},{14,6},{1,9},{3,11}... | collective-permute-start | bytes 12296 | tf_op jit(solution)/shard_map/ppermute | solution.py:20
  16.8 1.6 %collective-permute-done.4 = bf16[4,4,128]{2,1,0:T(4,128)(2,1)S(1)} collective-permute-done((bf16[4,4,128]{2,1,0:T(4,128)(2,1)S(1)}, bf16[4,4,128]{2,1,0:T(4,128)(2,1)S(1)}, u32[]{:S(2)}, u32[]{:S(2)}) %collective-permute-start.4) | collective-permute-done | bytes 4128 | tf_op jit(solution)/shard_map/ppermute | solution.py:20
  19.1 1.0 %gather_fusion = f32[512,3]{1,0:T(8,128)S(1)} fusion(f32[2048,3]{1,0:T(8,128)S(1)} %copy.27, s32[1024]{0:T(1024)S(1)} %pad_clamp_fusion), kind=kCustom, calls=%fused_computation | custom fusion | bytes 14336 | tf_op jit(solution)/shard_map/jit(_take)/gather | solution.py:97
  20.1 0.5 %multiply_reduce_fusion = (f32[512]{0:T(512)S(1)}, f32[512]{0:T(512)S(1)}, f32[512]{0:T(512)S(1)}, f32[512]{0:T(512)S(1)}) fusion(f32[512,3]{1,0:T(8,128)S(1)} %gather_fusion), kind=kLoop, calls=%fused_computation.39 | loop fusion | flops 2560 | bytes 14336 | tf_op jit(solution)/shard_map/mul | solution.py:102
  20.8 0.5 %fusion.8 = f32[4,4,128]{2,1,0:T(4,128)S(1)} fusion(bf16[4,4,128,128]{3,2,1,0:T(8,128)(2,1)S(1)} %copy-done, f32[4,128]{1,0:T(4,128)S(1)} %bitcast.125, f32[4,128]{1,0:T(4,128)S(1)} %bitcast.121, s32[4,4,128]{2,1,0:T(4,128)S(1)} %bitcast.135, s32[4,4,128]{2,1,0:T(4,128)S(1)} %bitcast.136, f32[4,128]{1,0:T(4,128)S(1)} %bitcast.123, ...), kind=kOutput, calls=%fused_computation.11 | convolution fusion | flops 70776832 | bytes 563216 | tf_op jit(solution)/shard_map/tkmi,tkip->tkmp/dot_general | solution.py:119
  21.9 2.9 %collective-permute-start.5 = (f32[8,64]{1,0:T(8,128)S(1)}, f32[8,64]{1,0:T(8,128)S(1)}, u32[]{:S(2)}, u32[]{:S(2)}) collective-permute-start(f32[8,64]{1,0:T(8,128)S(1)} %dynamic-slice_bitcast_fusion), channel_id=1, source_target_pairs={{0,8},{1,9},{2,10},{3,11},{4,12},{5,13},{6,14},{7,15},{8,0},{9,1},... | collective-permute-start | bytes 6152 | tf_op jit(solution)/shard_map/ppermute | solution.py:37
  24.8 1.5 %collective-permute-done.5 = f32[8,64]{1,0:T(8,128)S(1)} collective-permute-done((f32[8,64]{1,0:T(8,128)S(1)}, f32[8,64]{1,0:T(8,128)S(1)}, u32[]{:S(2)}, u32[]{:S(2)}) %collective-permute-start.5) | collective-permute-done | bytes 2080 | tf_op jit(solution)/shard_map/ppermute | solution.py:37
  26.4 1.9 %collective-permute-start.6 = (f32[4,64]{1,0:T(4,128)S(1)}, f32[4,64]{1,0:T(4,128)S(1)}, u32[]{:S(2)}, u32[]{:S(2)}) collective-permute-start(f32[4,64]{1,0:T(4,128)S(1)} %dynamic-slice_bitcast_fusion.1), channel_id=1, source_target_pairs={{0,4},{1,5},{2,6},{3,7},{4,0},{5,1},{6,2},{7,3},{8,12},{9,13},{10,... | collective-permute-start | bytes 3080 | tf_op jit(solution)/shard_map/ppermute | solution.py:37
  28.3 1.7 %collective-permute-done.6 = f32[4,64]{1,0:T(4,128)S(1)} collective-permute-done((f32[4,64]{1,0:T(4,128)S(1)}, f32[4,64]{1,0:T(4,128)S(1)}, u32[]{:S(2)}, u32[]{:S(2)}) %collective-permute-start.6) | collective-permute-done | bytes 1056 | tf_op jit(solution)/shard_map/ppermute | solution.py:37
  30.0 1.8 %collective-permute-start.7 = (f32[2,64]{1,0:T(2,128)S(1)}, f32[2,64]{1,0:T(2,128)S(1)}, u32[]{:S(2)}, u32[]{:S(2)}) collective-permute-start(f32[2,64]{1,0:T(2,128)S(1)} %fusion.52), channel_id=1, source_target_pairs={{0,2},{1,3},{2,0},{3,1},{4,6},{5,7},{6,4},{7,5},{8,10},{9,11},{10,... | collective-permute-start | bytes 1544 | tf_op jit(solution)/shard_map/ppermute | solution.py:37
  31.8 0.6 %fusion.9 = f32[4,128]{1,0:T(4,128)S(1)} fusion(bf16[4,4,128,128]{3,2,1,0:T(8,128)(2,1)S(1)} %copy-done, f32[4,128]{1,0:T(4,128)S(1)} %bitcast.126, f32[4,128]{1,0:T(4,128)S(1)} %bitcast.122, s32[4,4,128]{2,1,0:T(4,128)S(1)} %bitcast.134, s32[4,4,128]{2,1,0:T(4,128)S(1)} %bitcast.133, f32[4,128]{1,0:T(4,128)S(1)} %bitcast.124, ...), kind=kOutput, calls=%fused_computation.12 | convolution fusion | flops 70778368 | bytes 557072 | tf_op jit(solution)/shard_map/tkmi,tkip->tkmp/dot_general | solution.py:119
  32.4 1.2 %collective-permute-done.7 = f32[2,64]{1,0:T(2,128)S(1)} collective-permute-done((f32[2,64]{1,0:T(2,128)S(1)}, f32[2,64]{1,0:T(2,128)S(1)}, u32[]{:S(2)}, u32[]{:S(2)}) %collective-permute-start.7) | collective-permute-done | bytes 544 | tf_op jit(solution)/shard_map/ppermute | solution.py:37
  33.6 0.7 %fusion.49 = f32[512]{0:T(512)} fusion(f32[4,128]{1,0:T(4,128)S(1)} %fusion.9, f32[512]{0:T(512)S(1)} %get-tuple-element.6, pred[4]{0:T(512)(128)(4,1)S(1)} %not_reduce_fusion), kind=kLoop, calls=%fused_computation.93 | loop fusion | flops 1024 | bytes 6148 | tf_op jit(solution)/shard_map/sqrt | solution.py:147
  34.3 0.5 %collective-permute-done.8 = f32[1,64]{1,0:T(1,128)S(1)} collective-permute-done((f32[1,64]{1,0:T(1,128)S(1)}, f32[1,64]{1,0:T(1,128)S(1)}, u32[]{:S(2)}, u32[]{:S(2)}) %collective-permute-start.8) | collective-permute-done | bytes 288 | tf_op jit(solution)/shard_map/ppermute | solution.py:37
  34.8 0.5 %fusion.54 = f32[1,64]{1,0:T(1,128)} fusion(f32[1,64]{1,0:T(1,128)S(1)} %collective-permute-done.8, f32[2,64]{1,0:T(2,128)S(1)} %fusion.51, s32[]{:T(128)S(6)} %select_n.170), kind=kLoop, calls=%fused_computation.110 | loop fusion | flops 64 | bytes 772 | tf_op jit(solution)/shard_map/sqrt | solution.py:143
  (71 shorter events, 2.9 us)
Async XLA Ops:
  0.6 20.1 %copy-start = (bf16[4,4,128,128]{3,2,1,0:T(8,128)(2,1)S(1)}, bf16[4,4,128,128]{3,2,1,0:T(8,128)(2,1)}, u32[]{:S(2)}) copy-start(bf16[4,4,128,128]{3,2,1,0:T(8,128)(2,1)} %param.16) | copy-start | bytes 1572868
  0.6 0.8 %copy-start.1 = (f32[1024]{0:T(1024)S(1)}, f32[1024]{0:T(1024)}, u32[]{:S(2)}) copy-start(f32[1024]{0:T(1024)} %param.10) | copy-start | bytes 12292
  1.5 0.7 %copy-start.8 = (s32[1,128]{1,0:T(1,128)S(1)}, s32[1,128]{1,0:T(1,128)}, u32[]{:S(2)}) copy-start(s32[1,128]{1,0:T(1,128)} %param.17) | copy-start | bytes 1540
  2.1 0.9 %copy-start.3 = (f32[1024]{0:T(1024)S(1)}, f32[1024]{0:T(1024)}, u32[]{:S(2)}) copy-start(f32[1024]{0:T(1024)} %param.11) | copy-start | bytes 12292
  2.5 0.7 %copy-start.4 = (f32[1024]{0:T(1024)S(1)}, f32[1024]{0:T(1024)}, u32[]{:S(2)}) copy-start(f32[1024]{0:T(1024)} %param.12) | copy-start | bytes 12292
  2.5 0.7 %copy-start.5 = (f32[1024]{0:T(1024)S(1)}, f32[1024]{0:T(1024)}, u32[]{:S(2)}) copy-start(f32[1024]{0:T(1024)} %param.13) | copy-start | bytes 12292
  2.5 2.8 %collective-permute-start.1 = (f32[2,128]{1,0:T(2,128)S(1)}, f32[2,128]{1,0:T(2,128)S(1)}, u32[]{:S(2)}, u32[]{:S(2)}) collective-permute-start(f32[2,128]{1,0:T(2,128)S(1)} %bitcast.140), channel_id=1, source_target_pairs={{0,1},{1,0},{2,3},{3,2},{4,5},{5,4},{6,7},{7,6},{8,9},{9,8},{10,11... | collective-permute-start | bytes 3080 | tf_op jit(solution)/shard_map/ppermute | solution.py:79
  3.2 0.7 %copy-start.2 = (s32[4,4]{1,0:T(4,128)S(1)}, s32[4,4]{1,0:T(4,128)}, u32[]{:S(2)}) copy-start(s32[4,4]{1,0:T(4,128)} %param.15) | copy-start | bytes 196
  3.3 15.4 %collective-permute-start = (f32[1024,3]{0,1:T(4,128)S(1)}, f32[1024,3]{0,1:T(4,128)S(1)}, u32[]{:S(2)}, u32[]{:S(2)}) collective-permute-start(f32[1024,3]{0,1:T(4,128)S(1)} %pad_maximum_fusion.1), channel_id=1, source_target_pairs={{0,1},{1,0},{2,3},{3,2},{4,5},{5,4},{6,7},{7,6},{8,9},{9,8},{10,11... | collective-permute-start | bytes 36872 | tf_op jit(solution)/shard_map/ppermute | solution.py:94
  4.1 0.9 %copy-start.7 = (bf16[1,128,128]{2,1,0:T(8,128)(2,1)S(1)}, bf16[1,128,128]{2,1,0:T(8,128)(2,1)}, u32[]{:S(2)}) copy-start(bf16[1,128,128]{2,1,0:T(8,128)(2,1)} %param.18) | copy-start | bytes 98308
  4.1 0.7 %copy-start.6 = (s32[512]{0:T(512)S(1)}, s32[512]{0:T(512)}, u32[]{:S(2)}) copy-start(s32[512]{0:T(512)} %param.14) | copy-start | bytes 6148
  5.4 4.6 %collective-permute-start.2 = (bf16[1,4,128]{2,1,0:T(4,128)(2,1)S(1)}, bf16[1,4,128]{2,1,0:T(4,128)(2,1)S(1)}, u32[]{:S(2)}, u32[]{:S(2)}) collective-permute-start(bf16[1,4,128]{2,1,0:T(4,128)(2,1)S(1)} %maximum_convert_fusion), channel_id=1, source_target_pairs={{0,2},{2,0},{4,6},{6,4},{8,10},{10,8},{12,14},{14,12},{1,3},{3,1},... | collective-permute-start | bytes 3080 | tf_op jit(solution)/shard_map/ppermute | solution.py:20
  10.0 3.7 %collective-permute-start.3 = (bf16[2,4,128]{2,1,0:T(4,128)(2,1)S(1)}, bf16[2,4,128]{2,1,0:T(4,128)(2,1)S(1)}, u32[]{:S(2)}, u32[]{:S(2)}) collective-permute-start(bf16[2,4,128]{2,1,0:T(4,128)(2,1)S(1)} %maximum_select_fusion.4), channel_id=1, source_target_pairs={{0,4},{2,6},{4,0},{6,2},{8,12},{10,14},{12,8},{14,10},{1,5},{3,7},... | collective-permute-start | bytes 6152 | tf_op jit(solution)/shard_map/ppermute | solution.py:20
  13.7 4.7 %collective-permute-start.4 = (bf16[4,4,128]{2,1,0:T(4,128)(2,1)S(1)}, bf16[4,4,128]{2,1,0:T(4,128)(2,1)S(1)}, u32[]{:S(2)}, u32[]{:S(2)}) collective-permute-start(bf16[4,4,128]{2,1,0:T(4,128)(2,1)S(1)} %maximum_select_fusion.3), channel_id=1, source_target_pairs={{0,8},{2,10},{4,12},{6,14},{8,0},{10,2},{12,4},{14,6},{1,9},{3,11}... | collective-permute-start | bytes 12296 | tf_op jit(solution)/shard_map/ppermute | solution.py:20
  21.9 4.5 %collective-permute-start.5 = (f32[8,64]{1,0:T(8,128)S(1)}, f32[8,64]{1,0:T(8,128)S(1)}, u32[]{:S(2)}, u32[]{:S(2)}) collective-permute-start(f32[8,64]{1,0:T(8,128)S(1)} %dynamic-slice_bitcast_fusion), channel_id=1, source_target_pairs={{0,8},{1,9},{2,10},{3,11},{4,12},{5,13},{6,14},{7,15},{8,0},{9,1},... | collective-permute-start | bytes 6152 | tf_op jit(solution)/shard_map/ppermute | solution.py:37
  26.4 3.6 %collective-permute-start.6 = (f32[4,64]{1,0:T(4,128)S(1)}, f32[4,64]{1,0:T(4,128)S(1)}, u32[]{:S(2)}, u32[]{:S(2)}) collective-permute-start(f32[4,64]{1,0:T(4,128)S(1)} %dynamic-slice_bitcast_fusion.1), channel_id=1, source_target_pairs={{0,4},{1,5},{2,6},{3,7},{4,0},{5,1},{6,2},{7,3},{8,12},{9,13},{10,... | collective-permute-start | bytes 3080 | tf_op jit(solution)/shard_map/ppermute | solution.py:37
  30.0 3.6 %collective-permute-start.7 = (f32[2,64]{1,0:T(2,128)S(1)}, f32[2,64]{1,0:T(2,128)S(1)}, u32[]{:S(2)}, u32[]{:S(2)}) collective-permute-start(f32[2,64]{1,0:T(2,128)S(1)} %fusion.52), channel_id=1, source_target_pairs={{0,2},{1,3},{2,0},{3,1},{4,6},{5,7},{6,4},{7,5},{8,10},{9,11},{10,... | collective-permute-start | bytes 1544 | tf_op jit(solution)/shard_map/ppermute | solution.py:37
  33.6 1.2 %collective-permute-start.8 = (f32[1,64]{1,0:T(1,128)S(1)}, f32[1,64]{1,0:T(1,128)S(1)}, u32[]{:S(2)}, u32[]{:S(2)}) collective-permute-start(f32[1,64]{1,0:T(1,128)S(1)} %constant_dynamic-slice_fusion), channel_id=1, source_target_pairs={{0,1},{1,0},{2,3},{3,2},{4,5},{5,4},{6,7},{7,6},{8,9},{9,8},{10,11... | collective-permute-start | bytes 776 | tf_op jit(solution)/shard_map/ppermute | solution.py:37

commit v13 on v12

--- a/solution.py
+++ b/solution.py
@@ -15,12 +15,13 @@
     n = axes_size(axes)
     me = lax.axis_index(axes)
     cur = x[None]
-    bit = 1
-    while bit < n:
+    bit = n // 2
+    while bit >= 1:
         other = lax.ppermute(cur, axes, [(j, j ^ bit) for j in range(n)])
         low = (me & bit) == 0
-        cur = jnp.where(low, jnp.concatenate([cur, other]), jnp.concatenate([other, cur]))
-        bit *= 2
+        cur = jnp.where(low, jnp.stack([cur, other], axis=1), jnp.stack([other, cur], axis=1))
+        cur = cur.reshape((-1,) + x.shape)
+        bit //= 2
     return cur
 
 
@@ -61,39 +62,40 @@
     me_state = lax.axis_index("state")
     both = ("blk", "state")
 
+    partner = [(j, (j + 1) % halves) for j in range(halves)]
+    state_local = jnp.stack(
+        [base_real, base_reactive * base_reactive, voltage * rating], axis=1
+    )
+    other_half = lax.ppermute(state_local, "state", partner)
+    state_pos = jnp.concatenate([state_local, other_half])
+    pos_len = halves * half_len
+
     first_idx = outage_pairs[0, 0]
     second_idx = outage_pairs[0, 1]
-    local_at = outage_ids[0] - me_state * half_len
-    branch_iota = lax.broadcasted_iota(jnp.int32, (pair_count, half_len), 1)
-    pick_branch = (branch_iota == local_at[:, None]).astype(jnp.bfloat16)
-    flow_part = jnp.dot(
-        pick_branch, base_real.astype(jnp.bfloat16), preferred_element_type=jnp.float32
+    outage_at = (outage_ids[0] - me_state * half_len) % pos_len
+    branch_iota = lax.broadcasted_iota(jnp.int32, (pair_count, pos_len), 1)
+    pick_branch = (branch_iota == outage_at[:, None]).astype(jnp.bfloat16)
+    outage_flow = jnp.dot(
+        pick_branch, state_pos[:, 0].astype(jnp.bfloat16), preferred_element_type=jnp.float32
     )
     pair_at = jnp.concatenate([first_idx, second_idx])
     pair_to = jnp.concatenate([second_idx, first_idx])
     outage_iota = lax.broadcasted_iota(jnp.int32, (2 * pair_count, pair_count), 1)
     pick_at = (outage_iota == pair_at[:, None]).astype(jnp.bfloat16)
-    flow_pairs = jnp.dot(
-        pick_at, flow_part.astype(jnp.bfloat16), preferred_element_type=jnp.float32
+    flows = jnp.dot(
+        pick_at, outage_flow.astype(jnp.bfloat16), preferred_element_type=jnp.float32
     ).reshape(2, pair_count)
-    flow_other = lax.ppermute(
-        flow_pairs, "state", [(j, (j + 1) % halves) for j in range(halves)]
-    )
     coupled_rows = jnp.dot(pick_at, coupling[0], preferred_element_type=jnp.float32)
     coupled = jnp.sum(
         jnp.where(outage_iota == pair_to[:, None], coupled_rows, 0.0), axis=1
     ).reshape(2, pair_count)
-    flows = flow_pairs + flow_other
     determinant = 1.0 - coupled[0] * coupled[1]
     w_first = (flows[0] + coupled[0] * flows[1]) / determinant
     w_second = (flows[1] + coupled[1] * flows[0]) / determinant
     packed = jnp.stack([w_first, w_second, first_idx.astype(jnp.float32), second_idx.astype(jnp.float32)])
     table = gather_doubling(packed.astype(jnp.bfloat16), ("blk",))
 
-    state_local = jnp.stack([base_real, base_reactive * base_reactive, voltage * rating], axis=1)
-    other_half = lax.ppermute(state_local, "state", [(j, (j + 1) % halves) for j in range(halves)])
-    state_pos = jnp.concatenate([state_local, other_half])
-    mon_at = (monitored - me_state * half_len) % (halves * half_len)
+    mon_at = (monitored - me_state * half_len) % pos_len
     mon_vals = jnp.take(state_pos, mon_at, axis=0, mode="clip")
     mon_real = mon_vals[:, 0].reshape(tiles_dev, tile_size)
     react_sq = mon_vals[:, 1].reshape(tiles_dev, tile_size)

time: 35.6 us -> 33.7 us (0.947)
  starting transfers between devices: 16.1 us -> 14.5 us
  waiting for transfers between devices: 9.52 us -> 8.73 us
  local copies, waits for them, and re-layouts: 3.53 us -> 3.92 us
    ppermute x3, waiting for transfers between devices: 4.63 us -> 3.42 us  [gather_doubling(): other = lax.ppermute(cur, axes, [(j, j ^ bit) for j in range(n)])]
    mul x1, other arithmetic: 0.01 us -> 0.77 us  [body(): base_reactive * base_reactive]
    squeeze x1, other arithmetic: 0.76 us -> 0.01 us  [body(): second_idx = outage_pairs[0, 1]]
    ppermute x3, starting transfers between devices: 8.3 us -> 7.7 us  [gather_doubling(): other = lax.ppermute(cur, axes, [(j, j ^ bit) for j in range(n)])]
    ppermute x2 -> x1, starting transfers between devices: 1.09 us -> 0.56 us  [body(): other_half = lax.ppermute(state_local, 'state', partner)]
    ppermute x4, starting transfers between devices: 6.72 us -> 6.28 us  [scatter_max(): got = lax.ppermute(send, axes, [(j, j ^ bit) for j in range(n)])]
    ppermute x4, waiting for transfers between devices: 4.88 us -> 5.31 us  [scatter_max(): got = lax.ppermute(send, axes, [(j, j ^ bit) for j in range(n)])]
    unnamed x22 -> x18, local copies, waits for them, and re-layouts: 1.67 us -> 2.07 us
  transfers between devices with their start and end apart: 9 -> 8, of which waited for: 7 -> 6; matrix products, arithmetic and copies ran while one was open for 6% -> 12% of each run, Pallas kernels for 0% -> 0%
where the time goes in v13:
time: 33.7 us; the launch traced here: 33.5 us
  starting transfers between devices  14.5 us (43%)
  waiting for transfers between devices  8.73 us (26%)
  local copies, waits for them, and re-layouts  3.92 us (12%)
  other arithmetic  3.28 us (10%)
  matrix products  2.05 us (6%)
  between operations  0.96 us (3%)
    ppermute x3, starting transfers between devices, gather_doubling(): other = lax.ppermute(cur, axes, [(j, j ^ bit) for j in range(n)])  7.7 us
    ppermute x4, starting transfers between devices, scatter_max(): got = lax.ppermute(send, axes, [(j, j ^ bit) for j in range(n)])  6.28 us
    ppermute x4, waiting for transfers between devices, scatter_max(): got = lax.ppermute(send, axes, [(j, j ^ bit) for j in range(n)])  5.31 us
    ppermute x3, waiting for transfers between devices, gather_doubling(): other = lax.ppermute(cur, axes, [(j, j ^ bit) for j in range(n)])  3.42 us
    unnamed x18, local copies, waits for them, and re-layouts  2.07 us
    dot_general x2, matrix products, slot_squares(): jnp.einsum('tkmi,tkip->tkmp', values, weights, preferred_element_type=jnp...  1.11 us
    gather x1, local copies, waits for them, and re-layouts, body(): mon_vals = jnp.take(state_pos, mon_at, axis=0, mode='clip')  1.03 us
    mul x1, other arithmetic, body(): base_reactive * base_reactive  0.77 us
  transfers between devices with their start and end apart: 8, of which 6 were waited for; matrix products, arithmetic and copies ran while one was open for 12% of the time, Pallas kernels for 0%

profile of v13, /device:TPU:0, one launch (start us, length us, event | category | flops | bytes accessed | tf_op | source)
XLA Modules:
  0.0 33.5 jit_solution(8860223632545441990)
XLA Ops:
  0.7 0.8 %mul.86 = f32[1024]{0:T(1024)S(1)} multiply(f32[1024]{0:T(1024)} %param.11, f32[1024]{0:T(1024)} %param.11) | non-fusion elementwise | flops 1024 | bytes 12288 | tf_op jit(solution)/shard_map/mul | solution.py:67
  1.5 0.7 %copy-done.2 = f32[1024]{0:T(1024)S(1)} copy-done((f32[1024]{0:T(1024)S(1)}, f32[1024]{0:T(1024)}, u32[]{:S(2)}) %copy-start.2) | copy-done | bytes 4120
  2.2 0.6 %collective-permute-start = (f32[1024,3]{0,1:T(4,128)S(1)}, f32[1024,3]{0,1:T(4,128)S(1)}, u32[]{:S(2)}, u32[]{:S(2)}) collective-permute-start(f32[1024,3]{0,1:T(4,128)S(1)} %pad_maximum_fusion.1), channel_id=1, source_target_pairs={{0,1},{1,0},{2,3},{3,2},{4,5},{5,4},{6,7},{7,6},{8,9},{9,8},{10,11... | collective-permute-start | bytes 36872 | tf_op jit(solution)/shard_map/ppermute | solution.py:69
  2.9 0.6 %copy-done.6 = s32[1,2,128]{2,1,0:T(2,128)S(1)} copy-done((s32[1,2,128]{2,1,0:T(2,128)S(1)}, s32[1,2,128]{2,1,0:T(2,128)}, u32[]{:S(2)}) %copy-start.6) | copy-done | bytes 1048
  3.5 0.6 %copy-done.8 = s32[1,128]{1,0:T(1,128)S(1)} copy-done((s32[1,128]{1,0:T(1,128)S(1)}, s32[1,128]{1,0:T(1,128)}, u32[]{:S(2)}) %copy-start.8) | copy-done | bytes 536
  5.2 0.5 %fusion.17 = f32[1,256]{1,0:T(1,128)S(1)} fusion(s32[128]{0:T(128)S(1)} %and_select_fusion, s32[256]{0:T(256)S(1)} %get-tuple-element.22, f32[2048,3]{0,1:T(4,128)S(1)} %pad_maximum_fusion), kind=kOutput, calls=%fused_computation.28 | convolution fusion | flops 884864 | bytes 10752 | tf_op jit(solution)/shard_map/dot_general | solution.py:85
  5.7 4.1 %collective-permute-start.1 = (bf16[1,4,128]{2,1,0:T(4,128)(2,1)S(1)}, bf16[1,4,128]{2,1,0:T(4,128)(2,1)S(1)}, u32[]{:S(2)}, u32[]{:S(2)}) collective-permute-start(bf16[1,4,128]{2,1,0:T(4,128)(2,1)S(1)} %pad_maximum_fusion.2), channel_id=1, source_target_pairs={{0,8},{2,10},{4,12},{6,14},{8,0},{10,2},{12,4},{14,6},{1,9},{3,11}... | collective-permute-start | bytes 3080 | tf_op jit(solution)/shard_map/ppermute | solution.py:20
  9.9 1.0 %gather_fusion = f32[512,3]{1,0:T(8,128)S(1)} fusion(f32[2048,3]{1,0:T(8,128)S(1)} %copy.43, s32[1024]{0:T(1024)S(1)} %pad_clamp_fusion), kind=kCustom, calls=%fused_computation | custom fusion | bytes 14336 | tf_op jit(solution)/shard_map/jit(_take)/gather | solution.py:99
  10.9 0.5 %multiply_reduce_fusion = (f32[512]{0:T(512)S(1)}, f32[512]{0:T(512)S(1)}, f32[512]{0:T(512)S(1)}, f32[512]{0:T(512)S(1)}) fusion(f32[512,3]{1,0:T(8,128)S(1)} %gather_fusion), kind=kLoop, calls=%fused_computation.40 | loop fusion | flops 2560 | bytes 14336 | tf_op jit(solution)/shard_map/mul | solution.py:104
  11.6 1.8 %collective-permute-start.2 = (bf16[2,4,128]{2,1,0:T(4,128)(2,1)S(1)}, bf16[2,4,128]{2,1,0:T(4,128)(2,1)S(1)}, u32[]{:S(2)}, u32[]{:S(2)}) collective-permute-start(bf16[2,4,128]{2,1,0:T(4,128)(2,1)S(1)} %maximum_select_fusion.3), channel_id=1, source_target_pairs={{0,4},{2,6},{4,0},{6,2},{8,12},{10,14},{12,8},{14,10},{1,5},{3,7},... | collective-permute-start | bytes 6152 | tf_op jit(solution)/shard_map/ppermute | solution.py:20
  13.4 1.8 %collective-permute-done.2 = bf16[2,4,128]{2,1,0:T(4,128)(2,1)S(1)} collective-permute-done((bf16[2,4,128]{2,1,0:T(4,128)(2,1)S(1)}, bf16[2,4,128]{2,1,0:T(4,128)(2,1)S(1)}, u32[]{:S(2)}, u32[]{:S(2)}) %collective-permute-start.2) | collective-permute-done | bytes 2080 | tf_op jit(solution)/shard_map/ppermute | solution.py:20
  15.3 1.7 %collective-permute-start.3 = (bf16[4,4,128]{2,1,0:T(4,128)(2,1)S(1)}, bf16[4,4,128]{2,1,0:T(4,128)(2,1)S(1)}, u32[]{:S(2)}, u32[]{:S(2)}) collective-permute-start(bf16[4,4,128]{2,1,0:T(4,128)(2,1)S(1)} %bitcast.89), channel_id=1, source_target_pairs={{0,2},{2,0},{4,6},{6,4},{8,10},{10,8},{12,14},{14,12},{1,3},{3,1},... | collective-permute-start | bytes 12296 | tf_op jit(solution)/shard_map/ppermute | solution.py:20
  17.3 1.6 %collective-permute-done.3 = bf16[4,4,128]{2,1,0:T(4,128)(2,1)S(1)} collective-permute-done((bf16[4,4,128]{2,1,0:T(4,128)(2,1)S(1)}, bf16[4,4,128]{2,1,0:T(4,128)(2,1)S(1)}, u32[]{:S(2)}, u32[]{:S(2)}) %collective-permute-start.3) | collective-permute-done | bytes 4128 | tf_op jit(solution)/shard_map/ppermute | solution.py:20
  19.2 0.5 %fusion.8 = f32[4,4,128]{2,1,0:T(4,128)S(1)} fusion(bf16[4,4,128,128]{3,2,1,0:T(8,128)(2,1)S(1)} %copy-done, f32[4,128]{1,0:T(4,128)S(1)} %bitcast.97, f32[4,128]{1,0:T(4,128)S(1)} %bitcast.93, s32[4,4,128]{2,1,0:T(4,128)S(1)} %bitcast.104, s32[4,4,128]{2,1,0:T(4,128)S(1)} %bitcast.105, f32[4,128]{1,0:T(4,128)S(1)} %bitcast.95, ...), kind=kOutput, calls=%fused_computation.11 | convolution fusion | flops 70776832 | bytes 563216 | tf_op jit(solution)/shard_map/tkmi,tkip->tkmp/dot_general | solution.py:121
  20.0 2.8 %collective-permute-start.4 = (f32[8,64]{1,0:T(8,128)S(1)}, f32[8,64]{1,0:T(8,128)S(1)}, u32[]{:S(2)}, u32[]{:S(2)}) collective-permute-start(f32[8,64]{1,0:T(8,128)S(1)} %dynamic-slice_bitcast_fusion), channel_id=1, source_target_pairs={{0,8},{1,9},{2,10},{3,11},{4,12},{5,13},{6,14},{7,15},{8,0},{9,1},... | collective-permute-start | bytes 6152 | tf_op jit(solution)/shard_map/ppermute | solution.py:38
  22.9 1.7 %collective-permute-done.4 = f32[8,64]{1,0:T(8,128)S(1)} collective-permute-done((f32[8,64]{1,0:T(8,128)S(1)}, f32[8,64]{1,0:T(8,128)S(1)}, u32[]{:S(2)}, u32[]{:S(2)}) %collective-permute-start.4) | collective-permute-done | bytes 2080 | tf_op jit(solution)/shard_map/ppermute | solution.py:38
  24.6 1.8 %collective-permute-start.5 = (f32[4,64]{1,0:T(4,128)S(1)}, f32[4,64]{1,0:T(4,128)S(1)}, u32[]{:S(2)}, u32[]{:S(2)}) collective-permute-start(f32[4,64]{1,0:T(4,128)S(1)} %dynamic-slice_bitcast_fusion.1), channel_id=1, source_target_pairs={{0,4},{1,5},{2,6},{3,7},{4,0},{5,1},{6,2},{7,3},{8,12},{9,13},{10,... | collective-permute-start | bytes 3080 | tf_op jit(solution)/shard_map/ppermute | solution.py:38
  26.3 1.8 %collective-permute-done.5 = f32[4,64]{1,0:T(4,128)S(1)} collective-permute-done((f32[4,64]{1,0:T(4,128)S(1)}, f32[4,64]{1,0:T(4,128)S(1)}, u32[]{:S(2)}, u32[]{:S(2)}) %collective-permute-start.5) | collective-permute-done | bytes 1056 | tf_op jit(solution)/shard_map/ppermute | solution.py:38
  28.1 1.7 %collective-permute-start.6 = (f32[2,64]{1,0:T(2,128)S(1)}, f32[2,64]{1,0:T(2,128)S(1)}, u32[]{:S(2)}, u32[]{:S(2)}) collective-permute-start(f32[2,64]{1,0:T(2,128)S(1)} %fusion.48), channel_id=1, source_target_pairs={{0,2},{1,3},{2,0},{3,1},{4,6},{5,7},{6,4},{7,5},{8,10},{9,11},{10,... | collective-permute-start | bytes 1544 | tf_op jit(solution)/shard_map/ppermute | solution.py:38
  29.8 0.6 %fusion.9 = f32[4,128]{1,0:T(4,128)S(1)} fusion(bf16[4,4,128,128]{3,2,1,0:T(8,128)(2,1)S(1)} %copy-done, f32[4,128]{1,0:T(4,128)S(1)} %bitcast.98, f32[4,128]{1,0:T(4,128)S(1)} %bitcast.94, s32[4,4,128]{2,1,0:T(4,128)S(1)} %bitcast.103, s32[4,4,128]{2,1,0:T(4,128)S(1)} %bitcast.102, f32[4,128]{1,0:T(4,128)S(1)} %bitcast.96, ...), kind=kOutput, calls=%fused_computation.12 | convolution fusion | flops 70778368 | bytes 557072 | tf_op jit(solution)/shard_map/tkmi,tkip->tkmp/dot_general | solution.py:121
  30.4 1.3 %collective-permute-done.6 = f32[2,64]{1,0:T(2,128)S(1)} collective-permute-done((f32[2,64]{1,0:T(2,128)S(1)}, f32[2,64]{1,0:T(2,128)S(1)}, u32[]{:S(2)}, u32[]{:S(2)}) %collective-permute-start.6) | collective-permute-done | bytes 544 | tf_op jit(solution)/shard_map/ppermute | solution.py:38
  31.8 0.7 %fusion.45 = f32[512]{0:T(512)} fusion(f32[4,128]{1,0:T(4,128)S(1)} %fusion.9, f32[512]{0:T(512)S(1)} %get-tuple-element.6, pred[4]{0:T(512)(128)(4,1)S(1)} %not_reduce_fusion), kind=kLoop, calls=%fused_computation.86 | loop fusion | flops 1024 | bytes 6148 | tf_op jit(solution)/shard_map/sqrt | solution.py:149
  32.5 0.5 %collective-permute-done.7 = f32[1,64]{1,0:T(1,128)S(1)} collective-permute-done((f32[1,64]{1,0:T(1,128)S(1)}, f32[1,64]{1,0:T(1,128)S(1)}, u32[]{:S(2)}, u32[]{:S(2)}) %collective-permute-start.7) | collective-permute-done | bytes 288 | tf_op jit(solution)/shard_map/ppermute | solution.py:38
  33.0 0.5 %fusion.50 = f32[1,64]{1,0:T(1,128)} fusion(f32[1,64]{1,0:T(1,128)S(1)} %collective-permute-done.7, f32[2,64]{1,0:T(2,128)S(1)} %fusion.47, s32[]{:T(128)S(6)} %select_n.203), kind=kLoop, calls=%fused_computation.105 | loop fusion | flops 64 | bytes 772 | tf_op jit(solution)/shard_map/sqrt | solution.py:145
  (64 shorter events, 2.4 us)
Async XLA Ops:
  0.6 18.6 %copy-start = (bf16[4,4,128,128]{3,2,1,0:T(8,128)(2,1)S(1)}, bf16[4,4,128,128]{3,2,1,0:T(8,128)(2,1)}, u32[]{:S(2)}) copy-start(bf16[4,4,128,128]{3,2,1,0:T(8,128)(2,1)} %param.16) | copy-start | bytes 1572868
  0.6 0.8 %copy-start.3 = (f32[1024]{0:T(1024)S(1)}, f32[1024]{0:T(1024)}, u32[]{:S(2)}) copy-start(f32[1024]{0:T(1024)} %param.12) | copy-start | bytes 12292
  0.7 0.8 %copy-start.4 = (f32[1024]{0:T(1024)S(1)}, f32[1024]{0:T(1024)}, u32[]{:S(2)}) copy-start(f32[1024]{0:T(1024)} %param.13) | copy-start | bytes 12292
  1.4 0.7 %copy-start.2 = (f32[1024]{0:T(1024)S(1)}, f32[1024]{0:T(1024)}, u32[]{:S(2)}) copy-start(f32[1024]{0:T(1024)} %param.10) | copy-start | bytes 12292
  2.1 0.7 %copy-start.1 = (s32[4,4]{1,0:T(4,128)S(1)}, s32[4,4]{1,0:T(4,128)}, u32[]{:S(2)}) copy-start(s32[4,4]{1,0:T(4,128)} %param.15) | copy-start | bytes 196
  2.1 2.2 %copy-start.7 = (bf16[1,128,128]{2,1,0:T(8,128)(2,1)S(1)}, bf16[1,128,128]{2,1,0:T(8,128)(2,1)}, u32[]{:S(2)}) copy-start(bf16[1,128,128]{2,1,0:T(8,128)(2,1)} %param.18) | copy-start | bytes 98308
  2.2 2.7 %collective-permute-start = (f32[1024,3]{0,1:T(4,128)S(1)}, f32[1024,3]{0,1:T(4,128)S(1)}, u32[]{:S(2)}, u32[]{:S(2)}) collective-permute-start(f32[1024,3]{0,1:T(4,128)S(1)} %pad_maximum_fusion.1), channel_id=1, source_target_pairs={{0,1},{1,0},{2,3},{3,2},{4,5},{5,4},{6,7},{7,6},{8,9},{9,8},{10,11... | collective-permute-start | bytes 36872 | tf_op jit(solution)/shard_map/ppermute | solution.py:69
  2.8 0.7 %copy-start.6 = (s32[1,2,128]{2,1,0:T(2,128)S(1)}, s32[1,2,128]{2,1,0:T(2,128)}, u32[]{:S(2)}) copy-start(s32[1,2,128]{2,1,0:T(2,128)} %param.19) | copy-start | bytes 3076
  3.5 0.7 %copy-start.8 = (s32[1,128]{1,0:T(1,128)S(1)}, s32[1,128]{1,0:T(1,128)}, u32[]{:S(2)}) copy-start(s32[1,128]{1,0:T(1,128)} %param.17) | copy-start | bytes 1540
  3.5 0.7 %copy-start.5 = (s32[512]{0:T(512)S(1)}, s32[512]{0:T(512)}, u32[]{:S(2)}) copy-start(s32[512]{0:T(512)} %param.14) | copy-start | bytes 6148
  5.7 5.8 %collective-permute-start.1 = (bf16[1,4,128]{2,1,0:T(4,128)(2,1)S(1)}, bf16[1,4,128]{2,1,0:T(4,128)(2,1)S(1)}, u32[]{:S(2)}, u32[]{:S(2)}) collective-permute-start(bf16[1,4,128]{2,1,0:T(4,128)(2,1)S(1)} %pad_maximum_fusion.2), channel_id=1, source_target_pairs={{0,8},{2,10},{4,12},{6,14},{8,0},{10,2},{12,4},{14,6},{1,9},{3,11}... | collective-permute-start | bytes 3080 | tf_op jit(solution)/shard_map/ppermute | solution.py:20
  11.6 3.7 %collective-permute-start.2 = (bf16[2,4,128]{2,1,0:T(4,128)(2,1)S(1)}, bf16[2,4,128]{2,1,0:T(4,128)(2,1)S(1)}, u32[]{:S(2)}, u32[]{:S(2)}) collective-permute-start(bf16[2,4,128]{2,1,0:T(4,128)(2,1)S(1)} %maximum_select_fusion.3), channel_id=1, source_target_pairs={{0,4},{2,6},{4,0},{6,2},{8,12},{10,14},{12,8},{14,10},{1,5},{3,7},... | collective-permute-start | bytes 6152 | tf_op jit(solution)/shard_map/ppermute | solution.py:20
  15.3 3.7 %collective-permute-start.3 = (bf16[4,4,128]{2,1,0:T(4,128)(2,1)S(1)}, bf16[4,4,128]{2,1,0:T(4,128)(2,1)S(1)}, u32[]{:S(2)}, u32[]{:S(2)}) collective-permute-start(bf16[4,4,128]{2,1,0:T(4,128)(2,1)S(1)} %bitcast.89), channel_id=1, source_target_pairs={{0,2},{2,0},{4,6},{6,4},{8,10},{10,8},{12,14},{14,12},{1,3},{3,1},... | collective-permute-start | bytes 12296 | tf_op jit(solution)/shard_map/ppermute | solution.py:20
  20.0 4.5 %collective-permute-start.4 = (f32[8,64]{1,0:T(8,128)S(1)}, f32[8,64]{1,0:T(8,128)S(1)}, u32[]{:S(2)}, u32[]{:S(2)}) collective-permute-start(f32[8,64]{1,0:T(8,128)S(1)} %dynamic-slice_bitcast_fusion), channel_id=1, source_target_pairs={{0,8},{1,9},{2,10},{3,11},{4,12},{5,13},{6,14},{7,15},{8,0},{9,1},... | collective-permute-start | bytes 6152 | tf_op jit(solution)/shard_map/ppermute | solution.py:38
  24.6 3.6 %collective-permute-start.5 = (f32[4,64]{1,0:T(4,128)S(1)}, f32[4,64]{1,0:T(4,128)S(1)}, u32[]{:S(2)}, u32[]{:S(2)}) collective-permute-start(f32[4,64]{1,0:T(4,128)S(1)} %dynamic-slice_bitcast_fusion.1), channel_id=1, source_target_pairs={{0,4},{1,5},{2,6},{3,7},{4,0},{5,1},{6,2},{7,3},{8,12},{9,13},{10,... | collective-permute-start | bytes 3080 | tf_op jit(solution)/shard_map/ppermute | solution.py:38
  28.1 3.6 %collective-permute-start.6 = (f32[2,64]{1,0:T(2,128)S(1)}, f32[2,64]{1,0:T(2,128)S(1)}, u32[]{:S(2)}, u32[]{:S(2)}) collective-permute-start(f32[2,64]{1,0:T(2,128)S(1)} %fusion.48), channel_id=1, source_target_pairs={{0,2},{1,3},{2,0},{3,1},{4,6},{5,7},{6,4},{7,5},{8,10},{9,11},{10,... | collective-permute-start | bytes 1544 | tf_op jit(solution)/shard_map/ppermute | solution.py:38
  31.7 1.2 %collective-permute-start.7 = (f32[1,64]{1,0:T(1,128)S(1)}, f32[1,64]{1,0:T(1,128)S(1)}, u32[]{:S(2)}, u32[]{:S(2)}) collective-permute-start(f32[1,64]{1,0:T(1,128)S(1)} %constant_dynamic-slice_fusion), channel_id=1, source_target_pairs={{0,1},{1,0},{2,3},{3,2},{4,5},{5,4},{6,7},{7,6},{8,9},{9,8},{10,11... | collective-permute-start | bytes 776 | tf_op jit(solution)/shard_map/ppermute | solution.py:38

commit v14 on v8

--- a/solution.py
+++ b/solution.py
@@ -17,12 +17,13 @@
     n = axes_size(axes)
     me = lax.axis_index(axes)
     cur = x[None]
-    bit = 1
-    while bit < n:
+    bit = n // 2
+    while bit >= 1:
         other = lax.ppermute(cur, axes, [(j, j ^ bit) for j in range(n)])
         low = (me & bit) == 0
-        cur = jnp.where(low, jnp.concatenate([cur, other]), jnp.concatenate([other, cur]))
-        bit *= 2
+        cur = jnp.where(low, jnp.stack([cur, other], axis=1), jnp.stack([other, cur], axis=1))
+        cur = cur.reshape((-1,) + x.shape)
+        bit //= 2
     return cur
 
 
@@ -30,18 +31,30 @@
     n = axes_size(axes)
     me = lax.axis_index(axes)
     cur = x
-    bit = 1
-    while bit < n:
-        pairs = cur.reshape((cur.shape[0] // 2, 2) + cur.shape[1:])
+    bit = n // 2
+    while bit >= 1:
+        pairs = cur.reshape((2, cur.shape[0] // 2) + cur.shape[1:])
         mine = (me // bit) % 2
-        keep = lax.dynamic_index_in_dim(pairs, mine, 1, keepdims=False)
-        send = lax.dynamic_index_in_dim(pairs, 1 - mine, 1, keepdims=False)
-        cur = jnp.maximum(keep, lax.ppermute(send, axes, [(j, j ^ bit) for j in range(n)]))
-        bit *= 2
+        keep = lax.dynamic_index_in_dim(pairs, mine, 0, keepdims=False)
+        send = lax.dynamic_index_in_dim(pairs, 1 - mine, 0, keepdims=False)
+        got = lax.ppermute(send, axes, [(j, j ^ bit) for j in range(n)])
+        cur = jnp.maximum(keep, got)
+        bit //= 2
     return cur[0]
 
 
-def prep_kernel(me_ref, real_ref, ids_ref, pairs_ref, coupling_ref, flow_ref, coupled_ref):
+def prep_kernel(me_ref, real_hbm, ids_hbm, pairs_hbm, coupling_hbm, flow_ref, coupled_ref,
+                real_ref, ids_ref, pairs_ref, coupling_ref, sems):
+    copies = [
+        pltpu.make_async_copy(src, dst, sems.at[i])
+        for i, (src, dst) in enumerate(
+            ((real_hbm, real_ref), (ids_hbm, ids_ref), (pairs_hbm, pairs_ref), (coupling_hbm, coupling_ref))
+        )
+    ]
+    for copy in copies:
+        copy.start()
+    for copy in copies:
+        copy.wait()
     half_len = real_ref.shape[1]
     outages = ids_ref.shape[1]
     local_at = ids_ref[...] - me_ref[0] * half_len
@@ -64,16 +77,25 @@
 
 def prep_call(me_state, base_real, outage_ids, outage_pairs, coupling):
     pair_count = outage_pairs.shape[2]
+    real = base_real.reshape(1, -1)
     vmem = pl.BlockSpec(memory_space=pltpu.VMEM)
+    anywhere = pl.BlockSpec(memory_space=pl.ANY)
     flow, coupled = pl.pallas_call(
         prep_kernel,
         out_shape=(
             jax.ShapeDtypeStruct((1, 2 * pair_count), jnp.float32),
             jax.ShapeDtypeStruct((1, 2 * pair_count), jnp.float32),
         ),
-        in_specs=[pl.BlockSpec(memory_space=pltpu.SMEM), vmem, vmem, vmem, vmem],
+        in_specs=[pl.BlockSpec(memory_space=pltpu.SMEM), anywhere, anywhere, anywhere, anywhere],
         out_specs=(vmem, vmem),
-    )(me_state.reshape(1), base_real.reshape(1, -1), outage_ids, outage_pairs, coupling)
+        scratch_shapes=[
+            pltpu.VMEM(real.shape, real.dtype),
+            pltpu.VMEM(outage_ids.shape, outage_ids.dtype),
+            pltpu.VMEM(outage_pairs.shape, outage_pairs.dtype),
+            pltpu.VMEM(coupling.shape, coupling.dtype),
+            pltpu.SemaphoreType.DMA((4,)),
+        ],
+    )(me_state.reshape(1), real, outage_ids, outage_pairs, coupling)
     return flow.reshape(2, pair_count), coupled.reshape(2, pair_count)[::-1]
 
 
@@ -131,31 +153,30 @@
     pick_block = (block_of.reshape(-1, 1) == jnp.arange(blocks, dtype=jnp.int32)[None, :]).astype(jnp.bfloat16)
     chosen = jnp.dot(pick_block, table.reshape(blocks, -1), preferred_element_type=jnp.float32)
     chosen = chosen.astype(jnp.bfloat16).reshape(tiles_dev, slot_count, 4, pair_count)
-    rows_iota = lax.broadcasted_iota(jnp.int32, (1, 1, tile_size, pair_count), 2)
-    first_at = chosen[:, :, 2].astype(jnp.int32)[:, :, None, :]
-    second_at = chosen[:, :, 3].astype(jnp.int32)[:, :, None, :]
-    w_first = chosen[:, :, 0][:, :, None, :]
-    w_second = chosen[:, :, 1][:, :, None, :]
-    zero = jnp.zeros((), jnp.bfloat16)
-    weights = jnp.where(rows_iota == first_at, w_first, zero) + jnp.where(
-        rows_iota == second_at, w_second, zero
-    )
-    delta = jnp.einsum(
-        "tkmi,tkip->tkmp", tile_values, weights, preferred_element_type=jnp.float32
-    )
-    post = mon_real[:, None, :, None] + delta
-    squared = (post * post + react_sq[:, None, :, None]) * inv_limit_sq[:, None, :, None]
     neg = jnp.float32(-jnp.inf)
-    squared = jnp.where(valid[:, :, None, None], squared, neg)
+
+    def slot_squares(values, rows):
+        rows_iota = lax.broadcasted_iota(jnp.int32, (1, 1, tile_size, pair_count), 2)
+        first_at = rows[:, :, 2].astype(jnp.int32)[:, :, None, :]
+        second_at = rows[:, :, 3].astype(jnp.int32)[:, :, None, :]
+        zero = jnp.zeros((), jnp.bfloat16)
+        weights = jnp.where(rows_iota == first_at, rows[:, :, 0][:, :, None, :], zero) + jnp.where(
+            rows_iota == second_at, rows[:, :, 1][:, :, None, :], zero
+        )
+        delta = jnp.einsum(
+            "tkmi,tkip->tkmp", values, weights, preferred_element_type=jnp.float32
+        )
+        post = mon_real[:, None, :, None] + delta
+        squared = (post * post + react_sq[:, None, :, None]) * inv_limit_sq[:, None, :, None]
+        return jnp.where(valid[:, :, None, None], squared, neg)
+
+    squared = slot_squares(tile_values, chosen)
 
     block_iota = jnp.arange(blocks, dtype=jnp.int32)
     matches = tile_ids[:, :, None] == block_iota[None, None, :]
     absent = jnp.logical_not(jnp.any(matches, axis=1))
     any_absent = jnp.any(absent, axis=1)
 
-    peak_sq = jnp.max(squared, axis=(1, 3))
-    peak_sq = jnp.maximum(peak_sq, jnp.where(any_absent[:, None], base_sq, neg))
-    peak_load = jnp.sqrt(peak_sq)
 
     col_max = jnp.max(squared, axis=2)
     worst_local = jnp.max(
@@ -167,6 +188,10 @@
 
     worst_sq = scatter_max(worst_local.reshape(blocks * halves, half_width), both)
     worst_own = jnp.sqrt(worst_sq)[None, :]
+    values_again, rows_again = lax.optimization_barrier((tile_values, chosen))
+    peak_sq = jnp.max(slot_squares(values_again, rows_again), axis=(1, 3))
+    peak_sq = jnp.maximum(peak_sq, jnp.where(any_absent[:, None], base_sq, neg))
+    peak_load = jnp.sqrt(peak_sq)
     return (peak_load.reshape(-1), worst_own)
 
 

time: 39.6 us -> 37.2 us (0.939)
  matrix products: 2.38 us -> 1.3 us
  local copies, waits for them, and re-layouts: 5.68 us -> 4.9 us
  other arithmetic: 3.24 us -> 2.5 us
  starting transfers between devices: 15.3 us -> 15.8 us
    dot_general x1 -> x2, matrix products: 2.19 us -> 1.11 us  [slot_squares(): jnp.einsum('tkmi,tkip->tkmp', values, weights, preferred_element_type=jnp...]
    unnamed x24 -> x20, local copies, waits for them, and re-layouts: 4.06 us -> 3.04 us
    mul x1, other arithmetic: 0.77 us -> 0.01 us  [body(): base_reactive * base_reactive]
    ppermute x4, waiting for transfers between devices: 5.42 us -> 4.87 us  [scatter_max(): got = lax.ppermute(send, axes, [(j, j ^ bit) for j in range(n)])]
    ppermute x1, starting transfers between devices: 0.02 us -> 0.49 us  [body(): lax.ppermute(flow_pairs, 'state', [(j, (j + 1) % halves) for j in range(h...]
  transfers between devices with their start and end apart: 9 -> 9, of which waited for: 7 -> 7; matrix products, arithmetic and copies ran while one was open for 3% -> 5% of each run, Pallas kernels for 4% -> 0%
where the time goes in v14:
time: 37.2 us; the launch traced here: 36.9 us
  starting transfers between devices  15.8 us (42%)
  waiting for transfers between devices  9.79 us (26%)
  local copies, waits for them, and re-layouts  4.9 us (13%)
  other arithmetic  2.5 us (7%)
  Pallas kernels  1.76 us (5%)
  matrix products  1.3 us (3%)
  between operations  0.88 us (2%)
    ppermute x3, starting transfers between devices, gather_doubling(): other = lax.ppermute(cur, axes, [(j, j ^ bit) for j in range(n)])  7.99 us
    ppermute x4, starting transfers between devices, scatter_max(): got = lax.ppermute(send, axes, [(j, j ^ bit) for j in range(n)])  6.72 us
    ppermute x3, waiting for transfers between devices, gather_doubling(): other = lax.ppermute(cur, axes, [(j, j ^ bit) for j in range(n)])  4.91 us
    ppermute x4, waiting for transfers between devices, scatter_max(): got = lax.ppermute(send, axes, [(j, j ^ bit) for j in range(n)])  4.87 us
    unnamed x20, local copies, waits for them, and re-layouts  3.04 us
    pallas_call x1, Pallas kernels, prep_call(): pl.pallas_call(prep_kernel, out_shape=(jax.ShapeDtypeStruct((1, 2 * pair_...  1.76 us
    dot_general x2, matrix products, slot_squares(): jnp.einsum('tkmi,tkip->tkmp', values, weights, preferred_element_type=jnp...  1.11 us
    gather x1, local copies, waits for them, and re-layouts, body(): mon_vals = jnp.take(state_pos, mon_at, axis=0, mode='clip')  1.04 us
  transfers between devices with their start and end apart: 9, of which 7 were waited for; matrix products, arithmetic and copies ran while one was open for 5% of the time, Pallas kernels for 0%

profile of v14, /device:TPU:0, one launch (start us, length us, event | category | flops | bytes accessed | tf_op | source)
XLA Modules:
  0.0 36.9 jit_solution(6702990542630359378)
XLA Ops:
  0.7 1.8 %shard_map.113 = (f32[1,256]{1,0:T(1,128)}, f32[1,256]{1,0:T(1,128)}) custom-call(s32[1]{0:T(128)} %bitcast.3.me_ref, f32[1,1024]{1,0:T(1,128)} %bitcast.64, s32[1,128]{1,0:T(1,128)} %ids_hbm.1, s32[1,2,128]{2,1,0:T(2,128)} %pairs_hbm.1, bf16[1,128,128]{2,1,0:T(8,128)(2,1)} %coupling_hbm.1), custom_call_target="tpu_custom_call" | custom-call | tf_op jit(solution)/shard_map/pallas_call | solution.py:83
  2.4 0.7 %copy-done.9 = f32[1,256]{1,0:T(1,128)S(1)} copy-done((f32[1,256]{1,0:T(1,128)S(1)}, f32[1,256]{1,0:T(1,128)}, u32[]{:S(2)}) %copy-start.9) | copy-done | bytes 1048
  3.8 0.7 %copy-done.1 = f32[1024]{0:T(1024)S(1)} copy-done((f32[1024]{0:T(1024)S(1)}, f32[1024]{0:T(1024)}, u32[]{:S(2)}) %copy-start.1) | copy-done | bytes 4120
  4.5 0.6 %collective-permute-start = (f32[1024,3]{0,1:T(4,128)S(1)}, f32[1024,3]{0,1:T(4,128)S(1)}, u32[]{:S(2)}, u32[]{:S(2)}) collective-permute-start(f32[1024,3]{0,1:T(4,128)S(1)} %pad_maximum_fusion.1), channel_id=1, source_target_pairs={{0,1},{1,0},{2,3},{3,2},{4,5},{5,4},{6,7},{7,6},{8,9},{9,8},{10,11... | collective-permute-start | bytes 36872 | tf_op jit(solution)/shard_map/ppermute | solution.py:139
  5.3 0.7 %copy-done.7 = s32[512]{0:T(512)S(1)} copy-done((s32[512]{0:T(512)S(1)}, s32[512]{0:T(512)}, u32[]{:S(2)}) %copy-start.7) | copy-done | bytes 2072
  6.2 0.7 %copy-done.8 = f32[1,256]{1,0:T(1,128)S(1)} copy-done((f32[1,256]{1,0:T(1,128)S(1)}, f32[1,256]{1,0:T(1,128)}, u32[]{:S(2)}) %copy-start.8) | copy-done | bytes 1048
  6.9 4.1 %collective-permute-start.2 = (bf16[1,4,128]{2,1,0:T(4,128)(2,1)S(1)}, bf16[1,4,128]{2,1,0:T(4,128)(2,1)S(1)}, u32[]{:S(2)}, u32[]{:S(2)}) collective-permute-start(bf16[1,4,128]{2,1,0:T(4,128)(2,1)S(1)} %pad_maximum_fusion.2), channel_id=1, source_target_pairs={{0,8},{2,10},{4,12},{6,14},{8,0},{10,2},{12,4},{14,6},{1,9},{3,11}... | collective-permute-start | bytes 3080 | tf_op jit(solution)/shard_map/ppermute | solution.py:22
  11.0 1.5 %collective-permute-done.2 = bf16[1,4,128]{2,1,0:T(4,128)(2,1)S(1)} collective-permute-done((bf16[1,4,128]{2,1,0:T(4,128)(2,1)S(1)}, bf16[1,4,128]{2,1,0:T(4,128)(2,1)S(1)}, u32[]{:S(2)}, u32[]{:S(2)}) %collective-permute-start.2) | collective-permute-done | bytes 1056 | tf_op jit(solution)/shard_map/ppermute | solution.py:22
  12.6 2.0 %collective-permute-start.3 = (bf16[2,4,128]{2,1,0:T(4,128)(2,1)S(1)}, bf16[2,4,128]{2,1,0:T(4,128)(2,1)S(1)}, u32[]{:S(2)}, u32[]{:S(2)}) collective-permute-start(bf16[2,4,128]{2,1,0:T(4,128)(2,1)S(1)} %maximum_select_fusion.3), channel_id=1, source_target_pairs={{0,4},{2,6},{4,0},{6,2},{8,12},{10,14},{12,8},{14,10},{1,5},{3,7},... | collective-permute-start | bytes 6152 | tf_op jit(solution)/shard_map/ppermute | solution.py:22
  14.6 1.7 %collective-permute-done.3 = bf16[2,4,128]{2,1,0:T(4,128)(2,1)S(1)} collective-permute-done((bf16[2,4,128]{2,1,0:T(4,128)(2,1)S(1)}, bf16[2,4,128]{2,1,0:T(4,128)(2,1)S(1)}, u32[]{:S(2)}, u32[]{:S(2)}) %collective-permute-start.3) | collective-permute-done | bytes 2080 | tf_op jit(solution)/shard_map/ppermute | solution.py:22
  16.3 1.9 %collective-permute-start.4 = (bf16[4,4,128]{2,1,0:T(4,128)(2,1)S(1)}, bf16[4,4,128]{2,1,0:T(4,128)(2,1)S(1)}, u32[]{:S(2)}, u32[]{:S(2)}) collective-permute-start(bf16[4,4,128]{2,1,0:T(4,128)(2,1)S(1)} %bitcast.73), channel_id=1, source_target_pairs={{0,2},{2,0},{4,6},{6,4},{8,10},{10,8},{12,14},{14,12},{1,3},{3,1},... | collective-permute-start | bytes 12296 | tf_op jit(solution)/shard_map/ppermute | solution.py:22
  18.2 1.7 %collective-permute-done.4 = bf16[4,4,128]{2,1,0:T(4,128)(2,1)S(1)} collective-permute-done((bf16[4,4,128]{2,1,0:T(4,128)(2,1)S(1)}, bf16[4,4,128]{2,1,0:T(4,128)(2,1)S(1)}, u32[]{:S(2)}, u32[]{:S(2)}) %collective-permute-start.4) | collective-permute-done | bytes 4128 | tf_op jit(solution)/shard_map/ppermute | solution.py:22
  20.6 1.0 %gather_fusion = f32[512,3]{1,0:T(8,128)S(1)} fusion(f32[2048,3]{1,0:T(8,128)S(1)} %copy.43, s32[1024]{0:T(1024)S(1)} %pad_clamp_fusion), kind=kCustom, calls=%fused_computation | custom fusion | bytes 14336 | tf_op jit(solution)/shard_map/jit(_take)/gather | solution.py:144
  21.7 0.5 %multiply_reduce_fusion = (f32[512]{0:T(512)S(1)}, f32[512]{0:T(512)S(1)}, f32[512]{0:T(512)S(1)}, f32[512]{0:T(512)S(1)}) fusion(f32[512,3]{1,0:T(8,128)S(1)} %gather_fusion), kind=kLoop, calls=%fused_computation.32 | loop fusion | flops 2560 | bytes 14336 | tf_op jit(solution)/shard_map/mul | solution.py:149
  22.3 0.5 %fusion.8 = f32[4,4,128]{2,1,0:T(4,128)S(1)} fusion(bf16[4,4,128,128]{3,2,1,0:T(8,128)(2,1)S(1)} %copy-done, f32[4,128]{1,0:T(4,128)S(1)} %bitcast.79, f32[4,128]{1,0:T(4,128)S(1)} %bitcast.75, s32[4,4,128]{2,1,0:T(4,128)S(1)} %bitcast.86, s32[4,4,128]{2,1,0:T(4,128)S(1)} %bitcast.87, f32[4,128]{1,0:T(4,128)S(1)} %bitcast.77, ...), kind=kOutput, calls=%fused_computation.11 | convolution fusion | flops 70776832 | bytes 563216 | tf_op jit(solution)/shard_map/tkmi,tkip->tkmp/dot_general | solution.py:166
  23.4 2.9 %collective-permute-start.5 = (f32[8,64]{1,0:T(8,128)S(1)}, f32[8,64]{1,0:T(8,128)S(1)}, u32[]{:S(2)}, u32[]{:S(2)}) collective-permute-start(f32[8,64]{1,0:T(8,128)S(1)} %dynamic-slice_bitcast_fusion), channel_id=1, source_target_pairs={{0,8},{1,9},{2,10},{3,11},{4,12},{5,13},{6,14},{7,15},{8,0},{9,1},... | collective-permute-start | bytes 6152 | tf_op jit(solution)/shard_map/ppermute | solution.py:40
  26.4 1.5 %collective-permute-done.5 = f32[8,64]{1,0:T(8,128)S(1)} collective-permute-done((f32[8,64]{1,0:T(8,128)S(1)}, f32[8,64]{1,0:T(8,128)S(1)}, u32[]{:S(2)}, u32[]{:S(2)}) %collective-permute-start.5) | collective-permute-done | bytes 2080 | tf_op jit(solution)/shard_map/ppermute | solution.py:40
  28.0 1.9 %collective-permute-start.6 = (f32[4,64]{1,0:T(4,128)S(1)}, f32[4,64]{1,0:T(4,128)S(1)}, u32[]{:S(2)}, u32[]{:S(2)}) collective-permute-start(f32[4,64]{1,0:T(4,128)S(1)} %dynamic-slice_bitcast_fusion.1), channel_id=1, source_target_pairs={{0,4},{1,5},{2,6},{3,7},{4,0},{5,1},{6,2},{7,3},{8,12},{9,13},{10,... | collective-permute-start | bytes 3080 | tf_op jit(solution)/shard_map/ppermute | solution.py:40
  29.9 1.7 %collective-permute-done.6 = f32[4,64]{1,0:T(4,128)S(1)} collective-permute-done((f32[4,64]{1,0:T(4,128)S(1)}, f32[4,64]{1,0:T(4,128)S(1)}, u32[]{:S(2)}, u32[]{:S(2)}) %collective-permute-start.6) | collective-permute-done | bytes 1056 | tf_op jit(solution)/shard_map/ppermute | solution.py:40
  31.6 1.8 %collective-permute-start.7 = (f32[2,64]{1,0:T(2,128)S(1)}, f32[2,64]{1,0:T(2,128)S(1)}, u32[]{:S(2)}, u32[]{:S(2)}) collective-permute-start(f32[2,64]{1,0:T(2,128)S(1)} %fusion.39), channel_id=1, source_target_pairs={{0,2},{1,3},{2,0},{3,1},{4,6},{5,7},{6,4},{7,5},{8,10},{9,11},{10,... | collective-permute-start | bytes 1544 | tf_op jit(solution)/shard_map/ppermute | solution.py:40
  33.4 0.6 %fusion.9 = f32[4,128]{1,0:T(4,128)S(1)} fusion(bf16[4,4,128,128]{3,2,1,0:T(8,128)(2,1)S(1)} %copy-done, f32[4,128]{1,0:T(4,128)S(1)} %bitcast.80, f32[4,128]{1,0:T(4,128)S(1)} %bitcast.76, s32[4,4,128]{2,1,0:T(4,128)S(1)} %bitcast.85, s32[4,4,128]{2,1,0:T(4,128)S(1)} %bitcast.84, f32[4,128]{1,0:T(4,128)S(1)} %bitcast.78, ...), kind=kOutput, calls=%fused_computation.12 | convolution fusion | flops 70778368 | bytes 557072 | tf_op jit(solution)/shard_map/tkmi,tkip->tkmp/dot_general | solution.py:166
  34.0 1.2 %collective-permute-done.7 = f32[2,64]{1,0:T(2,128)S(1)} collective-permute-done((f32[2,64]{1,0:T(2,128)S(1)}, f32[2,64]{1,0:T(2,128)S(1)}, u32[]{:S(2)}, u32[]{:S(2)}) %collective-permute-start.7) | collective-permute-done | bytes 544 | tf_op jit(solution)/shard_map/ppermute | solution.py:40
  35.2 0.7 %fusion.36 = f32[512]{0:T(512)} fusion(f32[4,128]{1,0:T(4,128)S(1)} %fusion.9, f32[512]{0:T(512)S(1)} %get-tuple-element.10, pred[4]{0:T(512)(128)(4,1)S(1)} %not_reduce_fusion), kind=kLoop, calls=%fused_computation.70 | loop fusion | flops 1024 | bytes 6148 | tf_op jit(solution)/shard_map/sqrt | solution.py:194
  36.4 0.5 %fusion.41 = f32[1,64]{1,0:T(1,128)} fusion(f32[1,64]{1,0:T(1,128)S(1)} %collective-permute-done.8, f32[2,64]{1,0:T(2,128)S(1)} %fusion.38, s32[]{:T(128)S(6)} %select_n.187), kind=kLoop, calls=%fused_computation.86 | loop fusion | flops 64 | bytes 772 | tf_op jit(solution)/shard_map/sqrt | solution.py:190
  (66 shorter events, 3.2 us)
Async XLA Ops:
  0.6 21.7 %copy-start = (bf16[4,4,128,128]{3,2,1,0:T(8,128)(2,1)S(1)}, bf16[4,4,128,128]{3,2,1,0:T(8,128)(2,1)}, u32[]{:S(2)}) copy-start(bf16[4,4,128,128]{3,2,1,0:T(8,128)(2,1)} %param.16) | copy-start | bytes 1572868
  0.7 3.0 %copy-start.3 = (f32[1024]{0:T(1024)S(1)}, f32[1024]{0:T(1024)}, u32[]{:S(2)}) copy-start(f32[1024]{0:T(1024)} %param.11) | copy-start | bytes 12292
  2.4 0.7 %copy-start.9 = (f32[1,256]{1,0:T(1,128)S(1)}, f32[1,256]{1,0:T(1,128)}, u32[]{:S(2)}) copy-start(f32[1,256]{1,0:T(1,128)} %get-tuple-element.6) | copy-start | bytes 3076
  3.1 0.7 %copy-start.4 = (f32[1024]{0:T(1024)S(1)}, f32[1024]{0:T(1024)}, u32[]{:S(2)}) copy-start(f32[1024]{0:T(1024)} %param.12) | copy-start | bytes 12292
  3.1 0.7 %copy-start.5 = (f32[1024]{0:T(1024)S(1)}, f32[1024]{0:T(1024)}, u32[]{:S(2)}) copy-start(f32[1024]{0:T(1024)} %param.13) | copy-start | bytes 12292
  3.1 3.1 %collective-permute-start.1 = (f32[2,128]{1,0:T(2,128)S(1)}, f32[2,128]{1,0:T(2,128)S(1)}, u32[]{:S(2)}, u32[]{:S(2)}) collective-permute-start(f32[2,128]{1,0:T(2,128)S(1)} %bitcast.91), channel_id=1, source_target_pairs={{0,1},{1,0},{2,3},{3,2},{4,5},{5,4},{6,7},{7,6},{8,9},{9,8},{10,11... | collective-permute-start | bytes 3080 | tf_op jit(solution)/shard_map/ppermute | solution.py:126
  3.8 0.7 %copy-start.1 = (f32[1024]{0:T(1024)S(1)}, f32[1024]{0:T(1024)}, u32[]{:S(2)}) copy-start(f32[1024]{0:T(1024)} %param.10) | copy-start | bytes 12292
  4.5 0.7 %copy-start.6 = (s32[1,2,128]{2,1,0:T(2,128)S(1)}, s32[1,2,128]{2,1,0:T(2,128)}, u32[]{:S(2)}) copy-start(s32[1,2,128]{2,1,0:T(2,128)} %pairs_hbm.1) | copy-start | bytes 3076
  4.5 0.7 %copy-start.2 = (s32[4,4]{1,0:T(4,128)S(1)}, s32[4,4]{1,0:T(4,128)}, u32[]{:S(2)}) copy-start(s32[4,4]{1,0:T(4,128)} %param.15) | copy-start | bytes 196
  4.5 15.7 %collective-permute-start = (f32[1024,3]{0,1:T(4,128)S(1)}, f32[1024,3]{0,1:T(4,128)S(1)}, u32[]{:S(2)}, u32[]{:S(2)}) collective-permute-start(f32[1024,3]{0,1:T(4,128)S(1)} %pad_maximum_fusion.1), channel_id=1, source_target_pairs={{0,1},{1,0},{2,3},{3,2},{4,5},{5,4},{6,7},{7,6},{8,9},{9,8},{10,11... | collective-permute-start | bytes 36872 | tf_op jit(solution)/shard_map/ppermute | solution.py:139
  5.3 0.7 %copy-start.7 = (s32[512]{0:T(512)S(1)}, s32[512]{0:T(512)}, u32[]{:S(2)}) copy-start(s32[512]{0:T(512)} %param.14) | copy-start | bytes 6148
  6.2 0.7 %copy-start.8 = (f32[1,256]{1,0:T(1,128)S(1)}, f32[1,256]{1,0:T(1,128)}, u32[]{:S(2)}) copy-start(f32[1,256]{1,0:T(1,128)} %get-tuple-element.7) | copy-start | bytes 3076
  6.9 5.7 %collective-permute-start.2 = (bf16[1,4,128]{2,1,0:T(4,128)(2,1)S(1)}, bf16[1,4,128]{2,1,0:T(4,128)(2,1)S(1)}, u32[]{:S(2)}, u32[]{:S(2)}) collective-permute-start(bf16[1,4,128]{2,1,0:T(4,128)(2,1)S(1)} %pad_maximum_fusion.2), channel_id=1, source_target_pairs={{0,8},{2,10},{4,12},{6,14},{8,0},{10,2},{12,4},{14,6},{1,9},{3,11}... | collective-permute-start | bytes 3080 | tf_op jit(solution)/shard_map/ppermute | solution.py:22
  12.6 3.7 %collective-permute-start.3 = (bf16[2,4,128]{2,1,0:T(4,128)(2,1)S(1)}, bf16[2,4,128]{2,1,0:T(4,128)(2,1)S(1)}, u32[]{:S(2)}, u32[]{:S(2)}) collective-permute-start(bf16[2,4,128]{2,1,0:T(4,128)(2,1)S(1)} %maximum_select_fusion.3), channel_id=1, source_target_pairs={{0,4},{2,6},{4,0},{6,2},{8,12},{10,14},{12,8},{14,10},{1,5},{3,7},... | collective-permute-start | bytes 6152 | tf_op jit(solution)/shard_map/ppermute | solution.py:22
  16.3 3.7 %collective-permute-start.4 = (bf16[4,4,128]{2,1,0:T(4,128)(2,1)S(1)}, bf16[4,4,128]{2,1,0:T(4,128)(2,1)S(1)}, u32[]{:S(2)}, u32[]{:S(2)}) collective-permute-start(bf16[4,4,128]{2,1,0:T(4,128)(2,1)S(1)} %bitcast.73), channel_id=1, source_target_pairs={{0,2},{2,0},{4,6},{6,4},{8,10},{10,8},{12,14},{14,12},{1,3},{3,1},... | collective-permute-start | bytes 12296 | tf_op jit(solution)/shard_map/ppermute | solution.py:22
  23.4 4.5 %collective-permute-start.5 = (f32[8,64]{1,0:T(8,128)S(1)}, f32[8,64]{1,0:T(8,128)S(1)}, u32[]{:S(2)}, u32[]{:S(2)}) collective-permute-start(f32[8,64]{1,0:T(8,128)S(1)} %dynamic-slice_bitcast_fusion), channel_id=1, source_target_pairs={{0,8},{1,9},{2,10},{3,11},{4,12},{5,13},{6,14},{7,15},{8,0},{9,1},... | collective-permute-start | bytes 6152 | tf_op jit(solution)/shard_map/ppermute | solution.py:40
  28.0 3.6 %collective-permute-start.6 = (f32[4,64]{1,0:T(4,128)S(1)}, f32[4,64]{1,0:T(4,128)S(1)}, u32[]{:S(2)}, u32[]{:S(2)}) collective-permute-start(f32[4,64]{1,0:T(4,128)S(1)} %dynamic-slice_bitcast_fusion.1), channel_id=1, source_target_pairs={{0,4},{1,5},{2,6},{3,7},{4,0},{5,1},{6,2},{7,3},{8,12},{9,13},{10,... | collective-permute-start | bytes 3080 | tf_op jit(solution)/shard_map/ppermute | solution.py:40
  31.6 3.6 %collective-permute-start.7 = (f32[2,64]{1,0:T(2,128)S(1)}, f32[2,64]{1,0:T(2,128)S(1)}, u32[]{:S(2)}, u32[]{:S(2)}) collective-permute-start(f32[2,64]{1,0:T(2,128)S(1)} %fusion.39), channel_id=1, source_target_pairs={{0,2},{1,3},{2,0},{3,1},{4,6},{5,7},{6,4},{7,5},{8,10},{9,11},{10,... | collective-permute-start | bytes 1544 | tf_op jit(solution)/shard_map/ppermute | solution.py:40
  35.1 1.2 %collective-permute-start.8 = (f32[1,64]{1,0:T(1,128)S(1)}, f32[1,64]{1,0:T(1,128)S(1)}, u32[]{:S(2)}, u32[]{:S(2)}) collective-permute-start(f32[1,64]{1,0:T(1,128)S(1)} %constant_dynamic-slice_fusion), channel_id=1, source_target_pairs={{0,1},{1,0},{2,3},{3,2},{4,5},{5,4},{6,7},{7,6},{8,9},{9,8},{10,11... | collective-permute-start | bytes 776 | tf_op jit(solution)/shard_map/ppermute | solution.py:40

commit v15 on v13

--- a/solution.py
+++ b/solution.py
@@ -62,32 +62,26 @@
     me_state = lax.axis_index("state")
     both = ("blk", "state")
 
-    partner = [(j, (j + 1) % halves) for j in range(halves)]
-    state_local = jnp.stack(
-        [base_real, base_reactive * base_reactive, voltage * rating], axis=1
-    )
-    other_half = lax.ppermute(state_local, "state", partner)
-    state_pos = jnp.concatenate([state_local, other_half])
-    pos_len = halves * half_len
-
     first_idx = outage_pairs[0, 0]
     second_idx = outage_pairs[0, 1]
+    partner = [(j, (j + 1) % halves) for j in range(halves)]
+    real_other = lax.ppermute(base_real, "state", partner)
+    pos_len = halves * half_len
     outage_at = (outage_ids[0] - me_state * half_len) % pos_len
-    branch_iota = lax.broadcasted_iota(jnp.int32, (pair_count, pos_len), 1)
-    pick_branch = (branch_iota == outage_at[:, None]).astype(jnp.bfloat16)
-    outage_flow = jnp.dot(
-        pick_branch, state_pos[:, 0].astype(jnp.bfloat16), preferred_element_type=jnp.float32
-    )
     pair_at = jnp.concatenate([first_idx, second_idx])
     pair_to = jnp.concatenate([second_idx, first_idx])
     outage_iota = lax.broadcasted_iota(jnp.int32, (2 * pair_count, pair_count), 1)
     pick_at = (outage_iota == pair_at[:, None]).astype(jnp.bfloat16)
-    flows = jnp.dot(
-        pick_at, outage_flow.astype(jnp.bfloat16), preferred_element_type=jnp.float32
-    ).reshape(2, pair_count)
     coupled_rows = jnp.dot(pick_at, coupling[0], preferred_element_type=jnp.float32)
     coupled = jnp.sum(
         jnp.where(outage_iota == pair_to[:, None], coupled_rows, 0.0), axis=1
+    ).reshape(2, pair_count)
+    branch_iota = lax.broadcasted_iota(jnp.int32, (pair_count, pos_len), 1)
+    pick_branch = (branch_iota == outage_at[:, None]).astype(jnp.bfloat16)
+    real_pos = jnp.concatenate([base_real, real_other]).astype(jnp.bfloat16)
+    outage_flow = jnp.dot(pick_branch, real_pos, preferred_element_type=jnp.float32)
+    flows = jnp.dot(
+        pick_at, outage_flow.astype(jnp.bfloat16), preferred_element_type=jnp.float32
     ).reshape(2, pair_count)
     determinant = 1.0 - coupled[0] * coupled[1]
     w_first = (flows[0] + coupled[0] * flows[1]) / determinant
@@ -95,7 +89,10 @@
     packed = jnp.stack([w_first, w_second, first_idx.astype(jnp.float32), second_idx.astype(jnp.float32)])
     table = gather_doubling(packed.astype(jnp.bfloat16), ("blk",))
 
-    mon_at = (monitored - me_state * half_len) % pos_len
+    state_local = jnp.stack([base_real, base_reactive * base_reactive, voltage * rating], axis=1)
+    other_half = lax.ppermute(state_local, "state", [(j, (j + 1) % halves) for j in range(halves)])
+    state_pos = jnp.concatenate([state_local, other_half])
+    mon_at = (monitored - me_state * half_len) % (halves * half_len)
     mon_vals = jnp.take(state_pos, mon_at, axis=0, mode="clip")
     mon_real = mon_vals[:, 0].reshape(tiles_dev, tile_size)
     react_sq = mon_vals[:, 1].reshape(tiles_dev, tile_size)

time: 33.7 us -> 36.2 us (1.074)
  starting transfers between devices: 14.5 us -> 15.8 us
  waiting for transfers between devices: 8.73 us -> 9.79 us
    ppermute x3, waiting for transfers between devices: 3.42 us -> 4.91 us  [gather_doubling(): other = lax.ppermute(cur, axes, [(j, j ^ bit) for j in range(n)])]
    mul x1, other arithmetic: 0.77 us -> 0.01 us  [body(): base_reactive * base_reactive]
    another operation x0 -> x1, other arithmetic: none -> 0.75 us
    ppermute x1 -> x2, starting transfers between devices: 0.56 us -> 1.05 us  [the longest x1 0.56 us: body(): lax.ppermute(state_local, 'state', [(j, (j + 1) % halves) for j in range(...]
    ppermute x4, starting transfers between devices: 6.28 us -> 6.73 us  [scatter_max(): got = lax.ppermute(send, axes, [(j, j ^ bit) for j in range(n)])]
    ppermute x4, waiting for transfers between devices: 5.31 us -> 4.87 us  [scatter_max(): got = lax.ppermute(send, axes, [(j, j ^ bit) for j in range(n)])]
    unnamed x18 -> x20, local copies, waits for them, and re-layouts: 2.07 us -> 2.27 us
  transfers between devices with their start and end apart: 8 -> 9, of which waited for: 6 -> 7; matrix products, arithmetic and copies ran while one was open for 12% -> 8% of each run, Pallas kernels for 0% -> 0%
where the time goes in v15:
time: 36.2 us; the launch traced here: 35.9 us
  starting transfers between devices  15.8 us (44%)
  waiting for transfers between devices  9.79 us (27%)
  local copies, waits for them, and re-layouts  4.14 us (11%)
  other arithmetic  3.27 us (9%)
  matrix products  2.04 us (6%)
  between operations  0.89 us (2%)
    ppermute x3, starting transfers between devices, gather_doubling(): other = lax.ppermute(cur, axes, [(j, j ^ bit) for j in range(n)])  7.99 us
    ppermute x4, starting transfers between devices, scatter_max(): got = lax.ppermute(send, axes, [(j, j ^ bit) for j in range(n)])  6.73 us
    ppermute x3, waiting for transfers between devices, gather_doubling(): other = lax.ppermute(cur, axes, [(j, j ^ bit) for j in range(n)])  4.91 us
    ppermute x4, waiting for transfers between devices, scatter_max(): got = lax.ppermute(send, axes, [(j, j ^ bit) for j in range(n)])  4.87 us
    unnamed x20, local copies, waits for them, and re-layouts  2.27 us
    dot_general x2, matrix products, slot_squares(): jnp.einsum('tkmi,tkip->tkmp', values, weights, preferred_element_type=jnp...  1.11 us
    gather x1, local copies, waits for them, and re-layouts, body(): mon_vals = jnp.take(state_pos, mon_at, axis=0, mode='clip')  1.04 us
    another operation x1, other arithmetic  0.75 us
  transfers between devices with their start and end apart: 9, of which 7 were waited for; matrix products, arithmetic and copies ran while one was open for 8% of the time, Pallas kernels for 0%

profile of v15, /device:TPU:0, one launch (start us, length us, event | category | flops | bytes accessed | tf_op | source)
XLA Modules:
  0.0 35.9 jit_solution(16529049834498958260)
XLA Ops:
  0.7 0.8 %convert.38 = bf16[1024]{0:T(1024)(128)(2,1)S(1)} convert(f32[1024]{0:T(1024)} %param.10) | non-fusion elementwise | flops 1024 | bytes 6144 | tf_op jit(solution)/shard_map/convert.10
  1.4 0.5 %collective-permute-start.1 = (bf16[1024]{0:T(1024)(128)(2,1)S(1)}, bf16[1024]{0:T(1024)(128)(2,1)S(1)}, u32[]{:S(2)}, u32[]{:S(2)}) collective-permute-start(bf16[1024]{0:T(1024)(128)(2,1)S(1)} %convert.38), channel_id=1, source_target_pairs={{0,1},{1,0},{2,3},{3,2},{4,5},{5,4},{6,7},{7,6},{8,9},{9,8},{10,11... | collective-permute-start | bytes 6152 | tf_op jit(solution)/shard_map/ppermute | solution.py:68
  2.1 0.7 %copy-done.1 = f32[1024]{0:T(1024)S(1)} copy-done((f32[1024]{0:T(1024)S(1)}, f32[1024]{0:T(1024)}, u32[]{:S(2)}) %copy-start.1) | copy-done | bytes 4120
  2.8 0.6 %collective-permute-start = (f32[1024,3]{0,1:T(4,128)S(1)}, f32[1024,3]{0,1:T(4,128)S(1)}, u32[]{:S(2)}, u32[]{:S(2)}) collective-permute-start(f32[1024,3]{0,1:T(4,128)S(1)} %pad_maximum_fusion.1), channel_id=1, source_target_pairs={{0,1},{1,0},{2,3},{3,2},{4,5},{5,4},{6,7},{7,6},{8,9},{9,8},{10,11... | collective-permute-start | bytes 36872 | tf_op jit(solution)/shard_map/ppermute | solution.py:93
  3.6 0.6 %copy-done.7 = s32[1,2,128]{2,1,0:T(2,128)S(1)} copy-done((s32[1,2,128]{2,1,0:T(2,128)S(1)}, s32[1,2,128]{2,1,0:T(2,128)}, u32[]{:S(2)}) %copy-start.7) | copy-done | bytes 1048
  4.2 0.6 %copy-done.9 = s32[1,128]{1,0:T(1,128)S(1)} copy-done((s32[1,128]{1,0:T(1,128)S(1)}, s32[1,128]{1,0:T(1,128)}, u32[]{:S(2)}) %copy-start.9) | copy-done | bytes 536
  5.9 4.1 %collective-permute-start.2 = (bf16[1,4,128]{2,1,0:T(4,128)(2,1)S(1)}, bf16[1,4,128]{2,1,0:T(4,128)(2,1)S(1)}, u32[]{:S(2)}, u32[]{:S(2)}) collective-permute-start(bf16[1,4,128]{2,1,0:T(4,128)(2,1)S(1)} %pad_maximum_fusion.3), channel_id=1, source_target_pairs={{0,8},{2,10},{4,12},{6,14},{8,0},{10,2},{12,4},{14,6},{1,9},{3,11}... | collective-permute-start | bytes 3080 | tf_op jit(solution)/shard_map/ppermute | solution.py:20
  10.0 1.5 %collective-permute-done.2 = bf16[1,4,128]{2,1,0:T(4,128)(2,1)S(1)} collective-permute-done((bf16[1,4,128]{2,1,0:T(4,128)(2,1)S(1)}, bf16[1,4,128]{2,1,0:T(4,128)(2,1)S(1)}, u32[]{:S(2)}, u32[]{:S(2)}) %collective-permute-start.2) | collective-permute-done | bytes 1056 | tf_op jit(solution)/shard_map/ppermute | solution.py:20
  11.6 2.0 %collective-permute-start.3 = (bf16[2,4,128]{2,1,0:T(4,128)(2,1)S(1)}, bf16[2,4,128]{2,1,0:T(4,128)(2,1)S(1)}, u32[]{:S(2)}, u32[]{:S(2)}) collective-permute-start(bf16[2,4,128]{2,1,0:T(4,128)(2,1)S(1)} %maximum_select_fusion.3), channel_id=1, source_target_pairs={{0,4},{2,6},{4,0},{6,2},{8,12},{10,14},{12,8},{14,10},{1,5},{3,7},... | collective-permute-start | bytes 6152 | tf_op jit(solution)/shard_map/ppermute | solution.py:20
  13.6 1.7 %collective-permute-done.3 = bf16[2,4,128]{2,1,0:T(4,128)(2,1)S(1)} collective-permute-done((bf16[2,4,128]{2,1,0:T(4,128)(2,1)S(1)}, bf16[2,4,128]{2,1,0:T(4,128)(2,1)S(1)}, u32[]{:S(2)}, u32[]{:S(2)}) %collective-permute-start.3) | collective-permute-done | bytes 2080 | tf_op jit(solution)/shard_map/ppermute | solution.py:20
  15.3 1.9 %collective-permute-start.4 = (bf16[4,4,128]{2,1,0:T(4,128)(2,1)S(1)}, bf16[4,4,128]{2,1,0:T(4,128)(2,1)S(1)}, u32[]{:S(2)}, u32[]{:S(2)}) collective-permute-start(bf16[4,4,128]{2,1,0:T(4,128)(2,1)S(1)} %bitcast.92), channel_id=1, source_target_pairs={{0,2},{2,0},{4,6},{6,4},{8,10},{10,8},{12,14},{14,12},{1,3},{3,1},... | collective-permute-start | bytes 12296 | tf_op jit(solution)/shard_map/ppermute | solution.py:20
  17.2 1.7 %collective-permute-done.4 = bf16[4,4,128]{2,1,0:T(4,128)(2,1)S(1)} collective-permute-done((bf16[4,4,128]{2,1,0:T(4,128)(2,1)S(1)}, bf16[4,4,128]{2,1,0:T(4,128)(2,1)S(1)}, u32[]{:S(2)}, u32[]{:S(2)}) %collective-permute-start.4) | collective-permute-done | bytes 4128 | tf_op jit(solution)/shard_map/ppermute | solution.py:20
  19.7 1.0 %gather_fusion = f32[512,3]{1,0:T(8,128)S(1)} fusion(f32[2048,3]{1,0:T(8,128)S(1)} %copy.43, s32[1024]{0:T(1024)S(1)} %pad_clamp_fusion), kind=kCustom, calls=%fused_computation | custom fusion | bytes 14336 | tf_op jit(solution)/shard_map/jit(_take)/gather | solution.py:96
  20.7 0.5 %multiply_reduce_fusion = (f32[512]{0:T(512)S(1)}, f32[512]{0:T(512)S(1)}, f32[512]{0:T(512)S(1)}, f32[512]{0:T(512)S(1)}) fusion(f32[512,3]{1,0:T(8,128)S(1)} %gather_fusion), kind=kLoop, calls=%fused_computation.40 | loop fusion | flops 2560 | bytes 14336 | tf_op jit(solution)/shard_map/mul | solution.py:101
  21.3 0.5 %fusion.8 = f32[4,4,128]{2,1,0:T(4,128)S(1)} fusion(bf16[4,4,128,128]{3,2,1,0:T(8,128)(2,1)S(1)} %copy-done, f32[4,128]{1,0:T(4,128)S(1)} %bitcast.98, f32[4,128]{1,0:T(4,128)S(1)} %bitcast.94, s32[4,4,128]{2,1,0:T(4,128)S(1)} %bitcast.105, s32[4,4,128]{2,1,0:T(4,128)S(1)} %bitcast.106, f32[4,128]{1,0:T(4,128)S(1)} %bitcast.96, ...), kind=kOutput, calls=%fused_computation.11 | convolution fusion | flops 70776832 | bytes 563216 | tf_op jit(solution)/shard_map/tkmi,tkip->tkmp/dot_general | solution.py:118
  22.4 2.9 %collective-permute-start.5 = (f32[8,64]{1,0:T(8,128)S(1)}, f32[8,64]{1,0:T(8,128)S(1)}, u32[]{:S(2)}, u32[]{:S(2)}) collective-permute-start(f32[8,64]{1,0:T(8,128)S(1)} %dynamic-slice_bitcast_fusion), channel_id=1, source_target_pairs={{0,8},{1,9},{2,10},{3,11},{4,12},{5,13},{6,14},{7,15},{8,0},{9,1},... | collective-permute-start | bytes 6152 | tf_op jit(solution)/shard_map/ppermute | solution.py:38
  25.4 1.5 %collective-permute-done.5 = f32[8,64]{1,0:T(8,128)S(1)} collective-permute-done((f32[8,64]{1,0:T(8,128)S(1)}, f32[8,64]{1,0:T(8,128)S(1)}, u32[]{:S(2)}, u32[]{:S(2)}) %collective-permute-start.5) | collective-permute-done | bytes 2080 | tf_op jit(solution)/shard_map/ppermute | solution.py:38
  27.0 1.9 %collective-permute-start.6 = (f32[4,64]{1,0:T(4,128)S(1)}, f32[4,64]{1,0:T(4,128)S(1)}, u32[]{:S(2)}, u32[]{:S(2)}) collective-permute-start(f32[4,64]{1,0:T(4,128)S(1)} %dynamic-slice_bitcast_fusion.1), channel_id=1, source_target_pairs={{0,4},{1,5},{2,6},{3,7},{4,0},{5,1},{6,2},{7,3},{8,12},{9,13},{10,... | collective-permute-start | bytes 3080 | tf_op jit(solution)/shard_map/ppermute | solution.py:38
  28.9 1.7 %collective-permute-done.6 = f32[4,64]{1,0:T(4,128)S(1)} collective-permute-done((f32[4,64]{1,0:T(4,128)S(1)}, f32[4,64]{1,0:T(4,128)S(1)}, u32[]{:S(2)}, u32[]{:S(2)}) %collective-permute-start.6) | collective-permute-done | bytes 1056 | tf_op jit(solution)/shard_map/ppermute | solution.py:38
  30.6 1.8 %collective-permute-start.7 = (f32[2,64]{1,0:T(2,128)S(1)}, f32[2,64]{1,0:T(2,128)S(1)}, u32[]{:S(2)}, u32[]{:S(2)}) collective-permute-start(f32[2,64]{1,0:T(2,128)S(1)} %fusion.48), channel_id=1, source_target_pairs={{0,2},{1,3},{2,0},{3,1},{4,6},{5,7},{6,4},{7,5},{8,10},{9,11},{10,... | collective-permute-start | bytes 1544 | tf_op jit(solution)/shard_map/ppermute | solution.py:38
  32.4 0.6 %fusion.9 = f32[4,128]{1,0:T(4,128)S(1)} fusion(bf16[4,4,128,128]{3,2,1,0:T(8,128)(2,1)S(1)} %copy-done, f32[4,128]{1,0:T(4,128)S(1)} %bitcast.99, f32[4,128]{1,0:T(4,128)S(1)} %bitcast.95, s32[4,4,128]{2,1,0:T(4,128)S(1)} %bitcast.104, s32[4,4,128]{2,1,0:T(4,128)S(1)} %bitcast.103, f32[4,128]{1,0:T(4,128)S(1)} %bitcast.97, ...), kind=kOutput, calls=%fused_computation.12 | convolution fusion | flops 70778368 | bytes 557072 | tf_op jit(solution)/shard_map/tkmi,tkip->tkmp/dot_general | solution.py:118
  33.0 1.2 %collective-permute-done.7 = f32[2,64]{1,0:T(2,128)S(1)} collective-permute-done((f32[2,64]{1,0:T(2,128)S(1)}, f32[2,64]{1,0:T(2,128)S(1)}, u32[]{:S(2)}, u32[]{:S(2)}) %collective-permute-start.7) | collective-permute-done | bytes 544 | tf_op jit(solution)/shard_map/ppermute | solution.py:38
  34.2 0.7 %fusion.45 = f32[512]{0:T(512)} fusion(f32[4,128]{1,0:T(4,128)S(1)} %fusion.9, f32[512]{0:T(512)S(1)} %get-tuple-element.6, pred[4]{0:T(512)(128)(4,1)S(1)} %not_reduce_fusion), kind=kLoop, calls=%fused_computation.86 | loop fusion | flops 1024 | bytes 6148 | tf_op jit(solution)/shard_map/sqrt | solution.py:146
  35.4 0.5 %fusion.50 = f32[1,64]{1,0:T(1,128)} fusion(f32[1,64]{1,0:T(1,128)S(1)} %collective-permute-done.8, f32[2,64]{1,0:T(2,128)S(1)} %fusion.47, s32[]{:T(128)S(6)} %select_n.203), kind=kLoop, calls=%fused_computation.105 | loop fusion | flops 64 | bytes 772 | tf_op jit(solution)/shard_map/sqrt | solution.py:142
  (71 shorter events, 3.5 us)
Async XLA Ops:
  0.6 20.7 %copy-start = (bf16[4,4,128,128]{3,2,1,0:T(8,128)(2,1)S(1)}, bf16[4,4,128,128]{3,2,1,0:T(8,128)(2,1)}, u32[]{:S(2)}) copy-start(bf16[4,4,128,128]{3,2,1,0:T(8,128)(2,1)} %param.16) | copy-start | bytes 1572868
  0.6 1.3 %copy-start.3 = (f32[1024]{0:T(1024)S(1)}, f32[1024]{0:T(1024)}, u32[]{:S(2)}) copy-start(f32[1024]{0:T(1024)} %param.11) | copy-start | bytes 12292
  1.4 0.7 %copy-start.4 = (f32[1024]{0:T(1024)S(1)}, f32[1024]{0:T(1024)}, u32[]{:S(2)}) copy-start(f32[1024]{0:T(1024)} %param.12) | copy-start | bytes 12292
  1.4 0.7 %copy-start.5 = (f32[1024]{0:T(1024)S(1)}, f32[1024]{0:T(1024)}, u32[]{:S(2)}) copy-start(f32[1024]{0:T(1024)} %param.13) | copy-start | bytes 12292
  1.4 3.9 %collective-permute-start.1 = (bf16[1024]{0:T(1024)(128)(2,1)S(1)}, bf16[1024]{0:T(1024)(128)(2,1)S(1)}, u32[]{:S(2)}, u32[]{:S(2)}) collective-permute-start(bf16[1024]{0:T(1024)(128)(2,1)S(1)} %convert.38), channel_id=1, source_target_pairs={{0,1},{1,0},{2,3},{3,2},{4,5},{5,4},{6,7},{7,6},{8,9},{9,8},{10,11... | collective-permute-start | bytes 6152 | tf_op jit(solution)/shard_map/ppermute | solution.py:68
  2.1 0.7 %copy-start.1 = (f32[1024]{0:T(1024)S(1)}, f32[1024]{0:T(1024)}, u32[]{:S(2)}) copy-start(f32[1024]{0:T(1024)} %param.10) | copy-start | bytes 12292
  2.8 0.7 %copy-start.2 = (s32[4,4]{1,0:T(4,128)S(1)}, s32[4,4]{1,0:T(4,128)}, u32[]{:S(2)}) copy-start(s32[4,4]{1,0:T(4,128)} %param.15) | copy-start | bytes 196
  2.8 2.2 %copy-start.8 = (bf16[1,128,128]{2,1,0:T(8,128)(2,1)S(1)}, bf16[1,128,128]{2,1,0:T(8,128)(2,1)}, u32[]{:S(2)}) copy-start(bf16[1,128,128]{2,1,0:T(8,128)(2,1)} %param.18) | copy-start | bytes 98308
  2.8 16.4 %collective-permute-start = (f32[1024,3]{0,1:T(4,128)S(1)}, f32[1024,3]{0,1:T(4,128)S(1)}, u32[]{:S(2)}, u32[]{:S(2)}) collective-permute-start(f32[1024,3]{0,1:T(4,128)S(1)} %pad_maximum_fusion.1), channel_id=1, source_target_pairs={{0,1},{1,0},{2,3},{3,2},{4,5},{5,4},{6,7},{7,6},{8,9},{9,8},{10,11... | collective-permute-start | bytes 36872 | tf_op jit(solution)/shard_map/ppermute | solution.py:93
  3.5 0.7 %copy-start.7 = (s32[1,2,128]{2,1,0:T(2,128)S(1)}, s32[1,2,128]{2,1,0:T(2,128)}, u32[]{:S(2)}) copy-start(s32[1,2,128]{2,1,0:T(2,128)} %param.19) | copy-start | bytes 3076
  4.2 0.7 %copy-start.9 = (s32[1,128]{1,0:T(1,128)S(1)}, s32[1,128]{1,0:T(1,128)}, u32[]{:S(2)}) copy-start(s32[1,128]{1,0:T(1,128)} %param.17) | copy-start | bytes 1540
  4.2 0.7 %copy-start.6 = (s32[512]{0:T(512)S(1)}, s32[512]{0:T(512)}, u32[]{:S(2)}) copy-start(s32[512]{0:T(512)} %param.14) | copy-start | bytes 6148
  5.9 5.7 %collective-permute-start.2 = (bf16[1,4,128]{2,1,0:T(4,128)(2,1)S(1)}, bf16[1,4,128]{2,1,0:T(4,128)(2,1)S(1)}, u32[]{:S(2)}, u32[]{:S(2)}) collective-permute-start(bf16[1,4,128]{2,1,0:T(4,128)(2,1)S(1)} %pad_maximum_fusion.3), channel_id=1, source_target_pairs={{0,8},{2,10},{4,12},{6,14},{8,0},{10,2},{12,4},{14,6},{1,9},{3,11}... | collective-permute-start | bytes 3080 | tf_op jit(solution)/shard_map/ppermute | solution.py:20
  11.6 3.7 %collective-permute-start.3 = (bf16[2,4,128]{2,1,0:T(4,128)(2,1)S(1)}, bf16[2,4,128]{2,1,0:T(4,128)(2,1)S(1)}, u32[]{:S(2)}, u32[]{:S(2)}) collective-permute-start(bf16[2,4,128]{2,1,0:T(4,128)(2,1)S(1)} %maximum_select_fusion.3), channel_id=1, source_target_pairs={{0,4},{2,6},{4,0},{6,2},{8,12},{10,14},{12,8},{14,10},{1,5},{3,7},... | collective-permute-start | bytes 6152 | tf_op jit(solution)/shard_map/ppermute | solution.py:20
  15.3 3.7 %collective-permute-start.4 = (bf16[4,4,128]{2,1,0:T(4,128)(2,1)S(1)}, bf16[4,4,128]{2,1,0:T(4,128)(2,1)S(1)}, u32[]{:S(2)}, u32[]{:S(2)}) collective-permute-start(bf16[4,4,128]{2,1,0:T(4,128)(2,1)S(1)} %bitcast.92), channel_id=1, source_target_pairs={{0,2},{2,0},{4,6},{6,4},{8,10},{10,8},{12,14},{14,12},{1,3},{3,1},... | collective-permute-start | bytes 12296 | tf_op jit(solution)/shard_map/ppermute | solution.py:20
  22.4 4.5 %collective-permute-start.5 = (f32[8,64]{1,0:T(8,128)S(1)}, f32[8,64]{1,0:T(8,128)S(1)}, u32[]{:S(2)}, u32[]{:S(2)}) collective-permute-start(f32[8,64]{1,0:T(8,128)S(1)} %dynamic-slice_bitcast_fusion), channel_id=1, source_target_pairs={{0,8},{1,9},{2,10},{3,11},{4,12},{5,13},{6,14},{7,15},{8,0},{9,1},... | collective-permute-start | bytes 6152 | tf_op jit(solution)/shard_map/ppermute | solution.py:38
  27.0 3.6 %collective-permute-start.6 = (f32[4,64]{1,0:T(4,128)S(1)}, f32[4,64]{1,0:T(4,128)S(1)}, u32[]{:S(2)}, u32[]{:S(2)}) collective-permute-start(f32[4,64]{1,0:T(4,128)S(1)} %dynamic-slice_bitcast_fusion.1), channel_id=1, source_target_pairs={{0,4},{1,5},{2,6},{3,7},{4,0},{5,1},{6,2},{7,3},{8,12},{9,13},{10,... | collective-permute-start | bytes 3080 | tf_op jit(solution)/shard_map/ppermute | solution.py:38
  30.6 3.6 %collective-permute-start.7 = (f32[2,64]{1,0:T(2,128)S(1)}, f32[2,64]{1,0:T(2,128)S(1)}, u32[]{:S(2)}, u32[]{:S(2)}) collective-permute-start(f32[2,64]{1,0:T(2,128)S(1)} %fusion.48), channel_id=1, source_target_pairs={{0,2},{1,3},{2,0},{3,1},{4,6},{5,7},{6,4},{7,5},{8,10},{9,11},{10,... | collective-permute-start | bytes 1544 | tf_op jit(solution)/shard_map/ppermute | solution.py:38
  34.1 1.2 %collective-permute-start.8 = (f32[1,64]{1,0:T(1,128)S(1)}, f32[1,64]{1,0:T(1,128)S(1)}, u32[]{:S(2)}, u32[]{:S(2)}) collective-permute-start(f32[1,64]{1,0:T(1,128)S(1)} %constant_dynamic-slice_fusion), channel_id=1, source_target_pairs={{0,1},{1,0},{2,3},{3,2},{4,5},{5,4},{6,7},{7,6},{8,9},{9,8},{10,11... | collective-permute-start | bytes 776 | tf_op jit(solution)/shard_map/ppermute | solution.py:38

commit v16 on v12

--- a/solution.py
+++ b/solution.py
@@ -15,12 +15,13 @@
     n = axes_size(axes)
     me = lax.axis_index(axes)
     cur = x[None]
-    bit = 1
-    while bit < n:
+    bit = n // 2
+    while bit >= 1:
         other = lax.ppermute(cur, axes, [(j, j ^ bit) for j in range(n)])
         low = (me & bit) == 0
-        cur = jnp.where(low, jnp.concatenate([cur, other]), jnp.concatenate([other, cur]))
-        bit *= 2
+        cur = jnp.where(low, jnp.stack([cur, other], axis=1), jnp.stack([other, cur], axis=1))
+        cur = cur.reshape((-1,) + x.shape)
+        bit //= 2
     return cur
 
 
@@ -129,14 +130,14 @@
     matches = tile_ids[:, :, None] == block_iota[None, None, :]
     absent = jnp.logical_not(jnp.any(matches, axis=1))
     any_absent = jnp.any(absent, axis=1)
+    base_max = jnp.max(base_sq, axis=1)
+    absent_max = jnp.max(jnp.where(absent, base_max[:, None], neg), axis=0)
 
 
     col_max = jnp.max(squared, axis=2)
     worst_local = jnp.max(
         jnp.where(matches[:, :, :, None], col_max[:, :, None, :], neg), axis=(0, 1)
     )
-    base_max = jnp.max(base_sq, axis=1)
-    absent_max = jnp.max(jnp.where(absent, base_max[:, None], neg), axis=0)
     worst_local = jnp.maximum(worst_local, absent_max[:, None])
 
     worst_sq = scatter_max(worst_local.reshape(blocks * halves, half_width), both)

time: 35.6 us -> 35.5 us (level)
    unnamed x22 -> x18, local copies, waits for them, and re-layouts: 1.67 us -> 1.65 us
where the time goes in v16:
time: 35.5 us; the launch traced here: 35.2 us
  starting transfers between devices  15.8 us (45%)
  waiting for transfers between devices  9.8 us (28%)
  local copies, waits for them, and re-layouts  3.52 us (10%)
  other arithmetic  3.27 us (9%)
  matrix products  1.95 us (5%)
  between operations  0.89 us (3%)
    ppermute x3, starting transfers between devices, gather_doubling(): other = lax.ppermute(cur, axes, [(j, j ^ bit) for j in range(n)])  7.99 us
    ppermute x4, starting transfers between devices, scatter_max(): got = lax.ppermute(send, axes, [(j, j ^ bit) for j in range(n)])  6.72 us
    ppermute x3, waiting for transfers between devices, gather_doubling(): other = lax.ppermute(cur, axes, [(j, j ^ bit) for j in range(n)])  4.91 us
    ppermute x4, waiting for transfers between devices, scatter_max(): got = lax.ppermute(send, axes, [(j, j ^ bit) for j in range(n)])  4.88 us
    unnamed x18, local copies, waits for them, and re-layouts  1.65 us
    dot_general x2, matrix products, slot_squares(): jnp.einsum('tkmi,tkip->tkmp', values, weights, preferred_element_type=jnp...  1.11 us
    gather x1, local copies, waits for them, and re-layouts, body(): mon_vals = jnp.take(state_pos, mon_at, axis=0, mode='clip')  1.04 us
    squeeze x1, other arithmetic, body(): second_idx = outage_pairs[0, 1]  0.76 us
  transfers between devices with their start and end apart: 9, of which 7 were waited for; matrix products, arithmetic and copies ran while one was open for 6% of the time, Pallas kernels for 0%

profile of v16, /device:TPU:0, one launch (start us, length us, event | category | flops | bytes accessed | tf_op | source)
XLA Modules:
  0.0 35.2 jit_solution(652876308873108848)
XLA Ops:
  0.7 0.8 %slice_bitcast_fusion.2 = (s32[128]{0:T(128)S(1)}, bf16[1,1,128]{2,1,0:T(2,128)(2,1)S(1)}, bf16[1,1,128]{2,1,0:T(2,128)(2,1)S(1)}, s32[128]{0:T(128)S(1)}) fusion(s32[1,2,128]{2,1,0:T(2,128)} %param.19), kind=kLoop, calls=%fused_computation.114 | loop fusion | flops 512 | bytes 2560 | tf_op jit(solution)/shard_map/squeeze | solution.py:66
  1.5 0.6 %copy-done.8 = s32[1,128]{1,0:T(1,128)S(1)} copy-done((s32[1,128]{1,0:T(1,128)S(1)}, s32[1,128]{1,0:T(1,128)}, u32[]{:S(2)}) %copy-start.8) | copy-done | bytes 536
  2.5 0.5 %collective-permute-start.1 = (f32[2,128]{1,0:T(2,128)S(1)}, f32[2,128]{1,0:T(2,128)S(1)}, u32[]{:S(2)}, u32[]{:S(2)}) collective-permute-start(f32[2,128]{1,0:T(2,128)S(1)} %bitcast.134), channel_id=1, source_target_pairs={{0,1},{1,0},{2,3},{3,2},{4,5},{5,4},{6,7},{7,6},{8,9},{9,8},{10,11... | collective-permute-start | bytes 3080 | tf_op jit(solution)/shard_map/ppermute | solution.py:80
  3.3 0.6 %collective-permute-start = (f32[1024,3]{0,1:T(4,128)S(1)}, f32[1024,3]{0,1:T(4,128)S(1)}, u32[]{:S(2)}, u32[]{:S(2)}) collective-permute-start(f32[1024,3]{0,1:T(4,128)S(1)} %pad_maximum_fusion.1), channel_id=1, source_target_pairs={{0,1},{1,0},{2,3},{3,2},{4,5},{5,4},{6,7},{7,6},{8,9},{9,8},{10,11... | collective-permute-start | bytes 36872 | tf_op jit(solution)/shard_map/ppermute | solution.py:95
  4.0 0.7 %copy-done.6 = s32[512]{0:T(512)S(1)} copy-done((s32[512]{0:T(512)S(1)}, s32[512]{0:T(512)}, u32[]{:S(2)}) %copy-start.6) | copy-done | bytes 2072
  5.2 4.1 %collective-permute-start.2 = (bf16[1,4,128]{2,1,0:T(4,128)(2,1)S(1)}, bf16[1,4,128]{2,1,0:T(4,128)(2,1)S(1)}, u32[]{:S(2)}, u32[]{:S(2)}) collective-permute-start(bf16[1,4,128]{2,1,0:T(4,128)(2,1)S(1)} %pad_maximum_fusion.2), channel_id=1, source_target_pairs={{0,8},{2,10},{4,12},{6,14},{8,0},{10,2},{12,4},{14,6},{1,9},{3,11}... | collective-permute-start | bytes 3080 | tf_op jit(solution)/shard_map/ppermute | solution.py:20
  9.4 1.5 %collective-permute-done.2 = bf16[1,4,128]{2,1,0:T(4,128)(2,1)S(1)} collective-permute-done((bf16[1,4,128]{2,1,0:T(4,128)(2,1)S(1)}, bf16[1,4,128]{2,1,0:T(4,128)(2,1)S(1)}, u32[]{:S(2)}, u32[]{:S(2)}) %collective-permute-start.2) | collective-permute-done | bytes 1056 | tf_op jit(solution)/shard_map/ppermute | solution.py:20
  10.9 2.0 %collective-permute-start.3 = (bf16[2,4,128]{2,1,0:T(4,128)(2,1)S(1)}, bf16[2,4,128]{2,1,0:T(4,128)(2,1)S(1)}, u32[]{:S(2)}, u32[]{:S(2)}) collective-permute-start(bf16[2,4,128]{2,1,0:T(4,128)(2,1)S(1)} %maximum_select_fusion.3), channel_id=1, source_target_pairs={{0,4},{2,6},{4,0},{6,2},{8,12},{10,14},{12,8},{14,10},{1,5},{3,7},... | collective-permute-start | bytes 6152 | tf_op jit(solution)/shard_map/ppermute | solution.py:20
  12.9 1.7 %collective-permute-done.3 = bf16[2,4,128]{2,1,0:T(4,128)(2,1)S(1)} collective-permute-done((bf16[2,4,128]{2,1,0:T(4,128)(2,1)S(1)}, bf16[2,4,128]{2,1,0:T(4,128)(2,1)S(1)}, u32[]{:S(2)}, u32[]{:S(2)}) %collective-permute-start.3) | collective-permute-done | bytes 2080 | tf_op jit(solution)/shard_map/ppermute | solution.py:20
  14.6 1.9 %collective-permute-start.4 = (bf16[4,4,128]{2,1,0:T(4,128)(2,1)S(1)}, bf16[4,4,128]{2,1,0:T(4,128)(2,1)S(1)}, u32[]{:S(2)}, u32[]{:S(2)}) collective-permute-start(bf16[4,4,128]{2,1,0:T(4,128)(2,1)S(1)} %bitcast.116), channel_id=1, source_target_pairs={{0,2},{2,0},{4,6},{6,4},{8,10},{10,8},{12,14},{14,12},{1,3},{3,1},... | collective-permute-start | bytes 12296 | tf_op jit(solution)/shard_map/ppermute | solution.py:20
  16.6 1.7 %collective-permute-done.4 = bf16[4,4,128]{2,1,0:T(4,128)(2,1)S(1)} collective-permute-done((bf16[4,4,128]{2,1,0:T(4,128)(2,1)S(1)}, bf16[4,4,128]{2,1,0:T(4,128)(2,1)S(1)}, u32[]{:S(2)}, u32[]{:S(2)}) %collective-permute-start.4) | collective-permute-done | bytes 4128 | tf_op jit(solution)/shard_map/ppermute | solution.py:20
  19.0 1.0 %gather_fusion = f32[512,3]{1,0:T(8,128)S(1)} fusion(f32[2048,3]{1,0:T(8,128)S(1)} %copy.43, s32[1024]{0:T(1024)S(1)} %pad_clamp_fusion), kind=kCustom, calls=%fused_computation | custom fusion | bytes 14336 | tf_op jit(solution)/shard_map/jit(_take)/gather | solution.py:98
  20.0 0.5 %multiply_reduce_fusion = (f32[512]{0:T(512)S(1)}, f32[512]{0:T(512)S(1)}, f32[512]{0:T(512)S(1)}, f32[512]{0:T(512)S(1)}) fusion(f32[512,3]{1,0:T(8,128)S(1)} %gather_fusion), kind=kLoop, calls=%fused_computation.39 | loop fusion | flops 2560 | bytes 14336 | tf_op jit(solution)/shard_map/mul | solution.py:103
  20.6 0.5 %fusion.8 = f32[4,4,128]{2,1,0:T(4,128)S(1)} fusion(bf16[4,4,128,128]{3,2,1,0:T(8,128)(2,1)S(1)} %copy-done, f32[4,128]{1,0:T(4,128)S(1)} %bitcast.122, f32[4,128]{1,0:T(4,128)S(1)} %bitcast.118, s32[4,4,128]{2,1,0:T(4,128)S(1)} %bitcast.129, s32[4,4,128]{2,1,0:T(4,128)S(1)} %bitcast.130, f32[4,128]{1,0:T(4,128)S(1)} %bitcast.120, ...), kind=kOutput, calls=%fused_computation.11 | convolution fusion | flops 70776832 | bytes 563216 | tf_op jit(solution)/shard_map/tkmi,tkip->tkmp/dot_general | solution.py:120
  21.8 2.9 %collective-permute-start.5 = (f32[8,64]{1,0:T(8,128)S(1)}, f32[8,64]{1,0:T(8,128)S(1)}, u32[]{:S(2)}, u32[]{:S(2)}) collective-permute-start(f32[8,64]{1,0:T(8,128)S(1)} %dynamic-slice_bitcast_fusion), channel_id=1, source_target_pairs={{0,8},{1,9},{2,10},{3,11},{4,12},{5,13},{6,14},{7,15},{8,0},{9,1},... | collective-permute-start | bytes 6152 | tf_op jit(solution)/shard_map/ppermute | solution.py:38
  24.7 1.5 %collective-permute-done.5 = f32[8,64]{1,0:T(8,128)S(1)} collective-permute-done((f32[8,64]{1,0:T(8,128)S(1)}, f32[8,64]{1,0:T(8,128)S(1)}, u32[]{:S(2)}, u32[]{:S(2)}) %collective-permute-start.5) | collective-permute-done | bytes 2080 | tf_op jit(solution)/shard_map/ppermute | solution.py:38
  26.3 1.9 %collective-permute-start.6 = (f32[4,64]{1,0:T(4,128)S(1)}, f32[4,64]{1,0:T(4,128)S(1)}, u32[]{:S(2)}, u32[]{:S(2)}) collective-permute-start(f32[4,64]{1,0:T(4,128)S(1)} %dynamic-slice_bitcast_fusion.1), channel_id=1, source_target_pairs={{0,4},{1,5},{2,6},{3,7},{4,0},{5,1},{6,2},{7,3},{8,12},{9,13},{10,... | collective-permute-start | bytes 3080 | tf_op jit(solution)/shard_map/ppermute | solution.py:38
  28.2 1.7 %collective-permute-done.6 = f32[4,64]{1,0:T(4,128)S(1)} collective-permute-done((f32[4,64]{1,0:T(4,128)S(1)}, f32[4,64]{1,0:T(4,128)S(1)}, u32[]{:S(2)}, u32[]{:S(2)}) %collective-permute-start.6) | collective-permute-done | bytes 1056 | tf_op jit(solution)/shard_map/ppermute | solution.py:38
  29.9 1.8 %collective-permute-start.7 = (f32[2,64]{1,0:T(2,128)S(1)}, f32[2,64]{1,0:T(2,128)S(1)}, u32[]{:S(2)}, u32[]{:S(2)}) collective-permute-start(f32[2,64]{1,0:T(2,128)S(1)} %fusion.48), channel_id=1, source_target_pairs={{0,2},{1,3},{2,0},{3,1},{4,6},{5,7},{6,4},{7,5},{8,10},{9,11},{10,... | collective-permute-start | bytes 1544 | tf_op jit(solution)/shard_map/ppermute | solution.py:38
  31.7 0.6 %fusion.9 = f32[4,128]{1,0:T(4,128)S(1)} fusion(bf16[4,4,128,128]{3,2,1,0:T(8,128)(2,1)S(1)} %copy-done, f32[4,128]{1,0:T(4,128)S(1)} %bitcast.123, f32[4,128]{1,0:T(4,128)S(1)} %bitcast.119, s32[4,4,128]{2,1,0:T(4,128)S(1)} %bitcast.128, s32[4,4,128]{2,1,0:T(4,128)S(1)} %bitcast.127, f32[4,128]{1,0:T(4,128)S(1)} %bitcast.121, ...), kind=kOutput, calls=%fused_computation.12 | convolution fusion | flops 70778368 | bytes 557072 | tf_op jit(solution)/shard_map/tkmi,tkip->tkmp/dot_general | solution.py:120
  32.3 1.2 %collective-permute-done.7 = f32[2,64]{1,0:T(2,128)S(1)} collective-permute-done((f32[2,64]{1,0:T(2,128)S(1)}, f32[2,64]{1,0:T(2,128)S(1)}, u32[]{:S(2)}, u32[]{:S(2)}) %collective-permute-start.7) | collective-permute-done | bytes 544 | tf_op jit(solution)/shard_map/ppermute | solution.py:38
  33.5 0.7 %fusion.45 = f32[512]{0:T(512)} fusion(f32[4,128]{1,0:T(4,128)S(1)} %fusion.9, f32[512]{0:T(512)S(1)} %get-tuple-element.6, pred[4]{0:T(512)(128)(4,1)S(1)} %not_reduce_fusion), kind=kLoop, calls=%fused_computation.83 | loop fusion | flops 1024 | bytes 6148 | tf_op jit(solution)/shard_map/sqrt | solution.py:148
  34.2 0.5 %collective-permute-done.8 = f32[1,64]{1,0:T(1,128)S(1)} collective-permute-done((f32[1,64]{1,0:T(1,128)S(1)}, f32[1,64]{1,0:T(1,128)S(1)}, u32[]{:S(2)}, u32[]{:S(2)}) %collective-permute-start.8) | collective-permute-done | bytes 288 | tf_op jit(solution)/shard_map/ppermute | solution.py:38
  34.7 0.5 %fusion.50 = f32[1,64]{1,0:T(1,128)} fusion(f32[1,64]{1,0:T(1,128)S(1)} %collective-permute-done.8, f32[2,64]{1,0:T(2,128)S(1)} %fusion.47, s32[]{:T(128)S(6)} %select_n.192), kind=kLoop, calls=%fused_computation.101 | loop fusion | flops 64 | bytes 772 | tf_op jit(solution)/shard_map/sqrt | solution.py:144
  (69 shorter events, 2.9 us)
Async XLA Ops:
  0.6 20.0 %copy-start = (bf16[4,4,128,128]{3,2,1,0:T(8,128)(2,1)S(1)}, bf16[4,4,128,128]{3,2,1,0:T(8,128)(2,1)}, u32[]{:S(2)}) copy-start(bf16[4,4,128,128]{3,2,1,0:T(8,128)(2,1)} %param.16) | copy-start | bytes 1572868
  0.6 0.8 %copy-start.1 = (f32[1024]{0:T(1024)S(1)}, f32[1024]{0:T(1024)}, u32[]{:S(2)}) copy-start(f32[1024]{0:T(1024)} %param.10) | copy-start | bytes 12292
  1.5 0.7 %copy-start.8 = (s32[1,128]{1,0:T(1,128)S(1)}, s32[1,128]{1,0:T(1,128)}, u32[]{:S(2)}) copy-start(s32[1,128]{1,0:T(1,128)} %param.17) | copy-start | bytes 1540
  2.1 0.9 %copy-start.3 = (f32[1024]{0:T(1024)S(1)}, f32[1024]{0:T(1024)}, u32[]{:S(2)}) copy-start(f32[1024]{0:T(1024)} %param.11) | copy-start | bytes 12292
  2.5 0.7 %copy-start.4 = (f32[1024]{0:T(1024)S(1)}, f32[1024]{0:T(1024)}, u32[]{:S(2)}) copy-start(f32[1024]{0:T(1024)} %param.12) | copy-start | bytes 12292
  2.5 0.7 %copy-start.5 = (f32[1024]{0:T(1024)S(1)}, f32[1024]{0:T(1024)}, u32[]{:S(2)}) copy-start(f32[1024]{0:T(1024)} %param.13) | copy-start | bytes 12292
  2.5 2.7 %collective-permute-start.1 = (f32[2,128]{1,0:T(2,128)S(1)}, f32[2,128]{1,0:T(2,128)S(1)}, u32[]{:S(2)}, u32[]{:S(2)}) collective-permute-start(f32[2,128]{1,0:T(2,128)S(1)} %bitcast.134), channel_id=1, source_target_pairs={{0,1},{1,0},{2,3},{3,2},{4,5},{5,4},{6,7},{7,6},{8,9},{9,8},{10,11... | collective-permute-start | bytes 3080 | tf_op jit(solution)/shard_map/ppermute | solution.py:80
  3.2 0.7 %copy-start.2 = (s32[4,4]{1,0:T(4,128)S(1)}, s32[4,4]{1,0:T(4,128)}, u32[]{:S(2)}) copy-start(s32[4,4]{1,0:T(4,128)} %param.15) | copy-start | bytes 196
  3.2 1.6 %copy-start.7 = (bf16[1,128,128]{2,1,0:T(8,128)(2,1)S(1)}, bf16[1,128,128]{2,1,0:T(8,128)(2,1)}, u32[]{:S(2)}) copy-start(bf16[1,128,128]{2,1,0:T(8,128)(2,1)} %param.18) | copy-start | bytes 98308
  3.3 15.3 %collective-permute-start = (f32[1024,3]{0,1:T(4,128)S(1)}, f32[1024,3]{0,1:T(4,128)S(1)}, u32[]{:S(2)}, u32[]{:S(2)}) collective-permute-start(f32[1024,3]{0,1:T(4,128)S(1)} %pad_maximum_fusion.1), channel_id=1, source_target_pairs={{0,1},{1,0},{2,3},{3,2},{4,5},{5,4},{6,7},{7,6},{8,9},{9,8},{10,11... | collective-permute-start | bytes 36872 | tf_op jit(solution)/shard_map/ppermute | solution.py:95
  4.0 0.7 %copy-start.6 = (s32[512]{0:T(512)S(1)}, s32[512]{0:T(512)}, u32[]{:S(2)}) copy-start(s32[512]{0:T(512)} %param.14) | copy-start | bytes 6148
  5.2 5.7 %collective-permute-start.2 = (bf16[1,4,128]{2,1,0:T(4,128)(2,1)S(1)}, bf16[1,4,128]{2,1,0:T(4,128)(2,1)S(1)}, u32[]{:S(2)}, u32[]{:S(2)}) collective-permute-start(bf16[1,4,128]{2,1,0:T(4,128)(2,1)S(1)} %pad_maximum_fusion.2), channel_id=1, source_target_pairs={{0,8},{2,10},{4,12},{6,14},{8,0},{10,2},{12,4},{14,6},{1,9},{3,11}... | collective-permute-start | bytes 3080 | tf_op jit(solution)/shard_map/ppermute | solution.py:20
  10.9 3.7 %collective-permute-start.3 = (bf16[2,4,128]{2,1,0:T(4,128)(2,1)S(1)}, bf16[2,4,128]{2,1,0:T(4,128)(2,1)S(1)}, u32[]{:S(2)}, u32[]{:S(2)}) collective-permute-start(bf16[2,4,128]{2,1,0:T(4,128)(2,1)S(1)} %maximum_select_fusion.3), channel_id=1, source_target_pairs={{0,4},{2,6},{4,0},{6,2},{8,12},{10,14},{12,8},{14,10},{1,5},{3,7},... | collective-permute-start | bytes 6152 | tf_op jit(solution)/shard_map/ppermute | solution.py:20
  14.6 3.7 %collective-permute-start.4 = (bf16[4,4,128]{2,1,0:T(4,128)(2,1)S(1)}, bf16[4,4,128]{2,1,0:T(4,128)(2,1)S(1)}, u32[]{:S(2)}, u32[]{:S(2)}) collective-permute-start(bf16[4,4,128]{2,1,0:T(4,128)(2,1)S(1)} %bitcast.116), channel_id=1, source_target_pairs={{0,2},{2,0},{4,6},{6,4},{8,10},{10,8},{12,14},{14,12},{1,3},{3,1},... | collective-permute-start | bytes 12296 | tf_op jit(solution)/shard_map/ppermute | solution.py:20
  21.8 4.5 %collective-permute-start.5 = (f32[8,64]{1,0:T(8,128)S(1)}, f32[8,64]{1,0:T(8,128)S(1)}, u32[]{:S(2)}, u32[]{:S(2)}) collective-permute-start(f32[8,64]{1,0:T(8,128)S(1)} %dynamic-slice_bitcast_fusion), channel_id=1, source_target_pairs={{0,8},{1,9},{2,10},{3,11},{4,12},{5,13},{6,14},{7,15},{8,0},{9,1},... | collective-permute-start | bytes 6152 | tf_op jit(solution)/shard_map/ppermute | solution.py:38
  26.3 3.6 %collective-permute-start.6 = (f32[4,64]{1,0:T(4,128)S(1)}, f32[4,64]{1,0:T(4,128)S(1)}, u32[]{:S(2)}, u32[]{:S(2)}) collective-permute-start(f32[4,64]{1,0:T(4,128)S(1)} %dynamic-slice_bitcast_fusion.1), channel_id=1, source_target_pairs={{0,4},{1,5},{2,6},{3,7},{4,0},{5,1},{6,2},{7,3},{8,12},{9,13},{10,... | collective-permute-start | bytes 3080 | tf_op jit(solution)/shard_map/ppermute | solution.py:38
  29.9 3.6 %collective-permute-start.7 = (f32[2,64]{1,0:T(2,128)S(1)}, f32[2,64]{1,0:T(2,128)S(1)}, u32[]{:S(2)}, u32[]{:S(2)}) collective-permute-start(f32[2,64]{1,0:T(2,128)S(1)} %fusion.48), channel_id=1, source_target_pairs={{0,2},{1,3},{2,0},{3,1},{4,6},{5,7},{6,4},{7,5},{8,10},{9,11},{10,... | collective-permute-start | bytes 1544 | tf_op jit(solution)/shard_map/ppermute | solution.py:38
  33.5 1.2 %collective-permute-start.8 = (f32[1,64]{1,0:T(1,128)S(1)}, f32[1,64]{1,0:T(1,128)S(1)}, u32[]{:S(2)}, u32[]{:S(2)}) collective-permute-start(f32[1,64]{1,0:T(1,128)S(1)} %constant_dynamic-slice_fusion), channel_id=1, source_target_pairs={{0,1},{1,0},{2,3},{3,2},{4,5},{5,4},{6,7},{7,6},{8,9},{9,8},{10,11... | collective-permute-start | bytes 776 | tf_op jit(solution)/shard_map/ppermute | solution.py:38

commit v17 on v16

--- a/solution.py
+++ b/solution.py
@@ -91,8 +91,12 @@
     packed = jnp.stack([w_first, w_second, first_idx.astype(jnp.float32), second_idx.astype(jnp.float32)])
     table = gather_doubling(packed.astype(jnp.bfloat16), ("blk",))
 
-    state_local = jnp.stack([base_real, base_reactive * base_reactive, voltage * rating], axis=1)
-    other_half = lax.ppermute(state_local, "state", [(j, (j + 1) % halves) for j in range(halves)])
+    state_local = jnp.stack(
+        [base_real, base_reactive * base_reactive, voltage * rating], axis=1
+    )
+    other_half = lax.ppermute(
+        state_local, "state", [(j, (j + 1) % halves) for j in range(halves)]
+    )
     state_pos = jnp.concatenate([state_local, other_half])
     mon_at = (monitored - me_state * half_len) % (halves * half_len)
     mon_vals = jnp.take(state_pos, mon_at, axis=0, mode="clip")
@@ -130,18 +134,17 @@
     matches = tile_ids[:, :, None] == block_iota[None, None, :]
     absent = jnp.logical_not(jnp.any(matches, axis=1))
     any_absent = jnp.any(absent, axis=1)
-    base_max = jnp.max(base_sq, axis=1)
-    absent_max = jnp.max(jnp.where(absent, base_max[:, None], neg), axis=0)
 
 
     col_max = jnp.max(squared, axis=2)
     worst_local = jnp.max(
         jnp.where(matches[:, :, :, None], col_max[:, :, None, :], neg), axis=(0, 1)
     )
+    base_max = jnp.max(base_sq, axis=1)
+    absent_max = jnp.max(jnp.where(absent, base_max[:, None], neg), axis=0)
     worst_local = jnp.maximum(worst_local, absent_max[:, None])
 
-    worst_sq = scatter_max(worst_local.reshape(blocks * halves, half_width), both)
-    worst_own = jnp.sqrt(worst_sq)[None, :]
+    worst_own = scatter_max(jnp.sqrt(worst_local).reshape(blocks * halves, half_width), both)[None, :]
     values_again, rows_again = lax.optimization_barrier((tile_values, chosen))
     peak_sq = jnp.max(slot_squares(values_again, rows_again), axis=(1, 3))
     peak_sq = jnp.maximum(peak_sq, jnp.where(any_absent[:, None], base_sq, neg))

time: 35.5 us -> 35.5 us (level)
    max x3 -> x4, other arithmetic: 0.01 us -> 0.53 us  [scatter_max(): cur = jnp.maximum(keep, got)]
    sqrt x1, other arithmetic: 0.52 us -> 0.08 us  [body(): jnp.sqrt(worst_local).reshape(blocks * halves, half_width)]
where the time goes in v17:
time: 35.5 us; the launch traced here: 35.3 us
  starting transfers between devices  15.8 us (45%)
  waiting for transfers between devices  9.79 us (28%)
  local copies, waits for them, and re-layouts  3.52 us (10%)
  other arithmetic  3.27 us (9%)
  matrix products  1.95 us (5%)
  between operations  0.89 us (3%)
    ppermute x3, starting transfers between devices, gather_doubling(): other = lax.ppermute(cur, axes, [(j, j ^ bit) for j in range(n)])  7.99 us
    ppermute x4, starting transfers between devices, scatter_max(): got = lax.ppermute(send, axes, [(j, j ^ bit) for j in range(n)])  6.78 us
    ppermute x3, waiting for transfers between devices, gather_doubling(): other = lax.ppermute(cur, axes, [(j, j ^ bit) for j in range(n)])  4.91 us
    ppermute x4, waiting for transfers between devices, scatter_max(): got = lax.ppermute(send, axes, [(j, j ^ bit) for j in range(n)])  4.88 us
    unnamed x18, local copies, waits for them, and re-layouts  1.65 us
    dot_general x2, matrix products, slot_squares(): jnp.einsum('tkmi,tkip->tkmp', values, weights, preferred_element_type=jnp...  1.11 us
    gather x1, local copies, waits for them, and re-layouts, body(): mon_vals = jnp.take(state_pos, mon_at, axis=0, mode='clip')  1.04 us
    squeeze x1, other arithmetic, body(): second_idx = outage_pairs[0, 1]  0.76 us
  transfers between devices with their start and end apart: 9, of which 7 were waited for; matrix products, arithmetic and copies ran while one was open for 6% of the time, Pallas kernels for 0%

profile of v17, /device:TPU:0, one launch (start us, length us, event | category | flops | bytes accessed | tf_op | source)
XLA Modules:
  0.0 35.3 jit_solution(11500964562604537589)
XLA Ops:
  0.7 0.8 %slice_bitcast_fusion.2 = (s32[128]{0:T(128)S(1)}, bf16[1,1,128]{2,1,0:T(2,128)(2,1)S(1)}, bf16[1,1,128]{2,1,0:T(2,128)(2,1)S(1)}, s32[128]{0:T(128)S(1)}) fusion(s32[1,2,128]{2,1,0:T(2,128)} %param.19), kind=kLoop, calls=%fused_computation.113 | loop fusion | flops 512 | bytes 2560 | tf_op jit(solution)/shard_map/squeeze | solution.py:66
  1.5 0.6 %copy-done.8 = s32[1,128]{1,0:T(1,128)S(1)} copy-done((s32[1,128]{1,0:T(1,128)S(1)}, s32[1,128]{1,0:T(1,128)}, u32[]{:S(2)}) %copy-start.8) | copy-done | bytes 536
  2.5 0.5 %collective-permute-start.1 = (f32[2,128]{1,0:T(2,128)S(1)}, f32[2,128]{1,0:T(2,128)S(1)}, u32[]{:S(2)}, u32[]{:S(2)}) collective-permute-start(f32[2,128]{1,0:T(2,128)S(1)} %bitcast.134), channel_id=1, source_target_pairs={{0,1},{1,0},{2,3},{3,2},{4,5},{5,4},{6,7},{7,6},{8,9},{9,8},{10,11... | collective-permute-start | bytes 3080 | tf_op jit(solution)/shard_map/ppermute | solution.py:80
  3.3 0.6 %collective-permute-start = (f32[1024,3]{0,1:T(4,128)S(1)}, f32[1024,3]{0,1:T(4,128)S(1)}, u32[]{:S(2)}, u32[]{:S(2)}) collective-permute-start(f32[1024,3]{0,1:T(4,128)S(1)} %pad_maximum_fusion.1), channel_id=1, source_target_pairs={{0,1},{1,0},{2,3},{3,2},{4,5},{5,4},{6,7},{7,6},{8,9},{9,8},{10,11... | collective-permute-start | bytes 36872 | tf_op jit(solution)/shard_map/ppermute | solution.py:97
  4.0 0.7 %copy-done.6 = s32[512]{0:T(512)S(1)} copy-done((s32[512]{0:T(512)S(1)}, s32[512]{0:T(512)}, u32[]{:S(2)}) %copy-start.6) | copy-done | bytes 2072
  5.2 4.1 %collective-permute-start.2 = (bf16[1,4,128]{2,1,0:T(4,128)(2,1)S(1)}, bf16[1,4,128]{2,1,0:T(4,128)(2,1)S(1)}, u32[]{:S(2)}, u32[]{:S(2)}) collective-permute-start(bf16[1,4,128]{2,1,0:T(4,128)(2,1)S(1)} %pad_maximum_fusion.2), channel_id=1, source_target_pairs={{0,8},{2,10},{4,12},{6,14},{8,0},{10,2},{12,4},{14,6},{1,9},{3,11}... | collective-permute-start | bytes 3080 | tf_op jit(solution)/shard_map/ppermute | solution.py:20
  9.4 1.5 %collective-permute-done.2 = bf16[1,4,128]{2,1,0:T(4,128)(2,1)S(1)} collective-permute-done((bf16[1,4,128]{2,1,0:T(4,128)(2,1)S(1)}, bf16[1,4,128]{2,1,0:T(4,128)(2,1)S(1)}, u32[]{:S(2)}, u32[]{:S(2)}) %collective-permute-start.2) | collective-permute-done | bytes 1056 | tf_op jit(solution)/shard_map/ppermute | solution.py:20
  10.9 2.0 %collective-permute-start.3 = (bf16[2,4,128]{2,1,0:T(4,128)(2,1)S(1)}, bf16[2,4,128]{2,1,0:T(4,128)(2,1)S(1)}, u32[]{:S(2)}, u32[]{:S(2)}) collective-permute-start(bf16[2,4,128]{2,1,0:T(4,128)(2,1)S(1)} %maximum_select_fusion.3), channel_id=1, source_target_pairs={{0,4},{2,6},{4,0},{6,2},{8,12},{10,14},{12,8},{14,10},{1,5},{3,7},... | collective-permute-start | bytes 6152 | tf_op jit(solution)/shard_map/ppermute | solution.py:20
  12.9 1.7 %collective-permute-done.3 = bf16[2,4,128]{2,1,0:T(4,128)(2,1)S(1)} collective-permute-done((bf16[2,4,128]{2,1,0:T(4,128)(2,1)S(1)}, bf16[2,4,128]{2,1,0:T(4,128)(2,1)S(1)}, u32[]{:S(2)}, u32[]{:S(2)}) %collective-permute-start.3) | collective-permute-done | bytes 2080 | tf_op jit(solution)/shard_map/ppermute | solution.py:20
  14.6 1.9 %collective-permute-start.4 = (bf16[4,4,128]{2,1,0:T(4,128)(2,1)S(1)}, bf16[4,4,128]{2,1,0:T(4,128)(2,1)S(1)}, u32[]{:S(2)}, u32[]{:S(2)}) collective-permute-start(bf16[4,4,128]{2,1,0:T(4,128)(2,1)S(1)} %bitcast.116), channel_id=1, source_target_pairs={{0,2},{2,0},{4,6},{6,4},{8,10},{10,8},{12,14},{14,12},{1,3},{3,1},... | collective-permute-start | bytes 12296 | tf_op jit(solution)/shard_map/ppermute | solution.py:20
  16.6 1.7 %collective-permute-done.4 = bf16[4,4,128]{2,1,0:T(4,128)(2,1)S(1)} collective-permute-done((bf16[4,4,128]{2,1,0:T(4,128)(2,1)S(1)}, bf16[4,4,128]{2,1,0:T(4,128)(2,1)S(1)}, u32[]{:S(2)}, u32[]{:S(2)}) %collective-permute-start.4) | collective-permute-done | bytes 4128 | tf_op jit(solution)/shard_map/ppermute | solution.py:20
  19.0 1.0 %gather_fusion = f32[512,3]{1,0:T(8,128)S(1)} fusion(f32[2048,3]{1,0:T(8,128)S(1)} %copy.43, s32[1024]{0:T(1024)S(1)} %pad_clamp_fusion), kind=kCustom, calls=%fused_computation | custom fusion | bytes 14336 | tf_op jit(solution)/shard_map/jit(_take)/gather | solution.py:102
  20.0 0.5 %multiply_reduce_fusion = (f32[512]{0:T(512)S(1)}, f32[512]{0:T(512)S(1)}, f32[512]{0:T(512)S(1)}, f32[512]{0:T(512)S(1)}) fusion(f32[512,3]{1,0:T(8,128)S(1)} %gather_fusion), kind=kLoop, calls=%fused_computation.39 | loop fusion | flops 2560 | bytes 14336 | tf_op jit(solution)/shard_map/mul | solution.py:107
  20.6 0.5 %fusion.8 = f32[4,4,128]{2,1,0:T(4,128)S(1)} fusion(bf16[4,4,128,128]{3,2,1,0:T(8,128)(2,1)S(1)} %copy-done, f32[4,128]{1,0:T(4,128)S(1)} %bitcast.122, f32[4,128]{1,0:T(4,128)S(1)} %bitcast.118, s32[4,4,128]{2,1,0:T(4,128)S(1)} %bitcast.129, s32[4,4,128]{2,1,0:T(4,128)S(1)} %bitcast.130, f32[4,128]{1,0:T(4,128)S(1)} %bitcast.120, ...), kind=kOutput, calls=%fused_computation.11 | convolution fusion | flops 70776832 | bytes 563216 | tf_op jit(solution)/shard_map/tkmi,tkip->tkmp/dot_general | solution.py:124
  21.8 3.0 %collective-permute-start.5 = (f32[8,64]{1,0:T(8,128)S(1)}, f32[8,64]{1,0:T(8,128)S(1)}, u32[]{:S(2)}, u32[]{:S(2)}) collective-permute-start(f32[8,64]{1,0:T(8,128)S(1)} %dynamic-slice_bitcast_fusion), channel_id=1, source_target_pairs={{0,8},{1,9},{2,10},{3,11},{4,12},{5,13},{6,14},{7,15},{8,0},{9,1},... | collective-permute-start | bytes 6152 | tf_op jit(solution)/shard_map/ppermute | solution.py:38
  24.8 1.5 %collective-permute-done.5 = f32[8,64]{1,0:T(8,128)S(1)} collective-permute-done((f32[8,64]{1,0:T(8,128)S(1)}, f32[8,64]{1,0:T(8,128)S(1)}, u32[]{:S(2)}, u32[]{:S(2)}) %collective-permute-start.5) | collective-permute-done | bytes 2080 | tf_op jit(solution)/shard_map/ppermute | solution.py:38
  26.3 1.9 %collective-permute-start.6 = (f32[4,64]{1,0:T(4,128)S(1)}, f32[4,64]{1,0:T(4,128)S(1)}, u32[]{:S(2)}, u32[]{:S(2)}) collective-permute-start(f32[4,64]{1,0:T(4,128)S(1)} %dynamic-slice_bitcast_fusion.1), channel_id=1, source_target_pairs={{0,4},{1,5},{2,6},{3,7},{4,0},{5,1},{6,2},{7,3},{8,12},{9,13},{10,... | collective-permute-start | bytes 3080 | tf_op jit(solution)/shard_map/ppermute | solution.py:38
  28.3 1.7 %collective-permute-done.6 = f32[4,64]{1,0:T(4,128)S(1)} collective-permute-done((f32[4,64]{1,0:T(4,128)S(1)}, f32[4,64]{1,0:T(4,128)S(1)}, u32[]{:S(2)}, u32[]{:S(2)}) %collective-permute-start.6) | collective-permute-done | bytes 1056 | tf_op jit(solution)/shard_map/ppermute | solution.py:38
  29.9 1.8 %collective-permute-start.7 = (f32[2,64]{1,0:T(2,128)S(1)}, f32[2,64]{1,0:T(2,128)S(1)}, u32[]{:S(2)}, u32[]{:S(2)}) collective-permute-start(f32[2,64]{1,0:T(2,128)S(1)} %fusion.48), channel_id=1, source_target_pairs={{0,2},{1,3},{2,0},{3,1},{4,6},{5,7},{6,4},{7,5},{8,10},{9,11},{10,... | collective-permute-start | bytes 1544 | tf_op jit(solution)/shard_map/ppermute | solution.py:38
  31.8 0.6 %fusion.9 = f32[4,128]{1,0:T(4,128)S(1)} fusion(bf16[4,4,128,128]{3,2,1,0:T(8,128)(2,1)S(1)} %copy-done, f32[4,128]{1,0:T(4,128)S(1)} %bitcast.123, f32[4,128]{1,0:T(4,128)S(1)} %bitcast.119, s32[4,4,128]{2,1,0:T(4,128)S(1)} %bitcast.128, s32[4,4,128]{2,1,0:T(4,128)S(1)} %bitcast.127, f32[4,128]{1,0:T(4,128)S(1)} %bitcast.121, ...), kind=kOutput, calls=%fused_computation.12 | convolution fusion | flops 70778368 | bytes 557072 | tf_op jit(solution)/shard_map/tkmi,tkip->tkmp/dot_general | solution.py:124
  32.3 1.2 %collective-permute-done.7 = f32[2,64]{1,0:T(2,128)S(1)} collective-permute-done((f32[2,64]{1,0:T(2,128)S(1)}, f32[2,64]{1,0:T(2,128)S(1)}, u32[]{:S(2)}, u32[]{:S(2)}) %collective-permute-start.7) | collective-permute-done | bytes 544 | tf_op jit(solution)/shard_map/ppermute | solution.py:38
  33.6 0.7 %fusion.45 = f32[512]{0:T(512)} fusion(f32[4,128]{1,0:T(4,128)S(1)} %fusion.9, f32[512]{0:T(512)S(1)} %get-tuple-element.6, pred[4]{0:T(512)(128)(4,1)S(1)} %not_reduce_fusion), kind=kLoop, calls=%fused_computation.83 | loop fusion | flops 1024 | bytes 6148 | tf_op jit(solution)/shard_map/sqrt | solution.py:151
  34.3 0.5 %collective-permute-done.8 = f32[1,64]{1,0:T(1,128)S(1)} collective-permute-done((f32[1,64]{1,0:T(1,128)S(1)}, f32[1,64]{1,0:T(1,128)S(1)}, u32[]{:S(2)}, u32[]{:S(2)}) %collective-permute-start.8) | collective-permute-done | bytes 288 | tf_op jit(solution)/shard_map/ppermute | solution.py:38
  34.7 0.5 %fusion.49 = f32[1,64]{1,0:T(1,128)} fusion(f32[1,64]{1,0:T(1,128)S(1)} %collective-permute-done.8, f32[2,64]{1,0:T(2,128)S(1)} %fusion.47, s32[]{:T(128)S(6)} %select_n.192), kind=kLoop, calls=%fused_computation.100 | loop fusion | flops 64 | bytes 772 | tf_op jit(solution)/shard_map/max | solution.py:39
  (69 shorter events, 2.9 us)
Async XLA Ops:
  0.6 20.0 %copy-start = (bf16[4,4,128,128]{3,2,1,0:T(8,128)(2,1)S(1)}, bf16[4,4,128,128]{3,2,1,0:T(8,128)(2,1)}, u32[]{:S(2)}) copy-start(bf16[4,4,128,128]{3,2,1,0:T(8,128)(2,1)} %param.16) | copy-start | bytes 1572868
  0.6 0.8 %copy-start.1 = (f32[1024]{0:T(1024)S(1)}, f32[1024]{0:T(1024)}, u32[]{:S(2)}) copy-start(f32[1024]{0:T(1024)} %param.10) | copy-start | bytes 12292
  1.5 0.7 %copy-start.8 = (s32[1,128]{1,0:T(1,128)S(1)}, s32[1,128]{1,0:T(1,128)}, u32[]{:S(2)}) copy-start(s32[1,128]{1,0:T(1,128)} %param.17) | copy-start | bytes 1540
  2.1 0.9 %copy-start.3 = (f32[1024]{0:T(1024)S(1)}, f32[1024]{0:T(1024)}, u32[]{:S(2)}) copy-start(f32[1024]{0:T(1024)} %param.11) | copy-start | bytes 12292
  2.5 0.7 %copy-start.4 = (f32[1024]{0:T(1024)S(1)}, f32[1024]{0:T(1024)}, u32[]{:S(2)}) copy-start(f32[1024]{0:T(1024)} %param.12) | copy-start | bytes 12292
  2.5 0.7 %copy-start.5 = (f32[1024]{0:T(1024)S(1)}, f32[1024]{0:T(1024)}, u32[]{:S(2)}) copy-start(f32[1024]{0:T(1024)} %param.13) | copy-start | bytes 12292
  2.5 2.7 %collective-permute-start.1 = (f32[2,128]{1,0:T(2,128)S(1)}, f32[2,128]{1,0:T(2,128)S(1)}, u32[]{:S(2)}, u32[]{:S(2)}) collective-permute-start(f32[2,128]{1,0:T(2,128)S(1)} %bitcast.134), channel_id=1, source_target_pairs={{0,1},{1,0},{2,3},{3,2},{4,5},{5,4},{6,7},{7,6},{8,9},{9,8},{10,11... | collective-permute-start | bytes 3080 | tf_op jit(solution)/shard_map/ppermute | solution.py:80
  3.2 0.7 %copy-start.2 = (s32[4,4]{1,0:T(4,128)S(1)}, s32[4,4]{1,0:T(4,128)}, u32[]{:S(2)}) copy-start(s32[4,4]{1,0:T(4,128)} %param.15) | copy-start | bytes 196
  3.2 1.6 %copy-start.7 = (bf16[1,128,128]{2,1,0:T(8,128)(2,1)S(1)}, bf16[1,128,128]{2,1,0:T(8,128)(2,1)}, u32[]{:S(2)}) copy-start(bf16[1,128,128]{2,1,0:T(8,128)(2,1)} %param.18) | copy-start | bytes 98308
  3.3 15.3 %collective-permute-start = (f32[1024,3]{0,1:T(4,128)S(1)}, f32[1024,3]{0,1:T(4,128)S(1)}, u32[]{:S(2)}, u32[]{:S(2)}) collective-permute-start(f32[1024,3]{0,1:T(4,128)S(1)} %pad_maximum_fusion.1), channel_id=1, source_target_pairs={{0,1},{1,0},{2,3},{3,2},{4,5},{5,4},{6,7},{7,6},{8,9},{9,8},{10,11... | collective-permute-start | bytes 36872 | tf_op jit(solution)/shard_map/ppermute | solution.py:97
  4.0 0.7 %copy-start.6 = (s32[512]{0:T(512)S(1)}, s32[512]{0:T(512)}, u32[]{:S(2)}) copy-start(s32[512]{0:T(512)} %param.14) | copy-start | bytes 6148
  5.2 5.7 %collective-permute-start.2 = (bf16[1,4,128]{2,1,0:T(4,128)(2,1)S(1)}, bf16[1,4,128]{2,1,0:T(4,128)(2,1)S(1)}, u32[]{:S(2)}, u32[]{:S(2)}) collective-permute-start(bf16[1,4,128]{2,1,0:T(4,128)(2,1)S(1)} %pad_maximum_fusion.2), channel_id=1, source_target_pairs={{0,8},{2,10},{4,12},{6,14},{8,0},{10,2},{12,4},{14,6},{1,9},{3,11}... | collective-permute-start | bytes 3080 | tf_op jit(solution)/shard_map/ppermute | solution.py:20
  10.9 3.7 %collective-permute-start.3 = (bf16[2,4,128]{2,1,0:T(4,128)(2,1)S(1)}, bf16[2,4,128]{2,1,0:T(4,128)(2,1)S(1)}, u32[]{:S(2)}, u32[]{:S(2)}) collective-permute-start(bf16[2,4,128]{2,1,0:T(4,128)(2,1)S(1)} %maximum_select_fusion.3), channel_id=1, source_target_pairs={{0,4},{2,6},{4,0},{6,2},{8,12},{10,14},{12,8},{14,10},{1,5},{3,7},... | collective-permute-start | bytes 6152 | tf_op jit(solution)/shard_map/ppermute | solution.py:20
  14.6 3.7 %collective-permute-start.4 = (bf16[4,4,128]{2,1,0:T(4,128)(2,1)S(1)}, bf16[4,4,128]{2,1,0:T(4,128)(2,1)S(1)}, u32[]{:S(2)}, u32[]{:S(2)}) collective-permute-start(bf16[4,4,128]{2,1,0:T(4,128)(2,1)S(1)} %bitcast.116), channel_id=1, source_target_pairs={{0,2},{2,0},{4,6},{6,4},{8,10},{10,8},{12,14},{14,12},{1,3},{3,1},... | collective-permute-start | bytes 12296 | tf_op jit(solution)/shard_map/ppermute | solution.py:20
  21.8 4.6 %collective-permute-start.5 = (f32[8,64]{1,0:T(8,128)S(1)}, f32[8,64]{1,0:T(8,128)S(1)}, u32[]{:S(2)}, u32[]{:S(2)}) collective-permute-start(f32[8,64]{1,0:T(8,128)S(1)} %dynamic-slice_bitcast_fusion), channel_id=1, source_target_pairs={{0,8},{1,9},{2,10},{3,11},{4,12},{5,13},{6,14},{7,15},{8,0},{9,1},... | collective-permute-start | bytes 6152 | tf_op jit(solution)/shard_map/ppermute | solution.py:38
  26.3 3.6 %collective-permute-start.6 = (f32[4,64]{1,0:T(4,128)S(1)}, f32[4,64]{1,0:T(4,128)S(1)}, u32[]{:S(2)}, u32[]{:S(2)}) collective-permute-start(f32[4,64]{1,0:T(4,128)S(1)} %dynamic-slice_bitcast_fusion.1), channel_id=1, source_target_pairs={{0,4},{1,5},{2,6},{3,7},{4,0},{5,1},{6,2},{7,3},{8,12},{9,13},{10,... | collective-permute-start | bytes 3080 | tf_op jit(solution)/shard_map/ppermute | solution.py:38
  29.9 3.6 %collective-permute-start.7 = (f32[2,64]{1,0:T(2,128)S(1)}, f32[2,64]{1,0:T(2,128)S(1)}, u32[]{:S(2)}, u32[]{:S(2)}) collective-permute-start(f32[2,64]{1,0:T(2,128)S(1)} %fusion.48), channel_id=1, source_target_pairs={{0,2},{1,3},{2,0},{3,1},{4,6},{5,7},{6,4},{7,5},{8,10},{9,11},{10,... | collective-permute-start | bytes 1544 | tf_op jit(solution)/shard_map/ppermute | solution.py:38
  33.5 1.2 %collective-permute-start.8 = (f32[1,64]{1,0:T(1,128)S(1)}, f32[1,64]{1,0:T(1,128)S(1)}, u32[]{:S(2)}, u32[]{:S(2)}) collective-permute-start(f32[1,64]{1,0:T(1,128)S(1)} %constant_dynamic-slice_fusion), channel_id=1, source_target_pairs={{0,1},{1,0},{2,3},{3,2},{4,5},{5,4},{6,7},{7,6},{8,9},{9,8},{10,11... | collective-permute-start | bytes 776 | tf_op jit(solution)/shard_map/ppermute | solution.py:38

commit v18 on v16

--- a/solution.py
+++ b/solution.py
@@ -16,13 +16,14 @@
     me = lax.axis_index(axes)
     cur = x[None]
     bit = n // 2
-    while bit >= 1:
+    while bit >= 2:
         other = lax.ppermute(cur, axes, [(j, j ^ bit) for j in range(n)])
         low = (me & bit) == 0
         cur = jnp.where(low, jnp.stack([cur, other], axis=1), jnp.stack([other, cur], axis=1))
         cur = cur.reshape((-1,) + x.shape)
         bit //= 2
-    return cur
+    other = lax.ppermute(cur, axes, [(j, j ^ 1) for j in range(n)])
+    return cur, other
 
 
 def scatter_max(x, axes):
@@ -89,7 +90,8 @@
     w_first = (flows[0] + coupled[0] * flows[1]) / determinant
     w_second = (flows[1] + coupled[1] * flows[0]) / determinant
     packed = jnp.stack([w_first, w_second, first_idx.astype(jnp.float32), second_idx.astype(jnp.float32)])
-    table = gather_doubling(packed.astype(jnp.bfloat16), ("blk",))
+    own_rows, other_rows = gather_doubling(packed.astype(jnp.bfloat16), ("blk",))
+    me_low = lax.axis_index("blk") % 2
 
     state_local = jnp.stack([base_real, base_reactive * base_reactive, voltage * rating], axis=1)
     other_half = lax.ppermute(state_local, "state", [(j, (j + 1) % halves) for j in range(halves)])
@@ -104,8 +106,14 @@
 
     valid = tile_ids >= 0
     block_of = jnp.clip(tile_ids, 0, blocks - 1)
-    pick_block = (block_of.reshape(-1, 1) == jnp.arange(blocks, dtype=jnp.int32)[None, :]).astype(jnp.bfloat16)
-    chosen = jnp.dot(pick_block, table.reshape(blocks, -1), preferred_element_type=jnp.float32)
+    row_iota = jnp.arange(blocks // 2, dtype=jnp.int32)[None, :]
+    at_row = block_of.reshape(-1, 1) // 2 == row_iota
+    mine_low = (block_of.reshape(-1, 1) % 2) == me_low
+    pick_own = (at_row & mine_low).astype(jnp.bfloat16)
+    pick_other = (at_row & jnp.logical_not(mine_low)).astype(jnp.bfloat16)
+    chosen = jnp.dot(pick_own, own_rows.reshape(blocks // 2, -1), preferred_element_type=jnp.float32) + jnp.dot(
+        pick_other, other_rows.reshape(blocks // 2, -1), preferred_element_type=jnp.float32
+    )
     chosen = chosen.astype(jnp.bfloat16).reshape(tiles_dev, slot_count, 4, pair_count)
     neg = jnp.float32(-jnp.inf)
 
@@ -130,14 +138,14 @@
     matches = tile_ids[:, :, None] == block_iota[None, None, :]
     absent = jnp.logical_not(jnp.any(matches, axis=1))
     any_absent = jnp.any(absent, axis=1)
-    base_max = jnp.max(base_sq, axis=1)
-    absent_max = jnp.max(jnp.where(absent, base_max[:, None], neg), axis=0)
 
 
     col_max = jnp.max(squared, axis=2)
     worst_local = jnp.max(
         jnp.where(matches[:, :, :, None], col_max[:, :, None, :], neg), axis=(0, 1)
     )
+    base_max = jnp.max(base_sq, axis=1)
+    absent_max = jnp.max(jnp.where(absent, base_max[:, None], neg), axis=0)
     worst_local = jnp.maximum(worst_local, absent_max[:, None])
 
     worst_sq = scatter_max(worst_local.reshape(blocks * halves, half_width), both)

time: 35.5 us -> 35.8 us (level)
  local copies, waits for them, and re-layouts: 3.52 us -> 4.07 us
  starting transfers between devices: 15.8 us -> 15.3 us
    ppermute x3 -> x2, starting transfers between devices: 7.99 us -> 5.63 us  [gather_doubling(): other = lax.ppermute(cur, axes, [(j, j ^ bit) for j in range(n)])]
    ppermute x0 -> x1, starting transfers between devices: none -> 1.89 us  [gather_doubling(): other = lax.ppermute(cur, axes, [(j, j ^ 1) for j in range(n)])]
    ppermute x3 -> x2, waiting for transfers between devices: 4.91 us -> 3.21 us  [gather_doubling(): other = lax.ppermute(cur, axes, [(j, j ^ bit) for j in range(n)])]
    ppermute x0 -> x1, waiting for transfers between devices: none -> 1.6 us  [gather_doubling(): other = lax.ppermute(cur, axes, [(j, j ^ 1) for j in range(n)])]
    unnamed x18, local copies, waits for them, and re-layouts: 1.65 us -> 2.21 us
  transfers between devices with their start and end apart: 9 -> 9, of which waited for: 7 -> 7; matrix products, arithmetic and copies ran while one was open for 6% -> 7% of each run, Pallas kernels for 0% -> 0%
where the time goes in v18:
time: 35.8 us; the launch traced here: 35.5 us
  starting transfers between devices  15.3 us (43%)
  waiting for transfers between devices  9.68 us (27%)
  local copies, waits for them, and re-layouts  4.07 us (11%)
  other arithmetic  3.29 us (9%)
  matrix products  2.14 us (6%)
  between operations  1.01 us (3%)
    ppermute x4, starting transfers between devices, scatter_max(): got = lax.ppermute(send, axes, [(j, j ^ bit) for j in range(n)])  6.72 us
    ppermute x2, starting transfers between devices, gather_doubling(): other = lax.ppermute(cur, axes, [(j, j ^ bit) for j in range(n)])  5.63 us
    ppermute x4, waiting for transfers between devices, scatter_max(): got = lax.ppermute(send, axes, [(j, j ^ bit) for j in range(n)])  4.87 us
    ppermute x2, waiting for transfers between devices, gather_doubling(): other = lax.ppermute(cur, axes, [(j, j ^ bit) for j in range(n)])  3.21 us
    unnamed x18, local copies, waits for them, and re-layouts  2.21 us
    ppermute x1, starting transfers between devices, gather_doubling(): other = lax.ppermute(cur, axes, [(j, j ^ 1) for j in range(n)])  1.89 us
    ppermute x1, waiting for transfers between devices, gather_doubling(): other = lax.ppermute(cur, axes, [(j, j ^ 1) for j in range(n)])  1.6 us
    dot_general x2, matrix products, slot_squares(): jnp.einsum('tkmi,tkip->tkmp', values, weights, preferred_element_type=jnp...  1.11 us
  transfers between devices with their start and end apart: 9, of which 7 were waited for; matrix products, arithmetic and copies ran while one was open for 7% of the time, Pallas kernels for 0%

profile of v18, /device:TPU:0, one launch (start us, length us, event | category | flops | bytes accessed | tf_op | source)
XLA Modules:
  0.0 35.5 jit_solution(1710808748550705318)
XLA Ops:
  0.7 0.8 %slice_bitcast_fusion.2 = (s32[128]{0:T(128)S(1)}, bf16[1,1,128]{2,1,0:T(2,128)(2,1)S(1)}, bf16[1,1,128]{2,1,0:T(2,128)(2,1)S(1)}, s32[128]{0:T(128)S(1)}) fusion(s32[1,2,128]{2,1,0:T(2,128)} %param.19), kind=kLoop, calls=%fused_computation.128 | loop fusion | flops 512 | bytes 2560 | tf_op jit(solution)/shard_map/squeeze | solution.py:67
  1.5 0.6 %copy-done.8 = s32[1,128]{1,0:T(1,128)S(1)} copy-done((s32[1,128]{1,0:T(1,128)S(1)}, s32[1,128]{1,0:T(1,128)}, u32[]{:S(2)}) %copy-start.8) | copy-done | bytes 536
  2.5 0.5 %collective-permute-start.1 = (f32[2,128]{1,0:T(2,128)S(1)}, f32[2,128]{1,0:T(2,128)S(1)}, u32[]{:S(2)}, u32[]{:S(2)}) collective-permute-start(f32[2,128]{1,0:T(2,128)S(1)} %bitcast.134), channel_id=1, source_target_pairs={{0,1},{1,0},{2,3},{3,2},{4,5},{5,4},{6,7},{7,6},{8,9},{9,8},{10,11... | collective-permute-start | bytes 3080 | tf_op jit(solution)/shard_map/ppermute | solution.py:81
  3.3 0.6 %collective-permute-start = (f32[1024,3]{0,1:T(4,128)S(1)}, f32[1024,3]{0,1:T(4,128)S(1)}, u32[]{:S(2)}, u32[]{:S(2)}) collective-permute-start(f32[1024,3]{0,1:T(4,128)S(1)} %pad_maximum_fusion.1), channel_id=1, source_target_pairs={{0,1},{1,0},{2,3},{3,2},{4,5},{5,4},{6,7},{7,6},{8,9},{9,8},{10,11... | collective-permute-start | bytes 36872 | tf_op jit(solution)/shard_map/ppermute | solution.py:97
  3.8 0.7 %copy-done.2 = s32[4,4]{1,0:T(4,128)S(1)} copy-done((s32[4,4]{1,0:T(4,128)S(1)}, s32[4,4]{1,0:T(4,128)}, u32[]{:S(2)}) %copy-start.2) | copy-done | bytes 88
  4.8 0.7 %copy-done.6 = s32[512]{0:T(512)S(1)} copy-done((s32[512]{0:T(512)S(1)}, s32[512]{0:T(512)}, u32[]{:S(2)}) %copy-start.6) | copy-done | bytes 2072
  6.0 3.7 %collective-permute-start.2 = (bf16[1,4,128]{2,1,0:T(4,128)(2,1)S(1)}, bf16[1,4,128]{2,1,0:T(4,128)(2,1)S(1)}, u32[]{:S(2)}, u32[]{:S(2)}) collective-permute-start(bf16[1,4,128]{2,1,0:T(4,128)(2,1)S(1)} %pad_maximum_fusion.2), channel_id=1, source_target_pairs={{0,8},{2,10},{4,12},{6,14},{8,0},{10,2},{12,4},{14,6},{1,9},{3,11}... | collective-permute-start | bytes 3080 | tf_op jit(solution)/shard_map/ppermute | solution.py:20
  9.7 1.5 %collective-permute-done.2 = bf16[1,4,128]{2,1,0:T(4,128)(2,1)S(1)} collective-permute-done((bf16[1,4,128]{2,1,0:T(4,128)(2,1)S(1)}, bf16[1,4,128]{2,1,0:T(4,128)(2,1)S(1)}, u32[]{:S(2)}, u32[]{:S(2)}) %collective-permute-start.2) | collective-permute-done | bytes 1056 | tf_op jit(solution)/shard_map/ppermute | solution.py:20
  11.3 2.0 %collective-permute-start.3 = (bf16[2,4,128]{2,1,0:T(4,128)(2,1)S(1)}, bf16[2,4,128]{2,1,0:T(4,128)(2,1)S(1)}, u32[]{:S(2)}, u32[]{:S(2)}) collective-permute-start(bf16[2,4,128]{2,1,0:T(4,128)(2,1)S(1)} %maximum_select_fusion.2), channel_id=1, source_target_pairs={{0,4},{2,6},{4,0},{6,2},{8,12},{10,14},{12,8},{14,10},{1,5},{3,7},... | collective-permute-start | bytes 6152 | tf_op jit(solution)/shard_map/ppermute | solution.py:20
  13.2 1.7 %collective-permute-done.3 = bf16[2,4,128]{2,1,0:T(4,128)(2,1)S(1)} collective-permute-done((bf16[2,4,128]{2,1,0:T(4,128)(2,1)S(1)}, bf16[2,4,128]{2,1,0:T(4,128)(2,1)S(1)}, u32[]{:S(2)}, u32[]{:S(2)}) %collective-permute-start.3) | collective-permute-done | bytes 2080 | tf_op jit(solution)/shard_map/ppermute | solution.py:20
  14.9 1.9 %collective-permute-start.4 = (bf16[4,4,128]{2,1,0:T(4,128)(2,1)S(1)}, bf16[4,4,128]{2,1,0:T(4,128)(2,1)S(1)}, u32[]{:S(2)}, u32[]{:S(2)}) collective-permute-start(bf16[4,4,128]{2,1,0:T(4,128)(2,1)S(1)} %bitcast.130), channel_id=1, source_target_pairs={{0,2},{2,0},{4,6},{6,4},{8,10},{10,8},{12,14},{14,12},{1,3},{3,1},... | collective-permute-start | bytes 12296 | tf_op jit(solution)/shard_map/ppermute | solution.py:25
  17.0 1.6 %collective-permute-done.4 = bf16[4,4,128]{2,1,0:T(4,128)(2,1)S(1)} collective-permute-done((bf16[4,4,128]{2,1,0:T(4,128)(2,1)S(1)}, bf16[4,4,128]{2,1,0:T(4,128)(2,1)S(1)}, u32[]{:S(2)}, u32[]{:S(2)}) %collective-permute-start.4) | collective-permute-done | bytes 4128 | tf_op jit(solution)/shard_map/ppermute | solution.py:25
  19.3 1.0 %gather_fusion = f32[512,3]{1,0:T(8,128)S(1)} fusion(f32[2048,3]{1,0:T(8,128)S(1)} %copy.31, s32[1024]{0:T(1024)S(1)} %pad_clamp_fusion), kind=kCustom, calls=%fused_computation | custom fusion | bytes 14336 | tf_op jit(solution)/shard_map/jit(_take)/gather | solution.py:100
  20.3 0.5 %multiply_reduce_fusion = (f32[512]{0:T(512)S(1)}, f32[512]{0:T(512)S(1)}, f32[512]{0:T(512)S(1)}, f32[512]{0:T(512)S(1)}) fusion(f32[512,3]{1,0:T(8,128)S(1)} %gather_fusion), kind=kLoop, calls=%fused_computation.40 | loop fusion | flops 2560 | bytes 14336 | tf_op jit(solution)/shard_map/mul | solution.py:105
  21.0 0.5 %fusion.8 = f32[4,4,128]{2,1,0:T(4,128)S(1)} fusion(bf16[4,4,128,128]{3,2,1,0:T(8,128)(2,1)S(1)} %copy-done, f32[4,128]{1,0:T(4,128)S(1)} %bitcast.122, f32[4,128]{1,0:T(4,128)S(1)} %bitcast.118, s32[4,4,128]{2,1,0:T(4,128)S(1)} %bitcast.128, s32[4,4,128]{2,1,0:T(4,128)S(1)} %bitcast.129, f32[4,128]{1,0:T(4,128)S(1)} %bitcast.120, ...), kind=kOutput, calls=%fused_computation.11 | convolution fusion | flops 70776832 | bytes 563216 | tf_op jit(solution)/shard_map/tkmi,tkip->tkmp/dot_general | solution.py:128
  22.1 2.9 %collective-permute-start.5 = (f32[8,64]{1,0:T(8,128)S(1)}, f32[8,64]{1,0:T(8,128)S(1)}, u32[]{:S(2)}, u32[]{:S(2)}) collective-permute-start(f32[8,64]{1,0:T(8,128)S(1)} %dynamic-slice_bitcast_fusion), channel_id=1, source_target_pairs={{0,8},{1,9},{2,10},{3,11},{4,12},{5,13},{6,14},{7,15},{8,0},{9,1},... | collective-permute-start | bytes 6152 | tf_op jit(solution)/shard_map/ppermute | solution.py:39
  25.0 1.5 %collective-permute-done.5 = f32[8,64]{1,0:T(8,128)S(1)} collective-permute-done((f32[8,64]{1,0:T(8,128)S(1)}, f32[8,64]{1,0:T(8,128)S(1)}, u32[]{:S(2)}, u32[]{:S(2)}) %collective-permute-start.5) | collective-permute-done | bytes 2080 | tf_op jit(solution)/shard_map/ppermute | solution.py:39
  26.6 1.9 %collective-permute-start.6 = (f32[4,64]{1,0:T(4,128)S(1)}, f32[4,64]{1,0:T(4,128)S(1)}, u32[]{:S(2)}, u32[]{:S(2)}) collective-permute-start(f32[4,64]{1,0:T(4,128)S(1)} %dynamic-slice_bitcast_fusion.1), channel_id=1, source_target_pairs={{0,4},{1,5},{2,6},{3,7},{4,0},{5,1},{6,2},{7,3},{8,12},{9,13},{10,... | collective-permute-start | bytes 3080 | tf_op jit(solution)/shard_map/ppermute | solution.py:39
  28.5 1.7 %collective-permute-done.6 = f32[4,64]{1,0:T(4,128)S(1)} collective-permute-done((f32[4,64]{1,0:T(4,128)S(1)}, f32[4,64]{1,0:T(4,128)S(1)}, u32[]{:S(2)}, u32[]{:S(2)}) %collective-permute-start.6) | collective-permute-done | bytes 1056 | tf_op jit(solution)/shard_map/ppermute | solution.py:39
  30.2 1.8 %collective-permute-start.7 = (f32[2,64]{1,0:T(2,128)S(1)}, f32[2,64]{1,0:T(2,128)S(1)}, u32[]{:S(2)}, u32[]{:S(2)}) collective-permute-start(f32[2,64]{1,0:T(2,128)S(1)} %fusion.59), channel_id=1, source_target_pairs={{0,2},{1,3},{2,0},{3,1},{4,6},{5,7},{6,4},{7,5},{8,10},{9,11},{10,... | collective-permute-start | bytes 1544 | tf_op jit(solution)/shard_map/ppermute | solution.py:39
  32.0 0.6 %fusion.9 = f32[4,128]{1,0:T(4,128)S(1)} fusion(bf16[4,4,128,128]{3,2,1,0:T(8,128)(2,1)S(1)} %copy-done, f32[4,128]{1,0:T(4,128)S(1)} %bitcast.123, f32[4,128]{1,0:T(4,128)S(1)} %bitcast.119, s32[4,4,128]{2,1,0:T(4,128)S(1)} %bitcast.127, s32[4,4,128]{2,1,0:T(4,128)S(1)} %bitcast.126, f32[4,128]{1,0:T(4,128)S(1)} %bitcast.121, ...), kind=kOutput, calls=%fused_computation.12 | convolution fusion | flops 70778368 | bytes 557072 | tf_op jit(solution)/shard_map/tkmi,tkip->tkmp/dot_general | solution.py:128
  32.6 1.2 %collective-permute-done.7 = f32[2,64]{1,0:T(2,128)S(1)} collective-permute-done((f32[2,64]{1,0:T(2,128)S(1)}, f32[2,64]{1,0:T(2,128)S(1)}, u32[]{:S(2)}, u32[]{:S(2)}) %collective-permute-start.7) | collective-permute-done | bytes 544 | tf_op jit(solution)/shard_map/ppermute | solution.py:39
  33.9 0.7 %fusion.56 = f32[512]{0:T(512)} fusion(f32[4,128]{1,0:T(4,128)S(1)} %fusion.9, f32[512]{0:T(512)S(1)} %get-tuple-element.6, pred[4]{0:T(512)(128)(4,1)S(1)} %not_reduce_fusion), kind=kLoop, calls=%fused_computation.91 | loop fusion | flops 1024 | bytes 6148 | tf_op jit(solution)/shard_map/sqrt | solution.py:156
  35.0 0.5 %fusion.62 = f32[1,64]{1,0:T(1,128)} fusion(f32[1,64]{1,0:T(1,128)S(1)} %collective-permute-done.8, f32[2,64]{1,0:T(2,128)S(1)} %fusion.58, s32[]{:T(128)S(6)} %select_n.202), kind=kLoop, calls=%fused_computation.115 | loop fusion | flops 64 | bytes 772 | tf_op jit(solution)/shard_map/sqrt | solution.py:152
  (70 shorter events, 3.5 us)
Async XLA Ops:
  0.6 20.3 %copy-start = (bf16[4,4,128,128]{3,2,1,0:T(8,128)(2,1)S(1)}, bf16[4,4,128,128]{3,2,1,0:T(8,128)(2,1)}, u32[]{:S(2)}) copy-start(bf16[4,4,128,128]{3,2,1,0:T(8,128)(2,1)} %param.16) | copy-start | bytes 1572868
  0.6 0.8 %copy-start.1 = (f32[1024]{0:T(1024)S(1)}, f32[1024]{0:T(1024)}, u32[]{:S(2)}) copy-start(f32[1024]{0:T(1024)} %param.10) | copy-start | bytes 12292
  1.5 0.7 %copy-start.8 = (s32[1,128]{1,0:T(1,128)S(1)}, s32[1,128]{1,0:T(1,128)}, u32[]{:S(2)}) copy-start(s32[1,128]{1,0:T(1,128)} %param.17) | copy-start | bytes 1540
  2.1 0.9 %copy-start.3 = (f32[1024]{0:T(1024)S(1)}, f32[1024]{0:T(1024)}, u32[]{:S(2)}) copy-start(f32[1024]{0:T(1024)} %param.11) | copy-start | bytes 12292
  2.5 0.7 %copy-start.4 = (f32[1024]{0:T(1024)S(1)}, f32[1024]{0:T(1024)}, u32[]{:S(2)}) copy-start(f32[1024]{0:T(1024)} %param.12) | copy-start | bytes 12292
  2.5 0.7 %copy-start.5 = (f32[1024]{0:T(1024)S(1)}, f32[1024]{0:T(1024)}, u32[]{:S(2)}) copy-start(f32[1024]{0:T(1024)} %param.13) | copy-start | bytes 12292
  2.5 3.5 %collective-permute-start.1 = (f32[2,128]{1,0:T(2,128)S(1)}, f32[2,128]{1,0:T(2,128)S(1)}, u32[]{:S(2)}, u32[]{:S(2)}) collective-permute-start(f32[2,128]{1,0:T(2,128)S(1)} %bitcast.134), channel_id=1, source_target_pairs={{0,1},{1,0},{2,3},{3,2},{4,5},{5,4},{6,7},{7,6},{8,9},{9,8},{10,11... | collective-permute-start | bytes 3080 | tf_op jit(solution)/shard_map/ppermute | solution.py:81
  3.3 15.6 %collective-permute-start = (f32[1024,3]{0,1:T(4,128)S(1)}, f32[1024,3]{0,1:T(4,128)S(1)}, u32[]{:S(2)}, u32[]{:S(2)}) collective-permute-start(f32[1024,3]{0,1:T(4,128)S(1)} %pad_maximum_fusion.1), channel_id=1, source_target_pairs={{0,1},{1,0},{2,3},{3,2},{4,5},{5,4},{6,7},{7,6},{8,9},{9,8},{10,11... | collective-permute-start | bytes 36872 | tf_op jit(solution)/shard_map/ppermute | solution.py:97
  3.8 0.7 %copy-start.2 = (s32[4,4]{1,0:T(4,128)S(1)}, s32[4,4]{1,0:T(4,128)}, u32[]{:S(2)}) copy-start(s32[4,4]{1,0:T(4,128)} %param.15) | copy-start | bytes 196
  4.7 1.0 %copy-start.7 = (bf16[1,128,128]{2,1,0:T(8,128)(2,1)S(1)}, bf16[1,128,128]{2,1,0:T(8,128)(2,1)}, u32[]{:S(2)}) copy-start(bf16[1,128,128]{2,1,0:T(8,128)(2,1)} %param.18) | copy-start | bytes 98308
  4.8 0.7 %copy-start.6 = (s32[512]{0:T(512)S(1)}, s32[512]{0:T(512)}, u32[]{:S(2)}) copy-start(s32[512]{0:T(512)} %param.14) | copy-start | bytes 6148
  6.0 5.2 %collective-permute-start.2 = (bf16[1,4,128]{2,1,0:T(4,128)(2,1)S(1)}, bf16[1,4,128]{2,1,0:T(4,128)(2,1)S(1)}, u32[]{:S(2)}, u32[]{:S(2)}) collective-permute-start(bf16[1,4,128]{2,1,0:T(4,128)(2,1)S(1)} %pad_maximum_fusion.2), channel_id=1, source_target_pairs={{0,8},{2,10},{4,12},{6,14},{8,0},{10,2},{12,4},{14,6},{1,9},{3,11}... | collective-permute-start | bytes 3080 | tf_op jit(solution)/shard_map/ppermute | solution.py:20
  11.3 3.7 %collective-permute-start.3 = (bf16[2,4,128]{2,1,0:T(4,128)(2,1)S(1)}, bf16[2,4,128]{2,1,0:T(4,128)(2,1)S(1)}, u32[]{:S(2)}, u32[]{:S(2)}) collective-permute-start(bf16[2,4,128]{2,1,0:T(4,128)(2,1)S(1)} %maximum_select_fusion.2), channel_id=1, source_target_pairs={{0,4},{2,6},{4,0},{6,2},{8,12},{10,14},{12,8},{14,10},{1,5},{3,7},... | collective-permute-start | bytes 6152 | tf_op jit(solution)/shard_map/ppermute | solution.py:20
  14.9 3.7 %collective-permute-start.4 = (bf16[4,4,128]{2,1,0:T(4,128)(2,1)S(1)}, bf16[4,4,128]{2,1,0:T(4,128)(2,1)S(1)}, u32[]{:S(2)}, u32[]{:S(2)}) collective-permute-start(bf16[4,4,128]{2,1,0:T(4,128)(2,1)S(1)} %bitcast.130), channel_id=1, source_target_pairs={{0,2},{2,0},{4,6},{6,4},{8,10},{10,8},{12,14},{14,12},{1,3},{3,1},... | collective-permute-start | bytes 12296 | tf_op jit(solution)/shard_map/ppermute | solution.py:25
  22.1 4.5 %collective-permute-start.5 = (f32[8,64]{1,0:T(8,128)S(1)}, f32[8,64]{1,0:T(8,128)S(1)}, u32[]{:S(2)}, u32[]{:S(2)}) collective-permute-start(f32[8,64]{1,0:T(8,128)S(1)} %dynamic-slice_bitcast_fusion), channel_id=1, source_target_pairs={{0,8},{1,9},{2,10},{3,11},{4,12},{5,13},{6,14},{7,15},{8,0},{9,1},... | collective-permute-start | bytes 6152 | tf_op jit(solution)/shard_map/ppermute | solution.py:39
  26.6 3.6 %collective-permute-start.6 = (f32[4,64]{1,0:T(4,128)S(1)}, f32[4,64]{1,0:T(4,128)S(1)}, u32[]{:S(2)}, u32[]{:S(2)}) collective-permute-start(f32[4,64]{1,0:T(4,128)S(1)} %dynamic-slice_bitcast_fusion.1), channel_id=1, source_target_pairs={{0,4},{1,5},{2,6},{3,7},{4,0},{5,1},{6,2},{7,3},{8,12},{9,13},{10,... | collective-permute-start | bytes 3080 | tf_op jit(solution)/shard_map/ppermute | solution.py:39
  30.2 3.6 %collective-permute-start.7 = (f32[2,64]{1,0:T(2,128)S(1)}, f32[2,64]{1,0:T(2,128)S(1)}, u32[]{:S(2)}, u32[]{:S(2)}) collective-permute-start(f32[2,64]{1,0:T(2,128)S(1)} %fusion.59), channel_id=1, source_target_pairs={{0,2},{1,3},{2,0},{3,1},{4,6},{5,7},{6,4},{7,5},{8,10},{9,11},{10,... | collective-permute-start | bytes 1544 | tf_op jit(solution)/shard_map/ppermute | solution.py:39
  33.8 1.2 %collective-permute-start.8 = (f32[1,64]{1,0:T(1,128)S(1)}, f32[1,64]{1,0:T(1,128)S(1)}, u32[]{:S(2)}, u32[]{:S(2)}) collective-permute-start(f32[1,64]{1,0:T(1,128)S(1)} %constant_dynamic-slice_fusion), channel_id=1, source_target_pairs={{0,1},{1,0},{2,3},{3,2},{4,5},{5,4},{6,7},{7,6},{8,9},{9,8},{10,11... | collective-permute-start | bytes 776 | tf_op jit(solution)/shard_map/ppermute | solution.py:39
